TPU v7x, 32 devices: a whole 2x2x4 slice. The times are simulated.
32 devices in a mesh: seq: 8 (over y, x, core), head: 4 (over z).
Axes of the slice: x: 2, y: 2, z: 4, core: 2. Of those that a mesh axis runs over, the one named last changes fastest.
Arguments:
- query_rows: bfloat16 [1024, 2304], P(('seq', 'head')), may hold values from -6 to 6
- key_rows: bfloat16 [1024, 2304], P(('seq', 'head')), may hold values from -6 to 6
- value_rows: bfloat16 [1024, 2304], P(('seq', 'head')), may hold values from -6 to 6
- residual_in: bfloat16 [1024, 2304], P(('seq', 'head')), may hold values from -40 to 40
- norm_gain: float32 [2304], replicated, may hold values from 0.1 to 1.9
- router_weight: bfloat16 [2304, 8], replicated, may hold values from -0.125 to 0.125
- segment_ids: int32 [1024], P('seq'), may hold values from 0 to 3, never falling along the last dimension, each value on 1 to 897 neighbouring positions
- expert_ids: int32 [1024, 2], P(('seq', 'head')), may hold values from 0 to 7, all different within a row; in each aligned block of 32 rows (0 to 31, 32 to 63, ...) at most 9 rows name the same one
- gate_weight: bfloat16 [2304, 23040], P(None, ('seq', 'head')), may hold values from -0.125 to 0.125
- up_weight: bfloat16 [2304, 23040], P(None, ('seq', 'head')), may hold values from -0.125 to 0.125
- down_weight: bfloat16 [2304, 23040], P(None, ('seq', 'head')), may hold values from -0.109375 to 0.109375
- out_weight: bfloat16 [2304, 2304], P('head'), may hold values from -0.125 to 0.125
Outputs:
- residual_out: bfloat16 [1024, 2304], P(('seq', 'head'))
- key_cache: bfloat16 [1024, 2304], P('seq', 'head')
- value_cache: bfloat16 [1024, 2304], P('seq', 'head')
Inputs may be any that keep to these rules, and one draw needn't show every extreme that they name: `segment_ids`: each segment covers at most 897 tokens. `expert_ids`: in the rows of one device no expert is named more than 9 times.
All inputs are finite; a program needn't handle non-finite values.
Results may differ from a plain program's by a relative error of at most 0.005.
Values may be sent and summed in bfloat16 or wider, within the bound.
No kernel may reach another device: no remote copies, remote signals or barrier semaphores. Data moves between devices by JAX's collectives and lax.ppermute only.
A program may use at most 128 MiB of HBM per device.

v0:
```python
import math

import jax
import jax.numpy as jnp
from jax import lax
from jax.sharding import PartitionSpec as P

D = 2304
HDIM = 64
LEVELS = 4
CAP = 9


residual_scale = 1.4 / math.sqrt(40.0)
norm_epsilon = 1e-05


def passed_along(value, axis, by):
    length = lax.axis_size(axis)
    pairs = [(i, i + by) for i in range(length) if 0 <= i + by < length]
    return lax.ppermute(value, axis, pairs)


def score_piece(queries, key_piece, piece_allowed):
    raw_scores = jnp.einsum(
        "qhd,khd->hqk", queries, key_piece, preferred_element_type=jnp.float32
    ) * queries.shape[2] ** (-0.5)
    return jnp.where(piece_allowed[None], raw_scores, -jnp.inf)


def mix_piece(rounded_piece, value_piece):
    return jnp.einsum(
        "hqk,khd->qhd", rounded_piece, value_piece, preferred_element_type=jnp.float32
    )


def per_device(
    query_rows,
    key_rows,
    value_rows,
    residual_in,
    norm_gain,
    router_weight,
    segment_ids,
    expert_ids,
    gate_weight,
    up_weight,
    down_weight,
    out_weight,
):
    head_count = lax.axis_size("head")
    seq_count = lax.axis_size("seq")
    tok_local = query_rows.shape[0]
    group_width = query_rows.shape[1] // head_count
    heads_here = group_width // HDIM
    stretch_len = tok_local * head_count
    span_count = min(2**LEVELS * 32 // tok_local, seq_count)
    gate_full, up_full, down_full = (
        lax.all_gather(gate_weight, "head", axis=1, tiled=True),
        lax.all_gather(up_weight, "head", axis=1, tiled=True),
        lax.all_gather(down_weight, "head", axis=1, tiled=True),
    )
    expert_count = router_weight.shape[1]
    replicas = seq_count // expert_count
    seq_place = lax.axis_index("seq")
    query_head, key_head, value_head = (
        lax.all_to_all(
            query_rows.reshape(tok_local, head_count, group_width),
            "head",
            split_axis=1,
            concat_axis=0,
            tiled=True,
        ),
        lax.all_to_all(
            key_rows.reshape(tok_local, head_count, group_width),
            "head",
            split_axis=1,
            concat_axis=0,
            tiled=True,
        ),
        lax.all_to_all(
            value_rows.reshape(tok_local, head_count, group_width),
            "head",
            split_axis=1,
            concat_axis=0,
            tiled=True,
        ),
    )
    query_head = query_head.reshape(stretch_len, group_width)
    key_head = key_head.reshape(stretch_len, group_width)
    value_head = value_head.reshape(stretch_len, group_width)
    front_rows = (span_count - 1) * stretch_len
    key_window = jnp.concatenate((jnp.zeros((front_rows, group_width), jnp.bfloat16), key_head), 0)
    value_window = jnp.concatenate(
        (jnp.zeros((front_rows, group_width), jnp.bfloat16), value_head), 0
    )
    segment_window = jnp.concatenate((jnp.zeros((front_rows,), jnp.int32), segment_ids), 0)

    def advance(step_index, carried):
        moving, keys_held, values_held, segments_held = carried
        moving = passed_along((moving[0], moving[1], moving[2]), "seq", 1)
        write_place = (span_count - 1 - step_index) * stretch_len
        keys_held = lax.dynamic_update_slice_in_dim(keys_held, moving[0], write_place, 0)
        values_held = lax.dynamic_update_slice_in_dim(values_held, moving[1], write_place, 0)
        segments_held = lax.dynamic_update_slice_in_dim(segments_held, moving[2], write_place, 0)
        return (moving, keys_held, values_held, segments_held)

    moving_final, key_window, value_window, segment_window = lax.fori_loop(
        1,
        span_count,
        advance,
        ((key_head, value_head, segment_ids), key_window, value_window, segment_window),
    )
    key_total = span_count * stretch_len
    query_place = seq_place * stretch_len + jnp.arange(stretch_len, dtype=jnp.int32)
    key_place = (seq_place - span_count + 1) * stretch_len + jnp.arange(key_total, dtype=jnp.int32)
    allowed = (
        (segment_window[None, :] == segment_ids[:, None])
        & (key_place[None, :] <= query_place[:, None])
        & (key_place[None, :] >= 0)
    )
    queries = query_head.reshape(stretch_len, heads_here, HDIM)
    keys_all = key_window.reshape(key_total, heads_here, HDIM)
    values_all = value_window.reshape(key_total, heads_here, HDIM)
    masked = score_piece(queries, keys_all, allowed)
    row_max = jnp.max(masked, -1, keepdims=True)
    weights = jnp.where(allowed[None], jnp.exp(masked - row_max), 0.0)
    totals = jnp.sum(weights, -1)
    mixture = mix_piece(weights.astype(jnp.bfloat16), values_all)
    attention = (
        (mixture / jnp.transpose(totals)[:, :, None])
        .astype(jnp.bfloat16)
        .reshape(stretch_len, group_width)
    )
    attended_sum = lax.psum_scatter(
        jnp.dot(attention, out_weight, preferred_element_type=jnp.float32).astype(jnp.bfloat16),
        "head",
        scatter_dimension=0,
        tiled=True,
    ).astype(jnp.float32)
    middle = (residual_in.astype(jnp.float32) + residual_scale * attended_sum).astype(jnp.bfloat16)
    middle_wide = middle.astype(jnp.float32)
    mean_square = jnp.mean(middle_wide * middle_wide, -1, keepdims=True)
    normed = (middle_wide * lax.rsqrt(mean_square + norm_epsilon) * norm_gain).astype(jnp.bfloat16)
    route_count = expert_ids.shape[1]
    logits = jnp.dot(normed, router_weight, preferred_element_type=jnp.float32)
    route_hot = expert_ids[:, :, None] == jnp.arange(expert_count, dtype=jnp.int32)[None, None, :]
    chosen = jnp.sum(jnp.where(route_hot, logits[:, None, :], 0.0), -1)
    first_weight = 1.0 / (1.0 + jnp.exp(chosen[:, 1] - chosen[:, 0]))
    second_weight = 1.0 / (1.0 + jnp.exp(chosen[:, 0] - chosen[:, 1]))
    flat_hot = route_hot.reshape(tok_local * route_count, expert_count).astype(jnp.int32)
    before_count = jnp.cumsum(flat_hot, 0) - flat_hot
    route_rank = jnp.sum(before_count * flat_hot, -1)
    slot_ids = (expert_ids.reshape(-1) * CAP + route_rank).reshape(tok_local, route_count)
    slot_total = expert_count * CAP
    dispatch = jnp.any(
        slot_ids[None, :, :] == jnp.arange(slot_total, dtype=jnp.int32)[:, None, None], -1
    ).astype(jnp.bfloat16)
    packed = (
        jnp.dot(dispatch, normed, preferred_element_type=jnp.float32)
        .astype(jnp.bfloat16)
        .reshape(expert_count, CAP, D)
    )
    outgoing = jnp.broadcast_to(packed[:, None], (expert_count, replicas, CAP, D)).reshape(
        seq_count, CAP, D
    )
    arrived = lax.all_to_all(outgoing, "seq", split_axis=0, concat_axis=0, tiled=True)
    slot_count = arrived.shape[1]
    flat_rows = arrived.reshape(seq_count * slot_count, D)
    gate_act = jnp.dot(flat_rows, gate_full, preferred_element_type=jnp.float32)
    up_act = jnp.dot(flat_rows, up_full, preferred_element_type=jnp.float32)
    hidden = (jax.nn.silu(gate_act) * up_act).astype(jnp.bfloat16)
    shard_out = lax.dot_general(
        hidden, down_full, (((1,), (1,)), ((), ())), preferred_element_type=jnp.float32
    ).astype(jnp.bfloat16)
    returned = lax.all_to_all(
        shard_out.reshape(seq_count, slot_count, D), "seq", split_axis=0, concat_axis=0, tiled=True
    )
    expert_out = jnp.sum(
        returned.reshape(expert_count, replicas, CAP, D).astype(jnp.float32), 1
    ).reshape(slot_total, D)
    first_rows = expert_out[slot_ids[:, 0]]
    second_rows = expert_out[slot_ids[:, 1]]
    moe_sum = first_weight[:, None] * first_rows + second_weight[:, None] * second_rows
    residual_out = (middle_wide + residual_scale * moe_sum).astype(jnp.bfloat16)
    return (residual_out, key_head, value_head)


def solution(mesh):
    return jax.shard_map(
        per_device,
        mesh=mesh,
        in_specs=(
            P(("seq", "head"), None),
            P(("seq", "head"), None),
            P(("seq", "head"), None),
            P(("seq", "head"), None),
            P(),
            P(),
            P("seq"),
            P(("seq", "head"), None),
            P(None, ("seq", "head")),
            P(None, ("seq", "head")),
            P(None, ("seq", "head")),
            P("head", None),
        ),
        out_specs=(P(("seq", "head"), None), P("seq", "head"), P("seq", "head")),
        check_vma=False,
    )
```

profile of v0, /device:TPU:0, one launch (start us, length us, event | category | flops | bytes accessed | tf_op | source)
XLA Modules:
  0.0 894.4 jit_solution(14546956432762249407)
XLA Ops:
  7.2 1.3 reshape.156
  9.1 6.3 all-to-all-start
  16.1 1.1 reshape.158
  17.9 1.1 reshape.162
  19.8 2.1 all-to-all-done
  21.9 3.3 all-to-all-start.1
  25.9 1.2 concatenate.9
  27.1 4.1 all-to-all-done.1
  31.2 3.3 all-to-all-start.2
  34.6 1.2 concatenate.10
  36.5 88.6 %while.23 = (s32[]{:T(128)}, bf16[128,576]{1,0:T(8,128)(2,1)}, bf16[128,576]{1,0:T(8,128)(2,1)}, s32[128]{0:T(128)S(1)}, bf16[1024,576]{1,0:T(8,128)(2,1)}, /*in...) while((s32[]{:T(128)}, bf16[128,576]{1,0:T(8,128)(2,1)}, ...), condition=%wide.region_1.0_spmd, body=%wide.region_0.0_spmd.sunk | while | flops 7 | bytes 2396467 | solution.py:108
  36.5 1.3 collective-permute-start
  37.8 4.1 collective-permute-start.1
  41.9 1.9 collective-permute-start.2
  43.8 0.8 collective-permute-done.2
  47.5 3.4 collective-permute-start
  50.9 4.2 collective-permute-start.1
  55.0 1.9 collective-permute-start.2
  57.0 0.8 collective-permute-done.2
  60.6 4.3 collective-permute-start
  64.9 4.2 collective-permute-start.1
  69.1 1.9 collective-permute-start.2
  71.0 0.8 collective-permute-done.2
  74.7 2.8 collective-permute-start
  77.5 4.2 collective-permute-start.1
  81.7 1.9 collective-permute-start.2
  83.6 0.8 collective-permute-done.2
  87.3 2.8 collective-permute-start
  90.1 4.2 collective-permute-start.1
  94.3 1.9 collective-permute-start.2
  96.2 0.8 collective-permute-done.2
  99.8 2.8 collective-permute-start
  102.7 4.2 collective-permute-start.1
  106.9 1.9 collective-permute-start.2
  108.8 0.8 collective-permute-done.2
  112.5 2.8 collective-permute-start
  115.3 4.2 collective-permute-start.1
  119.5 1.9 collective-permute-start.2
  121.4 0.8 collective-permute-done.2
  125.0 2.4 copy.60
  127.4 1.1 reshape_reshape.3
  128.5 2.4 copy.59
  130.9 0.9 and_and_fusion
  131.8 5.3 fusion.41
  137.1 2.6 fusion.14
  139.7 1.5 convolution_convert_fusion
  144.2 21.1 %reduce-scatter.2.cloned.1.call-done = bf16[32,2304]{1,0:T(8,128)(2,1)} async-done(((bf16[128,2304]{1,0:T(8,128)(2,1)}), bf16[32,2304]{1,0:T(8,128)(2,1)}) %reduce-scatter.2.cloned.1.call-update) | async-done | bytes 147472 | tf_op jit(solution)/shard_map/reduce_scatter | solution.py:135
  165.3 1.1 fusion.20
  166.7 1.0 reshape_broadcast_in_dim_reshape.3
  167.7 3.8 all-to-all-start.3
  171.5 0.8 copy.66
  172.3 0.8 copy.67
  173.3 8.6 all-to-all-done.3
  182.1 212.7 %all-gather.4.cloned.1.call-done = bf16[2304,2880]{0,1:T(8,128)(2,1)} async-done(((bf16[2304,720]{0,1:T(8,128)(2,1)}), bf16[2304,2880]{0,1:T(8,128)(2,1)}) %all-gather.4.cloned.1.call-update) | async-done | bytes 13271056 | tf_op jit(solution)/shard_map/all_gather | solution.py:59
  394.8 8.8 fusion.46
  403.7 220.4 %all-gather.6.cloned.1.call-done = bf16[2304,2880]{0,1:T(8,128)(2,1)} async-done(((bf16[2304,720]{0,1:T(8,128)(2,1)}), bf16[2304,2880]{0,1:T(8,128)(2,1)}) %all-gather.6.cloned.1.call-update) | async-done | bytes 13271056 | tf_op jit(solution)/shard_map/all_gather | solution.py:60
  624.1 229.1 %all-gather.8.cloned.1.call-done = bf16[2304,2880]{0,1:T(8,128)(2,1)} async-done(((bf16[2304,720]{0,1:T(8,128)(2,1)}), bf16[2304,2880]{0,1:T(8,128)(2,1)}) %all-gather.8.cloned.1.call-update) | async-done | bytes 13271056 | tf_op jit(solution)/shard_map/all_gather | solution.py:61
  853.2 14.9 %convolution_convert_fusion.1 = bf16[72,2304]{1,0:T(8,128)(2,1)S(1)} fusion(bf16[2304,2880]{0,1:T(8,128)(2,1)} %all-gather.8.cloned.1.call-done, bf16[72,2304]{1,0:T(8,128)(2,1)S(1)} %reshape.164, bf16[2304,2880]{0,1:T(8,128)(2,1)} %all-gather.6.cloned.1.call-done, f32[72,2880]{1,0:T(8,128)S(1)} %fusion.46), kind=kOutput, calls=%fused_computation.11 | convolution fusion | flops 1912439808 | bytes 28035072 | tf_op jit(solution)/shard_map/dot_general | solution.py:173
  868.1 1.0 reshape.165
  869.0 3.7 all-to-all-start.4
  872.7 10.4 %all-to-all-done.4 = bf16[8,9,2304]{2,1,0:T(8,128)(2,1)S(1)} async-done(((bf16[8,9,2304]{2,1,0:T(8,128)(2,1)}), bf16[8,9,2304]{2,1,0:T(8,128)(2,1)S(1)}, u32[]{:S(2)}, u32[]{:S(2)}) %all-to-all-start.4) | async-done | bytes 331808 | tf_op jit(solution)/shard_map/all_to_all | solution.py:176
  883.3 1.4 gather_fusion
  884.6 1.4 gather_fusion.1
  886.0 1.8 fusion.23
  (108 shorter events, 27.9 us)
Async XLA Ops:
  7.2 132.5 %copy-start = (bf16[576,2304]{1,0:T(8,128)(2,1)S(1)}, bf16[576,2304]{1,0:T(8,128)(2,1)}, u32[]{:S(2)}) copy-start(bf16[576,2304]{1,0:T(8,128)(2,1)} %param.25) | copy-start | bytes 7962628
  9.1 12.7 %all-to-all-start = ((bf16[32,4,576]{2,0,1:T(8,128)(2,1)}), bf16[32,4,576]{2,0,1:T(8,128)(2,1)S(1)}, u32[]{:S(2)}, u32[]{:S(2)}) async-start(bf16[32,4,576]{2,0,1:T(8,128)(2,1)} %copy.57), calls=%async_computation | async-start | bytes 327680 | tf_op jit(solution)/shard_map/all_to_all | solution.py:74
  17.2 19.2 %copy-start.6 = (s32[128]{0:T(128)S(1)}, s32[128]{0:T(128)}, u32[]{:S(2)}) copy-start(s32[128]{0:T(128)} %param.20) | copy-start | bytes 1540
  21.9 9.3 %all-to-all-start.1 = ((bf16[32,4,576]{2,0,1:T(8,128)(2,1)}), bf16[32,4,576]{2,0,1:T(8,128)(2,1)S(1)}, u32[]{:S(2)}, u32[]{:S(2)}) async-start(bf16[32,4,576]{2,0,1:T(8,128)(2,1)} %copy.58), calls=%async_computation.1 | async-start | bytes 327680 | tf_op jit(solution)/shard_map/all_to_all | solution.py:81
  31.2 96.2 %all-to-all-start.2 = ((bf16[32,4,576]{2,0,1:T(8,128)(2,1)}), bf16[32,4,576]{2,0,1:T(8,128)(2,1)S(1)}, u32[]{:S(2)}, u32[]{:S(2)}) async-start(bf16[32,4,576]{2,0,1:T(8,128)(2,1)} %copy.61), calls=%async_computation.2 | async-start | bytes 327680 | tf_op jit(solution)/shard_map/all_to_all | solution.py:67
  34.6 130.7 %reduce-scatter.2.cloned.1.call-start = ((), (), s32[]{:S(2)}) async-start(), calls=%async_computation.6 | async-start | bytes 737280 | tf_op jit(solution)/shard_map/reduce_scatter | solution.py:135
  36.5 8.3 collective-permute-start
  37.8 8.4 collective-permute-start.1
  41.9 2.7 collective-permute-start.2
  47.5 10.5 %collective-permute-start = (bf16[128,576]{1,0:T(8,128)(2,1)}, bf16[128,576]{1,0:T(8,128)(2,1)S(1)}, u32[]{:S(2)}, u32[]{:S(2)}) collective-permute-start(bf16[128,576]{1,0:T(8,128)(2,1)} %get-tuple-element.230), channel_id=1, source_target_pairs={{0,4},{4,8},{8,12},{12,16},{16,20},{20,24},{24,28},{1,5},{5,9},{9,... | collective-permute-start | bytes 442376 | tf_op jit(solution)/shard_map/while/body/eval_jaxpr/ppermute | solution.py:21
  50.9 8.4 collective-permute-start.1
  55.0 2.7 collective-permute-start.2
  60.6 11.4 %collective-permute-start = (bf16[128,576]{1,0:T(8,128)(2,1)}, bf16[128,576]{1,0:T(8,128)(2,1)S(1)}, u32[]{:S(2)}, u32[]{:S(2)}) collective-permute-start(bf16[128,576]{1,0:T(8,128)(2,1)} %get-tuple-element.230), channel_id=1, source_target_pairs={{0,4},{4,8},{8,12},{12,16},{16,20},{20,24},{24,28},{1,5},{5,9},{9,... | collective-permute-start | bytes 442376 | tf_op jit(solution)/shard_map/while/body/eval_jaxpr/ppermute | solution.py:21
  64.9 8.4 collective-permute-start.1
  69.1 2.7 collective-permute-start.2
  74.7 9.9 %collective-permute-start = (bf16[128,576]{1,0:T(8,128)(2,1)}, bf16[128,576]{1,0:T(8,128)(2,1)S(1)}, u32[]{:S(2)}, u32[]{:S(2)}) collective-permute-start(bf16[128,576]{1,0:T(8,128)(2,1)} %get-tuple-element.230), channel_id=1, source_target_pairs={{0,4},{4,8},{8,12},{12,16},{16,20},{20,24},{24,28},{1,5},{5,9},{9,... | collective-permute-start | bytes 442376 | tf_op jit(solution)/shard_map/while/body/eval_jaxpr/ppermute | solution.py:21
  77.5 8.4 collective-permute-start.1
  81.7 2.7 collective-permute-start.2
  87.3 9.9 %collective-permute-start = (bf16[128,576]{1,0:T(8,128)(2,1)}, bf16[128,576]{1,0:T(8,128)(2,1)S(1)}, u32[]{:S(2)}, u32[]{:S(2)}) collective-permute-start(bf16[128,576]{1,0:T(8,128)(2,1)} %get-tuple-element.230), channel_id=1, source_target_pairs={{0,4},{4,8},{8,12},{12,16},{16,20},{20,24},{24,28},{1,5},{5,9},{9,... | collective-permute-start | bytes 442376 | tf_op jit(solution)/shard_map/while/body/eval_jaxpr/ppermute | solution.py:21
  90.1 8.4 collective-permute-start.1
  94.3 2.7 collective-permute-start.2
  99.8 9.9 %collective-permute-start = (bf16[128,576]{1,0:T(8,128)(2,1)}, bf16[128,576]{1,0:T(8,128)(2,1)S(1)}, u32[]{:S(2)}, u32[]{:S(2)}) collective-permute-start(bf16[128,576]{1,0:T(8,128)(2,1)} %get-tuple-element.230), channel_id=1, source_target_pairs={{0,4},{4,8},{8,12},{12,16},{16,20},{20,24},{24,28},{1,5},{5,9},{9,... | collective-permute-start | bytes 442376 | tf_op jit(solution)/shard_map/while/body/eval_jaxpr/ppermute | solution.py:21
  102.7 8.4 collective-permute-start.1
  106.9 2.7 collective-permute-start.2
  112.5 9.9 %collective-permute-start = (bf16[128,576]{1,0:T(8,128)(2,1)}, bf16[128,576]{1,0:T(8,128)(2,1)S(1)}, u32[]{:S(2)}, u32[]{:S(2)}) collective-permute-start(bf16[128,576]{1,0:T(8,128)(2,1)} %get-tuple-element.230), channel_id=1, source_target_pairs={{0,4},{4,8},{8,12},{12,16},{16,20},{20,24},{24,28},{1,5},{5,9},{9,... | collective-permute-start | bytes 442376 | tf_op jit(solution)/shard_map/while/body/eval_jaxpr/ppermute | solution.py:21
  115.3 8.4 collective-permute-start.1
  119.5 2.7 collective-permute-start.2
  125.0 5.9 copy-start.5
  141.2 253.6 %all-gather.4.cloned.1.call-start = ((), (), s32[]{:S(2)}) async-start(), calls=%async_computation.7 | async-start | bytes 16588800 | tf_op jit(solution)/shard_map/all_gather | solution.py:59
  142.0 1.3 copy-start.4
  142.0 23.3 %copy-start.2 = (bf16[32,2304]{1,0:T(8,128)(2,1)S(1)}, bf16[32,2304]{1,0:T(8,128)(2,1)}, u32[]{:S(2)}) copy-start(bf16[32,2304]{1,0:T(8,128)(2,1)} %param.17) | copy-start | bytes 442372
  142.0 482.1 %all-gather.6.cloned.1.call-start = ((), (), s32[]{:S(2)}) async-start(), calls=%async_computation.8 | async-start | bytes 16588800 | tf_op jit(solution)/shard_map/all_gather | solution.py:60
  142.7 23.7 %copy-start.3 = (f32[2304]{0:T(1024)S(1)}, f32[2304]{0:T(1024)}, u32[]{:S(2)}) copy-start(f32[2304]{0:T(1024)} %param.18) | copy-start | bytes 27652
  142.7 710.4 %all-gather.8.cloned.1.call-start = ((), (), s32[]{:S(2)}) async-start(), calls=%async_computation.9 | async-start | bytes 16588800 | tf_op jit(solution)/shard_map/all_gather | solution.py:61
  143.3 29.8 %copy-start.7 = (bf16[2304,8]{0,1:T(8,128)(2,1)S(1)}, bf16[2304,8]{0,1:T(8,128)(2,1)}, u32[]{:S(2)}) copy-start(bf16[2304,8]{0,1:T(8,128)(2,1)} %param.19) | copy-start | bytes 110596
  167.7 14.2 %all-to-all-start.3 = ((bf16[8,9,2304]{2,1,0:T(8,128)(2,1)}), bf16[8,9,2304]{2,1,0:T(8,128)(2,1)S(1)}, u32[]{:S(2)}, u32[]{:S(2)}) async-start(bf16[8,9,2304]{2,1,0:T(8,128)(2,1)} %reshape_broadcast_in_dim_reshape.3), calls=%async_computation.4 | async-start | bytes 1179648 | tf_op jit(solution)/shard_map/all_to_all | solution.py:167
  869.0 14.1 %all-to-all-start.4 = ((bf16[8,9,2304]{2,1,0:T(8,128)(2,1)}), bf16[8,9,2304]{2,1,0:T(8,128)(2,1)S(1)}, u32[]{:S(2)}, u32[]{:S(2)}) async-start(bf16[8,9,2304]{2,1,0:T(8,128)(2,1)} %reshape.165), calls=%async_computation.5 | async-start | bytes 1179648 | tf_op jit(solution)/shard_map/all_to_all | solution.py:176
  883.3 4.6 copy-start.1
Sparse Core Ops, SparseCore 0:
  141.3 23.9 reduce-scatter.1
  166.9 227.8 all-gather.3
  396.4 227.6 all-gather.5
  625.5 227.6 all-gather.7
where the time goes:
time: 896 us; the launch traced here: 894 us
  waiting for transfers between devices  716 us (80%)
  starting transfers between devices  83.3 us (9%)
  local copies, waits for them, and re-layouts  42.8 us (5%)
  matrix products  33.7 us (4%)
  between operations  14 us (2%)
    all_gather x1, waiting for transfers between devices, per_device(): lax.all_gather(down_weight, 'head', axis=1, tiled=True)  229 us
    all_gather x1, waiting for transfers between devices, per_device(): lax.all_gather(up_weight, 'head', axis=1, tiled=True)  220 us
    all_gather x1, waiting for transfers between devices, per_device(): lax.all_gather(gate_weight, 'head', axis=1, tiled=True)  213 us
    ppermute x21, starting transfers between devices, passed_along(): return lax.ppermute(value, axis, pairs)  62.7 us
    reduce_scatter x1, waiting for transfers between devices, per_device(): lax.psum_scatter(jnp.dot(attention, out_weight, preferred_element_type=jn...  21.1 us
  transfers between devices with their start and end apart: 30, of which 15 were waited for; matrix products, arithmetic and copies ran while one was open for 5% of the time, Pallas kernels for 0%

commit v1 on v0

--- a/solution.py
+++ b/solution.py
@@ -55,11 +55,6 @@
     heads_here = group_width // HDIM
     stretch_len = tok_local * head_count
     span_count = min(2**LEVELS * 32 // tok_local, seq_count)
-    gate_full, up_full, down_full = (
-        lax.all_gather(gate_weight, "head", axis=1, tiled=True),
-        lax.all_gather(up_weight, "head", axis=1, tiled=True),
-        lax.all_gather(down_weight, "head", axis=1, tiled=True),
-    )
     expert_count = router_weight.shape[1]
     replicas = seq_count // expert_count
     seq_place = lax.axis_index("seq")
@@ -167,12 +162,16 @@
     arrived = lax.all_to_all(outgoing, "seq", split_axis=0, concat_axis=0, tiled=True)
     slot_count = arrived.shape[1]
     flat_rows = arrived.reshape(seq_count * slot_count, D)
-    gate_act = jnp.dot(flat_rows, gate_full, preferred_element_type=jnp.float32)
-    up_act = jnp.dot(flat_rows, up_full, preferred_element_type=jnp.float32)
+    group_rows = lax.all_gather(flat_rows, "head", axis=0, tiled=True)
+    gate_act = jnp.dot(group_rows, gate_weight, preferred_element_type=jnp.float32)
+    up_act = jnp.dot(group_rows, up_weight, preferred_element_type=jnp.float32)
     hidden = (jax.nn.silu(gate_act) * up_act).astype(jnp.bfloat16)
-    shard_out = lax.dot_general(
-        hidden, down_full, (((1,), (1,)), ((), ())), preferred_element_type=jnp.float32
-    ).astype(jnp.bfloat16)
+    partial_out = lax.dot_general(
+        hidden, down_weight, (((1,), (1,)), ((), ())), preferred_element_type=jnp.float32
+    )
+    shard_out = lax.psum_scatter(partial_out, "head", scatter_dimension=0, tiled=True).astype(
+        jnp.bfloat16
+    )
     returned = lax.all_to_all(
         shard_out.reshape(seq_count, slot_count, D), "seq", split_axis=0, concat_axis=0, tiled=True
     )

time: 896 us -> 335 us (0.37)
  waiting for transfers between devices: 716 us -> 121 us
  local copies, waits for them, and re-layouts: 42.8 us -> 72.2 us
  blocking collectives: 0 us -> 14.6 us
  matrix products: 33.7 us -> 23 us
    all_gather x3 -> x1, waiting for transfers between devices: 662 us -> 29.6 us  [per_device(): group_rows = lax.all_gather(flat_rows, 'head', axis=0, tiled=True)]
    reduce_scatter x0 -> x1, waiting for transfers between devices: none -> 47.3 us  [per_device(): lax.psum_scatter(partial_out, 'head', scatter_dimension=0, tiled=True)]
    all_to_all x0 -> x1, blocking collectives: none -> 14.6 us  [per_device(): lax.all_to_all(outgoing, 'seq', split_axis=0, concat_axis=0, tiled=True)]
    dot_general x2, matrix products: 23.7 us -> 11.4 us  [the longest x1 6.94 us: per_device(): lax.dot_general(hidden, down_weight, (((1,), (1,)), ((), ())), preferred_...]
  transfers between devices with their start and end apart: 30 -> 28, of which waited for: 15 -> 12; matrix products, arithmetic and copies ran while one was open for 5% -> 16% of each run, Pallas kernels for 0% -> 0%
where the time goes in v1:
time: 335 us; the launch traced here: 333 us
  waiting for transfers between devices  121 us (36%)
  starting transfers between devices  82.5 us (25%)
  local copies, waits for them, and re-layouts  72.2 us (22%)
  matrix products  23 us (7%)
  blocking collectives  14.6 us (4%)
  between operations  13.9 us (4%)
  other arithmetic  6.15 us (2%)
    ppermute x21, starting transfers between devices, passed_along(): return lax.ppermute(value, axis, pairs)  62.8 us
    reduce_scatter x1, waiting for transfers between devices, per_device(): lax.psum_scatter(partial_out, 'head', scatter_dimension=0, tiled=True)  47.3 us
    all_gather x1, waiting for transfers between devices, per_device(): group_rows = lax.all_gather(flat_rows, 'head', axis=0, tiled=True)  29.6 us
    reduce_scatter x1, waiting for transfers between devices, per_device(): lax.psum_scatter(jnp.dot(attention, out_weight, preferred_element_type=jn...  23.3 us
    while x21, local copies, waits for them, and re-layouts  15.8 us
    all_to_all x1, blocking collectives, per_device(): lax.all_to_all(outgoing, 'seq', split_axis=0, concat_axis=0, tiled=True)  14.6 us
    dynamic_update_slice x7, local copies, waits for them, and re-layouts, advance(): lax.dynamic_update_slice_in_dim(keys_held, moving[0], write_place, 0)  11.1 us
    all_to_all x1, waiting for transfers between devices, per_device(): lax.all_to_all(shard_out.reshape(seq_count, slot_count, D), 'seq', split_...  10.4 us
  transfers between devices with their start and end apart: 28, of which 12 were waited for; matrix products, arithmetic and copies ran while one was open for 16% of the time, Pallas kernels for 0%

profile of v1, /device:TPU:0, one launch (start us, length us, event | category | flops | bytes accessed | tf_op | source)
XLA Modules:
  0.0 333.2 jit_solution(1250970378564809304)
XLA Ops:
  9.1 6.3 %all-to-all-start = ((bf16[32,4,576]{2,0,1:T(8,128)(2,1)}), bf16[32,4,576]{2,0,1:T(8,128)(2,1)S(1)}, u32[]{:S(2)}, u32[]{:S(2)}) async-start(bf16[32,4,576]{2,0,1:T(8,128)(2,1)} %copy.57), calls=%async_computation | async-start | bytes 327680 | tf_op jit(solution)/shard_map/all_to_all | solution.py:69
  16.1 1.8 reshape.158
  17.9 1.6 copy.58
  19.5 1.8 reshape.162
  21.3 1.6 copy.61
  22.9 5.1 %all-to-all-start.1 = ((bf16[32,4,576]{2,0,1:T(8,128)(2,1)}), bf16[32,4,576]{2,0,1:T(8,128)(2,1)}, u32[]{:S(2)}, u32[]{:S(2)}) async-start(bf16[32,4,576]{2,0,1:T(8,128)(2,1)} %copy.58), calls=%async_computation.1 | async-start | bytes 327680 | tf_op jit(solution)/shard_map/all_to_all | solution.py:76
  29.9 4.5 %all-to-all-done.1 = bf16[32,4,576]{2,0,1:T(8,128)(2,1)} async-done(((bf16[32,4,576]{2,0,1:T(8,128)(2,1)}), bf16[32,4,576]{2,0,1:T(8,128)(2,1)}, u32[]{:S(2)}, u32[]{:S(2)}) %all-to-all-start.1) | async-done | bytes 147488 | tf_op jit(solution)/shard_map/all_to_all | solution.py:76
  34.4 4.0 %all-to-all-start.2 = ((bf16[32,4,576]{2,0,1:T(8,128)(2,1)}), bf16[32,4,576]{2,0,1:T(8,128)(2,1)}, u32[]{:S(2)}, u32[]{:S(2)}) async-start(bf16[32,4,576]{2,0,1:T(8,128)(2,1)} %copy.61), calls=%async_computation.2 | async-start | bytes 327680 | tf_op jit(solution)/shard_map/all_to_all | solution.py:62
  38.4 2.1 concatenate.10
  40.5 1.6 copy.86
  42.1 101.5 %while.23 = (s32[]{:T(128)}, bf16[128,576]{1,0:T(8,128)(2,1)}, bf16[128,576]{1,0:T(8,128)(2,1)}, s32[128]{0:T(128)S(1)}, bf16[1024,576]{1,0:T(8,128)(2,1)}, /*in...) while((s32[]{:T(128)}, bf16[128,576]{1,0:T(8,128)(2,1)}, ...), condition=%wide.region_1.0_spmd, body=%wide.region_0.0_spmd.sunk | while | flops 7 | bytes 2412851 | solution.py:103
  42.1 2.0 collective-permute-start
  44.1 3.5 %collective-permute-start.1 = (bf16[128,576]{1,0:T(8,128)(2,1)}, bf16[128,576]{1,0:T(8,128)(2,1)S(1)}, u32[]{:S(2)}, u32[]{:S(2)}) collective-permute-start(bf16[128,576]{1,0:T(8,128)(2,1)} %get-tuple-element.231), channel_id=1, source_target_pairs={{0,4},{4,8},{8,12},{12,16},{16,20},{20,24},{24,28},{1,5},{5,9},{9,... | collective-permute-start | bytes 442376 | tf_op jit(solution)/shard_map/while/body/eval_jaxpr/ppermute | solution.py:21
  47.5 1.9 collective-permute-start.2
  50.4 1.6 copy.99
  52.0 1.6 constant_dynamic-update-slice_fusion.4
  55.0 4.1 %collective-permute-start = (bf16[128,576]{1,0:T(8,128)(2,1)}, bf16[128,576]{1,0:T(8,128)(2,1)}, u32[]{:S(2)}, u32[]{:S(2)}) collective-permute-start(bf16[128,576]{1,0:T(8,128)(2,1)} %get-tuple-element.230), channel_id=1, source_target_pairs={{0,4},{4,8},{8,12},{12,16},{16,20},{20,24},{24,28},{1,5},{5,9},{9,... | collective-permute-start | bytes 442376 | tf_op jit(solution)/shard_map/while/body/eval_jaxpr/ppermute | solution.py:21
  59.0 3.5 %collective-permute-start.1 = (bf16[128,576]{1,0:T(8,128)(2,1)}, bf16[128,576]{1,0:T(8,128)(2,1)S(1)}, u32[]{:S(2)}, u32[]{:S(2)}) collective-permute-start(bf16[128,576]{1,0:T(8,128)(2,1)} %get-tuple-element.231), channel_id=1, source_target_pairs={{0,4},{4,8},{8,12},{12,16},{16,20},{20,24},{24,28},{1,5},{5,9},{9,... | collective-permute-start | bytes 442376 | tf_op jit(solution)/shard_map/while/body/eval_jaxpr/ppermute | solution.py:21
  62.5 1.9 collective-permute-start.2
  65.4 1.6 copy.99
  67.0 1.6 constant_dynamic-update-slice_fusion.4
  70.0 5.0 %collective-permute-start = (bf16[128,576]{1,0:T(8,128)(2,1)}, bf16[128,576]{1,0:T(8,128)(2,1)}, u32[]{:S(2)}, u32[]{:S(2)}) collective-permute-start(bf16[128,576]{1,0:T(8,128)(2,1)} %get-tuple-element.230), channel_id=1, source_target_pairs={{0,4},{4,8},{8,12},{12,16},{16,20},{20,24},{24,28},{1,5},{5,9},{9,... | collective-permute-start | bytes 442376 | tf_op jit(solution)/shard_map/while/body/eval_jaxpr/ppermute | solution.py:21
  74.9 3.5 %collective-permute-start.1 = (bf16[128,576]{1,0:T(8,128)(2,1)}, bf16[128,576]{1,0:T(8,128)(2,1)S(1)}, u32[]{:S(2)}, u32[]{:S(2)}) collective-permute-start(bf16[128,576]{1,0:T(8,128)(2,1)} %get-tuple-element.231), channel_id=1, source_target_pairs={{0,4},{4,8},{8,12},{12,16},{16,20},{20,24},{24,28},{1,5},{5,9},{9,... | collective-permute-start | bytes 442376 | tf_op jit(solution)/shard_map/while/body/eval_jaxpr/ppermute | solution.py:21
  78.4 1.9 collective-permute-start.2
  81.3 1.6 copy.99
  82.9 1.6 constant_dynamic-update-slice_fusion.4
  85.9 3.5 %collective-permute-start = (bf16[128,576]{1,0:T(8,128)(2,1)}, bf16[128,576]{1,0:T(8,128)(2,1)}, u32[]{:S(2)}, u32[]{:S(2)}) collective-permute-start(bf16[128,576]{1,0:T(8,128)(2,1)} %get-tuple-element.230), channel_id=1, source_target_pairs={{0,4},{4,8},{8,12},{12,16},{16,20},{20,24},{24,28},{1,5},{5,9},{9,... | collective-permute-start | bytes 442376 | tf_op jit(solution)/shard_map/while/body/eval_jaxpr/ppermute | solution.py:21
  89.4 3.5 %collective-permute-start.1 = (bf16[128,576]{1,0:T(8,128)(2,1)}, bf16[128,576]{1,0:T(8,128)(2,1)S(1)}, u32[]{:S(2)}, u32[]{:S(2)}) collective-permute-start(bf16[128,576]{1,0:T(8,128)(2,1)} %get-tuple-element.231), channel_id=1, source_target_pairs={{0,4},{4,8},{8,12},{12,16},{16,20},{20,24},{24,28},{1,5},{5,9},{9,... | collective-permute-start | bytes 442376 | tf_op jit(solution)/shard_map/while/body/eval_jaxpr/ppermute | solution.py:21
  92.9 1.9 collective-permute-start.2
  95.8 1.6 copy.99
  100.3 3.5 %collective-permute-start = (bf16[128,576]{1,0:T(8,128)(2,1)}, bf16[128,576]{1,0:T(8,128)(2,1)}, u32[]{:S(2)}, u32[]{:S(2)}) collective-permute-start(bf16[128,576]{1,0:T(8,128)(2,1)} %get-tuple-element.230), channel_id=1, source_target_pairs={{0,4},{4,8},{8,12},{12,16},{16,20},{20,24},{24,28},{1,5},{5,9},{9,... | collective-permute-start | bytes 442376 | tf_op jit(solution)/shard_map/while/body/eval_jaxpr/ppermute | solution.py:21
  103.8 3.5 %collective-permute-start.1 = (bf16[128,576]{1,0:T(8,128)(2,1)}, bf16[128,576]{1,0:T(8,128)(2,1)S(1)}, u32[]{:S(2)}, u32[]{:S(2)}) collective-permute-start(bf16[128,576]{1,0:T(8,128)(2,1)} %get-tuple-element.231), channel_id=1, source_target_pairs={{0,4},{4,8},{8,12},{12,16},{16,20},{20,24},{24,28},{1,5},{5,9},{9,... | collective-permute-start | bytes 442376 | tf_op jit(solution)/shard_map/while/body/eval_jaxpr/ppermute | solution.py:21
  107.3 1.9 collective-permute-start.2
  111.8 1.6 constant_dynamic-update-slice_fusion.4
  114.7 3.5 %collective-permute-start = (bf16[128,576]{1,0:T(8,128)(2,1)}, bf16[128,576]{1,0:T(8,128)(2,1)}, u32[]{:S(2)}, u32[]{:S(2)}) collective-permute-start(bf16[128,576]{1,0:T(8,128)(2,1)} %get-tuple-element.230), channel_id=1, source_target_pairs={{0,4},{4,8},{8,12},{12,16},{16,20},{20,24},{24,28},{1,5},{5,9},{9,... | collective-permute-start | bytes 442376 | tf_op jit(solution)/shard_map/while/body/eval_jaxpr/ppermute | solution.py:21
  118.2 3.5 %collective-permute-start.1 = (bf16[128,576]{1,0:T(8,128)(2,1)}, bf16[128,576]{1,0:T(8,128)(2,1)S(1)}, u32[]{:S(2)}, u32[]{:S(2)}) collective-permute-start(bf16[128,576]{1,0:T(8,128)(2,1)} %get-tuple-element.231), channel_id=1, source_target_pairs={{0,4},{4,8},{8,12},{12,16},{16,20},{20,24},{24,28},{1,5},{5,9},{9,... | collective-permute-start | bytes 442376 | tf_op jit(solution)/shard_map/while/body/eval_jaxpr/ppermute | solution.py:21
  121.7 1.9 collective-permute-start.2
  126.2 1.6 constant_dynamic-update-slice_fusion.4
  129.2 3.5 %collective-permute-start = (bf16[128,576]{1,0:T(8,128)(2,1)}, bf16[128,576]{1,0:T(8,128)(2,1)}, u32[]{:S(2)}, u32[]{:S(2)}) collective-permute-start(bf16[128,576]{1,0:T(8,128)(2,1)} %get-tuple-element.230), channel_id=1, source_target_pairs={{0,4},{4,8},{8,12},{12,16},{16,20},{20,24},{24,28},{1,5},{5,9},{9,... | collective-permute-start | bytes 442376 | tf_op jit(solution)/shard_map/while/body/eval_jaxpr/ppermute | solution.py:21
  132.7 3.5 %collective-permute-start.1 = (bf16[128,576]{1,0:T(8,128)(2,1)}, bf16[128,576]{1,0:T(8,128)(2,1)S(1)}, u32[]{:S(2)}, u32[]{:S(2)}) collective-permute-start(bf16[128,576]{1,0:T(8,128)(2,1)} %get-tuple-element.231), channel_id=1, source_target_pairs={{0,4},{4,8},{8,12},{12,16},{16,20},{20,24},{24,28},{1,5},{5,9},{9,... | collective-permute-start | bytes 442376 | tf_op jit(solution)/shard_map/while/body/eval_jaxpr/ppermute | solution.py:21
  136.2 1.9 collective-permute-start.2
  140.7 1.6 constant_dynamic-update-slice_fusion.4
  143.6 2.4 copy.60
  146.0 2.0 reshape_reshape.3
  148.0 2.4 copy.59
  151.3 5.3 %fusion.42 = (f32[9,128]{1,0:T(8,128)S(1)}, bf16[9,128,1024]{1,2,0:T(8,128)(2,1)}) fusion(pred[128,1024]{0,1:T(8,128)(4,1)S(1)} %and_and_fusion, bf16[1024,9,64]{0,2,1:T(8,128)(2,1)} %bitcast.62, bf16[128,9,64]{2,1,0:T(8,128)(2,1)} %reshape_reshape.3), kind=kOutput, calls=%fused_computation.59 | convolution fusion | flops 158073856 | bytes 3822080 | tf_op jit(solution)/shard_map/sub | solution.py:122
  156.6 2.7 fusion.14
  161.8 23.3 %reduce-scatter.3.cloned.1.call-done = bf16[32,2304]{1,0:T(8,128)(2,1)} async-done(((bf16[128,2304]{1,0:T(8,128)(2,1)}), bf16[32,2304]{1,0:T(8,128)(2,1)}) %reduce-scatter.3.cloned.1.call-update) | async-done | bytes 147472 | tf_op jit(solution)/shard_map/reduce_scatter | solution.py:130
  187.8 1.9 reshape_broadcast_in_dim_reshape.3
  189.8 14.6 %all_to_all.55 = bf16[8,9,2304]{2,1,0:T(8,128)(2,1)} all-to-all(bf16[8,9,2304]{2,1,0:T(8,128)(2,1)} %reshape_broadcast_in_dim_reshape.3), channel_id=1, replica_groups=mesh['seq'=8,'head'=4] {'seq'}, dimensions={0} | all-to-all | bytes 663552 | tf_op jit(solution)/shard_map/all_to_all | solution.py:162
  204.4 1.9 reshape.164
  206.4 29.6 %all-gather.2.cloned.1.call-done = bf16[288,2304]{1,0:T(8,128)(2,1)} async-done(((bf16[72,2304]{1,0:T(8,128)(2,1)}), bf16[288,2304]{1,0:T(8,128)(2,1)}) %all-gather.2.cloned.1.call-update) | async-done | bytes 1327120 | tf_op jit(solution)/shard_map/all_gather | solution.py:165
  236.0 4.5 %fusion.47 = f32[288,720]{1,0:T(8,128)} fusion(bf16[288,2304]{1,0:T(8,128)(2,1)} %all-gather.2.cloned.1.call-done, bf16[2304,720]{0,1:T(8,128)(2,1)} %param.22), kind=kOutput, calls=%fused_computation.60 | convolution fusion | flops 955514880 | bytes 5474304 | tf_op jit(solution)/shard_map/dot_general | solution.py:166
  240.5 6.9 %fusion.17 = f32[288,2304]{1,0:T(8,128)} fusion(bf16[2304,720]{0,1:T(8,128)(2,1)S(1)} %copy-done, bf16[288,2304]{1,0:T(8,128)(2,1)} %all-gather.2.cloned.1.call-done, bf16[2304,720]{0,1:T(8,128)(2,1)} %param.23, f32[288,720]{1,0:T(8,128)} %fusion.47), kind=kOutput, calls=%fused_computation.20 | convolution fusion | flops 1912273920 | bytes 11446272 | tf_op jit(solution)/shard_map/dot_general | solution.py:169
  249.1 1.7 copy.67
  251.9 47.3 %reduce-scatter.5.cloned.1.call-done = f32[72,2304]{1,0:T(8,128)} async-done(((f32[288,2304]{1,0:T(8,128)}), f32[72,2304]{1,0:T(8,128)}) %reduce-scatter.5.cloned.1.call-update) | async-done | bytes 663568 | tf_op jit(solution)/shard_map/reduce_scatter | solution.py:172
  299.2 1.8 convert_element_type.53
  301.0 1.9 reshape.165
  303.0 4.2 %all-to-all-start.4 = ((bf16[8,9,2304]{2,1,0:T(8,128)(2,1)}), bf16[8,9,2304]{2,1,0:T(8,128)(2,1)}, u32[]{:S(2)}, u32[]{:S(2)}) async-start(bf16[8,9,2304]{2,1,0:T(8,128)(2,1)} %reshape.165), calls=%async_computation.6 | async-start | bytes 1179648 | tf_op jit(solution)/shard_map/all_to_all | solution.py:175
  307.2 10.4 %all-to-all-done.4 = bf16[8,9,2304]{2,1,0:T(8,128)(2,1)} async-done(((bf16[8,9,2304]{2,1,0:T(8,128)(2,1)}), bf16[8,9,2304]{2,1,0:T(8,128)(2,1)}, u32[]{:S(2)}, u32[]{:S(2)}) %all-to-all-start.4) | async-done | bytes 331808 | tf_op jit(solution)/shard_map/all_to_all | solution.py:175
  317.6 2.0 reshape.169
  319.7 2.6 gather_fusion
  322.3 2.6 gather_fusion.1
  324.9 1.8 fusion.24
  (111 shorter events, 36.1 us)
Async XLA Ops:
  7.2 233.3 %copy-start = (bf16[2304,720]{0,1:T(8,128)(2,1)S(1)}, bf16[2304,720]{0,1:T(8,128)(2,1)}, u32[]{:S(2)}) copy-start(bf16[2304,720]{0,1:T(8,128)(2,1)} %param.24) | copy-start | bytes 9953284
  9.1 13.8 %all-to-all-start = ((bf16[32,4,576]{2,0,1:T(8,128)(2,1)}), bf16[32,4,576]{2,0,1:T(8,128)(2,1)S(1)}, u32[]{:S(2)}, u32[]{:S(2)}) async-start(bf16[32,4,576]{2,0,1:T(8,128)(2,1)} %copy.57), calls=%async_computation | async-start | bytes 327680 | tf_op jit(solution)/shard_map/all_to_all | solution.py:69
  21.3 20.8 %copy-start.10 = (s32[128]{0:T(128)S(1)}, s32[128]{0:T(128)}, u32[]{:S(2)}) copy-start(s32[128]{0:T(128)} %param.20) | copy-start | bytes 1540
  22.9 19.2 %copy-start.2 = (bf16[32,4,576]{2,0,1:T(8,128)(2,1)}, bf16[32,4,576]{2,0,1:T(8,128)(2,1)S(1)}, u32[]{:S(2)}) copy-start(bf16[32,4,576]{2,0,1:T(8,128)(2,1)S(1)} %all-to-all-done) | copy-start | bytes 442372
  22.9 11.4 %all-to-all-start.1 = ((bf16[32,4,576]{2,0,1:T(8,128)(2,1)}), bf16[32,4,576]{2,0,1:T(8,128)(2,1)}, u32[]{:S(2)}, u32[]{:S(2)}) async-start(bf16[32,4,576]{2,0,1:T(8,128)(2,1)} %copy.58), calls=%async_computation.1 | async-start | bytes 327680 | tf_op jit(solution)/shard_map/all_to_all | solution.py:76
  34.4 111.6 %all-to-all-start.2 = ((bf16[32,4,576]{2,0,1:T(8,128)(2,1)}), bf16[32,4,576]{2,0,1:T(8,128)(2,1)}, u32[]{:S(2)}, u32[]{:S(2)}) async-start(bf16[32,4,576]{2,0,1:T(8,128)(2,1)} %copy.61), calls=%async_computation.2 | async-start | bytes 327680 | tf_op jit(solution)/shard_map/all_to_all | solution.py:62
  38.4 146.7 %reduce-scatter.3.cloned.1.call-start = ((), (), s32[]{:S(2)}) async-start(), calls=%async_computation.7 | async-start | bytes 737280 | tf_op jit(solution)/shard_map/reduce_scatter | solution.py:130
  42.1 8.3 %collective-permute-start = (bf16[128,576]{1,0:T(8,128)(2,1)}, bf16[128,576]{1,0:T(8,128)(2,1)}, u32[]{:S(2)}, u32[]{:S(2)}) collective-permute-start(bf16[128,576]{1,0:T(8,128)(2,1)} %get-tuple-element.230), channel_id=1, source_target_pairs={{0,4},{4,8},{8,12},{12,16},{16,20},{20,24},{24,28},{1,5},{5,9},{9,... | collective-permute-start | bytes 442376 | tf_op jit(solution)/shard_map/while/body/eval_jaxpr/ppermute | solution.py:21
  44.1 9.6 %collective-permute-start.1 = (bf16[128,576]{1,0:T(8,128)(2,1)}, bf16[128,576]{1,0:T(8,128)(2,1)S(1)}, u32[]{:S(2)}, u32[]{:S(2)}) collective-permute-start(bf16[128,576]{1,0:T(8,128)(2,1)} %get-tuple-element.231), channel_id=1, source_target_pairs={{0,4},{4,8},{8,12},{12,16},{16,20},{20,24},{24,28},{1,5},{5,9},{9,... | collective-permute-start | bytes 442376 | tf_op jit(solution)/shard_map/while/body/eval_jaxpr/ppermute | solution.py:21
  47.5 2.7 collective-permute-start.2
  55.0 10.5 %collective-permute-start = (bf16[128,576]{1,0:T(8,128)(2,1)}, bf16[128,576]{1,0:T(8,128)(2,1)}, u32[]{:S(2)}, u32[]{:S(2)}) collective-permute-start(bf16[128,576]{1,0:T(8,128)(2,1)} %get-tuple-element.230), channel_id=1, source_target_pairs={{0,4},{4,8},{8,12},{12,16},{16,20},{20,24},{24,28},{1,5},{5,9},{9,... | collective-permute-start | bytes 442376 | tf_op jit(solution)/shard_map/while/body/eval_jaxpr/ppermute | solution.py:21
  59.0 9.6 %collective-permute-start.1 = (bf16[128,576]{1,0:T(8,128)(2,1)}, bf16[128,576]{1,0:T(8,128)(2,1)S(1)}, u32[]{:S(2)}, u32[]{:S(2)}) collective-permute-start(bf16[128,576]{1,0:T(8,128)(2,1)} %get-tuple-element.231), channel_id=1, source_target_pairs={{0,4},{4,8},{8,12},{12,16},{16,20},{20,24},{24,28},{1,5},{5,9},{9,... | collective-permute-start | bytes 442376 | tf_op jit(solution)/shard_map/while/body/eval_jaxpr/ppermute | solution.py:21
  62.5 2.7 collective-permute-start.2
  70.0 11.4 %collective-permute-start = (bf16[128,576]{1,0:T(8,128)(2,1)}, bf16[128,576]{1,0:T(8,128)(2,1)}, u32[]{:S(2)}, u32[]{:S(2)}) collective-permute-start(bf16[128,576]{1,0:T(8,128)(2,1)} %get-tuple-element.230), channel_id=1, source_target_pairs={{0,4},{4,8},{8,12},{12,16},{16,20},{20,24},{24,28},{1,5},{5,9},{9,... | collective-permute-start | bytes 442376 | tf_op jit(solution)/shard_map/while/body/eval_jaxpr/ppermute | solution.py:21
  74.9 9.6 %collective-permute-start.1 = (bf16[128,576]{1,0:T(8,128)(2,1)}, bf16[128,576]{1,0:T(8,128)(2,1)S(1)}, u32[]{:S(2)}, u32[]{:S(2)}) collective-permute-start(bf16[128,576]{1,0:T(8,128)(2,1)} %get-tuple-element.231), channel_id=1, source_target_pairs={{0,4},{4,8},{8,12},{12,16},{16,20},{20,24},{24,28},{1,5},{5,9},{9,... | collective-permute-start | bytes 442376 | tf_op jit(solution)/shard_map/while/body/eval_jaxpr/ppermute | solution.py:21
  78.4 2.7 collective-permute-start.2
  85.9 9.9 %collective-permute-start = (bf16[128,576]{1,0:T(8,128)(2,1)}, bf16[128,576]{1,0:T(8,128)(2,1)}, u32[]{:S(2)}, u32[]{:S(2)}) collective-permute-start(bf16[128,576]{1,0:T(8,128)(2,1)} %get-tuple-element.230), channel_id=1, source_target_pairs={{0,4},{4,8},{8,12},{12,16},{16,20},{20,24},{24,28},{1,5},{5,9},{9,... | collective-permute-start | bytes 442376 | tf_op jit(solution)/shard_map/while/body/eval_jaxpr/ppermute | solution.py:21
  89.4 9.6 %collective-permute-start.1 = (bf16[128,576]{1,0:T(8,128)(2,1)}, bf16[128,576]{1,0:T(8,128)(2,1)S(1)}, u32[]{:S(2)}, u32[]{:S(2)}) collective-permute-start(bf16[128,576]{1,0:T(8,128)(2,1)} %get-tuple-element.231), channel_id=1, source_target_pairs={{0,4},{4,8},{8,12},{12,16},{16,20},{20,24},{24,28},{1,5},{5,9},{9,... | collective-permute-start | bytes 442376 | tf_op jit(solution)/shard_map/while/body/eval_jaxpr/ppermute | solution.py:21
  92.9 2.7 collective-permute-start.2
  100.3 9.9 %collective-permute-start = (bf16[128,576]{1,0:T(8,128)(2,1)}, bf16[128,576]{1,0:T(8,128)(2,1)}, u32[]{:S(2)}, u32[]{:S(2)}) collective-permute-start(bf16[128,576]{1,0:T(8,128)(2,1)} %get-tuple-element.230), channel_id=1, source_target_pairs={{0,4},{4,8},{8,12},{12,16},{16,20},{20,24},{24,28},{1,5},{5,9},{9,... | collective-permute-start | bytes 442376 | tf_op jit(solution)/shard_map/while/body/eval_jaxpr/ppermute | solution.py:21
  103.8 9.6 %collective-permute-start.1 = (bf16[128,576]{1,0:T(8,128)(2,1)}, bf16[128,576]{1,0:T(8,128)(2,1)S(1)}, u32[]{:S(2)}, u32[]{:S(2)}) collective-permute-start(bf16[128,576]{1,0:T(8,128)(2,1)} %get-tuple-element.231), channel_id=1, source_target_pairs={{0,4},{4,8},{8,12},{12,16},{16,20},{20,24},{24,28},{1,5},{5,9},{9,... | collective-permute-start | bytes 442376 | tf_op jit(solution)/shard_map/while/body/eval_jaxpr/ppermute | solution.py:21
  107.3 2.7 collective-permute-start.2
  114.7 9.9 %collective-permute-start = (bf16[128,576]{1,0:T(8,128)(2,1)}, bf16[128,576]{1,0:T(8,128)(2,1)}, u32[]{:S(2)}, u32[]{:S(2)}) collective-permute-start(bf16[128,576]{1,0:T(8,128)(2,1)} %get-tuple-element.230), channel_id=1, source_target_pairs={{0,4},{4,8},{8,12},{12,16},{16,20},{20,24},{24,28},{1,5},{5,9},{9,... | collective-permute-start | bytes 442376 | tf_op jit(solution)/shard_map/while/body/eval_jaxpr/ppermute | solution.py:21
  118.2 9.6 %collective-permute-start.1 = (bf16[128,576]{1,0:T(8,128)(2,1)}, bf16[128,576]{1,0:T(8,128)(2,1)S(1)}, u32[]{:S(2)}, u32[]{:S(2)}) collective-permute-start(bf16[128,576]{1,0:T(8,128)(2,1)} %get-tuple-element.231), channel_id=1, source_target_pairs={{0,4},{4,8},{8,12},{12,16},{16,20},{20,24},{24,28},{1,5},{5,9},{9,... | collective-permute-start | bytes 442376 | tf_op jit(solution)/shard_map/while/body/eval_jaxpr/ppermute | solution.py:21
  121.7 2.7 collective-permute-start.2
  129.2 9.9 %collective-permute-start = (bf16[128,576]{1,0:T(8,128)(2,1)}, bf16[128,576]{1,0:T(8,128)(2,1)}, u32[]{:S(2)}, u32[]{:S(2)}) collective-permute-start(bf16[128,576]{1,0:T(8,128)(2,1)} %get-tuple-element.230), channel_id=1, source_target_pairs={{0,4},{4,8},{8,12},{12,16},{16,20},{20,24},{24,28},{1,5},{5,9},{9,... | collective-permute-start | bytes 442376 | tf_op jit(solution)/shard_map/while/body/eval_jaxpr/ppermute | solution.py:21
  132.7 9.6 %collective-permute-start.1 = (bf16[128,576]{1,0:T(8,128)(2,1)}, bf16[128,576]{1,0:T(8,128)(2,1)S(1)}, u32[]{:S(2)}, u32[]{:S(2)}) collective-permute-start(bf16[128,576]{1,0:T(8,128)(2,1)} %get-tuple-element.231), channel_id=1, source_target_pairs={{0,4},{4,8},{8,12},{12,16},{16,20},{20,24},{24,28},{1,5},{5,9},{9,... | collective-permute-start | bytes 442376 | tf_op jit(solution)/shard_map/while/body/eval_jaxpr/ppermute | solution.py:21
  136.2 2.7 collective-permute-start.2
  143.6 6.8 %copy-start.9 = (s32[128]{0:T(128)S(1)}, s32[128]{0:T(128)}, u32[]{:S(2)}) copy-start(s32[128]{0:T(128)} %param.20) | copy-start | bytes 1540
  156.6 2.8 copy-start.1
  159.3 1.6 copy-start.8
  159.3 25.8 %copy-start.6 = (bf16[32,2304]{1,0:T(8,128)(2,1)S(1)}, bf16[32,2304]{1,0:T(8,128)(2,1)}, u32[]{:S(2)}) copy-start(bf16[32,2304]{1,0:T(8,128)(2,1)} %param.17) | copy-start | bytes 442372
  159.3 27.5 %copy-start.7 = (f32[2304]{0:T(1024)S(1)}, f32[2304]{0:T(1024)}, u32[]{:S(2)}) copy-start(f32[2304]{0:T(1024)} %param.18) | copy-start | bytes 27652
  160.9 75.1 %all-gather.2.cloned.1.call-start = ((), (), s32[]{:S(2)}) async-start(), calls=%async_computation.8 | async-start | bytes 1658880 | tf_op jit(solution)/shard_map/all_gather | solution.py:165
  186.1 0.7 copy-start.4
  206.4 92.8 %reduce-scatter.5.cloned.1.call-start = ((), (), s32[]{:S(2)}) async-start(), calls=%async_computation.9 | async-start | bytes 3317760 | tf_op jit(solution)/shard_map/reduce_scatter | solution.py:172
  247.4 0.9 copy-start.3
  303.0 14.7 %all-to-all-start.4 = ((bf16[8,9,2304]{2,1,0:T(8,128)(2,1)}), bf16[8,9,2304]{2,1,0:T(8,128)(2,1)}, u32[]{:S(2)}, u32[]{:S(2)}) async-start(bf16[8,9,2304]{2,1,0:T(8,128)(2,1)} %reshape.165), calls=%async_computation.6 | async-start | bytes 1179648 | tf_op jit(solution)/shard_map/all_to_all | solution.py:175
  319.7 5.2 %copy-start.5 = (bf16[32,2304]{1,0:T(8,128)(2,1)S(1)}, bf16[32,2304]{1,0:T(8,128)(2,1)}, u32[]{:S(2)}) copy-start(bf16[32,2304]{1,0:T(8,128)(2,1)} %copy-done.4) | copy-start | bytes 442372
Sparse Core Ops, SparseCore 0:
  161.0 24.0 reduce-scatter.2
  206.5 29.4 all-gather.1
  247.6 51.5 reduce-scatter.4

commit v2 on v1

--- a/solution.py
+++ b/solution.py
@@ -58,53 +58,32 @@
     expert_count = router_weight.shape[1]
     replicas = seq_count // expert_count
     seq_place = lax.axis_index("seq")
-    query_head, key_head, value_head = (
-        lax.all_to_all(
+    stacked = jnp.stack(
+        (
             query_rows.reshape(tok_local, head_count, group_width),
-            "head",
-            split_axis=1,
-            concat_axis=0,
-            tiled=True,
+            key_rows.reshape(tok_local, head_count, group_width),
+            value_rows.reshape(tok_local, head_count, group_width),
         ),
-        lax.all_to_all(
-            key_rows.reshape(tok_local, head_count, group_width),
-            "head",
-            split_axis=1,
-            concat_axis=0,
-            tiled=True,
-        ),
-        lax.all_to_all(
-            value_rows.reshape(tok_local, head_count, group_width),
-            "head",
-            split_axis=1,
-            concat_axis=0,
-            tiled=True,
-        ),
+        2,
     )
-    query_head = query_head.reshape(stretch_len, group_width)
-    key_head = key_head.reshape(stretch_len, group_width)
-    value_head = value_head.reshape(stretch_len, group_width)
+    by_head = lax.all_to_all(stacked, "head", split_axis=1, concat_axis=0, tiled=True)
+    query_head = by_head[:, 0, 0]
+    key_head = by_head[:, 0, 1]
+    value_head = by_head[:, 0, 2]
+    joined_head = by_head[:, 0, 1:].reshape(stretch_len, 2 * group_width)
+    pieces = [joined_head]
+    for distance in range(1, span_count):
+        pieces.append(passed_along(joined_head, "seq", distance))
+    joined_window = jnp.concatenate(pieces[::-1], 0)
+    key_window = joined_window[:, :group_width]
+    value_window = joined_window[:, group_width:]
     front_rows = (span_count - 1) * stretch_len
-    key_window = jnp.concatenate((jnp.zeros((front_rows, group_width), jnp.bfloat16), key_head), 0)
-    value_window = jnp.concatenate(
-        (jnp.zeros((front_rows, group_width), jnp.bfloat16), value_head), 0
-    )
-    segment_window = jnp.concatenate((jnp.zeros((front_rows,), jnp.int32), segment_ids), 0)
-
-    def advance(step_index, carried):
-        moving, keys_held, values_held, segments_held = carried
-        moving = passed_along((moving[0], moving[1], moving[2]), "seq", 1)
-        write_place = (span_count - 1 - step_index) * stretch_len
-        keys_held = lax.dynamic_update_slice_in_dim(keys_held, moving[0], write_place, 0)
-        values_held = lax.dynamic_update_slice_in_dim(values_held, moving[1], write_place, 0)
-        segments_held = lax.dynamic_update_slice_in_dim(segments_held, moving[2], write_place, 0)
-        return (moving, keys_held, values_held, segments_held)
-
-    moving_final, key_window, value_window, segment_window = lax.fori_loop(
-        1,
-        span_count,
-        advance,
-        ((key_head, value_head, segment_ids), key_window, value_window, segment_window),
+    all_segments = lax.all_gather(segment_ids, "seq", axis=0, tiled=True)
+    segment_window = lax.dynamic_slice_in_dim(
+        jnp.concatenate((jnp.zeros((front_rows,), jnp.int32), all_segments), 0),
+        seq_place * stretch_len,
+        span_count * stretch_len,
+        0,
     )
     key_total = span_count * stretch_len
     query_place = seq_place * stretch_len + jnp.arange(stretch_len, dtype=jnp.int32)

time: 335 us -> 257 us (0.77)
  starting transfers between devices: 82.5 us -> 25.8 us
  local copies, waits for them, and re-layouts: 72.2 us -> 36.9 us
  blocking collectives: 14.6 us -> 23.4 us
  waiting for transfers between devices: 121 us -> 126 us
    ppermute x21 -> x7, starting transfers between devices: 62.8 us -> 15.2 us  [passed_along(): return lax.ppermute(value, axis, pairs)]
    while x23 -> x0, local copies, waits for them, and re-layouts: 20.6 us -> none
    dynamic_update_slice x21 -> x0, local copies, waits for them, and re-layouts: 17.1 us -> none  [the longest x7 11.1 us: advance(): lax.dynamic_update_slice_in_dim(keys_held, moving[0], write_place, 0)]
    all_to_all x3 -> x1, starting transfers between devices: 15.4 us -> 6.32 us  [per_device(): lax.all_to_all(stacked, 'head', split_axis=1, concat_axis=0, tiled=True)]
    reshape x6 -> x0, local copies, waits for them, and re-layouts: 8.76 us -> none  [the longest x2 3.41 us: per_device(): query_rows.reshape(tok_local, head_count, group_width)]
    all_gather x0 -> x1, blocking collectives: none -> 8.76 us  [per_device(): all_segments = lax.all_gather(segment_ids, 'seq', axis=0, tiled=True)]
    ppermute x21 -> x7, waiting for transfers between devices: 5.6 us -> 12.7 us  [passed_along(): return lax.ppermute(value, axis, pairs)]
    slice x0 -> x4, local copies, waits for them, and re-layouts: none -> 5.03 us  [the longest x2 2.62 us: per_device(): joined_head = by_head[:, 0, 1:].reshape(stretch_len, 2 * group_width)]
  transfers between devices with their start and end apart: 28 -> 12, of which waited for: 12 -> 7; matrix products, arithmetic and copies ran while one was open for 16% -> 5% of each run, Pallas kernels for 0% -> 0%
where the time goes in v2:
time: 257 us; the launch traced here: 256 us
  waiting for transfers between devices  126 us (49%)
  local copies, waits for them, and re-layouts  36.9 us (14%)
  starting transfers between devices  25.8 us (10%)
  blocking collectives  23.4 us (9%)
  matrix products  22.1 us (9%)
  between operations  14 us (5%)
  other arithmetic  7.63 us (3%)
    reduce_scatter x1, waiting for transfers between devices, per_device(): lax.psum_scatter(partial_out, 'head', scatter_dimension=0, tiled=True)  48.1 us
    all_gather x1, waiting for transfers between devices, per_device(): group_rows = lax.all_gather(flat_rows, 'head', axis=0, tiled=True)  29.6 us
    reduce_scatter x1, waiting for transfers between devices, per_device(): lax.psum_scatter(jnp.dot(attention, out_weight, preferred_element_type=jn...  20.4 us
    ppermute x7, starting transfers between devices, passed_along(): return lax.ppermute(value, axis, pairs)  15.2 us
    all_to_all x1, blocking collectives, per_device(): lax.all_to_all(outgoing, 'seq', split_axis=0, concat_axis=0, tiled=True)  14.6 us
    ppermute x7, waiting for transfers between devices, passed_along(): return lax.ppermute(value, axis, pairs)  12.7 us
    all_to_all x1, waiting for transfers between devices, per_device(): lax.all_to_all(shard_out.reshape(seq_count, slot_count, D), 'seq', split_...  10.4 us
    unnamed x28, local copies, waits for them, and re-layouts  9.75 us
  transfers between devices with their start and end apart: 12, of which 7 were waited for; matrix products, arithmetic and copies ran while one was open for 5% of the time, Pallas kernels for 0%

profile of v2, /device:TPU:0, one launch (start us, length us, event | category | flops | bytes accessed | tf_op | source)
XLA Modules:
  0.0 256.2 jit_solution(2731430577743184152)
XLA Ops:
  7.2 1.3 stack_reshape.10
  8.5 1.8 stack_reshape.11
  10.3 1.8 stack_reshape.9
  12.0 1.4 pad_maximum_fusion
  13.5 0.8 copy.77
  14.3 6.3 %all-to-all-start = ((bf16[32,4,3,576]{3,0,2,1:T(8,128)(2,1)}), bf16[32,4,3,576]{3,0,2,1:T(8,128)(2,1)}, u32[]{:S(2)}, u32[]{:S(2)}) async-start(bf16[32,4,3,576]{3,0,2,1:T(8,128)(2,1)} %copy.77), calls=%async_computation | async-start | bytes 983040 | tf_op jit(solution)/shard_map/all_to_all | solution.py:69
  20.6 8.8 %all-gather = s32[8,1,128]{2,1,0:T(1,128)S(1)} all-gather(s32[1,1,128]{2,1,0:T(1,128)S(1)} %bitcast.60), channel_id=1, replica_groups=mesh['seq'=8,'head'=4] {'seq'}, dimensions={0}, use_global_device_ids=true | all-gather | bytes 4608 | tf_op jit(solution)/shard_map/all_gather | solution.py:81
  29.4 0.1 pad_dynamic-slice_fusion
  29.5 5.0 %all-to-all-done = bf16[32,4,3,576]{3,0,2,1:T(8,128)(2,1)} async-done(((bf16[32,4,3,576]{3,0,2,1:T(8,128)(2,1)}), bf16[32,4,3,576]{3,0,2,1:T(8,128)(2,1)}, u32[]{:S(2)}, u32[]{:S(2)}) %all-to-all-start) | async-done | bytes 442400 | tf_op jit(solution)/shard_map/all_to_all | solution.py:69
  34.5 1.1 copy.78
  35.6 0.8 copy-done.1
  36.4 0.8 slice.46
  37.1 1.9 copy.79
  39.0 3.7 %collective-permute-start = (bf16[128,1152]{0,1:T(8,128)(2,1)}, bf16[128,1152]{0,1:T(8,128)(2,1)}, u32[]{:S(2)}, u32[]{:S(2)}) collective-permute-start(bf16[128,1152]{0,1:T(8,128)(2,1)} %bitcast.47), channel_id=1, source_target_pairs={{0,28},{1,29},{2,30},{3,31}} | collective-permute-start | bytes 884744 | tf_op jit(solution)/shard_map/ppermute | solution.py:21
  42.7 0.8 and_and_fusion
  43.6 2.7 %collective-permute-start.1 = (bf16[128,1152]{0,1:T(8,128)(2,1)}, bf16[128,1152]{0,1:T(8,128)(2,1)}, u32[]{:S(2)}, u32[]{:S(2)}) collective-permute-start(bf16[128,1152]{0,1:T(8,128)(2,1)} %bitcast.48), channel_id=1, source_target_pairs={{0,24},{4,28},{1,25},{5,29},{2,26},{6,30},{3,27},{7,31}} | collective-permute-start | bytes 884744 | tf_op jit(solution)/shard_map/ppermute | solution.py:21
  46.3 2.0 collective-permute-start.2
  48.3 2.0 collective-permute-start.3
  50.3 2.0 collective-permute-start.4
  52.3 1.8 slice_bitcast_fusion
  54.2 0.8 copy.80
  54.9 1.4 collective-permute-start.5
  56.4 1.0 constant_dynamic-update-slice_fusion.7
  57.4 1.3 collective-permute-start.6
  58.8 1.1 constant_dynamic-update-slice_fusion.6
  59.8 7.4 %collective-permute-done.2 = bf16[128,1152]{0,1:T(8,128)(2,1)} collective-permute-done((bf16[128,1152]{0,1:T(8,128)(2,1)}, bf16[128,1152]{0,1:T(8,128)(2,1)}, u32[]{:S(2)}, u32[]{:S(2)}) %collective-permute-start.2) | collective-permute-done | bytes 294944 | tf_op jit(solution)/shard_map/ppermute | solution.py:21
  67.3 1.1 constant_dynamic-update-slice_fusion.5
  68.3 5.3 %collective-permute-done.3 = bf16[128,1152]{0,1:T(8,128)(2,1)} collective-permute-done((bf16[128,1152]{0,1:T(8,128)(2,1)}, bf16[128,1152]{0,1:T(8,128)(2,1)}, u32[]{:S(2)}, u32[]{:S(2)}) %collective-permute-start.3) | collective-permute-done | bytes 294944 | tf_op jit(solution)/shard_map/ppermute | solution.py:21
  73.6 1.1 constant_dynamic-update-slice_fusion.4
  74.7 1.1 constant_dynamic-update-slice_fusion.3
  75.7 0.1 constant_dynamic-update-slice_fusion.2
  75.8 0.1 constant_dynamic-update-slice_fusion.1
  76.0 0.1 constant_dynamic-update-slice_fusion
  76.1 1.6 fusion.35
  77.7 4.9 %fusion.36 = (f32[9,128]{1,0:T(8,128)S(1)}, bf16[9,128,1024]{2,1,0:T(8,128)(2,1)}) fusion(pred[128,1024]{1,0:T(8,128)(4,1)} %and_and_fusion, bf16[128,9,64]{0,2,1:T(8,128)(2,1)S(1)} %bitcast.58, bf16[1024,9,64]{0,2,1:T(8,128)(2,1)} %bitcast.56), kind=kOutput, calls=%fused_computation.67 | convolution fusion | flops 158073856 | bytes 3822080 | tf_op jit(solution)/shard_map/sub | solution.py:101
  82.6 3.1 %fusion.14 = bf16[128,9,64]{0,2,1:T(8,128)(2,1)S(1)} fusion(bf16[1024,9,64]{0,2,1:T(8,128)(2,1)} %bitcast.55, bf16[9,128,1024]{2,1,0:T(8,128)(2,1)} %get-tuple-element.33, f32[128,9]{0,1:T(8,128)S(1)} %bitcast.61), kind=kOutput, calls=%fused_computation.17 | convolution fusion | flops 151142400 | bytes 3691008 | tf_op jit(solution)/shard_map/hqk,khd->qhd/dot_general | solution.py:32
  85.8 1.5 convolution_convert_fusion
  87.3 0.1 copy.81
  87.4 0.1 eq.58
  87.6 0.1 reduce_window_sum.11
  87.7 0.2 select_reduce_fusion
  87.9 0.1 reduce_sum.46
  88.1 0.1 fusion.29
  88.2 20.4 %reduce-scatter.3.cloned.1.call-done = bf16[32,2304]{1,0:T(8,128)(2,1)} async-done(((bf16[128,2304]{1,0:T(8,128)(2,1)}), bf16[32,2304]{1,0:T(8,128)(2,1)}) %reduce-scatter.3.cloned.1.call-update) | async-done | bytes 147472 | tf_op jit(solution)/shard_map/reduce_scatter | solution.py:109
  108.6 1.2 fusion.21
  109.8 1.0 convolution_convert_fusion.1
  110.8 1.9 reshape_broadcast_in_dim_reshape.3
  112.7 14.6 %all_to_all.28 = bf16[8,9,2304]{2,1,0:T(8,128)(2,1)} all-to-all(bf16[8,9,2304]{2,1,0:T(8,128)(2,1)} %reshape_broadcast_in_dim_reshape.3), channel_id=1, replica_groups=mesh['seq'=8,'head'=4] {'seq'}, dimensions={0} | all-to-all | bytes 663552 | tf_op jit(solution)/shard_map/all_to_all | solution.py:141
  127.3 1.9 reshape.141
  129.4 29.6 %all-gather.3.cloned.1.call-done = bf16[288,2304]{1,0:T(8,128)(2,1)} async-done(((bf16[72,2304]{1,0:T(8,128)(2,1)}), bf16[288,2304]{1,0:T(8,128)(2,1)}) %all-gather.3.cloned.1.call-update) | async-done | bytes 1327120 | tf_op jit(solution)/shard_map/all_gather | solution.py:144
  159.0 4.5 %fusion.37 = f32[288,720]{1,0:T(8,128)} fusion(bf16[288,2304]{1,0:T(8,128)(2,1)} %all-gather.3.cloned.1.call-done, bf16[2304,720]{0,1:T(8,128)(2,1)} %param.20), kind=kOutput, calls=%fused_computation.68 | convolution fusion | flops 955514880 | bytes 5474304 | tf_op jit(solution)/shard_map/dot_general | solution.py:145
  163.4 6.9 %fusion.17 = f32[288,2304]{1,0:T(8,128)} fusion(bf16[2304,720]{0,1:T(8,128)(2,1)S(1)} %copy-done, bf16[288,2304]{1,0:T(8,128)(2,1)} %all-gather.3.cloned.1.call-done, bf16[2304,720]{0,1:T(8,128)(2,1)} %param.21, f32[288,720]{1,0:T(8,128)} %fusion.37), kind=kOutput, calls=%fused_computation.18 | convolution fusion | flops 1912273920 | bytes 11446272 | tf_op jit(solution)/shard_map/dot_general | solution.py:148
  170.4 1.7 copy.83
  172.1 1.7 copy.84
  173.8 0.2 fusion.26
  174.0 48.1 %reduce-scatter.5.cloned.1.call-done = f32[72,2304]{1,0:T(8,128)} async-done(((f32[288,2304]{1,0:T(8,128)}), f32[72,2304]{1,0:T(8,128)}) %reduce-scatter.5.cloned.1.call-update) | async-done | bytes 663568 | tf_op jit(solution)/shard_map/reduce_scatter | solution.py:151
  222.2 1.8 convert_element_type.53
  224.0 1.9 reshape.142
  225.9 4.2 %all-to-all-start.2 = ((bf16[8,9,2304]{2,1,0:T(8,128)(2,1)}), bf16[8,9,2304]{2,1,0:T(8,128)(2,1)}, u32[]{:S(2)}, u32[]{:S(2)}) async-start(bf16[8,9,2304]{2,1,0:T(8,128)(2,1)} %reshape.142), calls=%async_computation.4 | async-start | bytes 1179648 | tf_op jit(solution)/shard_map/all_to_all | solution.py:154
  230.2 10.4 %all-to-all-done.2 = bf16[8,9,2304]{2,1,0:T(8,128)(2,1)} async-done(((bf16[8,9,2304]{2,1,0:T(8,128)(2,1)}), bf16[8,9,2304]{2,1,0:T(8,128)(2,1)}, u32[]{:S(2)}, u32[]{:S(2)}) %all-to-all-start.2) | async-done | bytes 331808 | tf_op jit(solution)/shard_map/all_to_all | solution.py:154
  240.6 2.0 reshape.146
  242.7 2.6 %gather_fusion = f32[32,2304]{1,0:T(8,128)} fusion(f32[72,2304]{1,0:T(8,128)} %reshape.146, s32[1024]{0:T(1024)S(1)} %get-tuple-element.35), kind=kCustom, calls=%fused_computation | custom fusion | bytes 589952 | tf_op jit(solution)/shard_map/gather | solution.py:160
  245.2 2.6 %gather_fusion.1 = f32[32,2304]{1,0:T(8,128)} fusion(f32[72,2304]{1,0:T(8,128)} %reshape.146, s32[1024]{0:T(1024)S(1)} %get-tuple-element.34), kind=kCustom, calls=%fused_computation.1 | custom fusion | bytes 589952 | tf_op jit(solution)/shard_map/gather | solution.py:161
  247.8 1.8 fusion.24
  (39 shorter events, 0.4 us)
Async XLA Ops:
  7.2 156.3 %copy-start = (bf16[2304,720]{0,1:T(8,128)(2,1)S(1)}, bf16[2304,720]{0,1:T(8,128)(2,1)}, u32[]{:S(2)}) copy-start(bf16[2304,720]{0,1:T(8,128)(2,1)} %param.22) | copy-start | bytes 9953284
  7.2 13.4 %copy-start.7 = (s32[128]{0:T(128)S(1)}, s32[128]{0:T(128)}, u32[]{:S(2)}) copy-start(s32[128]{0:T(128)} %param.18) | copy-start | bytes 1540
  14.3 20.2 %all-to-all-start = ((bf16[32,4,3,576]{3,0,2,1:T(8,128)(2,1)}), bf16[32,4,3,576]{3,0,2,1:T(8,128)(2,1)}, u32[]{:S(2)}, u32[]{:S(2)}) async-start(bf16[32,4,3,576]{3,0,2,1:T(8,128)(2,1)} %copy.77), calls=%async_computation | async-start | bytes 983040 | tf_op jit(solution)/shard_map/all_to_all | solution.py:69
  20.6 88.0 %reduce-scatter.3.cloned.1.call-start = ((), (), s32[]{:S(2)}) async-start(), calls=%async_computation.5 | async-start | bytes 737280 | tf_op jit(solution)/shard_map/reduce_scatter | solution.py:109
  35.6 0.8 copy-start.1
  39.0 15.9 %collective-permute-start = (bf16[128,1152]{0,1:T(8,128)(2,1)}, bf16[128,1152]{0,1:T(8,128)(2,1)}, u32[]{:S(2)}, u32[]{:S(2)}) collective-permute-start(bf16[128,1152]{0,1:T(8,128)(2,1)} %bitcast.47), channel_id=1, source_target_pairs={{0,28},{1,29},{2,30},{3,31}} | collective-permute-start | bytes 884744 | tf_op jit(solution)/shard_map/ppermute | solution.py:21
  43.6 13.9 %collective-permute-start.1 = (bf16[128,1152]{0,1:T(8,128)(2,1)}, bf16[128,1152]{0,1:T(8,128)(2,1)}, u32[]{:S(2)}, u32[]{:S(2)}) collective-permute-start(bf16[128,1152]{0,1:T(8,128)(2,1)} %bitcast.48), channel_id=1, source_target_pairs={{0,24},{4,28},{1,25},{5,29},{2,26},{6,30},{3,27},{7,31}} | collective-permute-start | bytes 884744 | tf_op jit(solution)/shard_map/ppermute | solution.py:21
  46.3 21.0 %collective-permute-start.2 = (bf16[128,1152]{0,1:T(8,128)(2,1)}, bf16[128,1152]{0,1:T(8,128)(2,1)}, u32[]{:S(2)}, u32[]{:S(2)}) collective-permute-start(bf16[128,1152]{0,1:T(8,128)(2,1)} %bitcast.49), channel_id=1, source_target_pairs={{0,20},{4,24},{8,28},{1,21},{5,25},{9,29},{2,22},{6,26},{10,30},{3... | collective-permute-start | bytes 884744 | tf_op jit(solution)/shard_map/ppermute | solution.py:21
  48.3 25.3 %collective-permute-start.3 = (bf16[128,1152]{0,1:T(8,128)(2,1)}, bf16[128,1152]{0,1:T(8,128)(2,1)}, u32[]{:S(2)}, u32[]{:S(2)}) collective-permute-start(bf16[128,1152]{0,1:T(8,128)(2,1)} %bitcast.50), channel_id=1, source_target_pairs={{0,16},{4,20},{8,24},{12,28},{1,17},{5,21},{9,25},{13,29},{2,18},{... | collective-permute-start | bytes 884744 | tf_op jit(solution)/shard_map/ppermute | solution.py:21
  50.3 24.4 %collective-permute-start.4 = (bf16[128,1152]{0,1:T(8,128)(2,1)}, bf16[128,1152]{0,1:T(8,128)(2,1)}, u32[]{:S(2)}, u32[]{:S(2)}) collective-permute-start(bf16[128,1152]{0,1:T(8,128)(2,1)} %bitcast.51), channel_id=1, source_target_pairs={{0,12},{4,16},{8,20},{12,24},{16,28},{1,13},{5,17},{9,21},{13,25},... | collective-permute-start | bytes 884744 | tf_op jit(solution)/shard_map/ppermute | solution.py:21
  54.9 21.0 %copy-start.3 = (bf16[128,1,2,576]{0,3,2,1:T(8,128)(2,1)S(1)}, bf16[128,1,2,576]{0,3,2,1:T(8,128)(2,1)}, u32[]{:S(2)}) copy-start(bf16[128,1,2,576]{0,3,2,1:T(8,128)(2,1)} %copy.79) | copy-start | bytes 884740
  54.9 20.8 %collective-permute-start.5 = (bf16[128,1152]{0,1:T(8,128)(2,1)}, bf16[128,1152]{0,1:T(8,128)(2,1)S(1)}, u32[]{:S(2)}, u32[]{:S(2)}) collective-permute-start(bf16[128,1152]{0,1:T(8,128)(2,1)} %bitcast.52), channel_id=1, source_target_pairs={{0,8},{4,12},{8,16},{12,20},{16,24},{20,28},{1,9},{5,13},{9,17},{1... | collective-permute-start | bytes 884744 | tf_op jit(solution)/shard_map/ppermute | solution.py:21
  57.4 18.4 %collective-permute-start.6 = (bf16[128,1152]{0,1:T(8,128)(2,1)}, bf16[128,1152]{0,1:T(8,128)(2,1)S(1)}, u32[]{:S(2)}, u32[]{:S(2)}) collective-permute-start(bf16[128,1152]{0,1:T(8,128)(2,1)} %bitcast.53), channel_id=1, source_target_pairs={{0,4},{4,8},{8,12},{12,16},{16,20},{20,24},{24,28},{1,5},{5,9},{9,... | collective-permute-start | bytes 884744 | tf_op jit(solution)/shard_map/ppermute | solution.py:21
  76.1 1.6 copy-start.4
  82.6 3.1 %copy-start.2 = (bf16[576,2304]{1,0:T(8,128)(2,1)S(1)}, bf16[576,2304]{1,0:T(8,128)(2,1)}, u32[]{:S(2)}) copy-start(bf16[576,2304]{1,0:T(8,128)(2,1)} %param.23) | copy-start | bytes 7962628
  85.7 1.6 copy-start.6
  85.7 24.0 %copy-start.5 = (f32[2304]{0:T(1024)S(1)}, f32[2304]{0:T(1024)}, u32[]{:S(2)}) copy-start(f32[2304]{0:T(1024)} %param.16) | copy-start | bytes 27652
  87.3 71.7 %all-gather.3.cloned.1.call-start = ((), (), s32[]{:S(2)}) async-start(), calls=%async_computation.6 | async-start | bytes 1658880 | tf_op jit(solution)/shard_map/all_gather | solution.py:144
  129.3 92.8 %reduce-scatter.5.cloned.1.call-start = ((), (), s32[]{:S(2)}) async-start(), calls=%async_computation.7 | async-start | bytes 3317760 | tf_op jit(solution)/shard_map/reduce_scatter | solution.py:151
  170.4 3.4 %copy-start.8 = (bf16[2304,8]{0,1:T(8,128)(2,1)S(1)}, bf16[2304,8]{0,1:T(8,128)(2,1)}, u32[]{:S(2)}) copy-start(bf16[2304,8]{0,1:T(8,128)(2,1)} %param.17) | copy-start | bytes 110596
  225.9 14.7 %all-to-all-start.2 = ((bf16[8,9,2304]{2,1,0:T(8,128)(2,1)}), bf16[8,9,2304]{2,1,0:T(8,128)(2,1)}, u32[]{:S(2)}, u32[]{:S(2)}) async-start(bf16[8,9,2304]{2,1,0:T(8,128)(2,1)} %reshape.142), calls=%async_computation.4 | async-start | bytes 1179648 | tf_op jit(solution)/shard_map/all_to_all | solution.py:154
Sparse Core Ops, SparseCore 0:
  87.4 21.1 reduce-scatter.2
  129.4 29.4 all-gather.2
  170.5 51.5 reduce-scatter.4

commit v3 on v2

--- a/solution.py
+++ b/solution.py
@@ -147,10 +147,8 @@
     hidden = (jax.nn.silu(gate_act) * up_act).astype(jnp.bfloat16)
     partial_out = lax.dot_general(
         hidden, down_weight, (((1,), (1,)), ((), ())), preferred_element_type=jnp.float32
-    )
-    shard_out = lax.psum_scatter(partial_out, "head", scatter_dimension=0, tiled=True).astype(
-        jnp.bfloat16
-    )
+    ).astype(jnp.bfloat16)
+    shard_out = lax.psum_scatter(partial_out, "head", scatter_dimension=0, tiled=True)
     returned = lax.all_to_all(
         shard_out.reshape(seq_count, slot_count, D), "seq", split_axis=0, concat_axis=0, tiled=True
     )

time: 257 us -> 234 us (0.911)
  waiting for transfers between devices: 126 us -> 105 us
    reduce_scatter x1, waiting for transfers between devices: 48.1 us -> 27.1 us  [per_device(): lax.psum_scatter(partial_out, 'head', scatter_dimension=0, tiled=True)]
  transfers between devices with their start and end apart: 12 -> 12, of which waited for: 7 -> 7; matrix products, arithmetic and copies ran while one was open for 5% -> 6% of each run, Pallas kernels for 0% -> 0%
where the time goes in v3:
time: 234 us; the launch traced here: 233 us
  waiting for transfers between devices  105 us (45%)
  local copies, waits for them, and re-layouts  36.9 us (16%)
  starting transfers between devices  25.8 us (11%)
  blocking collectives  23.4 us (10%)
  matrix products  21.7 us (9%)
  between operations  14 us (6%)
  other arithmetic  5.79 us (2%)
    all_gather x1, waiting for transfers between devices, per_device(): group_rows = lax.all_gather(flat_rows, 'head', axis=0, tiled=True)  29.6 us
    reduce_scatter x1, waiting for transfers between devices, per_device(): lax.psum_scatter(partial_out, 'head', scatter_dimension=0, tiled=True)  27.1 us
    reduce_scatter x1, waiting for transfers between devices, per_device(): lax.psum_scatter(jnp.dot(attention, out_weight, preferred_element_type=jn...  20.4 us
    ppermute x7, starting transfers between devices, passed_along(): return lax.ppermute(value, axis, pairs)  15.2 us
    all_to_all x1, blocking collectives, per_device(): lax.all_to_all(outgoing, 'seq', split_axis=0, concat_axis=0, tiled=True)  14.6 us
    ppermute x7, waiting for transfers between devices, passed_along(): return lax.ppermute(value, axis, pairs)  12.7 us
    all_to_all x1, waiting for transfers between devices, per_device(): lax.all_to_all(shard_out.reshape(seq_count, slot_count, D), 'seq', split_...  10.4 us
    unnamed x28, local copies, waits for them, and re-layouts  9.75 us
  transfers between devices with their start and end apart: 12, of which 7 were waited for; matrix products, arithmetic and copies ran while one was open for 6% of the time, Pallas kernels for 0%

profile of v3, /device:TPU:0, one launch (start us, length us, event | category | flops | bytes accessed | tf_op | source)
XLA Modules:
  0.0 233.0 jit_solution(6231626913665201842)
XLA Ops:
  7.2 1.3 stack_reshape.10
  8.5 1.8 stack_reshape.11
  10.3 1.8 stack_reshape.9
  12.0 1.4 pad_maximum_fusion
  13.5 0.8 copy.77
  14.3 6.3 %all-to-all-start = ((bf16[32,4,3,576]{3,0,2,1:T(8,128)(2,1)}), bf16[32,4,3,576]{3,0,2,1:T(8,128)(2,1)}, u32[]{:S(2)}, u32[]{:S(2)}) async-start(bf16[32,4,3,576]{3,0,2,1:T(8,128)(2,1)} %copy.77), calls=%async_computation | async-start | bytes 983040 | tf_op jit(solution)/shard_map/all_to_all | solution.py:69
  20.6 8.8 %all-gather = s32[8,1,128]{2,1,0:T(1,128)S(1)} all-gather(s32[1,1,128]{2,1,0:T(1,128)S(1)} %bitcast.60), channel_id=1, replica_groups=mesh['seq'=8,'head'=4] {'seq'}, dimensions={0}, use_global_device_ids=true | all-gather | bytes 4608 | tf_op jit(solution)/shard_map/all_gather | solution.py:81
  29.4 0.1 pad_dynamic-slice_fusion
  29.5 5.0 %all-to-all-done = bf16[32,4,3,576]{3,0,2,1:T(8,128)(2,1)} async-done(((bf16[32,4,3,576]{3,0,2,1:T(8,128)(2,1)}), bf16[32,4,3,576]{3,0,2,1:T(8,128)(2,1)}, u32[]{:S(2)}, u32[]{:S(2)}) %all-to-all-start) | async-done | bytes 442400 | tf_op jit(solution)/shard_map/all_to_all | solution.py:69
  34.5 1.1 copy.78
  35.6 0.8 copy-done.1
  36.4 0.8 slice.46
  37.1 1.9 copy.79
  39.0 3.7 %collective-permute-start = (bf16[128,1152]{0,1:T(8,128)(2,1)}, bf16[128,1152]{0,1:T(8,128)(2,1)}, u32[]{:S(2)}, u32[]{:S(2)}) collective-permute-start(bf16[128,1152]{0,1:T(8,128)(2,1)} %bitcast.47), channel_id=1, source_target_pairs={{0,28},{1,29},{2,30},{3,31}} | collective-permute-start | bytes 884744 | tf_op jit(solution)/shard_map/ppermute | solution.py:21
  42.7 0.8 and_and_fusion
  43.6 2.7 %collective-permute-start.1 = (bf16[128,1152]{0,1:T(8,128)(2,1)}, bf16[128,1152]{0,1:T(8,128)(2,1)}, u32[]{:S(2)}, u32[]{:S(2)}) collective-permute-start(bf16[128,1152]{0,1:T(8,128)(2,1)} %bitcast.48), channel_id=1, source_target_pairs={{0,24},{4,28},{1,25},{5,29},{2,26},{6,30},{3,27},{7,31}} | collective-permute-start | bytes 884744 | tf_op jit(solution)/shard_map/ppermute | solution.py:21
  46.3 2.0 collective-permute-start.2
  48.3 2.0 collective-permute-start.3
  50.3 2.0 collective-permute-start.4
  52.3 1.9 slice_bitcast_fusion
  54.2 0.8 copy.80
  55.0 1.4 collective-permute-start.5
  56.4 1.0 constant_dynamic-update-slice_fusion.7
  57.5 1.3 collective-permute-start.6
  58.8 1.1 constant_dynamic-update-slice_fusion.6
  59.8 7.4 %collective-permute-done.2 = bf16[128,1152]{0,1:T(8,128)(2,1)} collective-permute-done((bf16[128,1152]{0,1:T(8,128)(2,1)}, bf16[128,1152]{0,1:T(8,128)(2,1)}, u32[]{:S(2)}, u32[]{:S(2)}) %collective-permute-start.2) | collective-permute-done | bytes 294944 | tf_op jit(solution)/shard_map/ppermute | solution.py:21
  67.3 1.1 constant_dynamic-update-slice_fusion.5
  68.3 5.3 %collective-permute-done.3 = bf16[128,1152]{0,1:T(8,128)(2,1)} collective-permute-done((bf16[128,1152]{0,1:T(8,128)(2,1)}, bf16[128,1152]{0,1:T(8,128)(2,1)}, u32[]{:S(2)}, u32[]{:S(2)}) %collective-permute-start.3) | collective-permute-done | bytes 294944 | tf_op jit(solution)/shard_map/ppermute | solution.py:21
  73.6 1.1 constant_dynamic-update-slice_fusion.4
  74.7 1.1 constant_dynamic-update-slice_fusion.3
  75.7 0.1 constant_dynamic-update-slice_fusion.2
  75.8 0.1 constant_dynamic-update-slice_fusion.1
  76.0 0.1 constant_dynamic-update-slice_fusion
  76.1 1.6 fusion.34
  77.7 4.9 %fusion.35 = (f32[9,128]{1,0:T(8,128)S(1)}, bf16[9,128,1024]{2,1,0:T(8,128)(2,1)}) fusion(pred[128,1024]{1,0:T(8,128)(4,1)} %and_and_fusion, bf16[128,9,64]{0,2,1:T(8,128)(2,1)S(1)} %bitcast.58, bf16[1024,9,64]{0,2,1:T(8,128)(2,1)} %bitcast.56), kind=kOutput, calls=%fused_computation.67 | convolution fusion | flops 158073856 | bytes 3822080 | tf_op jit(solution)/shard_map/sub | solution.py:101
  82.6 3.1 %fusion.14 = bf16[128,9,64]{0,2,1:T(8,128)(2,1)S(1)} fusion(bf16[1024,9,64]{0,2,1:T(8,128)(2,1)} %bitcast.55, bf16[9,128,1024]{2,1,0:T(8,128)(2,1)} %get-tuple-element.33, f32[128,9]{0,1:T(8,128)S(1)} %bitcast.61), kind=kOutput, calls=%fused_computation.18 | convolution fusion | flops 151142400 | bytes 3691008 | tf_op jit(solution)/shard_map/hqk,khd->qhd/dot_general | solution.py:32
  85.8 1.5 convolution_convert_fusion.1
  87.3 0.1 copy.81
  87.4 0.1 eq.58
  87.6 0.1 reduce_window_sum.11
  87.7 0.2 select_reduce_fusion
  87.9 0.1 reduce_sum.46
  88.0 0.1 copy.82
  88.1 0.1 fusion.28
  88.2 20.4 %reduce-scatter.3.cloned.1.call-done = bf16[32,2304]{1,0:T(8,128)(2,1)} async-done(((bf16[128,2304]{1,0:T(8,128)(2,1)}), bf16[32,2304]{1,0:T(8,128)(2,1)}) %reduce-scatter.3.cloned.1.call-update) | async-done | bytes 147472 | tf_op jit(solution)/shard_map/reduce_scatter | solution.py:109
  108.6 1.2 fusion.20
  109.8 1.0 convolution_convert_fusion.2
  110.8 1.9 reshape_broadcast_in_dim_reshape.3
  112.7 14.6 %all_to_all.28 = bf16[8,9,2304]{2,1,0:T(8,128)(2,1)} all-to-all(bf16[8,9,2304]{2,1,0:T(8,128)(2,1)} %reshape_broadcast_in_dim_reshape.3), channel_id=1, replica_groups=mesh['seq'=8,'head'=4] {'seq'}, dimensions={0} | all-to-all | bytes 663552 | tf_op jit(solution)/shard_map/all_to_all | solution.py:141
  127.3 1.9 reshape.141
  129.4 29.6 %all-gather.3.cloned.1.call-done = bf16[288,2304]{1,0:T(8,128)(2,1)} async-done(((bf16[72,2304]{1,0:T(8,128)(2,1)}), bf16[288,2304]{1,0:T(8,128)(2,1)}) %all-gather.3.cloned.1.call-update) | async-done | bytes 1327120 | tf_op jit(solution)/shard_map/all_gather | solution.py:144
  159.0 4.5 %fusion.36 = f32[288,720]{1,0:T(8,128)} fusion(bf16[288,2304]{1,0:T(8,128)(2,1)} %all-gather.3.cloned.1.call-done, bf16[2304,720]{0,1:T(8,128)(2,1)} %param.20), kind=kOutput, calls=%fused_computation.68 | convolution fusion | flops 955514880 | bytes 5474304 | tf_op jit(solution)/shard_map/dot_general | solution.py:145
  163.5 6.5 %convolution_convert_fusion = bf16[288,2304]{1,0:T(8,128)(2,1)} fusion(bf16[2304,720]{0,1:T(8,128)(2,1)S(1)} %copy-done, bf16[288,2304]{1,0:T(8,128)(2,1)} %all-gather.3.cloned.1.call-done, bf16[2304,720]{0,1:T(8,128)(2,1)} %param.21, f32[288,720]{1,0:T(8,128)} %fusion.36), kind=kOutput, calls=%fused_computation.5 | convolution fusion | flops 1912937472 | bytes 10119168 | tf_op jit(solution)/shard_map/dot_general | solution.py:148
  170.0 1.7 copy.83
  171.7 1.7 copy.84
  173.4 0.2 fusion.25
  173.6 27.1 %reduce-scatter.5.cloned.1.call-done = bf16[72,2304]{1,0:T(8,128)(2,1)} async-done(((bf16[288,2304]{1,0:T(8,128)(2,1)}), bf16[72,2304]{1,0:T(8,128)(2,1)}) %reduce-scatter.5.cloned.1.call-update) | async-done | bytes 331792 | tf_op jit(solution)/shard_map/reduce_scatter | solution.py:151
  200.8 1.9 reshape.142
  202.7 4.2 %all-to-all-start.2 = ((bf16[8,9,2304]{2,1,0:T(8,128)(2,1)}), bf16[8,9,2304]{2,1,0:T(8,128)(2,1)}, u32[]{:S(2)}, u32[]{:S(2)}) async-start(bf16[8,9,2304]{2,1,0:T(8,128)(2,1)} %reshape.142), calls=%async_computation.4 | async-start | bytes 1179648 | tf_op jit(solution)/shard_map/all_to_all | solution.py:152
  206.9 10.4 %all-to-all-done.2 = bf16[8,9,2304]{2,1,0:T(8,128)(2,1)} async-done(((bf16[8,9,2304]{2,1,0:T(8,128)(2,1)}), bf16[8,9,2304]{2,1,0:T(8,128)(2,1)}, u32[]{:S(2)}, u32[]{:S(2)}) %all-to-all-start.2) | async-done | bytes 331808 | tf_op jit(solution)/shard_map/all_to_all | solution.py:152
  217.4 2.0 reshape.146
  219.4 2.6 %gather_fusion = f32[32,2304]{1,0:T(8,128)} fusion(f32[72,2304]{1,0:T(8,128)} %reshape.146, s32[1024]{0:T(1024)S(1)} %get-tuple-element.35), kind=kCustom, calls=%fused_computation | custom fusion | bytes 589952 | tf_op jit(solution)/shard_map/gather | solution.py:158
  222.0 2.6 %gather_fusion.1 = f32[32,2304]{1,0:T(8,128)} fusion(f32[72,2304]{1,0:T(8,128)} %reshape.146, s32[1024]{0:T(1024)S(1)} %get-tuple-element.34), kind=kCustom, calls=%fused_computation.1 | custom fusion | bytes 589952 | tf_op jit(solution)/shard_map/gather | solution.py:159
  224.6 1.8 fusion.23
  (38 shorter events, 0.3 us)
Async XLA Ops:
  7.2 156.3 %copy-start = (bf16[2304,720]{0,1:T(8,128)(2,1)S(1)}, bf16[2304,720]{0,1:T(8,128)(2,1)}, u32[]{:S(2)}) copy-start(bf16[2304,720]{0,1:T(8,128)(2,1)} %param.22) | copy-start | bytes 9953284
  7.2 13.4 %copy-start.7 = (s32[128]{0:T(128)S(1)}, s32[128]{0:T(128)}, u32[]{:S(2)}) copy-start(s32[128]{0:T(128)} %param.18) | copy-start | bytes 1540
  14.3 20.2 %all-to-all-start = ((bf16[32,4,3,576]{3,0,2,1:T(8,128)(2,1)}), bf16[32,4,3,576]{3,0,2,1:T(8,128)(2,1)}, u32[]{:S(2)}, u32[]{:S(2)}) async-start(bf16[32,4,3,576]{3,0,2,1:T(8,128)(2,1)} %copy.77), calls=%async_computation | async-start | bytes 983040 | tf_op jit(solution)/shard_map/all_to_all | solution.py:69
  20.6 88.0 %reduce-scatter.3.cloned.1.call-start = ((), (), s32[]{:S(2)}) async-start(), calls=%async_computation.5 | async-start | bytes 737280 | tf_op jit(solution)/shard_map/reduce_scatter | solution.py:109
  35.6 0.8 copy-start.1
  39.0 16.0 %collective-permute-start = (bf16[128,1152]{0,1:T(8,128)(2,1)}, bf16[128,1152]{0,1:T(8,128)(2,1)}, u32[]{:S(2)}, u32[]{:S(2)}) collective-permute-start(bf16[128,1152]{0,1:T(8,128)(2,1)} %bitcast.47), channel_id=1, source_target_pairs={{0,28},{1,29},{2,30},{3,31}} | collective-permute-start | bytes 884744 | tf_op jit(solution)/shard_map/ppermute | solution.py:21
  43.6 13.9 %collective-permute-start.1 = (bf16[128,1152]{0,1:T(8,128)(2,1)}, bf16[128,1152]{0,1:T(8,128)(2,1)}, u32[]{:S(2)}, u32[]{:S(2)}) collective-permute-start(bf16[128,1152]{0,1:T(8,128)(2,1)} %bitcast.48), channel_id=1, source_target_pairs={{0,24},{4,28},{1,25},{5,29},{2,26},{6,30},{3,27},{7,31}} | collective-permute-start | bytes 884744 | tf_op jit(solution)/shard_map/ppermute | solution.py:21
  46.3 21.0 %collective-permute-start.2 = (bf16[128,1152]{0,1:T(8,128)(2,1)}, bf16[128,1152]{0,1:T(8,128)(2,1)}, u32[]{:S(2)}, u32[]{:S(2)}) collective-permute-start(bf16[128,1152]{0,1:T(8,128)(2,1)} %bitcast.49), channel_id=1, source_target_pairs={{0,20},{4,24},{8,28},{1,21},{5,25},{9,29},{2,22},{6,26},{10,30},{3... | collective-permute-start | bytes 884744 | tf_op jit(solution)/shard_map/ppermute | solution.py:21
  48.3 25.3 %collective-permute-start.3 = (bf16[128,1152]{0,1:T(8,128)(2,1)}, bf16[128,1152]{0,1:T(8,128)(2,1)}, u32[]{:S(2)}, u32[]{:S(2)}) collective-permute-start(bf16[128,1152]{0,1:T(8,128)(2,1)} %bitcast.50), channel_id=1, source_target_pairs={{0,16},{4,20},{8,24},{12,28},{1,17},{5,21},{9,25},{13,29},{2,18},{... | collective-permute-start | bytes 884744 | tf_op jit(solution)/shard_map/ppermute | solution.py:21
  50.3 24.4 %collective-permute-start.4 = (bf16[128,1152]{0,1:T(8,128)(2,1)}, bf16[128,1152]{0,1:T(8,128)(2,1)}, u32[]{:S(2)}, u32[]{:S(2)}) collective-permute-start(bf16[128,1152]{0,1:T(8,128)(2,1)} %bitcast.51), channel_id=1, source_target_pairs={{0,12},{4,16},{8,20},{12,24},{16,28},{1,13},{5,17},{9,21},{13,25},... | collective-permute-start | bytes 884744 | tf_op jit(solution)/shard_map/ppermute | solution.py:21
  55.0 21.0 %copy-start.3 = (bf16[128,1,2,576]{0,3,2,1:T(8,128)(2,1)S(1)}, bf16[128,1,2,576]{0,3,2,1:T(8,128)(2,1)}, u32[]{:S(2)}) copy-start(bf16[128,1,2,576]{0,3,2,1:T(8,128)(2,1)} %copy.79) | copy-start | bytes 884740
  55.0 20.8 %collective-permute-start.5 = (bf16[128,1152]{0,1:T(8,128)(2,1)}, bf16[128,1152]{0,1:T(8,128)(2,1)S(1)}, u32[]{:S(2)}, u32[]{:S(2)}) collective-permute-start(bf16[128,1152]{0,1:T(8,128)(2,1)} %bitcast.52), channel_id=1, source_target_pairs={{0,8},{4,12},{8,16},{12,20},{16,24},{20,28},{1,9},{5,13},{9,17},{1... | collective-permute-start | bytes 884744 | tf_op jit(solution)/shard_map/ppermute | solution.py:21
  57.5 18.4 %collective-permute-start.6 = (bf16[128,1152]{0,1:T(8,128)(2,1)}, bf16[128,1152]{0,1:T(8,128)(2,1)S(1)}, u32[]{:S(2)}, u32[]{:S(2)}) collective-permute-start(bf16[128,1152]{0,1:T(8,128)(2,1)} %bitcast.53), channel_id=1, source_target_pairs={{0,4},{4,8},{8,12},{12,16},{16,20},{20,24},{24,28},{1,5},{5,9},{9,... | collective-permute-start | bytes 884744 | tf_op jit(solution)/shard_map/ppermute | solution.py:21
  76.1 1.6 copy-start.4
  82.6 3.1 %copy-start.2 = (bf16[576,2304]{1,0:T(8,128)(2,1)S(1)}, bf16[576,2304]{1,0:T(8,128)(2,1)}, u32[]{:S(2)}) copy-start(bf16[576,2304]{1,0:T(8,128)(2,1)} %param.23) | copy-start | bytes 7962628
  85.7 1.6 copy-start.6
  85.7 24.0 %copy-start.5 = (f32[2304]{0:T(1024)S(1)}, f32[2304]{0:T(1024)}, u32[]{:S(2)}) copy-start(f32[2304]{0:T(1024)} %param.16) | copy-start | bytes 27652
  87.3 71.7 %all-gather.3.cloned.1.call-start = ((), (), s32[]{:S(2)}) async-start(), calls=%async_computation.6 | async-start | bytes 1658880 | tf_op jit(solution)/shard_map/all_gather | solution.py:144
  129.3 71.5 %reduce-scatter.5.cloned.1.call-start = ((), (), s32[]{:S(2)}) async-start(), calls=%async_computation.7 | async-start | bytes 1658880 | tf_op jit(solution)/shard_map/reduce_scatter | solution.py:151
  163.5 10.0 %copy-start.8 = (bf16[2304,8]{0,1:T(8,128)(2,1)S(1)}, bf16[2304,8]{0,1:T(8,128)(2,1)}, u32[]{:S(2)}) copy-start(bf16[2304,8]{0,1:T(8,128)(2,1)} %param.17) | copy-start | bytes 110596
  202.7 14.7 %all-to-all-start.2 = ((bf16[8,9,2304]{2,1,0:T(8,128)(2,1)}), bf16[8,9,2304]{2,1,0:T(8,128)(2,1)}, u32[]{:S(2)}, u32[]{:S(2)}) async-start(bf16[8,9,2304]{2,1,0:T(8,128)(2,1)} %reshape.142), calls=%async_computation.4 | async-start | bytes 1179648 | tf_op jit(solution)/shard_map/all_to_all | solution.py:152
Sparse Core Ops, SparseCore 0:
  87.4 21.1 reduce-scatter.2
  129.4 29.4 all-gather.2
  170.1 30.6 reduce-scatter.4

commit v4 on v3

--- a/solution.py
+++ b/solution.py
@@ -138,20 +138,32 @@
     outgoing = jnp.broadcast_to(packed[:, None], (expert_count, replicas, CAP, D)).reshape(
         seq_count, CAP, D
     )
-    arrived = lax.all_to_all(outgoing, "seq", split_axis=0, concat_axis=0, tiled=True)
-    slot_count = arrived.shape[1]
-    flat_rows = arrived.reshape(seq_count * slot_count, D)
-    group_rows = lax.all_gather(flat_rows, "head", axis=0, tiled=True)
-    gate_act = jnp.dot(group_rows, gate_weight, preferred_element_type=jnp.float32)
-    up_act = jnp.dot(group_rows, up_weight, preferred_element_type=jnp.float32)
-    hidden = (jax.nn.silu(gate_act) * up_act).astype(jnp.bfloat16)
-    partial_out = lax.dot_general(
-        hidden, down_weight, (((1,), (1,)), ((), ())), preferred_element_type=jnp.float32
-    ).astype(jnp.bfloat16)
-    shard_out = lax.psum_scatter(partial_out, "head", scatter_dimension=0, tiled=True)
-    returned = lax.all_to_all(
-        shard_out.reshape(seq_count, slot_count, D), "seq", split_axis=0, concat_axis=0, tiled=True
-    )
+    chunk_edges = (0, (CAP + 1) // 2, CAP)
+    returned_parts = []
+    for chunk_start, chunk_end in zip(chunk_edges[:-1], chunk_edges[1:]):
+        slot_count = chunk_end - chunk_start
+        arrived = lax.all_to_all(
+            outgoing[:, chunk_start:chunk_end], "seq", split_axis=0, concat_axis=0, tiled=True
+        )
+        flat_rows = arrived.reshape(seq_count * slot_count, D)
+        group_rows = lax.all_gather(flat_rows, "head", axis=0, tiled=True)
+        gate_act = jnp.dot(group_rows, gate_weight, preferred_element_type=jnp.float32)
+        up_act = jnp.dot(group_rows, up_weight, preferred_element_type=jnp.float32)
+        hidden = (jax.nn.silu(gate_act) * up_act).astype(jnp.bfloat16)
+        partial_out = lax.dot_general(
+            hidden, down_weight, (((1,), (1,)), ((), ())), preferred_element_type=jnp.float32
+        ).astype(jnp.bfloat16)
+        shard_out = lax.psum_scatter(partial_out, "head", scatter_dimension=0, tiled=True)
+        returned_parts.append(
+            lax.all_to_all(
+                shard_out.reshape(seq_count, slot_count, D),
+                "seq",
+                split_axis=0,
+                concat_axis=0,
+                tiled=True,
+            )
+        )
+    returned = jnp.concatenate(returned_parts, 1)
     expert_out = jnp.sum(
         returned.reshape(expert_count, replicas, CAP, D).astype(jnp.float32), 1
     ).reshape(slot_total, D)

time: 234 us -> 249 us (1.064)
  waiting for transfers between devices: 105 us -> 62.4 us
  blocking collectives: 23.4 us -> 50.9 us
  starting transfers between devices: 25.8 us -> 37.8 us
  local copies, waits for them, and re-layouts: 36.9 us -> 45.1 us
  matrix products: 21.7 us -> 29.1 us
    all_gather x0 -> x2, blocking collectives: none -> 42.1 us  [per_device(): group_rows = lax.all_gather(flat_rows, 'head', axis=0, tiled=True)]
    all_gather x1 -> x0, waiting for transfers between devices: 29.6 us -> none  [per_device(): group_rows = lax.all_gather(flat_rows, 'head', axis=0, tiled=True)]
    all_to_all x1 -> x0, blocking collectives: 14.6 us -> none  [per_device(): lax.all_to_all(outgoing, 'seq', split_axis=0, concat_axis=0, tiled=True)]
    reduce_scatter x1 -> x2, waiting for transfers between devices: 27.1 us -> 12.9 us  [per_device(): lax.psum_scatter(partial_out, 'head', scatter_dimension=0, tiled=True)]
    all_to_all x0 -> x2, starting transfers between devices: none -> 8.07 us  [per_device(): lax.all_to_all(outgoing[:, chunk_start:chunk_end], 'seq', split_axis=0, c...]
    dot_general x1 -> x2, matrix products: 6.52 us -> 10.7 us  [per_device(): lax.dot_general(hidden, down_weight, (((1,), (1,)), ((), ())), preferred_...]
    all_to_all x0 -> x2, waiting for transfers between devices: none -> 4.02 us  [per_device(): lax.all_to_all(outgoing[:, chunk_start:chunk_end], 'seq', split_axis=0, c...]
    all_to_all x1 -> x2, starting transfers between devices: 4.2 us -> 8.07 us  [per_device(): lax.all_to_all(shard_out.reshape(seq_count, slot_count, D), 'seq', split_...]
  transfers between devices with their start and end apart: 12 -> 15, of which waited for: 7 -> 7; matrix products, arithmetic and copies ran while one was open for 6% -> 16% of each run, Pallas kernels for 0% -> 0%
where the time goes in v4:
time: 249 us; the launch traced here: 247 us
  waiting for transfers between devices  62.4 us (25%)
  blocking collectives  50.9 us (20%)
  local copies, waits for them, and re-layouts  45.1 us (18%)
  starting transfers between devices  37.8 us (15%)
  matrix products  29.1 us (12%)
  between operations  14.1 us (6%)
  other arithmetic  8.05 us (3%)
    all_gather x2, blocking collectives, per_device(): group_rows = lax.all_gather(flat_rows, 'head', axis=0, tiled=True)  42.1 us
    reduce_scatter x1, waiting for transfers between devices, per_device(): lax.psum_scatter(jnp.dot(attention, out_weight, preferred_element_type=jn...  20.4 us
    ppermute x7, starting transfers between devices, passed_along(): return lax.ppermute(value, axis, pairs)  15.2 us
    reduce_scatter x2, waiting for transfers between devices, per_device(): lax.psum_scatter(partial_out, 'head', scatter_dimension=0, tiled=True)  12.9 us
    ppermute x7, waiting for transfers between devices, passed_along(): return lax.ppermute(value, axis, pairs)  12.7 us
    unnamed x32, local copies, waits for them, and re-layouts  11.5 us
    dot_general x2, matrix products, per_device(): lax.dot_general(hidden, down_weight, (((1,), (1,)), ((), ())), preferred_...  10.7 us
    all_gather x1, blocking collectives, per_device(): all_segments = lax.all_gather(segment_ids, 'seq', axis=0, tiled=True)  8.76 us
  transfers between devices with their start and end apart: 15, of which 7 were waited for; matrix products, arithmetic and copies ran while one was open for 16% of the time, Pallas kernels for 0%

profile of v4, /device:TPU:0, one launch (start us, length us, event | category | flops | bytes accessed | tf_op | source)
XLA Modules:
  0.0 247.2 jit_solution(7513430961776093302)
XLA Ops:
  7.2 1.3 stack_reshape.10
  8.5 1.8 stack_reshape.11
  10.3 1.8 stack_reshape.9
  12.1 1.4 pad_maximum_fusion
  13.5 0.8 copy.77
  14.3 6.3 %all-to-all-start = ((bf16[32,4,3,576]{3,0,2,1:T(8,128)(2,1)}), bf16[32,4,3,576]{3,0,2,1:T(8,128)(2,1)}, u32[]{:S(2)}, u32[]{:S(2)}) async-start(bf16[32,4,3,576]{3,0,2,1:T(8,128)(2,1)} %copy.77), calls=%async_computation | async-start | bytes 983040 | tf_op jit(solution)/shard_map/all_to_all | solution.py:69
  20.6 8.8 %all-gather = s32[8,1,128]{2,1,0:T(1,128)S(1)} all-gather(s32[1,1,128]{2,1,0:T(1,128)S(1)} %bitcast.69), channel_id=1, replica_groups=mesh['seq'=8,'head'=4] {'seq'}, dimensions={0}, use_global_device_ids=true | all-gather | bytes 4608 | tf_op jit(solution)/shard_map/all_gather | solution.py:81
  29.5 5.0 %all-to-all-done = bf16[32,4,3,576]{3,0,2,1:T(8,128)(2,1)} async-done(((bf16[32,4,3,576]{3,0,2,1:T(8,128)(2,1)}), bf16[32,4,3,576]{3,0,2,1:T(8,128)(2,1)}, u32[]{:S(2)}, u32[]{:S(2)}) %all-to-all-start) | async-done | bytes 442400 | tf_op jit(solution)/shard_map/all_to_all | solution.py:69
  34.5 1.1 copy.78
  35.6 0.8 copy-done.2
  37.1 1.9 copy.79
  39.0 3.7 %collective-permute-start = (bf16[128,1152]{0,1:T(8,128)(2,1)}, bf16[128,1152]{0,1:T(8,128)(2,1)}, u32[]{:S(2)}, u32[]{:S(2)}) collective-permute-start(bf16[128,1152]{0,1:T(8,128)(2,1)} %bitcast.56), channel_id=1, source_target_pairs={{0,28},{1,29},{2,30},{3,31}} | collective-permute-start | bytes 884744 | tf_op jit(solution)/shard_map/ppermute | solution.py:21
  42.8 0.8 and_and_fusion
  43.6 2.7 %collective-permute-start.1 = (bf16[128,1152]{0,1:T(8,128)(2,1)}, bf16[128,1152]{0,1:T(8,128)(2,1)}, u32[]{:S(2)}, u32[]{:S(2)}) collective-permute-start(bf16[128,1152]{0,1:T(8,128)(2,1)} %bitcast.57), channel_id=1, source_target_pairs={{0,24},{4,28},{1,25},{5,29},{2,26},{6,30},{3,27},{7,31}} | collective-permute-start | bytes 884744 | tf_op jit(solution)/shard_map/ppermute | solution.py:21
  46.3 2.0 collective-permute-start.2
  48.3 2.0 collective-permute-start.3
  50.3 2.0 collective-permute-start.4
  52.3 1.9 slice_bitcast_fusion
  54.2 0.8 copy.80
  55.0 1.4 collective-permute-start.5
  56.4 1.0 constant_dynamic-update-slice_fusion.7
  57.5 1.3 collective-permute-start.6
  58.8 1.1 constant_dynamic-update-slice_fusion.6
  59.9 7.4 %collective-permute-done.2 = bf16[128,1152]{0,1:T(8,128)(2,1)} collective-permute-done((bf16[128,1152]{0,1:T(8,128)(2,1)}, bf16[128,1152]{0,1:T(8,128)(2,1)}, u32[]{:S(2)}, u32[]{:S(2)}) %collective-permute-start.2) | collective-permute-done | bytes 294944 | tf_op jit(solution)/shard_map/ppermute | solution.py:21
  67.3 1.1 constant_dynamic-update-slice_fusion.5
  68.3 5.3 %collective-permute-done.3 = bf16[128,1152]{0,1:T(8,128)(2,1)} collective-permute-done((bf16[128,1152]{0,1:T(8,128)(2,1)}, bf16[128,1152]{0,1:T(8,128)(2,1)}, u32[]{:S(2)}, u32[]{:S(2)}) %collective-permute-start.3) | collective-permute-done | bytes 294944 | tf_op jit(solution)/shard_map/ppermute | solution.py:21
  73.6 1.1 constant_dynamic-update-slice_fusion.4
  74.7 1.1 constant_dynamic-update-slice_fusion.3
  76.1 1.6 fusion.47
  77.7 4.9 %fusion.48 = (f32[9,128]{1,0:T(8,128)S(1)}, bf16[9,128,1024]{2,1,0:T(8,128)(2,1)}) fusion(pred[128,1024]{1,0:T(8,128)(4,1)} %and_and_fusion, bf16[128,9,64]{0,2,1:T(8,128)(2,1)S(1)} %bitcast.67, bf16[1024,9,64]{0,2,1:T(8,128)(2,1)} %bitcast.65), kind=kOutput, calls=%fused_computation.83 | convolution fusion | flops 158073856 | bytes 3822080 | tf_op jit(solution)/shard_map/sub | solution.py:101
  82.6 3.1 %fusion.15 = bf16[128,9,64]{0,2,1:T(8,128)(2,1)S(1)} fusion(bf16[1024,9,64]{0,2,1:T(8,128)(2,1)} %bitcast.64, bf16[9,128,1024]{2,1,0:T(8,128)(2,1)} %get-tuple-element.33, f32[128,9]{0,1:T(8,128)S(1)} %bitcast.70), kind=kOutput, calls=%fused_computation.21 | convolution fusion | flops 151142400 | bytes 3691008 | tf_op jit(solution)/shard_map/hqk,khd->qhd/dot_general | solution.py:32
  85.8 1.5 convolution_convert_fusion.1
  88.1 20.4 %reduce-scatter.4.cloned.1.call-done = bf16[32,2304]{1,0:T(8,128)(2,1)} async-done(((bf16[128,2304]{1,0:T(8,128)(2,1)}), bf16[32,2304]{1,0:T(8,128)(2,1)}) %reduce-scatter.4.cloned.1.call-update) | async-done | bytes 147472 | tf_op jit(solution)/shard_map/reduce_scatter | solution.py:109
  108.6 1.2 fusion.30
  109.8 1.0 convolution_convert_fusion.3
  110.8 1.9 reshape_broadcast_in_dim_reshape.3
  112.7 1.8 slice.59
  114.6 4.0 %all-to-all-start.3 = ((bf16[8,4,2304]{2,1,0:T(4,128)(2,1)}), bf16[8,4,2304]{2,1,0:T(4,128)(2,1)}, u32[]{:S(2)}, u32[]{:S(2)}) async-start(bf16[8,4,2304]{2,1,0:T(4,128)(2,1)} %slice.59), calls=%async_computation.5 | async-start | bytes 294912 | tf_op jit(solution)/shard_map/all_to_all | solution.py:145
  118.6 1.7 slice.58
  120.3 4.0 %all-to-all-done.3 = bf16[8,4,2304]{2,1,0:T(4,128)(2,1)} async-done(((bf16[8,4,2304]{2,1,0:T(4,128)(2,1)}), bf16[8,4,2304]{2,1,0:T(4,128)(2,1)}, u32[]{:S(2)}, u32[]{:S(2)}) %all-to-all-start.3) | async-done | bytes 147488 | tf_op jit(solution)/shard_map/all_to_all | solution.py:145
  124.3 4.1 %all-to-all-start.1 = ((bf16[8,5,2304]{2,1,0:T(8,128)(2,1)}), bf16[8,5,2304]{2,1,0:T(8,128)(2,1)}, u32[]{:S(2)}, u32[]{:S(2)}) async-start(bf16[8,5,2304]{2,1,0:T(8,128)(2,1)} %slice.58), calls=%async_computation.2 | async-start | bytes 589824 | tf_op jit(solution)/shard_map/all_to_all | solution.py:145
  128.4 1.6 reshape.148
  130.0 16.7 %all_gather.11 = bf16[128,2304]{1,0:T(8,128)(2,1)S(1)} all-gather(bf16[32,2304]{1,0:T(8,128)(2,1)} %reshape.148), channel_id=1, replica_groups=mesh['seq'=8,'head'=4] {'head'}, dimensions={0}, use_global_device_ids=true | all-gather | bytes 737280 | tf_op jit(solution)/shard_map/all_gather | solution.py:149
  146.7 0.8 copy-done.1
  147.5 3.7 %fusion.50 = f32[128,720]{0,1:T(8,128)} fusion(bf16[128,2304]{1,0:T(8,128)(2,1)S(1)} %all_gather.11, bf16[2304,720]{0,1:T(8,128)(2,1)} %param.20), kind=kOutput, calls=%fused_computation.85 | convolution fusion | flops 424673280 | bytes 4276224 | tf_op jit(solution)/shard_map/dot_general | solution.py:150
  151.2 5.4 %convolution_convert_fusion.2 = bf16[128,2304]{1,0:T(8,128)(2,1)} fusion(bf16[2304,720]{0,1:T(8,128)(2,1)S(1)} %copy-done, bf16[128,2304]{1,0:T(8,128)(2,1)} %copy-done.1, bf16[2304,720]{0,1:T(8,128)(2,1)} %param.21, f32[128,720]{0,1:T(8,128)} %fusion.50), kind=kOutput, calls=%fused_computation.7 | convolution fusion | flops 850194432 | bytes 8183808 | tf_op jit(solution)/shard_map/dot_general | solution.py:153
  156.7 1.7 reshape.146
  158.4 25.5 %all_gather.10 = bf16[160,2304]{1,0:T(8,128)(2,1)S(1)} all-gather(bf16[40,2304]{1,0:T(8,128)(2,1)} %reshape.146), channel_id=1, replica_groups=mesh['seq'=8,'head'=4] {'head'}, dimensions={0}, use_global_device_ids=true | all-gather | bytes 921600 | tf_op jit(solution)/shard_map/all_gather | solution.py:149
  183.9 0.9 copy-done.3
  184.8 3.9 %fusion.49 = f32[160,720]{1,0:T(8,128)} fusion(bf16[160,2304]{1,0:T(8,128)(2,1)S(1)} %all_gather.10, bf16[2304,720]{0,1:T(8,128)(2,1)} %param.20), kind=kOutput, calls=%fused_computation.84 | convolution fusion | flops 530841600 | bytes 4515840 | tf_op jit(solution)/shard_map/dot_general | solution.py:150
  188.6 5.3 %convolution_convert_fusion = bf16[160,2304]{1,0:T(8,128)(2,1)} fusion(bf16[2304,720]{0,1:T(8,128)(2,1)S(1)} %copy-done, bf16[160,2304]{1,0:T(8,128)(2,1)} %copy-done.3, bf16[2304,720]{0,1:T(8,128)(2,1)} %param.21, f32[160,720]{1,0:T(8,128)} %fusion.49), kind=kOutput, calls=%fused_computation.5 | convolution fusion | flops 1062743040 | bytes 8570880 | tf_op jit(solution)/shard_map/dot_general | solution.py:153
  194.0 1.7 copy.83
  195.7 1.7 copy.84
  197.4 1.6 reshape.149
  199.0 4.0 %all-to-all-start.4 = ((bf16[8,4,2304]{2,1,0:T(4,128)(2,1)}), bf16[8,4,2304]{2,1,0:T(4,128)(2,1)}, u32[]{:S(2)}, u32[]{:S(2)}) async-start(bf16[8,4,2304]{2,1,0:T(4,128)(2,1)} %reshape.149), calls=%async_computation.7 | async-start | bytes 294912 | tf_op jit(solution)/shard_map/all_to_all | solution.py:158
  203.3 12.9 %reduce-scatter.6.cloned.1.call-done = bf16[40,2304]{1,0:T(8,128)(2,1)} async-done(((bf16[160,2304]{1,0:T(8,128)(2,1)}), bf16[40,2304]{1,0:T(8,128)(2,1)}) %reduce-scatter.6.cloned.1.call-update) | async-done | bytes 184336 | tf_op jit(solution)/shard_map/reduce_scatter | solution.py:156
  216.1 1.7 reshape.147
  217.8 4.1 %all-to-all-start.2 = ((bf16[8,5,2304]{2,1,0:T(8,128)(2,1)}), bf16[8,5,2304]{2,1,0:T(8,128)(2,1)}, u32[]{:S(2)}, u32[]{:S(2)}) async-start(bf16[8,5,2304]{2,1,0:T(8,128)(2,1)} %reshape.147), calls=%async_computation.4 | async-start | bytes 589824 | tf_op jit(solution)/shard_map/all_to_all | solution.py:158
  221.9 7.3 %all-to-all-done.2 = bf16[8,5,2304]{2,1,0:T(8,128)(2,1)} async-done(((bf16[8,5,2304]{2,1,0:T(8,128)(2,1)}), bf16[8,5,2304]{2,1,0:T(8,128)(2,1)}, u32[]{:S(2)}, u32[]{:S(2)}) %all-to-all-start.2) | async-done | bytes 184352 | tf_op jit(solution)/shard_map/all_to_all | solution.py:158
  229.2 2.3 maximum_convert_fusion
  231.5 2.3 reshape.150
  233.7 2.6 %gather_fusion = f32[32,2304]{1,0:T(8,128)} fusion(f32[72,2304]{1,0:T(8,128)} %reshape.150, s32[1024]{0:T(1024)S(1)} %get-tuple-element.35), kind=kCustom, calls=%fused_computation | custom fusion | bytes 589952 | tf_op jit(solution)/shard_map/gather | solution.py:170
  236.3 2.6 %gather_fusion.1 = f32[32,2304]{1,0:T(8,128)} fusion(f32[72,2304]{1,0:T(8,128)} %reshape.150, s32[1024]{0:T(1024)S(1)} %get-tuple-element.34), kind=kCustom, calls=%fused_computation.1 | custom fusion | bytes 589952 | tf_op jit(solution)/shard_map/gather | solution.py:171
  238.9 1.8 fusion.33
  (56 shorter events, 2.4 us)
Async XLA Ops:
  7.2 144.0 %copy-start = (bf16[2304,720]{0,1:T(8,128)(2,1)S(1)}, bf16[2304,720]{0,1:T(8,128)(2,1)}, u32[]{:S(2)}) copy-start(bf16[2304,720]{0,1:T(8,128)(2,1)} %param.22) | copy-start | bytes 9953284
  7.2 13.4 %copy-start.9 = (s32[128]{0:T(128)S(1)}, s32[128]{0:T(128)}, u32[]{:S(2)}) copy-start(s32[128]{0:T(128)} %param.18) | copy-start | bytes 1540
  14.3 20.2 %all-to-all-start = ((bf16[32,4,3,576]{3,0,2,1:T(8,128)(2,1)}), bf16[32,4,3,576]{3,0,2,1:T(8,128)(2,1)}, u32[]{:S(2)}, u32[]{:S(2)}) async-start(bf16[32,4,3,576]{3,0,2,1:T(8,128)(2,1)} %copy.77), calls=%async_computation | async-start | bytes 983040 | tf_op jit(solution)/shard_map/all_to_all | solution.py:69
  20.6 88.0 %reduce-scatter.4.cloned.1.call-start = ((), (), s32[]{:S(2)}) async-start(), calls=%async_computation.8 | async-start | bytes 737280 | tf_op jit(solution)/shard_map/reduce_scatter | solution.py:109
  35.6 0.8 copy-start.2
  39.0 16.0 %collective-permute-start = (bf16[128,1152]{0,1:T(8,128)(2,1)}, bf16[128,1152]{0,1:T(8,128)(2,1)}, u32[]{:S(2)}, u32[]{:S(2)}) collective-permute-start(bf16[128,1152]{0,1:T(8,128)(2,1)} %bitcast.56), channel_id=1, source_target_pairs={{0,28},{1,29},{2,30},{3,31}} | collective-permute-start | bytes 884744 | tf_op jit(solution)/shard_map/ppermute | solution.py:21
  43.6 13.9 %collective-permute-start.1 = (bf16[128,1152]{0,1:T(8,128)(2,1)}, bf16[128,1152]{0,1:T(8,128)(2,1)}, u32[]{:S(2)}, u32[]{:S(2)}) collective-permute-start(bf16[128,1152]{0,1:T(8,128)(2,1)} %bitcast.57), channel_id=1, source_target_pairs={{0,24},{4,28},{1,25},{5,29},{2,26},{6,30},{3,27},{7,31}} | collective-permute-start | bytes 884744 | tf_op jit(solution)/shard_map/ppermute | solution.py:21
  46.3 21.0 %collective-permute-start.2 = (bf16[128,1152]{0,1:T(8,128)(2,1)}, bf16[128,1152]{0,1:T(8,128)(2,1)}, u32[]{:S(2)}, u32[]{:S(2)}) collective-permute-start(bf16[128,1152]{0,1:T(8,128)(2,1)} %bitcast.58), channel_id=1, source_target_pairs={{0,20},{4,24},{8,28},{1,21},{5,25},{9,29},{2,22},{6,26},{10,30},{3... | collective-permute-start | bytes 884744 | tf_op jit(solution)/shard_map/ppermute | solution.py:21
  48.3 25.3 %collective-permute-start.3 = (bf16[128,1152]{0,1:T(8,128)(2,1)}, bf16[128,1152]{0,1:T(8,128)(2,1)}, u32[]{:S(2)}, u32[]{:S(2)}) collective-permute-start(bf16[128,1152]{0,1:T(8,128)(2,1)} %bitcast.59), channel_id=1, source_target_pairs={{0,16},{4,20},{8,24},{12,28},{1,17},{5,21},{9,25},{13,29},{2,18},{... | collective-permute-start | bytes 884744 | tf_op jit(solution)/shard_map/ppermute | solution.py:21
  50.3 24.3 %collective-permute-start.4 = (bf16[128,1152]{0,1:T(8,128)(2,1)}, bf16[128,1152]{0,1:T(8,128)(2,1)}, u32[]{:S(2)}, u32[]{:S(2)}) collective-permute-start(bf16[128,1152]{0,1:T(8,128)(2,1)} %bitcast.60), channel_id=1, source_target_pairs={{0,12},{4,16},{8,20},{12,24},{16,28},{1,13},{5,17},{9,21},{13,25},... | collective-permute-start | bytes 884744 | tf_op jit(solution)/shard_map/ppermute | solution.py:21
  55.0 21.0 %copy-start.5 = (bf16[128,1,2,576]{0,3,2,1:T(8,128)(2,1)S(1)}, bf16[128,1,2,576]{0,3,2,1:T(8,128)(2,1)}, u32[]{:S(2)}) copy-start(bf16[128,1,2,576]{0,3,2,1:T(8,128)(2,1)} %copy.79) | copy-start | bytes 884740
  55.0 20.8 %collective-permute-start.5 = (bf16[128,1152]{0,1:T(8,128)(2,1)}, bf16[128,1152]{0,1:T(8,128)(2,1)S(1)}, u32[]{:S(2)}, u32[]{:S(2)}) collective-permute-start(bf16[128,1152]{0,1:T(8,128)(2,1)} %bitcast.61), channel_id=1, source_target_pairs={{0,8},{4,12},{8,16},{12,20},{16,24},{20,28},{1,9},{5,13},{9,17},{1... | collective-permute-start | bytes 884744 | tf_op jit(solution)/shard_map/ppermute | solution.py:21
  57.5 18.4 %collective-permute-start.6 = (bf16[128,1152]{0,1:T(8,128)(2,1)}, bf16[128,1152]{0,1:T(8,128)(2,1)S(1)}, u32[]{:S(2)}, u32[]{:S(2)}) collective-permute-start(bf16[128,1152]{0,1:T(8,128)(2,1)} %bitcast.62), channel_id=1, source_target_pairs={{0,4},{4,8},{8,12},{12,16},{16,20},{20,24},{24,28},{1,5},{5,9},{9,... | collective-permute-start | bytes 884744 | tf_op jit(solution)/shard_map/ppermute | solution.py:21
  76.1 1.6 copy-start.6
  82.6 3.1 %copy-start.4 = (bf16[576,2304]{1,0:T(8,128)(2,1)S(1)}, bf16[576,2304]{1,0:T(8,128)(2,1)}, u32[]{:S(2)}) copy-start(bf16[576,2304]{1,0:T(8,128)(2,1)} %param.23) | copy-start | bytes 7962628
  85.7 1.5 copy-start.8
  85.7 24.0 %copy-start.7 = (f32[2304]{0:T(1024)S(1)}, f32[2304]{0:T(1024)}, u32[]{:S(2)}) copy-start(f32[2304]{0:T(1024)} %param.16) | copy-start | bytes 27652
  114.6 9.7 %all-to-all-start.3 = ((bf16[8,4,2304]{2,1,0:T(4,128)(2,1)}), bf16[8,4,2304]{2,1,0:T(4,128)(2,1)}, u32[]{:S(2)}, u32[]{:S(2)}) async-start(bf16[8,4,2304]{2,1,0:T(4,128)(2,1)} %slice.59), calls=%async_computation.5 | async-start | bytes 294912 | tf_op jit(solution)/shard_map/all_to_all | solution.py:145
  124.3 32.4 %all-to-all-start.1 = ((bf16[8,5,2304]{2,1,0:T(8,128)(2,1)}), bf16[8,5,2304]{2,1,0:T(8,128)(2,1)}, u32[]{:S(2)}, u32[]{:S(2)}) async-start(bf16[8,5,2304]{2,1,0:T(8,128)(2,1)} %slice.58), calls=%async_computation.2 | async-start | bytes 589824 | tf_op jit(solution)/shard_map/all_to_all | solution.py:145
  128.4 69.0 %reduce-scatter.8.cloned.1.call-start = ((), (), s32[]{:S(2)}) async-start(), calls=%async_computation.10 | async-start | bytes 737280 | tf_op jit(solution)/shard_map/reduce_scatter | solution.py:156
  146.7 0.8 copy-start.1
  156.7 59.5 %reduce-scatter.6.cloned.1.call-start = ((), (), s32[]{:S(2)}) async-start(), calls=%async_computation.9 | async-start | bytes 921600 | tf_op jit(solution)/shard_map/reduce_scatter | solution.py:156
  183.9 0.9 copy-start.3
  188.6 14.4 %copy-start.10 = (bf16[2304,8]{0,1:T(8,128)(2,1)S(1)}, bf16[2304,8]{0,1:T(8,128)(2,1)}, u32[]{:S(2)}) copy-start(bf16[2304,8]{0,1:T(8,128)(2,1)} %param.17) | copy-start | bytes 110596
  199.0 18.8 %all-to-all-start.4 = ((bf16[8,4,2304]{2,1,0:T(4,128)(2,1)}), bf16[8,4,2304]{2,1,0:T(4,128)(2,1)}, u32[]{:S(2)}, u32[]{:S(2)}) async-start(bf16[8,4,2304]{2,1,0:T(4,128)(2,1)} %reshape.149), calls=%async_computation.7 | async-start | bytes 294912 | tf_op jit(solution)/shard_map/all_to_all | solution.py:158
  217.8 11.4 %all-to-all-start.2 = ((bf16[8,5,2304]{2,1,0:T(8,128)(2,1)}), bf16[8,5,2304]{2,1,0:T(8,128)(2,1)}, u32[]{:S(2)}, u32[]{:S(2)}) async-start(bf16[8,5,2304]{2,1,0:T(8,128)(2,1)} %reshape.147), calls=%async_computation.4 | async-start | bytes 589824 | tf_op jit(solution)/shard_map/all_to_all | solution.py:158
Sparse Core Ops, SparseCore 0:
  87.4 21.1 reduce-scatter.3
  156.8 26.6 reduce-scatter.7
  194.1 21.9 reduce-scatter.5

commit v5 on v3

--- a/solution.py
+++ b/solution.py
@@ -71,23 +71,29 @@
     key_head = by_head[:, 0, 1]
     value_head = by_head[:, 0, 2]
     joined_head = by_head[:, 0, 1:].reshape(stretch_len, 2 * group_width)
-    pieces = [joined_head]
-    for distance in range(1, span_count):
-        pieces.append(passed_along(joined_head, "seq", distance))
-    joined_window = jnp.concatenate(pieces[::-1], 0)
+    all_segments = lax.all_gather(segment_ids, "seq", axis=0, tiled=True)
+    if span_count == seq_count:
+        joined_window = lax.all_gather(joined_head, "seq", axis=0, tiled=True)
+        segment_window = all_segments
+        window_first = 0
+    else:
+        pieces = [joined_head]
+        for distance in range(1, span_count):
+            pieces.append(passed_along(joined_head, "seq", distance))
+        joined_window = jnp.concatenate(pieces[::-1], 0)
+        front_rows = (span_count - 1) * stretch_len
+        segment_window = lax.dynamic_slice_in_dim(
+            jnp.concatenate((jnp.zeros((front_rows,), jnp.int32), all_segments), 0),
+            seq_place * stretch_len,
+            span_count * stretch_len,
+            0,
+        )
+        window_first = (seq_place - span_count + 1) * stretch_len
     key_window = joined_window[:, :group_width]
     value_window = joined_window[:, group_width:]
-    front_rows = (span_count - 1) * stretch_len
-    all_segments = lax.all_gather(segment_ids, "seq", axis=0, tiled=True)
-    segment_window = lax.dynamic_slice_in_dim(
-        jnp.concatenate((jnp.zeros((front_rows,), jnp.int32), all_segments), 0),
-        seq_place * stretch_len,
-        span_count * stretch_len,
-        0,
-    )
     key_total = span_count * stretch_len
     query_place = seq_place * stretch_len + jnp.arange(stretch_len, dtype=jnp.int32)
-    key_place = (seq_place - span_count + 1) * stretch_len + jnp.arange(key_total, dtype=jnp.int32)
+    key_place = window_first + jnp.arange(key_total, dtype=jnp.int32)
     allowed = (
         (segment_window[None, :] == segment_ids[:, None])
         & (key_place[None, :] <= query_place[:, None])

time: 234 us -> 226 us (0.966)
  starting transfers between devices: 25.8 us -> 4.36 us
  blocking collectives: 23.4 us -> 43.3 us
  local copies, waits for them, and re-layouts: 36.9 us -> 31.1 us
    all_to_all x0 -> x1, blocking collectives: none -> 19.9 us  [per_device(): lax.all_to_all(stacked, 'head', split_axis=1, concat_axis=0, tiled=True)]
    all_gather x0 -> x1, waiting for transfers between devices: none -> 16.3 us  [per_device(): joined_window = lax.all_gather(joined_head, 'seq', axis=0, tiled=True)]
    ppermute x7 -> x0, starting transfers between devices: 15.2 us -> none  [passed_along(): return lax.ppermute(value, axis, pairs)]
    ppermute x7 -> x0, waiting for transfers between devices: 12.7 us -> none  [passed_along(): return lax.ppermute(value, axis, pairs)]
    all_to_all x1 -> x0, starting transfers between devices: 6.32 us -> none  [per_device(): lax.all_to_all(stacked, 'head', split_axis=1, concat_axis=0, tiled=True)]
    unnamed x28 -> x19, local copies, waits for them, and re-layouts: 9.75 us -> 4.32 us
    all_to_all x1 -> x0, waiting for transfers between devices: 5.03 us -> none  [per_device(): lax.all_to_all(stacked, 'head', split_axis=1, concat_axis=0, tiled=True)]
  transfers between devices with their start and end apart: 12 -> 5, of which waited for: 7 -> 5; matrix products, arithmetic and copies ran while one was open for 6% -> 4% of each run, Pallas kernels for 0% -> 0%
where the time goes in v5:
time: 226 us; the launch traced here: 225 us
  waiting for transfers between devices  105 us (46%)
  blocking collectives  43.3 us (19%)
  local copies, waits for them, and re-layouts  31.1 us (14%)
  matrix products  21.7 us (10%)
  between operations  13.9 us (6%)
  other arithmetic  5.8 us (3%)
  starting transfers between devices  4.36 us (2%)
    all_gather x1, waiting for transfers between devices, per_device(): group_rows = lax.all_gather(flat_rows, 'head', axis=0, tiled=True)  29.6 us
    reduce_scatter x1, waiting for transfers between devices, per_device(): lax.psum_scatter(partial_out, 'head', scatter_dimension=0, tiled=True)  27.1 us
    reduce_scatter x1, waiting for transfers between devices, per_device(): lax.psum_scatter(jnp.dot(attention, out_weight, preferred_element_type=jn...  21.3 us
    all_to_all x1, blocking collectives, per_device(): lax.all_to_all(stacked, 'head', split_axis=1, concat_axis=0, tiled=True)  19.9 us
    all_gather x1, waiting for transfers between devices, per_device(): joined_window = lax.all_gather(joined_head, 'seq', axis=0, tiled=True)  16.3 us
    all_to_all x1, blocking collectives, per_device(): lax.all_to_all(outgoing, 'seq', split_axis=0, concat_axis=0, tiled=True)  14.6 us
    all_to_all x1, waiting for transfers between devices, per_device(): lax.all_to_all(shard_out.reshape(seq_count, slot_count, D), 'seq', split_...  10.4 us
    all_gather x1, blocking collectives, per_device(): all_segments = lax.all_gather(segment_ids, 'seq', axis=0, tiled=True)  8.76 us
  transfers between devices with their start and end apart: 5, of which 5 were waited for; matrix products, arithmetic and copies ran while one was open for 4% of the time, Pallas kernels for 0%

profile of v5, /device:TPU:0, one launch (start us, length us, event | category | flops | bytes accessed | tf_op | source)
XLA Modules:
  0.0 224.9 jit_solution(7894496712606518567)
XLA Ops:
  7.2 0.0 copy-start
  7.2 0.0 all-gather.4.cloned.1.call-start
  7.2 1.3 stack_reshape.11
  8.5 1.8 stack_reshape.10
  10.3 1.8 stack_reshape.9
  12.1 1.4 pad_maximum_fusion
  13.5 0.0 copy-start.6
  13.5 0.1 copy.77
  13.6 19.9 %all_to_all.28 = bf16[32,4,3,576]{3,0,2,1:T(8,128)(2,1)S(1)} all-to-all(bf16[32,4,3,576]{3,0,2,1:T(8,128)(2,1)S(1)} %copy.77), channel_id=1, replica_groups=mesh['seq'=8,'head'=4] {'head'}, dimensions={1} | all-to-all | bytes 884736 | tf_op jit(solution)/shard_map/all_to_all | solution.py:69
  33.6 0.0 copy-start.1
  33.6 0.8 copy-done.1
  34.4 0.7 slice.46
  35.1 1.9 copy.79
  37.0 0.0 all-gather.4.cloned.1.call-update
  37.0 0.0 reduce-scatter.3.cloned.1.call-start
  37.1 0.0 copy-done.6
  37.1 8.8 %all-gather = s32[8,1,128]{2,1,0:T(1,128)S(1)} all-gather(s32[1,1,128]{2,1,0:T(1,128)S(1)} %bitcast.54), channel_id=1, replica_groups=mesh['seq'=8,'head'=4] {'seq'}, dimensions={0}, use_global_device_ids=true | all-gather | bytes 4608 | tf_op jit(solution)/shard_map/all_gather | solution.py:74
  45.8 0.9 fusion.17
  46.7 1.9 slice_bitcast_fusion
  48.6 0.8 copy.80
  49.4 16.3 %all-gather.4.cloned.1.call-done = bf16[1024,1152]{0,1:T(8,128)(2,1)} async-done(((bf16[128,1152]{0,1:T(8,128)(2,1)}), bf16[1024,1152]{0,1:T(8,128)(2,1)}) %all-gather.4.cloned.1.call-update) | async-done | bytes 2359312 | tf_op jit(solution)/shard_map/all_gather | solution.py:76
  65.6 3.2 %fusion.35 = (bf16[1024,576]{0,1:T(8,128)(2,1)}, bf16[1024,576]{0,1:T(8,128)(2,1)}) fusion(bf16[1024,1152]{0,1:T(8,128)(2,1)} %all-gather.4.cloned.1.call-done), kind=kLoop, calls=%fused_computation.56 | loop fusion | bytes 4718592 | tf_op jit(solution)/shard_map/slice | solution.py:92
  68.9 0.0 copy-done.3
  68.9 4.9 %fusion.36 = (f32[9,128]{1,0:T(8,128)S(1)}, bf16[9,128,1024]{2,1,0:T(8,128)(2,1)}) fusion(pred[128,1024]{1,0:T(8,128)(4,1)} %fusion.17, bf16[128,9,64]{0,2,1:T(8,128)(2,1)S(1)} %bitcast.52, bf16[1024,9,64]{0,2,1:T(8,128)(2,1)} %bitcast.50), kind=kOutput, calls=%fused_computation.57 | convolution fusion | flops 158073856 | bytes 3822080 | tf_op jit(solution)/shard_map/sub | solution.py:107
  73.8 3.1 %fusion.14 = bf16[128,9,64]{0,2,1:T(8,128)(2,1)S(1)} fusion(bf16[1024,9,64]{0,2,1:T(8,128)(2,1)} %bitcast.49, bf16[9,128,1024]{2,1,0:T(8,128)(2,1)} %get-tuple-element.33, f32[128,9]{0,1:T(8,128)S(1)} %bitcast.55), kind=kOutput, calls=%fused_computation.18 | convolution fusion | flops 151142400 | bytes 3691008 | tf_op jit(solution)/shard_map/hqk,khd->qhd/dot_general | solution.py:32
  76.9 0.0 copy-start.5
  76.9 0.0 copy-start.4
  76.9 0.0 copy-done.2
  76.9 1.5 convolution_convert_fusion.1
  78.4 0.0 reduce-scatter.3.cloned.1.call-update
  78.4 0.0 all-gather.6.cloned.1.call-start
  78.5 0.0 copy-done.5
  78.5 0.1 copy.81
  78.6 0.1 eq.58
  78.7 0.1 fusion.28
  78.7 0.1 reduce_window_sum.11
  78.8 0.2 select_reduce_fusion
  79.0 0.1 reduce_sum.46
  79.1 0.1 copy.82
  79.2 0.1 fusion.29
  79.3 21.3 %reduce-scatter.3.cloned.1.call-done = bf16[32,2304]{1,0:T(8,128)(2,1)} async-done(((bf16[128,2304]{1,0:T(8,128)(2,1)}), bf16[32,2304]{1,0:T(8,128)(2,1)}) %reduce-scatter.3.cloned.1.call-update) | async-done | bytes 147472 | tf_op jit(solution)/shard_map/reduce_scatter | solution.py:115
  100.6 1.2 fusion.21
  101.8 0.0 copy-done.4
  101.8 1.0 convolution_convert_fusion.2
  102.8 1.9 reshape_broadcast_in_dim_reshape.3
  104.7 14.6 %all_to_all.29 = bf16[8,9,2304]{2,1,0:T(8,128)(2,1)} all-to-all(bf16[8,9,2304]{2,1,0:T(8,128)(2,1)} %reshape_broadcast_in_dim_reshape.3), channel_id=1, replica_groups=mesh['seq'=8,'head'=4] {'seq'}, dimensions={0} | all-to-all | bytes 663552 | tf_op jit(solution)/shard_map/all_to_all | solution.py:147
  119.4 1.9 reshape.113
  121.3 0.0 all-gather.6.cloned.1.call-update
  121.3 0.0 reduce-scatter.5.cloned.1.call-start
  121.4 29.6 %all-gather.6.cloned.1.call-done = bf16[288,2304]{1,0:T(8,128)(2,1)} async-done(((bf16[72,2304]{1,0:T(8,128)(2,1)}), bf16[288,2304]{1,0:T(8,128)(2,1)}) %all-gather.6.cloned.1.call-update) | async-done | bytes 1327120 | tf_op jit(solution)/shard_map/all_gather | solution.py:150
  151.0 4.5 %fusion.37 = f32[288,720]{1,0:T(8,128)} fusion(bf16[288,2304]{1,0:T(8,128)(2,1)} %all-gather.6.cloned.1.call-done, bf16[2304,720]{0,1:T(8,128)(2,1)} %param.20), kind=kOutput, calls=%fused_computation.58 | convolution fusion | flops 955514880 | bytes 5474304 | tf_op jit(solution)/shard_map/dot_general | solution.py:151
  155.5 6.5 %convolution_convert_fusion = bf16[288,2304]{1,0:T(8,128)(2,1)} fusion(bf16[2304,720]{0,1:T(8,128)(2,1)S(1)} %copy-done, bf16[288,2304]{1,0:T(8,128)(2,1)} %all-gather.6.cloned.1.call-done, bf16[2304,720]{0,1:T(8,128)(2,1)} %param.21, f32[288,720]{1,0:T(8,128)} %fusion.37), kind=kOutput, calls=%fused_computation.5 | convolution fusion | flops 1912937472 | bytes 10119168 | tf_op jit(solution)/shard_map/dot_general | solution.py:154
  161.9 0.0 reduce-scatter.5.cloned.1.call-update
  162.0 1.7 copy.83
  163.7 1.7 copy.84
  165.4 0.2 fusion.26
  165.6 27.1 %reduce-scatter.5.cloned.1.call-done = bf16[72,2304]{1,0:T(8,128)(2,1)} async-done(((bf16[288,2304]{1,0:T(8,128)(2,1)}), bf16[72,2304]{1,0:T(8,128)(2,1)}) %reduce-scatter.5.cloned.1.call-update) | async-done | bytes 331792 | tf_op jit(solution)/shard_map/reduce_scatter | solution.py:157
  192.7 1.9 reshape.114
  194.7 4.2 %all-to-all-start.2 = ((bf16[8,9,2304]{2,1,0:T(8,128)(2,1)}), bf16[8,9,2304]{2,1,0:T(8,128)(2,1)}, u32[]{:S(2)}, u32[]{:S(2)}) async-start(bf16[8,9,2304]{2,1,0:T(8,128)(2,1)} %reshape.114), calls=%async_computation.4 | async-start | bytes 1179648 | tf_op jit(solution)/shard_map/all_to_all | solution.py:158
  198.9 10.4 %all-to-all-done.2 = bf16[8,9,2304]{2,1,0:T(8,128)(2,1)} async-done(((bf16[8,9,2304]{2,1,0:T(8,128)(2,1)}), bf16[8,9,2304]{2,1,0:T(8,128)(2,1)}, u32[]{:S(2)}, u32[]{:S(2)}) %all-to-all-start.2) | async-done | bytes 331808 | tf_op jit(solution)/shard_map/all_to_all | solution.py:158
  209.3 2.0 reshape.118
  211.4 2.6 %gather_fusion.1 = f32[32,2304]{1,0:T(8,128)} fusion(f32[72,2304]{1,0:T(8,128)} %reshape.118, s32[1024]{0:T(1024)S(1)} %get-tuple-element.34), kind=kCustom, calls=%fused_computation.1 | custom fusion | bytes 589952 | tf_op jit(solution)/shard_map/gather | solution.py:165
  214.0 2.6 %gather_fusion = f32[32,2304]{1,0:T(8,128)} fusion(f32[72,2304]{1,0:T(8,128)} %reshape.118, s32[1024]{0:T(1024)S(1)} %get-tuple-element.35), kind=kCustom, calls=%fused_computation | custom fusion | bytes 589952 | tf_op jit(solution)/shard_map/gather | solution.py:164
  216.6 1.8 fusion.24
  (13 shorter events, 0.1 us)
Async XLA Ops:
  7.2 148.3 %copy-start = (bf16[2304,720]{0,1:T(8,128)(2,1)S(1)}, bf16[2304,720]{0,1:T(8,128)(2,1)}, u32[]{:S(2)}) copy-start(bf16[2304,720]{0,1:T(8,128)(2,1)} %param.22) | copy-start | bytes 9953284
  7.2 58.4 %all-gather.4.cloned.1.call-start = ((), (), s32[]{:S(2)}) async-start(), calls=%async_computation.5 | async-start | bytes 2654208 | tf_op jit(solution)/shard_map/all_gather | solution.py:76
  13.5 23.5 %copy-start.6 = (s32[128]{0:T(128)S(1)}, s32[128]{0:T(128)}, u32[]{:S(2)}) copy-start(s32[128]{0:T(128)} %param.18) | copy-start | bytes 1540
  33.6 0.8 copy-start.1
  37.0 63.6 %reduce-scatter.3.cloned.1.call-start = ((), (), s32[]{:S(2)}) async-start(), calls=%async_computation.6 | async-start | bytes 737280 | tf_op jit(solution)/shard_map/reduce_scatter | solution.py:115
  49.3 19.5 %copy-start.3 = (bf16[128,1,1,576]{0,3,2,1:T(8,128)(2,1)S(1)}, bf16[128,1,1,576]{0,3,2,1:T(8,128)(2,1)}, u32[]{:S(2)}) copy-start(bf16[128,1,1,576]{0,3,2,1:T(8,128)(2,1)} %copy.80) | copy-start | bytes 442372
  73.8 3.1 %copy-start.2 = (bf16[576,2304]{1,0:T(8,128)(2,1)S(1)}, bf16[576,2304]{1,0:T(8,128)(2,1)}, u32[]{:S(2)}) copy-start(bf16[576,2304]{1,0:T(8,128)(2,1)} %param.23) | copy-start | bytes 7962628
  76.9 1.6 copy-start.5
  76.9 24.9 %copy-start.4 = (f32[2304]{0:T(1024)S(1)}, f32[2304]{0:T(1024)}, u32[]{:S(2)}) copy-start(f32[2304]{0:T(1024)} %param.16) | copy-start | bytes 27652
  78.4 72.6 %all-gather.6.cloned.1.call-start = ((), (), s32[]{:S(2)}) async-start(), calls=%async_computation.7 | async-start | bytes 1658880 | tf_op jit(solution)/shard_map/all_gather | solution.py:150
  121.3 71.4 %reduce-scatter.5.cloned.1.call-start = ((), (), s32[]{:S(2)}) async-start(), calls=%async_computation.8 | async-start | bytes 1658880 | tf_op jit(solution)/shard_map/reduce_scatter | solution.py:157
  155.5 9.9 %copy-start.7 = (bf16[2304,8]{0,1:T(8,128)(2,1)S(1)}, bf16[2304,8]{0,1:T(8,128)(2,1)}, u32[]{:S(2)}) copy-start(bf16[2304,8]{0,1:T(8,128)(2,1)} %param.17) | copy-start | bytes 110596
  194.7 14.7 %all-to-all-start.2 = ((bf16[8,9,2304]{2,1,0:T(8,128)(2,1)}), bf16[8,9,2304]{2,1,0:T(8,128)(2,1)}, u32[]{:S(2)}, u32[]{:S(2)}) async-start(bf16[8,9,2304]{2,1,0:T(8,128)(2,1)} %reshape.114), calls=%async_computation.4 | async-start | bytes 1179648 | tf_op jit(solution)/shard_map/all_to_all | solution.py:158
Sparse Core Ops, SparseCore 0:
  37.1 28.4 all-gather.3
  78.5 22.0 reduce-scatter.2
  121.5 29.4 all-gather.5
  162.1 30.6 reduce-scatter.4

commit v6 on v5

--- a/solution.py
+++ b/solution.py
@@ -58,19 +58,24 @@
     expert_count = router_weight.shape[1]
     replicas = seq_count // expert_count
     seq_place = lax.axis_index("seq")
-    stacked = jnp.stack(
+    joined_stack = jnp.stack(
         (
-            query_rows.reshape(tok_local, head_count, group_width),
             key_rows.reshape(tok_local, head_count, group_width),
             value_rows.reshape(tok_local, head_count, group_width),
         ),
         2,
     )
-    by_head = lax.all_to_all(stacked, "head", split_axis=1, concat_axis=0, tiled=True)
-    query_head = by_head[:, 0, 0]
-    key_head = by_head[:, 0, 1]
-    value_head = by_head[:, 0, 2]
-    joined_head = by_head[:, 0, 1:].reshape(stretch_len, 2 * group_width)
+    joined_by_head = lax.all_to_all(joined_stack, "head", split_axis=1, concat_axis=0, tiled=True)
+    key_head = joined_by_head[:, 0, 0]
+    value_head = joined_by_head[:, 0, 1]
+    joined_head = joined_by_head.reshape(stretch_len, 2 * group_width)
+    query_head = lax.all_to_all(
+        query_rows.reshape(tok_local, head_count, group_width),
+        "head",
+        split_axis=1,
+        concat_axis=0,
+        tiled=True,
+    ).reshape(stretch_len, group_width)
     all_segments = lax.all_gather(segment_ids, "seq", axis=0, tiled=True)
     if span_count == seq_count:
         joined_window = lax.all_gather(joined_head, "seq", axis=0, tiled=True)
@@ -158,11 +163,18 @@
     returned = lax.all_to_all(
         shard_out.reshape(seq_count, slot_count, D), "seq", split_axis=0, concat_axis=0, tiled=True
     )
-    expert_out = jnp.sum(
-        returned.reshape(expert_count, replicas, CAP, D).astype(jnp.float32), 1
-    ).reshape(slot_total, D)
-    first_rows = expert_out[slot_ids[:, 0]]
-    second_rows = expert_out[slot_ids[:, 1]]
+    by_slot = jnp.swapaxes(returned.reshape(expert_count, replicas, CAP, D), 1, 2).reshape(
+        slot_total, replicas, D
+    )
+    slot_range = jnp.arange(slot_total, dtype=jnp.int32)[None, :]
+    first_hot = (slot_ids[:, 0:1] == slot_range).astype(jnp.bfloat16)
+    second_hot = (slot_ids[:, 1:2] == slot_range).astype(jnp.bfloat16)
+    first_rows = jnp.sum(
+        jnp.einsum("ts,srd->trd", first_hot, by_slot, preferred_element_type=jnp.float32), 1
+    )
+    second_rows = jnp.sum(
+        jnp.einsum("ts,srd->trd", second_hot, by_slot, preferred_element_type=jnp.float32), 1
+    )
     moe_sum = first_weight[:, None] * first_rows + second_weight[:, None] * second_rows
     residual_out = (middle_wide + residual_scale * moe_sum).astype(jnp.bfloat16)
     return (residual_out, key_head, value_head)

time: 226 us -> 222 us (0.982)
  waiting for transfers between devices: 105 us -> 99.1 us
  blocking collectives: 43.3 us -> 39.8 us
  starting transfers between devices: 4.36 us -> 7.7 us
  matrix products: 21.7 us -> 24.8 us
    gather x2 -> x0, local copies, waits for them, and re-layouts: 5.19 us -> none  [the longest x1 2.6 us: per_device(): first_rows = expert_out[slot_ids[:, 0]]]
    all_gather x1, waiting for transfers between devices: 16.3 us -> 12.4 us  [per_device(): joined_window = lax.all_gather(joined_head, 'seq', axis=0, tiled=True)]
    all_to_all x1, blocking collectives: 19.9 us -> 16.4 us  [per_device(): lax.all_to_all(joined_stack, 'head', split_axis=1, concat_axis=0, tiled=T...]
    all_to_all x0 -> x1, starting transfers between devices: none -> 3.34 us  [per_device(): lax.all_to_all(query_rows.reshape(tok_local, head_count, group_width), 'h...]
    dot_general x0 -> x2, matrix products: none -> 3.11 us  [the longest x1 1.9 us: per_device(): jnp.einsum('ts,srd->trd', second_hot, by_slot, preferred_element_type=jnp...]
    slice x1 -> x2, local copies, waits for them, and re-layouts: 3.24 us -> 6.31 us  [per_device(): key_window = joined_window[:, :group_width]]
    another operation x4 -> x5, local copies, waits for them, and re-layouts: 4.91 us -> 6.09 us  [the longest x3 3.1 us: per_device(): jnp.stack((key_rows.reshape(tok_local, head_count, group_width), value_ro...]
  transfers between devices with their start and end apart: 5 -> 6, of which waited for: 5 -> 5; matrix products, arithmetic and copies ran while one was open for 4% -> 4% of each run, Pallas kernels for 0% -> 0%
where the time goes in v6:
time: 222 us; the launch traced here: 221 us
  waiting for transfers between devices  99.1 us (45%)
  blocking collectives  39.8 us (18%)
  local copies, waits for them, and re-layouts  31.7 us (14%)
  matrix products  24.8 us (11%)
  between operations  13.9 us (6%)
  starting transfers between devices  7.7 us (3%)
  other arithmetic  3.69 us (2%)
    all_gather x1, waiting for transfers between devices, per_device(): group_rows = lax.all_gather(flat_rows, 'head', axis=0, tiled=True)  29.6 us
    reduce_scatter x1, waiting for transfers between devices, per_device(): lax.psum_scatter(partial_out, 'head', scatter_dimension=0, tiled=True)  25.4 us
    reduce_scatter x1, waiting for transfers between devices, per_device(): lax.psum_scatter(jnp.dot(attention, out_weight, preferred_element_type=jn...  21.3 us
    all_to_all x1, blocking collectives, per_device(): lax.all_to_all(joined_stack, 'head', split_axis=1, concat_axis=0, tiled=T...  16.4 us
    all_to_all x1, blocking collectives, per_device(): lax.all_to_all(outgoing, 'seq', split_axis=0, concat_axis=0, tiled=True)  14.6 us
    all_gather x1, waiting for transfers between devices, per_device(): joined_window = lax.all_gather(joined_head, 'seq', axis=0, tiled=True)  12.4 us
    all_to_all x1, waiting for transfers between devices, per_device(): lax.all_to_all(shard_out.reshape(seq_count, slot_count, D), 'seq', split_...  10.4 us
    all_gather x1, blocking collectives, per_device(): all_segments = lax.all_gather(segment_ids, 'seq', axis=0, tiled=True)  8.76 us
  transfers between devices with their start and end apart: 6, of which 5 were waited for; matrix products, arithmetic and copies ran while one was open for 4% of the time, Pallas kernels for 0%

profile of v6, /device:TPU:0, one launch (start us, length us, event | category | flops | bytes accessed | tf_op | source)
XLA Modules:
  0.0 220.8 jit_solution(7136279273830050331)
XLA Ops:
  7.2 0.0 copy-start
  7.2 0.0 all-gather.4.cloned.1.call-start
  7.2 1.3 stack_reshape.7
  8.5 0.0 copy-start.6
  8.5 1.8 stack_reshape.6
  10.3 1.2 pad_maximum_fusion
  11.5 16.4 %all_to_all.43 = bf16[32,4,2,576]{3,0,2,1:T(8,128)(2,1)S(1)} all-to-all(bf16[32,4,2,576]{3,0,2,1:T(8,128)(2,1)S(1)} %copy.82), channel_id=1, replica_groups=mesh['seq'=8,'head'=4] {'head'}, dimensions={1} | all-to-all | bytes 589824 | tf_op jit(solution)/shard_map/all_to_all | solution.py:68
  27.9 0.7 copy-done.1
  28.6 1.0 copy.83
  29.6 1.9 reshape.119
  31.5 0.0 all-gather.4.cloned.1.call-update
  31.6 1.1 reshape.122
  32.7 0.7 copy.86
  33.4 3.3 %all-to-all-start.1 = ((bf16[32,4,576]{2,0,1:T(8,128)(2,1)}), bf16[32,4,576]{2,0,1:T(8,128)(2,1)S(1)}, u32[]{:S(2)}, u32[]{:S(2)}) async-start(bf16[32,4,576]{2,0,1:T(8,128)(2,1)} %copy.86), calls=%async_computation.1 | async-start | bytes 327680 | tf_op jit(solution)/shard_map/all_to_all | solution.py:72
  36.7 0.0 reduce-scatter.3.cloned.1.call-start
  36.8 8.8 %all-gather = s32[8,1,128]{2,1,0:T(1,128)S(1)} all-gather(s32[1,1,128]{2,1,0:T(1,128)S(1)} %bitcast.71), channel_id=1, replica_groups=mesh['seq'=8,'head'=4] {'seq'}, dimensions={0}, use_global_device_ids=true | all-gather | bytes 4608 | tf_op jit(solution)/shard_map/all_gather | solution.py:79
  45.6 0.9 fusion.21
  46.4 0.0 all-to-all-done.1
  46.4 1.1 reshape_reshape.3
  47.5 12.4 %all-gather.4.cloned.1.call-done = bf16[1024,1152]{1,0:T(8,128)(2,1)} async-done(((bf16[128,1152]{1,0:T(8,128)(2,1)}), bf16[1024,1152]{1,0:T(8,128)(2,1)}) %all-gather.4.cloned.1.call-update) | async-done | bytes 2359312 | tf_op jit(solution)/shard_map/all_gather | solution.py:81
  59.9 3.9 %fusion.45 = (bf16[1024,576]{1,0:T(8,128)(2,1)}, bf16[1024,576]{1,0:T(8,128)(2,1)}) fusion(bf16[1024,1152]{1,0:T(8,128)(2,1)} %all-gather.4.cloned.1.call-done), kind=kLoop, calls=%fused_computation.61 | loop fusion | bytes 4718592 | tf_op jit(solution)/shard_map/slice | solution.py:97
  63.8 2.5 %copy.84 = bf16[1024,576]{0,1:T(8,128)(2,1)} copy(bf16[1024,576]{1,0:T(8,128)(2,1)} %get-tuple-element.21) | data formatting | bytes 2359296 | tf_op jit(solution)/shard_map/slice | solution.py:98
  66.2 2.4 %copy.85 = bf16[1024,576]{0,1:T(8,128)(2,1)} copy(bf16[1024,576]{1,0:T(8,128)(2,1)} %get-tuple-element.20) | data formatting | bytes 2359296 | tf_op jit(solution)/shard_map/slice | solution.py:97
  68.7 0.0 copy-done.3
  68.7 5.3 %fusion.46 = (f32[9,128]{1,0:T(8,128)S(1)}, bf16[9,128,1024]{1,2,0:T(8,128)(2,1)}) fusion(pred[128,1024]{0,1:T(8,128)(4,1)S(1)} %copy-done.3, bf16[1024,9,64]{0,2,1:T(8,128)(2,1)} %bitcast.67, bf16[128,9,64]{2,1,0:T(8,128)(2,1)} %reshape_reshape.3), kind=kOutput, calls=%fused_computation.62 | convolution fusion | flops 158073856 | bytes 3822080 | tf_op jit(solution)/shard_map/sub | solution.py:112
  73.9 2.7 %fusion.18 = bf16[128,9,64]{0,2,1:T(8,128)(2,1)S(1)} fusion(bf16[1024,9,64]{0,2,1:T(8,128)(2,1)} %bitcast.66, bf16[9,128,1024]{1,2,0:T(8,128)(2,1)} %get-tuple-element.29, f32[128,9]{0,1:T(8,128)S(1)} %bitcast.72), kind=kOutput, calls=%fused_computation.22 | convolution fusion | flops 151142400 | bytes 3691008 | tf_op jit(solution)/shard_map/hqk,khd->qhd/dot_general | solution.py:32
  76.6 0.0 copy-start.5
  76.7 0.0 copy-start.4
  76.7 0.1 copy-done.2
  76.7 1.5 convolution_convert_fusion.1
  78.2 0.0 reduce-scatter.3.cloned.1.call-update
  78.3 0.0 all-gather.6.cloned.1.call-start
  78.3 0.1 copy.89
  78.4 0.1 eq.88
  78.5 0.1 fusion.38
  78.6 0.1 reduce_window_sum.11
  78.7 0.2 select_reduce_fusion
  78.9 0.1 reduce_sum.50
  79.0 0.1 copy.90
  79.1 0.1 fusion.39
  79.2 21.3 %reduce-scatter.3.cloned.1.call-done = bf16[32,2304]{1,0:T(8,128)(2,1)} async-done(((bf16[128,2304]{1,0:T(8,128)(2,1)}), bf16[32,2304]{1,0:T(8,128)(2,1)}) %reduce-scatter.3.cloned.1.call-update) | async-done | bytes 147472 | tf_op jit(solution)/shard_map/reduce_scatter | solution.py:120
  100.4 1.2 fusion.25
  101.6 1.1 convolution_convert_fusion.2
  102.7 1.9 reshape_broadcast_in_dim_reshape.3
  104.6 14.6 %all_to_all.44 = bf16[8,9,2304]{2,1,0:T(8,128)(2,1)} all-to-all(bf16[8,9,2304]{2,1,0:T(8,128)(2,1)} %reshape_broadcast_in_dim_reshape.3), channel_id=1, replica_groups=mesh['seq'=8,'head'=4] {'seq'}, dimensions={0} | all-to-all | bytes 663552 | tf_op jit(solution)/shard_map/all_to_all | solution.py:152
  119.2 1.9 reshape.124
  121.2 0.0 all-gather.6.cloned.1.call-update
  121.2 0.0 reduce-scatter.5.cloned.1.call-start
  121.2 29.6 %all-gather.6.cloned.1.call-done = bf16[288,2304]{1,0:T(8,128)(2,1)} async-done(((bf16[72,2304]{1,0:T(8,128)(2,1)}), bf16[288,2304]{1,0:T(8,128)(2,1)}) %all-gather.6.cloned.1.call-update) | async-done | bytes 1327120 | tf_op jit(solution)/shard_map/all_gather | solution.py:155
  150.8 4.5 %fusion.51 = f32[288,720]{1,0:T(8,128)} fusion(bf16[288,2304]{1,0:T(8,128)(2,1)} %all-gather.6.cloned.1.call-done, bf16[2304,720]{0,1:T(8,128)(2,1)} %param.20), kind=kOutput, calls=%fused_computation.63 | convolution fusion | flops 955514880 | bytes 5474304 | tf_op jit(solution)/shard_map/dot_general | solution.py:156
  155.3 6.5 %convolution_convert_fusion = bf16[288,2304]{1,0:T(8,128)(2,1)} fusion(bf16[2304,720]{0,1:T(8,128)(2,1)S(1)} %copy-done, bf16[288,2304]{1,0:T(8,128)(2,1)} %all-gather.6.cloned.1.call-done, bf16[2304,720]{0,1:T(8,128)(2,1)} %param.21, f32[288,720]{1,0:T(8,128)} %fusion.51), kind=kOutput, calls=%fused_computation.3 | convolution fusion | flops 1912937472 | bytes 10119168 | tf_op jit(solution)/shard_map/dot_general | solution.py:159
  161.8 0.0 reduce-scatter.5.cloned.1.call-update
  161.8 1.0 copy.91
  162.8 0.7 slice_bitcast_fusion
  163.6 1.7 copy.92
  165.3 1.7 copy.93
  167.0 0.2 fusion.36
  167.2 25.4 %reduce-scatter.5.cloned.1.call-done = bf16[72,2304]{1,0:T(8,128)(2,1)} async-done(((bf16[288,2304]{1,0:T(8,128)(2,1)}), bf16[72,2304]{1,0:T(8,128)(2,1)}) %reduce-scatter.5.cloned.1.call-update) | async-done | bytes 331792 | tf_op jit(solution)/shard_map/reduce_scatter | solution.py:162
  192.6 1.9 reshape.125
  194.5 4.2 %all-to-all-start.3 = ((bf16[8,9,2304]{2,1,0:T(8,128)(2,1)}), bf16[8,9,2304]{2,1,0:T(8,128)(2,1)}, u32[]{:S(2)}, u32[]{:S(2)}) async-start(bf16[8,9,2304]{2,1,0:T(8,128)(2,1)} %reshape.125), calls=%async_computation.5 | async-start | bytes 1179648 | tf_op jit(solution)/shard_map/all_to_all | solution.py:163
  198.8 10.4 %all-to-all-done.3 = bf16[8,9,2304]{2,1,0:T(8,128)(2,1)} async-done(((bf16[8,9,2304]{2,1,0:T(8,128)(2,1)}), bf16[8,9,2304]{2,1,0:T(8,128)(2,1)}, u32[]{:S(2)}, u32[]{:S(2)}) %all-to-all-start.3) | async-done | bytes 331808 | tf_op jit(solution)/shard_map/all_to_all | solution.py:163
  209.2 1.9 reshape.126
  211.1 1.2 convolution_multiply_fusion.1
  212.3 1.9 fusion.5
  (16 shorter events, 0.1 us)
Async XLA Ops:
  7.2 148.2 %copy-start = (bf16[2304,720]{0,1:T(8,128)(2,1)S(1)}, bf16[2304,720]{0,1:T(8,128)(2,1)}, u32[]{:S(2)}) copy-start(bf16[2304,720]{0,1:T(8,128)(2,1)} %param.22) | copy-start | bytes 9953284
  7.2 52.7 %all-gather.4.cloned.1.call-start = ((), (), s32[]{:S(2)}) async-start(), calls=%async_computation.6 | async-start | bytes 2654208 | tf_op jit(solution)/shard_map/all_gather | solution.py:81
  8.5 28.3 %copy-start.6 = (s32[128]{0:T(128)S(1)}, s32[128]{0:T(128)}, u32[]{:S(2)}) copy-start(s32[128]{0:T(128)} %param.18) | copy-start | bytes 1540
  27.9 0.7 copy-start.1
  33.4 13.0 %all-to-all-start.1 = ((bf16[32,4,576]{2,0,1:T(8,128)(2,1)}), bf16[32,4,576]{2,0,1:T(8,128)(2,1)S(1)}, u32[]{:S(2)}, u32[]{:S(2)}) async-start(bf16[32,4,576]{2,0,1:T(8,128)(2,1)} %copy.86), calls=%async_computation.1 | async-start | bytes 327680 | tf_op jit(solution)/shard_map/all_to_all | solution.py:72
  36.7 63.7 %reduce-scatter.3.cloned.1.call-start = ((), (), s32[]{:S(2)}) async-start(), calls=%async_computation.7 | async-start | bytes 737280 | tf_op jit(solution)/shard_map/reduce_scatter | solution.py:120
  63.8 4.9 %copy-start.3 = (pred[128,1024]{0,1:T(8,128)(4,1)S(1)}, pred[128,1024]{0,1:T(8,128)(4,1)}, u32[]{:S(2)}) copy-start(pred[128,1024]{0,1:T(8,128)(4,1)} %fusion.21) | copy-start | bytes 393220
  73.9 2.8 %copy-start.2 = (bf16[576,2304]{1,0:T(8,128)(2,1)S(1)}, bf16[576,2304]{1,0:T(8,128)(2,1)}, u32[]{:S(2)}) copy-start(bf16[576,2304]{1,0:T(8,128)(2,1)} %param.23) | copy-start | bytes 7962628
  76.6 1.7 copy-start.5
  76.7 24.9 %copy-start.4 = (f32[2304]{0:T(1024)S(1)}, f32[2304]{0:T(1024)}, u32[]{:S(2)}) copy-start(f32[2304]{0:T(1024)} %param.16) | copy-start | bytes 27652
  78.3 72.6 %all-gather.6.cloned.1.call-start = ((), (), s32[]{:S(2)}) async-start(), calls=%async_computation.8 | async-start | bytes 1658880 | tf_op jit(solution)/shard_map/all_gather | solution.py:155
  121.2 71.4 %reduce-scatter.5.cloned.1.call-start = ((), (), s32[]{:S(2)}) async-start(), calls=%async_computation.9 | async-start | bytes 1658880 | tf_op jit(solution)/shard_map/reduce_scatter | solution.py:162
  161.8 5.2 %copy-start.7 = (bf16[2304,8]{0,1:T(8,128)(2,1)S(1)}, bf16[2304,8]{0,1:T(8,128)(2,1)}, u32[]{:S(2)}) copy-start(bf16[2304,8]{0,1:T(8,128)(2,1)} %param.17) | copy-start | bytes 110596
  194.5 14.7 %all-to-all-start.3 = ((bf16[8,9,2304]{2,1,0:T(8,128)(2,1)}), bf16[8,9,2304]{2,1,0:T(8,128)(2,1)}, u32[]{:S(2)}, u32[]{:S(2)}) async-start(bf16[8,9,2304]{2,1,0:T(8,128)(2,1)} %reshape.125), calls=%async_computation.5 | async-start | bytes 1179648 | tf_op jit(solution)/shard_map/all_to_all | solution.py:163
Sparse Core Ops, SparseCore 0:
  31.7 28.1 all-gather.3
  78.4 22.0 reduce-scatter.2
  121.3 29.4 all-gather.5
  161.9 30.6 reduce-scatter.4

commit v7 on v6

--- a/solution.py
+++ b/solution.py
@@ -138,21 +138,35 @@
     route_rank = jnp.sum(before_count * flat_hot, -1)
     slot_ids = (expert_ids.reshape(-1) * CAP + route_rank).reshape(tok_local, route_count)
     slot_total = expert_count * CAP
-    dispatch = jnp.any(
-        slot_ids[None, :, :] == jnp.arange(slot_total, dtype=jnp.int32)[:, None, None], -1
+    normed_group = lax.all_gather(normed, "head", axis=0, tiled=True)
+    ids_group = lax.all_gather(expert_ids, "head", axis=0, tiled=True).reshape(
+        head_count, tok_local * route_count
+    )
+    group_hot = (
+        ids_group[:, :, None] == jnp.arange(expert_count, dtype=jnp.int32)[None, None, :]
+    ).astype(jnp.int32)
+    group_rank = jnp.sum((jnp.cumsum(group_hot, 1) - group_hot) * group_hot, -1)
+    source_place = jnp.arange(head_count, dtype=jnp.int32)[:, None]
+    row_ids = ((ids_group * head_count + source_place) * CAP + group_rank).reshape(
+        head_count * tok_local, route_count
+    )
+    row_total = expert_count * head_count * CAP
+    group_dispatch = jnp.any(
+        row_ids[None, :, :] == jnp.arange(row_total, dtype=jnp.int32)[:, None, None], -1
     ).astype(jnp.bfloat16)
     packed = (
-        jnp.dot(dispatch, normed, preferred_element_type=jnp.float32)
+        jnp.dot(group_dispatch, normed_group, preferred_element_type=jnp.float32)
         .astype(jnp.bfloat16)
-        .reshape(expert_count, CAP, D)
-    )
-    outgoing = jnp.broadcast_to(packed[:, None], (expert_count, replicas, CAP, D)).reshape(
-        seq_count, CAP, D
-    )
+        .reshape(expert_count, head_count * CAP, D)
+    )
+    outgoing = jnp.broadcast_to(
+        packed[:, None], (expert_count, replicas, head_count * CAP, D)
+    ).reshape(seq_count, head_count * CAP, D)
     arrived = lax.all_to_all(outgoing, "seq", split_axis=0, concat_axis=0, tiled=True)
-    slot_count = arrived.shape[1]
-    flat_rows = arrived.reshape(seq_count * slot_count, D)
-    group_rows = lax.all_gather(flat_rows, "head", axis=0, tiled=True)
+    slot_count = CAP
+    group_rows = jnp.swapaxes(arrived.reshape(seq_count, head_count, CAP, D), 0, 1).reshape(
+        head_count * seq_count * CAP, D
+    )
     gate_act = jnp.dot(group_rows, gate_weight, preferred_element_type=jnp.float32)
     up_act = jnp.dot(group_rows, up_weight, preferred_element_type=jnp.float32)
     hidden = (jax.nn.silu(gate_act) * up_act).astype(jnp.bfloat16)

time: 222 us -> 221 us (level)
  waiting for transfers between devices: 99.1 us -> 51.7 us
  blocking collectives: 39.8 us -> 75.9 us
  local copies, waits for them, and re-layouts: 31.7 us -> 36.3 us
  other arithmetic: 3.69 us -> 8.18 us
    all_gather x1 -> x0, waiting for transfers between devices: 29.6 us -> none  [per_device(): group_rows = lax.all_gather(flat_rows, 'head', axis=0, tiled=True)]
    all_gather x0 -> x2, blocking collectives: none -> 27.1 us  [the longest x1 16.2 us: per_device(): normed_group = lax.all_gather(normed, 'head', axis=0, tiled=True)]
    reduce_scatter x1, waiting for transfers between devices: 21.3 us -> 6.99 us  [per_device(): lax.psum_scatter(jnp.dot(attention, out_weight, preferred_element_type=jn...]
    all_to_all x1, blocking collectives: 14.6 us -> 23.6 us  [per_device(): lax.all_to_all(outgoing, 'seq', split_axis=0, concat_axis=0, tiled=True)]
    reduce_scatter x1, waiting for transfers between devices: 25.4 us -> 21.9 us  [per_device(): lax.psum_scatter(partial_out, 'head', scatter_dimension=0, tiled=True)]
    unnamed x19 -> x21, local copies, waits for them, and re-layouts: 4.31 us -> 5.01 us
  transfers between devices with their start and end apart: 6 -> 5, of which waited for: 5 -> 4; matrix products, arithmetic and copies ran while one was open for 4% -> 7% of each run, Pallas kernels for 0% -> 0%
where the time goes in v7:
time: 221 us; the launch traced here: 220 us
  blocking collectives  75.9 us (34%)
  waiting for transfers between devices  51.7 us (23%)
  local copies, waits for them, and re-layouts  36.3 us (16%)
  matrix products  26.2 us (12%)
  between operations  13.9 us (6%)
  other arithmetic  8.18 us (4%)
  starting transfers between devices  7.65 us (3%)
    all_to_all x1, blocking collectives, per_device(): lax.all_to_all(outgoing, 'seq', split_axis=0, concat_axis=0, tiled=True)  23.6 us
    reduce_scatter x1, waiting for transfers between devices, per_device(): lax.psum_scatter(partial_out, 'head', scatter_dimension=0, tiled=True)  21.9 us
    all_to_all x1, blocking collectives, per_device(): lax.all_to_all(joined_stack, 'head', split_axis=1, concat_axis=0, tiled=T...  16.4 us
    all_gather x1, blocking collectives, per_device(): normed_group = lax.all_gather(normed, 'head', axis=0, tiled=True)  16.2 us
    all_gather x1, waiting for transfers between devices, per_device(): joined_window = lax.all_gather(joined_head, 'seq', axis=0, tiled=True)  12.4 us
    all_gather x1, blocking collectives, per_device(): lax.all_gather(expert_ids, 'head', axis=0, tiled=True)  10.9 us
    all_to_all x1, waiting for transfers between devices, per_device(): lax.all_to_all(shard_out.reshape(seq_count, slot_count, D), 'seq', split_...  10.4 us
    all_gather x1, blocking collectives, per_device(): all_segments = lax.all_gather(segment_ids, 'seq', axis=0, tiled=True)  8.76 us
  transfers between devices with their start and end apart: 5, of which 4 were waited for; matrix products, arithmetic and copies ran while one was open for 7% of the time, Pallas kernels for 0%

profile of v7, /device:TPU:0, one launch (start us, length us, event | category | flops | bytes accessed | tf_op | source)
XLA Modules:
  0.0 219.9 jit_solution(18395998172098133359)
XLA Ops:
  7.2 1.3 stack_reshape.7
  8.5 1.8 stack_reshape.6
  10.3 1.2 pad_maximum_fusion
  11.5 16.4 %all_to_all.43 = bf16[32,4,2,576]{3,0,2,1:T(8,128)(2,1)S(1)} all-to-all(bf16[32,4,2,576]{3,0,2,1:T(8,128)(2,1)S(1)} %copy.108), channel_id=1, replica_groups=mesh['seq'=8,'head'=4] {'head'}, dimensions={1} | all-to-all | bytes 589824 | tf_op jit(solution)/shard_map/all_to_all | solution.py:68
  27.9 0.7 copy-done.1
  28.6 1.0 copy.109
  29.6 1.9 reshape.130
  31.6 1.1 reshape.133
  32.7 0.7 copy.112
  33.4 3.3 %all-to-all-start.1 = ((bf16[32,4,576]{2,0,1:T(8,128)(2,1)}), bf16[32,4,576]{2,0,1:T(8,128)(2,1)S(1)}, u32[]{:S(2)}, u32[]{:S(2)}) async-start(bf16[32,4,576]{2,0,1:T(8,128)(2,1)} %copy.112), calls=%async_computation.1 | async-start | bytes 327680 | tf_op jit(solution)/shard_map/all_to_all | solution.py:72
  36.8 8.8 %all-gather = s32[8,1,128]{2,1,0:T(1,128)S(1)} all-gather(s32[1,1,128]{2,1,0:T(1,128)S(1)} %bitcast.83), channel_id=1, replica_groups=mesh['seq'=8,'head'=4] {'seq'}, dimensions={0}, use_global_device_ids=true | all-gather | bytes 4608 | tf_op jit(solution)/shard_map/all_gather | solution.py:79
  45.5 0.9 fusion.21
  46.4 1.1 reshape_reshape.3
  47.5 12.4 %all-gather.4.cloned.1.call-done = bf16[1024,1152]{1,0:T(8,128)(2,1)} async-done(((bf16[128,1152]{1,0:T(8,128)(2,1)}), bf16[1024,1152]{1,0:T(8,128)(2,1)}) %all-gather.4.cloned.1.call-update) | async-done | bytes 2359312 | tf_op jit(solution)/shard_map/all_gather | solution.py:81
  59.9 3.9 %fusion.43 = (bf16[1024,576]{1,0:T(8,128)(2,1)}, bf16[1024,576]{1,0:T(8,128)(2,1)}) fusion(bf16[1024,1152]{1,0:T(8,128)(2,1)} %all-gather.4.cloned.1.call-done), kind=kLoop, calls=%fused_computation.65 | loop fusion | bytes 4718592 | tf_op jit(solution)/shard_map/slice | solution.py:97
  63.8 2.5 %copy.110 = bf16[1024,576]{0,1:T(8,128)(2,1)} copy(bf16[1024,576]{1,0:T(8,128)(2,1)} %get-tuple-element.19) | data formatting | bytes 2359296 | tf_op jit(solution)/shard_map/slice | solution.py:98
  66.2 2.4 %copy.111 = bf16[1024,576]{0,1:T(8,128)(2,1)} copy(bf16[1024,576]{1,0:T(8,128)(2,1)} %get-tuple-element.18) | data formatting | bytes 2359296 | tf_op jit(solution)/shard_map/slice | solution.py:97
  68.7 5.3 %fusion.44 = (f32[9,128]{1,0:T(8,128)S(1)}, bf16[9,128,1024]{1,2,0:T(8,128)(2,1)}) fusion(pred[128,1024]{0,1:T(8,128)(4,1)S(1)} %copy-done.5, bf16[1024,9,64]{0,2,1:T(8,128)(2,1)} %bitcast.77, bf16[128,9,64]{2,1,0:T(8,128)(2,1)} %reshape_reshape.3), kind=kOutput, calls=%fused_computation.66 | convolution fusion | flops 158073856 | bytes 3822080 | tf_op jit(solution)/shard_map/sub | solution.py:112
  73.9 2.7 %fusion.18 = bf16[128,9,64]{0,2,1:T(8,128)(2,1)S(1)} fusion(bf16[1024,9,64]{0,2,1:T(8,128)(2,1)} %bitcast.76, bf16[9,128,1024]{1,2,0:T(8,128)(2,1)} %get-tuple-element.27, f32[128,9]{0,1:T(8,128)S(1)} %bitcast.84), kind=kOutput, calls=%fused_computation.22 | convolution fusion | flops 151142400 | bytes 3691008 | tf_op jit(solution)/shard_map/hqk,khd->qhd/dot_general | solution.py:32
  76.7 0.1 copy-done.2
  76.8 1.5 convolution_convert_fusion.2
  78.3 10.9 %all-gather.1 = s32[4,32,2]{1,2,0:T(2,128)S(1)} all-gather(s32[1,32,2]{1,2,0:T(2,128)S(1)} %bitcast.82), channel_id=1, replica_groups=mesh['seq'=8,'head'=4] {'head'}, dimensions={0}, use_global_device_ids=true | all-gather | bytes 1280 | tf_op jit(solution)/shard_map/all_gather | solution.py:142
  89.3 0.1 copy.118
  89.4 0.1 copy.119
  89.4 0.8 fusion.36
  90.2 1.7 reduce_window_sum.23
  91.9 1.1 select_reduce_fusion
  93.0 0.1 reduce_sum.63
  93.1 0.1 copy.120
  93.2 0.1 reshape.145
  93.3 0.1 add.77
  93.4 0.1 fusion.28
  93.4 7.0 %reduce-scatter.3.cloned.1.call-done = bf16[32,2304]{1,0:T(8,128)(2,1)} async-done(((bf16[128,2304]{1,0:T(8,128)(2,1)}), bf16[32,2304]{1,0:T(8,128)(2,1)}) %reduce-scatter.3.cloned.1.call-update) | async-done | bytes 147472 | tf_op jit(solution)/shard_map/reduce_scatter | solution.py:120
  100.4 1.1 fusion.25
  101.5 1.0 fusion.27
  102.6 0.7 copy-done.4
  103.2 16.2 %all_gather.15 = bf16[128,2304]{1,0:T(8,128)(2,1)S(1)} all-gather(bf16[32,2304]{1,0:T(8,128)(2,1)S(1)} %fusion.27), channel_id=1, replica_groups=mesh['seq'=8,'head'=4] {'head'}, dimensions={0}, use_global_device_ids=true | all-gather | bytes 737280 | tf_op jit(solution)/shard_map/all_gather | solution.py:141
  119.4 1.6 convolution_convert_fusion.1
  121.0 2.4 %reshape_broadcast_in_dim_reshape.3 = bf16[8,36,2304]{2,1,0:T(8,128)(2,1)} reshape(bf16[288,2304]{1,0:T(8,128)(2,1)} %convolution_convert_fusion.1) | data formatting | bytes 2654208 | tf_op jit(solution)/shard_map/reshape;broadcast_in_dim;reshape | solution.py:164
  123.4 23.6 %all_to_all.44 = bf16[8,36,2304]{2,1,0:T(8,128)(2,1)S(1)} all-to-all(bf16[8,36,2304]{2,1,0:T(8,128)(2,1)} %reshape_broadcast_in_dim_reshape.3), channel_id=1, replica_groups=mesh['seq'=8,'head'=4] {'seq'}, dimensions={0} | all-to-all | bytes 2654208 | tf_op jit(solution)/shard_map/all_to_all | solution.py:165
  147.0 0.2 copy.121
  147.2 1.8 copy.122
  149.0 2.8 %reshape.136 = bf16[288,2304]{1,0:T(8,128)(2,1)} reshape(bf16[4,8,9,2304]{3,2,1,0:T(8,128)(2,1)} %copy.122) | data formatting | bytes 2654208 | tf_op jit(solution)/shard_map/reshape | solution.py:167
  151.8 4.5 %fusion.50 = f32[288,720]{1,0:T(8,128)} fusion(bf16[288,2304]{1,0:T(8,128)(2,1)} %reshape.136, bf16[2304,720]{0,1:T(8,128)(2,1)} %param.20), kind=kOutput, calls=%fused_computation.68 | convolution fusion | flops 955514880 | bytes 5474304 | tf_op jit(solution)/shard_map/dot_general | solution.py:170
  156.3 6.5 %convolution_convert_fusion = bf16[288,2304]{1,0:T(8,128)(2,1)} fusion(bf16[2304,720]{0,1:T(8,128)(2,1)S(1)} %copy-done, bf16[288,2304]{1,0:T(8,128)(2,1)} %reshape.136, bf16[2304,720]{0,1:T(8,128)(2,1)} %param.21, f32[288,720]{1,0:T(8,128)} %fusion.50), kind=kOutput, calls=%fused_computation.3 | convolution fusion | flops 1912937472 | bytes 10119168 | tf_op jit(solution)/shard_map/dot_general | solution.py:173
  162.8 0.1 copy.115
  162.9 0.1 eq.103
  163.0 0.1 fusion.37
  163.1 0.1 reduce_window_sum.22
  163.2 0.2 select_reduce_fusion.1
  163.4 0.1 reduce_sum.61
  163.5 0.1 copy.116
  163.6 1.0 copy.123
  164.6 0.7 slice_bitcast_fusion
  165.3 1.7 copy.124
  167.1 1.7 copy.125
  168.8 1.0 fusion.49
  169.8 21.9 %reduce-scatter.5.cloned.1.call-done = bf16[72,2304]{1,0:T(8,128)(2,1)} async-done(((bf16[288,2304]{1,0:T(8,128)(2,1)}), bf16[72,2304]{1,0:T(8,128)(2,1)}) %reduce-scatter.5.cloned.1.call-update) | async-done | bytes 331792 | tf_op jit(solution)/shard_map/reduce_scatter | solution.py:176
  191.7 1.9 reshape.137
  193.6 4.2 %all-to-all-start.3 = ((bf16[8,9,2304]{2,1,0:T(8,128)(2,1)}), bf16[8,9,2304]{2,1,0:T(8,128)(2,1)}, u32[]{:S(2)}, u32[]{:S(2)}) async-start(bf16[8,9,2304]{2,1,0:T(8,128)(2,1)} %reshape.137), calls=%async_computation.5 | async-start | bytes 1179648 | tf_op jit(solution)/shard_map/all_to_all | solution.py:177
  197.8 10.4 %all-to-all-done.3 = bf16[8,9,2304]{2,1,0:T(8,128)(2,1)} async-done(((bf16[8,9,2304]{2,1,0:T(8,128)(2,1)}), bf16[8,9,2304]{2,1,0:T(8,128)(2,1)}, u32[]{:S(2)}, u32[]{:S(2)}) %all-to-all-start.3) | async-done | bytes 331808 | tf_op jit(solution)/shard_map/all_to_all | solution.py:177
  208.3 1.9 reshape.138
  210.2 1.2 convolution_multiply_fusion.1
  211.4 1.9 fusion.5
  (32 shorter events, 0.3 us)
Async XLA Ops:
  7.2 149.1 %copy-start = (bf16[2304,720]{0,1:T(8,128)(2,1)S(1)}, bf16[2304,720]{0,1:T(8,128)(2,1)}, u32[]{:S(2)}) copy-start(bf16[2304,720]{0,1:T(8,128)(2,1)} %param.22) | copy-start | bytes 9953284
  7.2 52.7 %all-gather.4.cloned.1.call-start = ((), (), s32[]{:S(2)}) async-start(), calls=%async_computation.6 | async-start | bytes 2654208 | tf_op jit(solution)/shard_map/all_gather | solution.py:81
  8.5 28.3 %copy-start.8 = (s32[128]{0:T(128)S(1)}, s32[128]{0:T(128)}, u32[]{:S(2)}) copy-start(s32[128]{0:T(128)} %param.18) | copy-start | bytes 1540
  27.9 0.7 copy-start.1
  33.4 13.0 %all-to-all-start.1 = ((bf16[32,4,576]{2,0,1:T(8,128)(2,1)}), bf16[32,4,576]{2,0,1:T(8,128)(2,1)S(1)}, u32[]{:S(2)}, u32[]{:S(2)}) async-start(bf16[32,4,576]{2,0,1:T(8,128)(2,1)} %copy.112), calls=%async_computation.1 | async-start | bytes 327680 | tf_op jit(solution)/shard_map/all_to_all | solution.py:72
  36.7 63.7 %reduce-scatter.3.cloned.1.call-start = ((), (), s32[]{:S(2)}) async-start(), calls=%async_computation.7 | async-start | bytes 737280 | tf_op jit(solution)/shard_map/reduce_scatter | solution.py:120
  63.8 4.9 %copy-start.5 = (pred[128,1024]{0,1:T(8,128)(4,1)S(1)}, pred[128,1024]{0,1:T(8,128)(4,1)}, u32[]{:S(2)}) copy-start(pred[128,1024]{0,1:T(8,128)(4,1)} %fusion.21) | copy-start | bytes 393220
  73.9 2.8 %copy-start.2 = (bf16[576,2304]{1,0:T(8,128)(2,1)S(1)}, bf16[576,2304]{1,0:T(8,128)(2,1)}, u32[]{:S(2)}) copy-start(bf16[576,2304]{1,0:T(8,128)(2,1)} %param.23) | copy-start | bytes 7962628
  76.7 1.7 copy-start.6
  76.8 23.7 %copy-start.3 = (bf16[32,2304]{1,0:T(8,128)(2,1)S(1)}, bf16[32,2304]{1,0:T(8,128)(2,1)}, u32[]{:S(2)}) copy-start(bf16[32,2304]{1,0:T(8,128)(2,1)} %param.15) | copy-start | bytes 442372
  76.8 24.8 %copy-start.7 = (f32[2304]{0:T(1024)S(1)}, f32[2304]{0:T(1024)}, u32[]{:S(2)}) copy-start(f32[2304]{0:T(1024)} %param.16) | copy-start | bytes 27652
  78.3 113.4 %reduce-scatter.5.cloned.1.call-start = ((), (), s32[]{:S(2)}) async-start(), calls=%async_computation.8 | async-start | bytes 1658880 | tf_op jit(solution)/shard_map/reduce_scatter | solution.py:176
  102.5 0.7 copy-start.4
  193.6 14.7 %all-to-all-start.3 = ((bf16[8,9,2304]{2,1,0:T(8,128)(2,1)}), bf16[8,9,2304]{2,1,0:T(8,128)(2,1)}, u32[]{:S(2)}, u32[]{:S(2)}) async-start(bf16[8,9,2304]{2,1,0:T(8,128)(2,1)} %reshape.137), calls=%async_computation.5 | async-start | bytes 1179648 | tf_op jit(solution)/shard_map/all_to_all | solution.py:177
Sparse Core Ops, SparseCore 0:
  31.7 28.1 all-gather.3
  78.4 21.9 reduce-scatter.2
  162.9 28.6 reduce-scatter.4

commit v8 on v6

--- a/solution.py
+++ b/solution.py
@@ -58,17 +58,18 @@
     expert_count = router_weight.shape[1]
     replicas = seq_count // expert_count
     seq_place = lax.axis_index("seq")
-    joined_stack = jnp.stack(
+    joined_rows = jnp.concatenate(
         (
             key_rows.reshape(tok_local, head_count, group_width),
             value_rows.reshape(tok_local, head_count, group_width),
         ),
         2,
     )
-    joined_by_head = lax.all_to_all(joined_stack, "head", split_axis=1, concat_axis=0, tiled=True)
-    key_head = joined_by_head[:, 0, 0]
-    value_head = joined_by_head[:, 0, 1]
-    joined_head = joined_by_head.reshape(stretch_len, 2 * group_width)
+    joined_head = lax.all_to_all(
+        joined_rows, "head", split_axis=1, concat_axis=0, tiled=True
+    ).reshape(stretch_len, 2 * group_width)
+    key_head = joined_head[:, :group_width]
+    value_head = joined_head[:, group_width:]
     query_head = lax.all_to_all(
         query_rows.reshape(tok_local, head_count, group_width),
         "head",
@@ -152,17 +153,33 @@
     arrived = lax.all_to_all(outgoing, "seq", split_axis=0, concat_axis=0, tiled=True)
     slot_count = arrived.shape[1]
     flat_rows = arrived.reshape(seq_count * slot_count, D)
-    group_rows = lax.all_gather(flat_rows, "head", axis=0, tiled=True)
-    gate_act = jnp.dot(group_rows, gate_weight, preferred_element_type=jnp.float32)
-    up_act = jnp.dot(group_rows, up_weight, preferred_element_type=jnp.float32)
-    hidden = (jax.nn.silu(gate_act) * up_act).astype(jnp.bfloat16)
-    partial_out = lax.dot_general(
-        hidden, down_weight, (((1,), (1,)), ((), ())), preferred_element_type=jnp.float32
-    ).astype(jnp.bfloat16)
-    shard_out = lax.psum_scatter(partial_out, "head", scatter_dimension=0, tiled=True)
-    returned = lax.all_to_all(
-        shard_out.reshape(seq_count, slot_count, D), "seq", split_axis=0, concat_axis=0, tiled=True
-    )
+    group_rows = lax.all_gather(flat_rows, "head", axis=0, tiled=True).reshape(
+        head_count, seq_count, slot_count, D
+    )
+    chunk_edges = (0, (slot_count + 1) // 2, slot_count)
+    returned_parts = []
+    for chunk_start, chunk_end in zip(chunk_edges[:-1], chunk_edges[1:]):
+        chunk_slots = chunk_end - chunk_start
+        chunk_rows = group_rows[:, :, chunk_start:chunk_end].reshape(
+            head_count * seq_count * chunk_slots, D
+        )
+        gate_act = jnp.dot(chunk_rows, gate_weight, preferred_element_type=jnp.float32)
+        up_act = jnp.dot(chunk_rows, up_weight, preferred_element_type=jnp.float32)
+        hidden = (jax.nn.silu(gate_act) * up_act).astype(jnp.bfloat16)
+        partial_out = lax.dot_general(
+            hidden, down_weight, (((1,), (1,)), ((), ())), preferred_element_type=jnp.float32
+        ).astype(jnp.bfloat16)
+        shard_out = lax.psum_scatter(partial_out, "head", scatter_dimension=0, tiled=True)
+        returned_parts.append(
+            lax.all_to_all(
+                shard_out.reshape(seq_count, chunk_slots, D),
+                "seq",
+                split_axis=0,
+                concat_axis=0,
+                tiled=True,
+            )
+        )
+    returned = jnp.concatenate(returned_parts, 1)
     by_slot = jnp.swapaxes(returned.reshape(expert_count, replicas, CAP, D), 1, 2).reshape(
         slot_total, replicas, D
     )

time: 222 us -> 236 us (1.063)
  local copies, waits for them, and re-layouts: 31.7 us -> 42 us
  waiting for transfers between devices: 99.1 us -> 89.7 us
  matrix products: 24.8 us -> 32.6 us
  starting transfers between devices: 7.7 us -> 11.8 us
    reshape x2 -> x7, local copies, waits for them, and re-layouts: 3.86 us -> 13.6 us  [the longest x2 4.47 us: per_device(): group_rows[:, :, chunk_start:chunk_end]]
    slice x0 -> x3, local copies, waits for them, and re-layouts: none -> 7.02 us  [the longest x2 5.22 us: per_device(): group_rows[:, :, chunk_start:chunk_end]]
    reduce_scatter x1 -> x2, waiting for transfers between devices: 25.4 us -> 19.1 us  [per_device(): lax.psum_scatter(partial_out, 'head', scatter_dimension=0, tiled=True)]
    dot_general x1 -> x2, matrix products: 6.48 us -> 10.7 us  [per_device(): lax.dot_general(hidden, down_weight, (((1,), (1,)), ((), ())), preferred_...]
    all_to_all x1 -> x2, starting transfers between devices: 4.19 us -> 8.07 us  [per_device(): lax.all_to_all(shard_out.reshape(seq_count, chunk_slots, D), 'seq', split...]
    dot_general x1 -> x2, matrix products: 4.48 us -> 8.01 us  [per_device(): jnp.dot(chunk_rows, gate_weight, preferred_element_type=jnp.float32)]
    concatenate x0 -> x2, other arithmetic: none -> 3.15 us  [the longest x1 2.05 us: per_device(): returned = jnp.concatenate(returned_parts, 1)]
    all_to_all x1 -> x2, waiting for transfers between devices: 10.4 us -> 7.28 us  [per_device(): lax.all_to_all(shard_out.reshape(seq_count, chunk_slots, D), 'seq', split...]
  transfers between devices with their start and end apart: 6 -> 8, of which waited for: 5 -> 6; matrix products, arithmetic and copies ran while one was open for 4% -> 12% of each run, Pallas kernels for 0% -> 0%
where the time goes in v8:
time: 236 us; the launch traced here: 235 us
  waiting for transfers between devices  89.7 us (38%)
  local copies, waits for them, and re-layouts  42 us (18%)
  blocking collectives  39.2 us (17%)
  matrix products  32.6 us (14%)
  between operations  14 us (6%)
  starting transfers between devices  11.8 us (5%)
  other arithmetic  5.67 us (2%)
    all_gather x1, waiting for transfers between devices, per_device(): lax.all_gather(flat_rows, 'head', axis=0, tiled=True)  29.6 us
    reduce_scatter x1, waiting for transfers between devices, per_device(): lax.psum_scatter(jnp.dot(attention, out_weight, preferred_element_type=jn...  21.3 us
    reduce_scatter x2, waiting for transfers between devices, per_device(): lax.psum_scatter(partial_out, 'head', scatter_dimension=0, tiled=True)  19.1 us
    all_to_all x1, blocking collectives, per_device(): lax.all_to_all(joined_rows, 'head', split_axis=1, concat_axis=0, tiled=True)  15.8 us
    all_to_all x1, blocking collectives, per_device(): lax.all_to_all(outgoing, 'seq', split_axis=0, concat_axis=0, tiled=True)  14.6 us
    all_gather x1, waiting for transfers between devices, per_device(): joined_window = lax.all_gather(joined_head, 'seq', axis=0, tiled=True)  12.4 us
    dot_general x2, matrix products, per_device(): lax.dot_general(hidden, down_weight, (((1,), (1,)), ((), ())), preferred_...  10.7 us
    all_gather x1, blocking collectives, per_device(): all_segments = lax.all_gather(segment_ids, 'seq', axis=0, tiled=True)  8.76 us
  transfers between devices with their start and end apart: 8, of which 6 were waited for; matrix products, arithmetic and copies ran while one was open for 12% of the time, Pallas kernels for 0%

profile of v8, /device:TPU:0, one launch (start us, length us, event | category | flops | bytes accessed | tf_op | source)
XLA Modules:
  0.0 234.9 jit_solution(4722647167637197679)
XLA Ops:
  7.2 0.0 all-gather.4.cloned.1.call-start
  7.2 1.3 reshape.138
  8.5 1.8 reshape.137
  10.3 1.1 pad_maximum_fusion.1
  11.4 15.8 %all_to_all.45 = bf16[32,4,1152]{2,0,1:T(8,128)(2,1)} all-to-all(bf16[32,4,1152]{2,0,1:T(8,128)(2,1)S(1)} %copy.74), channel_id=1, replica_groups=mesh['seq'=8,'head'=4] {'head'}, dimensions={1} | all-to-all | bytes 589824 | tf_op jit(solution)/shard_map/all_to_all | solution.py:68
  27.2 0.0 all-gather.4.cloned.1.call-update
  27.3 1.1 reshape.142
  28.4 0.7 copy.77
  29.1 3.3 %all-to-all-start.1 = ((bf16[32,4,576]{2,0,1:T(8,128)(2,1)}), bf16[32,4,576]{2,0,1:T(8,128)(2,1)S(1)}, u32[]{:S(2)}, u32[]{:S(2)}) async-start(bf16[32,4,576]{2,0,1:T(8,128)(2,1)} %copy.77), calls=%async_computation.1 | async-start | bytes 327680 | tf_op jit(solution)/shard_map/all_to_all | solution.py:73
  32.4 0.0 reduce-scatter.4.cloned.1.call-start
  32.5 8.8 %all-gather = s32[8,1,128]{2,1,0:T(1,128)S(1)} all-gather(s32[1,1,128]{2,1,0:T(1,128)S(1)} %bitcast.70), channel_id=1, replica_groups=mesh['seq'=8,'head'=4] {'seq'}, dimensions={0}, use_global_device_ids=true | all-gather | bytes 4608 | tf_op jit(solution)/shard_map/all_gather | solution.py:80
  41.3 0.9 fusion.22
  42.1 1.1 reshape_reshape.3
  43.2 12.4 %all-gather.4.cloned.1.call-done = bf16[1024,1152]{1,0:T(8,128)(2,1)} async-done(((bf16[128,1152]{1,0:T(8,128)(2,1)}), bf16[1024,1152]{1,0:T(8,128)(2,1)}) %all-gather.4.cloned.1.call-update) | async-done | bytes 2359312 | tf_op jit(solution)/shard_map/all_gather | solution.py:82
  55.6 3.9 %fusion.58 = (bf16[1024,576]{1,0:T(8,128)(2,1)}, bf16[1024,576]{1,0:T(8,128)(2,1)}) fusion(bf16[1024,1152]{1,0:T(8,128)(2,1)} %all-gather.4.cloned.1.call-done), kind=kLoop, calls=%fused_computation.75 | loop fusion | bytes 4718592 | tf_op jit(solution)/shard_map/slice | solution.py:98
  59.5 2.5 %copy.75 = bf16[1024,576]{0,1:T(8,128)(2,1)} copy(bf16[1024,576]{1,0:T(8,128)(2,1)} %get-tuple-element.21) | data formatting | bytes 2359296 | tf_op jit(solution)/shard_map/slice | solution.py:99
  62.0 2.4 %copy.76 = bf16[1024,576]{0,1:T(8,128)(2,1)} copy(bf16[1024,576]{1,0:T(8,128)(2,1)} %get-tuple-element.20) | data formatting | bytes 2359296 | tf_op jit(solution)/shard_map/slice | solution.py:98
  64.4 5.3 %fusion.60 = (f32[9,128]{1,0:T(8,128)S(1)}, bf16[9,128,1024]{1,2,0:T(8,128)(2,1)}) fusion(pred[128,1024]{0,1:T(8,128)(4,1)S(1)} %copy-done.2, bf16[1024,9,64]{0,2,1:T(8,128)(2,1)} %bitcast.66, bf16[128,9,64]{2,1,0:T(8,128)(2,1)} %reshape_reshape.3), kind=kOutput, calls=%fused_computation.77 | convolution fusion | flops 158073856 | bytes 3822080 | tf_op jit(solution)/shard_map/sub | solution.py:113
  69.6 2.7 %fusion.19 = bf16[128,9,64]{0,2,1:T(8,128)(2,1)S(1)} fusion(bf16[1024,9,64]{0,2,1:T(8,128)(2,1)} %bitcast.65, bf16[9,128,1024]{1,2,0:T(8,128)(2,1)} %get-tuple-element.29, f32[128,9]{0,1:T(8,128)S(1)} %bitcast.71), kind=kOutput, calls=%fused_computation.25 | convolution fusion | flops 151142400 | bytes 3691008 | tf_op jit(solution)/shard_map/hqk,khd->qhd/dot_general | solution.py:32
  72.4 0.1 copy-done.1
  72.5 1.5 convolution_convert_fusion.1
  73.9 0.0 reduce-scatter.4.cloned.1.call-update
  74.0 0.0 all-gather.6.cloned.1.call-start
  74.0 0.1 copy.80
  74.1 0.1 eq.88
  74.2 0.1 fusion.50
  74.3 0.1 reduce_window_sum.11
  74.4 0.2 select_reduce_fusion
  74.6 0.1 reduce_sum.50
  74.7 0.1 copy.81
  74.8 0.1 fusion.51
  74.9 21.3 %reduce-scatter.4.cloned.1.call-done = bf16[32,2304]{1,0:T(8,128)(2,1)} async-done(((bf16[128,2304]{1,0:T(8,128)(2,1)}), bf16[32,2304]{1,0:T(8,128)(2,1)}) %reduce-scatter.4.cloned.1.call-update) | async-done | bytes 147472 | tf_op jit(solution)/shard_map/reduce_scatter | solution.py:121
  96.2 1.2 fusion.35
  97.3 1.1 convolution_convert_fusion.3
  98.4 1.9 reshape_broadcast_in_dim_reshape.3
  100.3 14.6 %all_to_all.46 = bf16[8,9,2304]{2,1,0:T(8,128)(2,1)} all-to-all(bf16[8,9,2304]{2,1,0:T(8,128)(2,1)} %reshape_broadcast_in_dim_reshape.3), channel_id=1, replica_groups=mesh['seq'=8,'head'=4] {'seq'}, dimensions={0} | all-to-all | bytes 663552 | tf_op jit(solution)/shard_map/all_to_all | solution.py:153
  115.0 1.9 reshape.144
  116.9 0.0 reduce-scatter.8.cloned.1.call-start
  117.0 29.6 %all-gather.6.cloned.1.call-done = bf16[288,2304]{1,0:T(8,128)(2,1)} async-done(((bf16[72,2304]{1,0:T(8,128)(2,1)}), bf16[288,2304]{1,0:T(8,128)(2,1)}) %all-gather.6.cloned.1.call-update) | async-done | bytes 1327120 | tf_op jit(solution)/shard_map/all_gather | solution.py:156
  146.6 2.8 %reshape.145 = bf16[4,8,9,2304]{3,2,1,0:T(8,128)(2,1)} reshape(bf16[288,2304]{1,0:T(8,128)(2,1)} %all-gather.6.cloned.1.call-done) | data formatting | bytes 2654208 | tf_op jit(solution)/shard_map/reshape | solution.py:156
  149.3 2.9 %slice.45 = bf16[4,8,4,2304]{3,2,1,0:T(4,128)(2,1)} slice(bf16[4,8,9,2304]{3,2,1,0:T(8,128)(2,1)} %reshape.145), slice={[0:4], [0:8], [5:9], [0:2304]} | slice | bytes 1179648 | tf_op jit(solution)/shard_map/slice | solution.py:163
  152.2 2.2 reshape.148
  154.4 3.9 %fusion.66 = f32[128,720]{0,1:T(8,128)} fusion(bf16[128,2304]{1,0:T(8,128)(2,1)} %reshape.148, bf16[2304,720]{0,1:T(8,128)(2,1)} %param.20), kind=kOutput, calls=%fused_computation.79 | convolution fusion | flops 424673280 | bytes 4276224 | tf_op jit(solution)/shard_map/dot_general | solution.py:166
  158.3 5.4 %convolution_convert_fusion.2 = bf16[128,2304]{1,0:T(8,128)(2,1)} fusion(bf16[2304,720]{0,1:T(8,128)(2,1)S(1)} %copy-done, bf16[128,2304]{1,0:T(8,128)(2,1)} %reshape.148, bf16[2304,720]{0,1:T(8,128)(2,1)} %param.21, f32[128,720]{0,1:T(8,128)} %fusion.66), kind=kOutput, calls=%fused_computation.5 | convolution fusion | flops 850194432 | bytes 8183808 | tf_op jit(solution)/shard_map/dot_general | solution.py:169
  163.7 0.2 reduce-scatter.6.cloned.1.call-start
  163.9 2.4 %slice.44 = bf16[4,8,5,2304]{3,2,1,0:T(8,128)(2,1)} slice(bf16[4,8,9,2304]{3,2,1,0:T(8,128)(2,1)} %reshape.145), slice={[0:4], [0:8], [0:5], [0:2304]} | slice | bytes 1474560 | tf_op jit(solution)/shard_map/slice | solution.py:163
  166.3 2.3 reshape.146
  168.6 4.1 %fusion.65 = f32[160,720]{1,0:T(8,128)} fusion(bf16[160,2304]{1,0:T(8,128)(2,1)} %reshape.146, bf16[2304,720]{0,1:T(8,128)(2,1)} %param.20), kind=kOutput, calls=%fused_computation.78 | convolution fusion | flops 530841600 | bytes 4515840 | tf_op jit(solution)/shard_map/dot_general | solution.py:166
  172.7 5.3 %convolution_convert_fusion = bf16[160,2304]{1,0:T(8,128)(2,1)} fusion(bf16[2304,720]{0,1:T(8,128)(2,1)S(1)} %copy-done, bf16[160,2304]{1,0:T(8,128)(2,1)} %reshape.146, bf16[2304,720]{0,1:T(8,128)(2,1)} %param.21, f32[160,720]{1,0:T(8,128)} %fusion.65), kind=kOutput, calls=%fused_computation.3 | convolution fusion | flops 1062743040 | bytes 8570880 | tf_op jit(solution)/shard_map/dot_general | solution.py:169
  178.1 1.8 fusion.59
  179.9 1.7 copy.82
  181.6 1.7 copy.83
  183.3 1.6 reduce-scatter.8.cloned.1.call-done
  184.8 1.6 reshape.149
  186.4 4.0 %all-to-all-start.4 = ((bf16[8,4,2304]{2,1,0:T(4,128)(2,1)}), bf16[8,4,2304]{2,1,0:T(4,128)(2,1)}, u32[]{:S(2)}, u32[]{:S(2)}) async-start(bf16[8,4,2304]{2,1,0:T(4,128)(2,1)} %reshape.149), calls=%async_computation.7 | async-start | bytes 294912 | tf_op jit(solution)/shard_map/all_to_all | solution.py:174
  190.4 0.2 fusion.48
  190.7 17.5 %reduce-scatter.6.cloned.1.call-done = bf16[40,2304]{1,0:T(8,128)(2,1)} async-done(((bf16[160,2304]{1,0:T(8,128)(2,1)}), bf16[40,2304]{1,0:T(8,128)(2,1)}) %reduce-scatter.6.cloned.1.call-update) | async-done | bytes 184336 | tf_op jit(solution)/shard_map/reduce_scatter | solution.py:172
  208.2 1.7 reshape.147
  209.9 4.1 %all-to-all-start.3 = ((bf16[8,5,2304]{2,1,0:T(8,128)(2,1)}), bf16[8,5,2304]{2,1,0:T(8,128)(2,1)}, u32[]{:S(2)}, u32[]{:S(2)}) async-start(bf16[8,5,2304]{2,1,0:T(8,128)(2,1)} %reshape.147), calls=%async_computation.5 | async-start | bytes 589824 | tf_op jit(solution)/shard_map/all_to_all | solution.py:174
  214.0 7.3 %all-to-all-done.3 = bf16[8,5,2304]{2,1,0:T(8,128)(2,1)} async-done(((bf16[8,5,2304]{2,1,0:T(8,128)(2,1)}), bf16[8,5,2304]{2,1,0:T(8,128)(2,1)}, u32[]{:S(2)}, u32[]{:S(2)}) %all-to-all-start.3) | async-done | bytes 184352 | tf_op jit(solution)/shard_map/all_to_all | solution.py:174
  221.3 2.0 pad_maximum_fusion
  223.3 1.9 reshape.150
  225.3 1.2 convolution_multiply_fusion.1
  226.5 1.9 fusion.5
  (25 shorter events, 0.2 us)
Async XLA Ops:
  7.2 151.1 %copy-start = (bf16[2304,720]{0,1:T(8,128)(2,1)S(1)}, bf16[2304,720]{0,1:T(8,128)(2,1)}, u32[]{:S(2)}) copy-start(bf16[2304,720]{0,1:T(8,128)(2,1)} %param.22) | copy-start | bytes 9953284
  7.2 25.3 %copy-start.5 = (s32[128]{0:T(128)S(1)}, s32[128]{0:T(128)}, u32[]{:S(2)}) copy-start(s32[128]{0:T(128)} %param.18) | copy-start | bytes 1540
  7.2 48.4 %all-gather.4.cloned.1.call-start = ((), (), s32[]{:S(2)}) async-start(), calls=%async_computation.8 | async-start | bytes 2654208 | tf_op jit(solution)/shard_map/all_gather | solution.py:82
  29.1 13.0 %all-to-all-start.1 = ((bf16[32,4,576]{2,0,1:T(8,128)(2,1)}), bf16[32,4,576]{2,0,1:T(8,128)(2,1)S(1)}, u32[]{:S(2)}, u32[]{:S(2)}) async-start(bf16[32,4,576]{2,0,1:T(8,128)(2,1)} %copy.77), calls=%async_computation.1 | async-start | bytes 327680 | tf_op jit(solution)/shard_map/all_to_all | solution.py:73
  32.4 63.7 %reduce-scatter.4.cloned.1.call-start = ((), (), s32[]{:S(2)}) async-start(), calls=%async_computation.9 | async-start | bytes 737280 | tf_op jit(solution)/shard_map/reduce_scatter | solution.py:121
  59.5 4.9 %copy-start.2 = (pred[128,1024]{0,1:T(8,128)(4,1)S(1)}, pred[128,1024]{0,1:T(8,128)(4,1)}, u32[]{:S(2)}) copy-start(pred[128,1024]{0,1:T(8,128)(4,1)} %fusion.22) | copy-start | bytes 393220
  69.6 2.8 %copy-start.1 = (bf16[576,2304]{1,0:T(8,128)(2,1)S(1)}, bf16[576,2304]{1,0:T(8,128)(2,1)}, u32[]{:S(2)}) copy-start(bf16[576,2304]{1,0:T(8,128)(2,1)} %param.23) | copy-start | bytes 7962628
  72.4 1.7 copy-start.4
  72.4 25.0 %copy-start.3 = (f32[2304]{0:T(1024)S(1)}, f32[2304]{0:T(1024)}, u32[]{:S(2)}) copy-start(f32[2304]{0:T(1024)} %param.16) | copy-start | bytes 27652
  74.0 72.6 %all-gather.6.cloned.1.call-start = ((), (), s32[]{:S(2)}) async-start(), calls=%async_computation.10 | async-start | bytes 1658880 | tf_op jit(solution)/shard_map/all_gather | solution.py:156
  116.9 67.9 %reduce-scatter.8.cloned.1.call-start = ((), (), s32[]{:S(2)}) async-start(), calls=%async_computation.12 | async-start | bytes 737280 | tf_op jit(solution)/shard_map/reduce_scatter | solution.py:172
  163.7 44.5 %reduce-scatter.6.cloned.1.call-start = ((), (), s32[]{:S(2)}) async-start(), calls=%async_computation.11 | async-start | bytes 921600 | tf_op jit(solution)/shard_map/reduce_scatter | solution.py:172
  172.7 17.7 %copy-start.6 = (bf16[2304,8]{0,1:T(8,128)(2,1)S(1)}, bf16[2304,8]{0,1:T(8,128)(2,1)}, u32[]{:S(2)}) copy-start(bf16[2304,8]{0,1:T(8,128)(2,1)} %param.17) | copy-start | bytes 110596
  186.4 23.5 %all-to-all-start.4 = ((bf16[8,4,2304]{2,1,0:T(4,128)(2,1)}), bf16[8,4,2304]{2,1,0:T(4,128)(2,1)}, u32[]{:S(2)}, u32[]{:S(2)}) async-start(bf16[8,4,2304]{2,1,0:T(4,128)(2,1)} %reshape.149), calls=%async_computation.7 | async-start | bytes 294912 | tf_op jit(solution)/shard_map/all_to_all | solution.py:174
  209.9 11.4 %all-to-all-start.3 = ((bf16[8,5,2304]{2,1,0:T(8,128)(2,1)}), bf16[8,5,2304]{2,1,0:T(8,128)(2,1)}, u32[]{:S(2)}, u32[]{:S(2)}) async-start(bf16[8,5,2304]{2,1,0:T(8,128)(2,1)} %reshape.147), calls=%async_computation.5 | async-start | bytes 589824 | tf_op jit(solution)/shard_map/all_to_all | solution.py:174
Sparse Core Ops, SparseCore 0:
  27.4 28.1 all-gather.3
  74.1 22.0 reduce-scatter.3
  117.1 29.4 all-gather.5
  163.8 20.9 reduce-scatter.7
  187.0 21.2 reduce-scatter.5

commit v9 on v6

--- a/solution.py
+++ b/solution.py
@@ -58,17 +58,18 @@
     expert_count = router_weight.shape[1]
     replicas = seq_count // expert_count
     seq_place = lax.axis_index("seq")
-    joined_stack = jnp.stack(
+    joined_rows = jnp.concatenate(
         (
             key_rows.reshape(tok_local, head_count, group_width),
             value_rows.reshape(tok_local, head_count, group_width),
         ),
         2,
     )
-    joined_by_head = lax.all_to_all(joined_stack, "head", split_axis=1, concat_axis=0, tiled=True)
-    key_head = joined_by_head[:, 0, 0]
-    value_head = joined_by_head[:, 0, 1]
-    joined_head = joined_by_head.reshape(stretch_len, 2 * group_width)
+    joined_head = lax.all_to_all(
+        joined_rows, "head", split_axis=1, concat_axis=0, tiled=True
+    ).reshape(stretch_len, 2 * group_width)
+    key_head = joined_head[:, :group_width]
+    value_head = joined_head[:, group_width:]
     query_head = lax.all_to_all(
         query_rows.reshape(tok_local, head_count, group_width),
         "head",
@@ -146,26 +147,30 @@
         .astype(jnp.bfloat16)
         .reshape(expert_count, CAP, D)
     )
-    outgoing = jnp.broadcast_to(packed[:, None], (expert_count, replicas, CAP, D)).reshape(
-        seq_count, CAP, D
-    )
-    arrived = lax.all_to_all(outgoing, "seq", split_axis=0, concat_axis=0, tiled=True)
-    slot_count = arrived.shape[1]
-    flat_rows = arrived.reshape(seq_count * slot_count, D)
-    group_rows = lax.all_gather(flat_rows, "head", axis=0, tiled=True)
-    gate_act = jnp.dot(group_rows, gate_weight, preferred_element_type=jnp.float32)
-    up_act = jnp.dot(group_rows, up_weight, preferred_element_type=jnp.float32)
+    device_count = seq_count * head_count
+    outgoing = jnp.broadcast_to(
+        packed[:, None, None], (expert_count, replicas, head_count, CAP, D)
+    ).reshape(device_count, CAP, D)
+    arrived = lax.all_to_all(
+        outgoing, ("seq", "head"), split_axis=0, concat_axis=0, tiled=True
+    )
+    flat_rows = arrived.reshape(device_count * CAP, D)
+    gate_act = jnp.dot(flat_rows, gate_weight, preferred_element_type=jnp.float32)
+    up_act = jnp.dot(flat_rows, up_weight, preferred_element_type=jnp.float32)
     hidden = (jax.nn.silu(gate_act) * up_act).astype(jnp.bfloat16)
     partial_out = lax.dot_general(
         hidden, down_weight, (((1,), (1,)), ((), ())), preferred_element_type=jnp.float32
     ).astype(jnp.bfloat16)
-    shard_out = lax.psum_scatter(partial_out, "head", scatter_dimension=0, tiled=True)
     returned = lax.all_to_all(
-        shard_out.reshape(seq_count, slot_count, D), "seq", split_axis=0, concat_axis=0, tiled=True
-    )
-    by_slot = jnp.swapaxes(returned.reshape(expert_count, replicas, CAP, D), 1, 2).reshape(
-        slot_total, replicas, D
-    )
+        partial_out.reshape(device_count, CAP, D),
+        ("seq", "head"),
+        split_axis=0,
+        concat_axis=0,
+        tiled=True,
+    )
+    by_slot = jnp.swapaxes(
+        returned.reshape(expert_count, replicas * head_count, CAP, D), 1, 2
+    ).reshape(slot_total, replicas * head_count, D)
     slot_range = jnp.arange(slot_total, dtype=jnp.int32)[None, :]
     first_hot = (slot_ids[:, 0:1] == slot_range).astype(jnp.bfloat16)
     second_hot = (slot_ids[:, 1:2] == slot_range).astype(jnp.bfloat16)

time: 222 us -> 244 us (1.099)
  blocking collectives: 39.8 us -> 81.9 us
  waiting for transfers between devices: 99.1 us -> 81.6 us
    all_to_all x2, blocking collectives: 31 us -> 73.1 us  [the longest x1 57.3 us: per_device(): lax.all_to_all(outgoing, ('seq', 'head'), split_axis=0, concat_axis=0, ti...]
    all_to_all x1, waiting for transfers between devices: 10.4 us -> 47.9 us  [per_device(): lax.all_to_all(partial_out.reshape(device_count, CAP, D), ('seq', 'head')...]
    all_gather x1 -> x0, waiting for transfers between devices: 29.6 us -> none  [per_device(): group_rows = lax.all_gather(flat_rows, 'head', axis=0, tiled=True)]
    reduce_scatter x1 -> x0, waiting for transfers between devices: 25.4 us -> none  [per_device(): lax.psum_scatter(partial_out, 'head', scatter_dimension=0, tiled=True)]
    another operation x5 -> x0, local copies, waits for them, and re-layouts: 6.99 us -> none  [the longest x3 3.1 us: per_device(): jnp.stack((key_rows.reshape(tok_local, head_count, group_width), value_ro...]
    reshape x3 -> x5, local copies, waits for them, and re-layouts: 5.79 us -> 11 us  [the longest x1 2.79 us: per_device(): partial_out.reshape(device_count, CAP, D)]
    broadcast_in_dim x0 -> x2, local copies, waits for them, and re-layouts: none -> 3.17 us  [per_device(): jnp.broadcast_to(packed[:, None, None], (expert_count, replicas, head_cou...]
  transfers between devices with their start and end apart: 6 -> 4, of which waited for: 5 -> 3; matrix products, arithmetic and copies ran while one was open for 4% -> 4% of each run, Pallas kernels for 0% -> 0%
where the time goes in v9:
time: 244 us; the launch traced here: 243 us
  blocking collectives  81.9 us (34%)
  waiting for transfers between devices  81.6 us (33%)
  local copies, waits for them, and re-layouts  31.5 us (13%)
  matrix products  22.5 us (9%)
  between operations  14.2 us (6%)
  starting transfers between devices  7.07 us (3%)
  other arithmetic  4.42 us (2%)
    all_to_all x1, blocking collectives, per_device(): lax.all_to_all(outgoing, ('seq', 'head'), split_axis=0, concat_axis=0, ti...  57.3 us
    all_to_all x1, waiting for transfers between devices, per_device(): lax.all_to_all(partial_out.reshape(device_count, CAP, D), ('seq', 'head')...  47.9 us
    reduce_scatter x1, waiting for transfers between devices, per_device(): lax.psum_scatter(jnp.dot(attention, out_weight, preferred_element_type=jn...  21.3 us
    all_to_all x1, blocking collectives, per_device(): lax.all_to_all(joined_rows, 'head', split_axis=1, concat_axis=0, tiled=True)  15.8 us
    all_gather x1, waiting for transfers between devices, per_device(): joined_window = lax.all_gather(joined_head, 'seq', axis=0, tiled=True)  12.4 us
    all_gather x1, blocking collectives, per_device(): all_segments = lax.all_gather(segment_ids, 'seq', axis=0, tiled=True)  8.76 us
    dot_general x1, matrix products, per_device(): lax.dot_general(hidden, down_weight, (((1,), (1,)), ((), ())), preferred_...  6.48 us
    slice x2, local copies, waits for them, and re-layouts, per_device(): key_window = joined_window[:, :group_width]  6.35 us
  transfers between devices with their start and end apart: 4, of which 3 were waited for; matrix products, arithmetic and copies ran while one was open for 4% of the time, Pallas kernels for 0%

profile of v9, /device:TPU:0, one launch (start us, length us, event | category | flops | bytes accessed | tf_op | source)
XLA Modules:
  0.0 243.1 jit_solution(8425663896053532357)
XLA Ops:
  7.2 0.0 copy-start
  7.2 0.0 copy-start.5
  7.2 0.0 all-gather.3.cloned.1.call-start
  7.2 1.3 reshape.126
  8.5 1.8 reshape.125
  10.3 1.1 pad_maximum_fusion
  11.4 15.8 %all_to_all.40 = bf16[32,4,1152]{2,0,1:T(8,128)(2,1)} all-to-all(bf16[32,4,1152]{2,0,1:T(8,128)(2,1)S(1)} %copy.87), channel_id=1, replica_groups=mesh['seq'=8,'head'=4] {'head'}, dimensions={1} | all-to-all | bytes 589824 | tf_op jit(solution)/shard_map/all_to_all | solution.py:68
  27.2 0.0 all-gather.3.cloned.1.call-update
  27.3 1.1 reshape.130
  28.4 0.7 copy.90
  29.1 3.3 %all-to-all-start.1 = ((bf16[32,4,576]{2,0,1:T(8,128)(2,1)}), bf16[32,4,576]{2,0,1:T(8,128)(2,1)S(1)}, u32[]{:S(2)}, u32[]{:S(2)}) async-start(bf16[32,4,576]{2,0,1:T(8,128)(2,1)} %copy.90), calls=%async_computation.1 | async-start | bytes 327680 | tf_op jit(solution)/shard_map/all_to_all | solution.py:73
  32.4 0.0 reduce-scatter.2.cloned.1.call-start
  32.5 0.0 copy-done.5
  32.5 8.8 %all-gather = s32[8,1,128]{2,1,0:T(1,128)S(1)} all-gather(s32[1,1,128]{2,1,0:T(1,128)S(1)} %bitcast.77), channel_id=1, replica_groups=mesh['seq'=8,'head'=4] {'seq'}, dimensions={0}, use_global_device_ids=true | all-gather | bytes 4608 | tf_op jit(solution)/shard_map/all_gather | solution.py:80
  41.3 0.9 fusion.19
  42.1 0.0 all-to-all-done.1
  42.1 1.0 reshape_reshape.3
  43.2 12.4 %all-gather.3.cloned.1.call-done = bf16[1024,1152]{1,0:T(8,128)(2,1)} async-done(((bf16[128,1152]{1,0:T(8,128)(2,1)}), bf16[1024,1152]{1,0:T(8,128)(2,1)}) %all-gather.3.cloned.1.call-update) | async-done | bytes 2359312 | tf_op jit(solution)/shard_map/all_gather | solution.py:82
  55.6 3.9 %fusion.48 = (bf16[1024,576]{1,0:T(8,128)(2,1)}, bf16[1024,576]{1,0:T(8,128)(2,1)}) fusion(bf16[1024,1152]{1,0:T(8,128)(2,1)} %all-gather.3.cloned.1.call-done), kind=kLoop, calls=%fused_computation.61 | loop fusion | bytes 4718592 | tf_op jit(solution)/shard_map/slice | solution.py:98
  59.5 0.0 copy-start.2
  59.5 2.5 %copy.88 = bf16[1024,576]{0,1:T(8,128)(2,1)} copy(bf16[1024,576]{1,0:T(8,128)(2,1)} %get-tuple-element.21) | data formatting | bytes 2359296 | tf_op jit(solution)/shard_map/slice | solution.py:99
  61.9 2.4 %copy.89 = bf16[1024,576]{0,1:T(8,128)(2,1)} copy(bf16[1024,576]{1,0:T(8,128)(2,1)} %get-tuple-element.20) | data formatting | bytes 2359296 | tf_op jit(solution)/shard_map/slice | solution.py:98
  64.4 0.0 copy-done.2
  64.4 5.3 %fusion.50 = (f32[9,128]{1,0:T(8,128)S(1)}, bf16[9,128,1024]{1,2,0:T(8,128)(2,1)}) fusion(pred[128,1024]{0,1:T(8,128)(4,1)S(1)} %copy-done.2, bf16[1024,9,64]{0,2,1:T(8,128)(2,1)} %bitcast.73, bf16[128,9,64]{2,1,0:T(8,128)(2,1)} %reshape_reshape.3), kind=kOutput, calls=%fused_computation.63 | convolution fusion | flops 158073856 | bytes 3822080 | tf_op jit(solution)/shard_map/sub | solution.py:113
  69.6 0.0 copy-start.1
  69.6 2.7 %fusion.16 = bf16[128,9,64]{0,2,1:T(8,128)(2,1)S(1)} fusion(bf16[1024,9,64]{0,2,1:T(8,128)(2,1)} %bitcast.72, bf16[9,128,1024]{1,2,0:T(8,128)(2,1)} %get-tuple-element.29, f32[128,9]{0,1:T(8,128)S(1)} %bitcast.78), kind=kOutput, calls=%fused_computation.20 | convolution fusion | flops 151142400 | bytes 3691008 | tf_op jit(solution)/shard_map/hqk,khd->qhd/dot_general | solution.py:32
  72.4 0.0 copy-start.4
  72.4 0.0 copy-start.3
  72.4 0.1 copy-done.1
  72.5 1.5 convolution_convert_fusion.1
  73.9 0.0 reduce-scatter.2.cloned.1.call-update
  74.0 0.0 copy-done.4
  74.0 0.1 copy.93
  74.1 0.1 eq.88
  74.2 0.1 fusion.37
  74.2 0.1 reduce_window_sum.11
  74.3 0.2 select_reduce_fusion
  74.5 0.1 reduce_sum.60
  74.6 0.1 copy.94
  74.7 0.1 fusion.38
  74.8 21.3 %reduce-scatter.2.cloned.1.call-done = bf16[32,2304]{1,0:T(8,128)(2,1)} async-done(((bf16[128,2304]{1,0:T(8,128)(2,1)}), bf16[32,2304]{1,0:T(8,128)(2,1)}) %reduce-scatter.2.cloned.1.call-update) | async-done | bytes 147472 | tf_op jit(solution)/shard_map/reduce_scatter | solution.py:121
  96.1 1.2 fusion.23
  97.3 0.0 copy-done.3
  97.3 1.0 convolution_convert_fusion.2
  98.3 1.9 broadcast_in_dim.60
  100.3 1.2 broadcast_in_dim.61
  101.5 57.3 %all_to_all.41 = bf16[32,9,2304]{2,1,0:T(8,128)(2,1)} all-to-all(bf16[32,9,2304]{2,1,0:T(8,128)(2,1)S(1)} %bitcast.69), channel_id=1, replica_groups=mesh['seq'=8,'head'=4] {'seq','head'}, dimensions={0} | all-to-all | bytes 2654208 | tf_op jit(solution)/shard_map/all_to_all | solution.py:154
  158.8 2.8 %reshape.133 = bf16[288,2304]{1,0:T(8,128)(2,1)} reshape(bf16[32,9,2304]{2,1,0:T(8,128)(2,1)} %all_to_all.41) | data formatting | bytes 2654208 | tf_op jit(solution)/shard_map/reshape | solution.py:157
  161.6 4.5 %fusion.55 = f32[288,720]{1,0:T(8,128)} fusion(bf16[288,2304]{1,0:T(8,128)(2,1)} %reshape.133, bf16[2304,720]{0,1:T(8,128)(2,1)} %param.20), kind=kOutput, calls=%fused_computation.64 | convolution fusion | flops 955514880 | bytes 5474304 | tf_op jit(solution)/shard_map/dot_general | solution.py:158
  166.1 0.0 copy-done
  166.1 6.5 %convolution_convert_fusion = bf16[288,2304]{1,0:T(8,128)(2,1)} fusion(bf16[2304,720]{0,1:T(8,128)(2,1)S(1)} %copy-done, bf16[288,2304]{1,0:T(8,128)(2,1)} %reshape.133, bf16[2304,720]{0,1:T(8,128)(2,1)} %param.21, f32[288,720]{1,0:T(8,128)} %fusion.55), kind=kOutput, calls=%fused_computation.3 | convolution fusion | flops 1912937472 | bytes 10119168 | tf_op jit(solution)/shard_map/dot_general | solution.py:161
  172.5 2.8 %reshape.134 = bf16[32,9,2304]{2,1,0:T(8,128)(2,1)} reshape(bf16[288,2304]{1,0:T(8,128)(2,1)} %convolution_convert_fusion) | data formatting | bytes 2654208 | tf_op jit(solution)/shard_map/reshape | solution.py:165
  175.3 0.0 copy-start.6
  175.3 3.6 %all-to-all-start.3 = ((bf16[32,9,2304]{2,1,0:T(8,128)(2,1)}), bf16[32,9,2304]{2,1,0:T(8,128)(2,1)}, u32[]{:S(2)}, u32[]{:S(2)}) async-start(bf16[32,9,2304]{2,1,0:T(8,128)(2,1)} %reshape.134), calls=%async_computation.4 | async-start | bytes 4718592 | tf_op jit(solution)/shard_map/all_to_all | solution.py:164
  179.0 1.8 fusion.49
  180.8 1.7 copy.98
  182.5 1.7 copy.99
  184.2 0.0 copy-done.6
  184.2 0.2 fusion.35
  184.4 47.9 %all-to-all-done.3 = bf16[32,9,2304]{2,1,0:T(8,128)(2,1)} async-done(((bf16[32,9,2304]{2,1,0:T(8,128)(2,1)}), bf16[32,9,2304]{2,1,0:T(8,128)(2,1)}, u32[]{:S(2)}, u32[]{:S(2)}) %all-to-all-start.3) | async-done | bytes 1327136 | tf_op jit(solution)/shard_map/all_to_all | solution.py:164
  232.3 2.4 copy.95
  234.7 0.4 convolution_reduce_fusion
  235.1 0.4 convolution_reduce_fusion.1
  235.5 0.8 fusion.26
  (7 shorter events, 0.1 us)
Async XLA Ops:
  7.2 158.9 %copy-start = (bf16[2304,720]{0,1:T(8,128)(2,1)S(1)}, bf16[2304,720]{0,1:T(8,128)(2,1)}, u32[]{:S(2)}) copy-start(bf16[2304,720]{0,1:T(8,128)(2,1)} %param.22) | copy-start | bytes 9953284
  7.2 25.3 %copy-start.5 = (s32[128]{0:T(128)S(1)}, s32[128]{0:T(128)}, u32[]{:S(2)}) copy-start(s32[128]{0:T(128)} %param.18) | copy-start | bytes 1540
  7.2 48.4 %all-gather.3.cloned.1.call-start = ((), (), s32[]{:S(2)}) async-start(), calls=%async_computation.5 | async-start | bytes 2654208 | tf_op jit(solution)/shard_map/all_gather | solution.py:82
  29.1 13.0 %all-to-all-start.1 = ((bf16[32,4,576]{2,0,1:T(8,128)(2,1)}), bf16[32,4,576]{2,0,1:T(8,128)(2,1)S(1)}, u32[]{:S(2)}, u32[]{:S(2)}) async-start(bf16[32,4,576]{2,0,1:T(8,128)(2,1)} %copy.90), calls=%async_computation.1 | async-start | bytes 327680 | tf_op jit(solution)/shard_map/all_to_all | solution.py:73
  32.4 63.7 %reduce-scatter.2.cloned.1.call-start = ((), (), s32[]{:S(2)}) async-start(), calls=%async_computation.6 | async-start | bytes 737280 | tf_op jit(solution)/shard_map/reduce_scatter | solution.py:121
  59.5 4.9 %copy-start.2 = (pred[128,1024]{0,1:T(8,128)(4,1)S(1)}, pred[128,1024]{0,1:T(8,128)(4,1)}, u32[]{:S(2)}) copy-start(pred[128,1024]{0,1:T(8,128)(4,1)} %fusion.19) | copy-start | bytes 393220
  69.6 2.8 %copy-start.1 = (bf16[576,2304]{1,0:T(8,128)(2,1)S(1)}, bf16[576,2304]{1,0:T(8,128)(2,1)}, u32[]{:S(2)}) copy-start(bf16[576,2304]{1,0:T(8,128)(2,1)} %param.23) | copy-start | bytes 7962628
  72.4 1.6 copy-start.4
  72.4 24.9 %copy-start.3 = (f32[2304]{0:T(1024)S(1)}, f32[2304]{0:T(1024)}, u32[]{:S(2)}) copy-start(f32[2304]{0:T(1024)} %param.16) | copy-start | bytes 27652
  175.3 8.8 %copy-start.6 = (bf16[2304,8]{0,1:T(8,128)(2,1)S(1)}, bf16[2304,8]{0,1:T(8,128)(2,1)}, u32[]{:S(2)}) copy-start(bf16[2304,8]{0,1:T(8,128)(2,1)} %param.17) | copy-start | bytes 110596
  175.3 57.0 %all-to-all-start.3 = ((bf16[32,9,2304]{2,1,0:T(8,128)(2,1)}), bf16[32,9,2304]{2,1,0:T(8,128)(2,1)}, u32[]{:S(2)}, u32[]{:S(2)}) async-start(bf16[32,9,2304]{2,1,0:T(8,128)(2,1)} %reshape.134), calls=%async_computation.4 | async-start | bytes 4718592 | tf_op jit(solution)/shard_map/all_to_all | solution.py:164
Sparse Core Ops, SparseCore 0:
  27.4 28.1 all-gather.2
  74.1 22.0 reduce-scatter.1

commit v10 on v6

--- a/solution.py
+++ b/solution.py
@@ -58,17 +58,18 @@
     expert_count = router_weight.shape[1]
     replicas = seq_count // expert_count
     seq_place = lax.axis_index("seq")
-    joined_stack = jnp.stack(
+    joined_rows = jnp.concatenate(
         (
             key_rows.reshape(tok_local, head_count, group_width),
             value_rows.reshape(tok_local, head_count, group_width),
         ),
         2,
     )
-    joined_by_head = lax.all_to_all(joined_stack, "head", split_axis=1, concat_axis=0, tiled=True)
-    key_head = joined_by_head[:, 0, 0]
-    value_head = joined_by_head[:, 0, 1]
-    joined_head = joined_by_head.reshape(stretch_len, 2 * group_width)
+    joined_head = lax.all_to_all(
+        joined_rows, "head", split_axis=1, concat_axis=0, tiled=True
+    ).reshape(stretch_len, 2 * group_width)
+    key_head = joined_head[:, :group_width]
+    value_head = joined_head[:, group_width:]
     query_head = lax.all_to_all(
         query_rows.reshape(tok_local, head_count, group_width),
         "head",

time: 222 us -> 217 us (0.977)
  local copies, waits for them, and re-layouts: 31.7 us -> 28.2 us
    another operation x4 -> x1, local copies, waits for them, and re-layouts: 5.04 us -> 1.94 us  [the longest x3 3.1 us: per_device(): jnp.stack((key_rows.reshape(tok_local, head_count, group_width), value_ro...]
  transfers between devices with their start and end apart: 6 -> 6, of which waited for: 5 -> 5; matrix products, arithmetic and copies ran while one was open for 4% -> 5% of each run, Pallas kernels for 0% -> 0%
where the time goes in v10:
time: 217 us; the launch traced here: 216 us
  waiting for transfers between devices  99.1 us (46%)
  blocking collectives  39.2 us (18%)
  local copies, waits for them, and re-layouts  28.2 us (13%)
  matrix products  24.8 us (11%)
  between operations  13.9 us (6%)
  starting transfers between devices  7.69 us (4%)
  other arithmetic  3.62 us (2%)
    all_gather x1, waiting for transfers between devices, per_device(): group_rows = lax.all_gather(flat_rows, 'head', axis=0, tiled=True)  29.6 us
    reduce_scatter x1, waiting for transfers between devices, per_device(): lax.psum_scatter(partial_out, 'head', scatter_dimension=0, tiled=True)  25.4 us
    reduce_scatter x1, waiting for transfers between devices, per_device(): lax.psum_scatter(jnp.dot(attention, out_weight, preferred_element_type=jn...  21.3 us
    all_to_all x1, blocking collectives, per_device(): lax.all_to_all(joined_rows, 'head', split_axis=1, concat_axis=0, tiled=True)  15.8 us
    all_to_all x1, blocking collectives, per_device(): lax.all_to_all(outgoing, 'seq', split_axis=0, concat_axis=0, tiled=True)  14.6 us
    all_gather x1, waiting for transfers between devices, per_device(): joined_window = lax.all_gather(joined_head, 'seq', axis=0, tiled=True)  12.4 us
    all_to_all x1, waiting for transfers between devices, per_device(): lax.all_to_all(shard_out.reshape(seq_count, slot_count, D), 'seq', split_...  10.4 us
    all_gather x1, blocking collectives, per_device(): all_segments = lax.all_gather(segment_ids, 'seq', axis=0, tiled=True)  8.76 us
  transfers between devices with their start and end apart: 6, of which 5 were waited for; matrix products, arithmetic and copies ran while one was open for 5% of the time, Pallas kernels for 0%

profile of v10, /device:TPU:0, one launch (start us, length us, event | category | flops | bytes accessed | tf_op | source)
XLA Modules:
  0.0 216.5 jit_solution(9283446151723942940)
XLA Ops:
  7.2 0.0 copy-start
  7.2 0.0 copy-start.5
  7.2 0.0 all-gather.4.cloned.1.call-start
  7.2 1.3 reshape.126
  8.5 1.8 reshape.125
  10.3 1.1 pad_maximum_fusion
  11.5 15.8 %all_to_all.40 = bf16[32,4,1152]{2,0,1:T(8,128)(2,1)} all-to-all(bf16[32,4,1152]{2,0,1:T(8,128)(2,1)S(1)} %copy.74), channel_id=1, replica_groups=mesh['seq'=8,'head'=4] {'head'}, dimensions={1} | all-to-all | bytes 589824 | tf_op jit(solution)/shard_map/all_to_all | solution.py:68
  27.2 0.0 all-gather.4.cloned.1.call-update
  27.3 1.1 reshape.130
  28.4 0.7 copy.77
  29.1 3.3 %all-to-all-start.1 = ((bf16[32,4,576]{2,0,1:T(8,128)(2,1)}), bf16[32,4,576]{2,0,1:T(8,128)(2,1)S(1)}, u32[]{:S(2)}, u32[]{:S(2)}) async-start(bf16[32,4,576]{2,0,1:T(8,128)(2,1)} %copy.77), calls=%async_computation.1 | async-start | bytes 327680 | tf_op jit(solution)/shard_map/all_to_all | solution.py:73
  32.4 0.0 reduce-scatter.3.cloned.1.call-start
  32.5 0.0 copy-done.5
  32.5 8.8 %all-gather = s32[8,1,128]{2,1,0:T(1,128)S(1)} all-gather(s32[1,1,128]{2,1,0:T(1,128)S(1)} %bitcast.65), channel_id=1, replica_groups=mesh['seq'=8,'head'=4] {'seq'}, dimensions={0}, use_global_device_ids=true | all-gather | bytes 4608 | tf_op jit(solution)/shard_map/all_gather | solution.py:80
  41.3 0.9 fusion.21
  42.1 0.0 all-to-all-done.1
  42.1 1.0 reshape_reshape.3
  43.2 12.4 %all-gather.4.cloned.1.call-done = bf16[1024,1152]{1,0:T(8,128)(2,1)} async-done(((bf16[128,1152]{1,0:T(8,128)(2,1)}), bf16[1024,1152]{1,0:T(8,128)(2,1)}) %all-gather.4.cloned.1.call-update) | async-done | bytes 2359312 | tf_op jit(solution)/shard_map/all_gather | solution.py:82
  55.6 3.9 %fusion.45 = (bf16[1024,576]{1,0:T(8,128)(2,1)}, bf16[1024,576]{1,0:T(8,128)(2,1)}) fusion(bf16[1024,1152]{1,0:T(8,128)(2,1)} %all-gather.4.cloned.1.call-done), kind=kLoop, calls=%fused_computation.59 | loop fusion | bytes 4718592 | tf_op jit(solution)/shard_map/slice | solution.py:98
  59.5 2.5 %copy.75 = bf16[1024,576]{0,1:T(8,128)(2,1)} copy(bf16[1024,576]{1,0:T(8,128)(2,1)} %get-tuple-element.21) | data formatting | bytes 2359296 | tf_op jit(solution)/shard_map/slice | solution.py:99
  61.9 2.4 %copy.76 = bf16[1024,576]{0,1:T(8,128)(2,1)} copy(bf16[1024,576]{1,0:T(8,128)(2,1)} %get-tuple-element.20) | data formatting | bytes 2359296 | tf_op jit(solution)/shard_map/slice | solution.py:98
  64.4 0.0 copy-done.2
  64.4 5.3 %fusion.47 = (f32[9,128]{1,0:T(8,128)S(1)}, bf16[9,128,1024]{1,2,0:T(8,128)(2,1)}) fusion(pred[128,1024]{0,1:T(8,128)(4,1)S(1)} %copy-done.2, bf16[1024,9,64]{0,2,1:T(8,128)(2,1)} %bitcast.61, bf16[128,9,64]{2,1,0:T(8,128)(2,1)} %reshape_reshape.3), kind=kOutput, calls=%fused_computation.61 | convolution fusion | flops 158073856 | bytes 3822080 | tf_op jit(solution)/shard_map/sub | solution.py:113
  69.6 2.7 %fusion.18 = bf16[128,9,64]{0,2,1:T(8,128)(2,1)S(1)} fusion(bf16[1024,9,64]{0,2,1:T(8,128)(2,1)} %bitcast.60, bf16[9,128,1024]{1,2,0:T(8,128)(2,1)} %get-tuple-element.29, f32[128,9]{0,1:T(8,128)S(1)} %bitcast.66), kind=kOutput, calls=%fused_computation.22 | convolution fusion | flops 151142400 | bytes 3691008 | tf_op jit(solution)/shard_map/hqk,khd->qhd/dot_general | solution.py:32
  72.3 0.0 copy-start.4
  72.4 0.0 copy-start.3
  72.4 0.1 copy-done.1
  72.4 1.5 convolution_convert_fusion.1
  73.9 0.0 reduce-scatter.3.cloned.1.call-update
  74.0 0.0 all-gather.6.cloned.1.call-start
  74.0 0.0 copy-done.4
  74.0 0.1 copy.80
  74.1 0.1 eq.88
  74.2 0.1 fusion.38
  74.3 0.1 reduce_window_sum.11
  74.4 0.2 select_reduce_fusion
  74.6 0.1 reduce_sum.50
  74.7 0.1 copy.81
  74.8 0.1 fusion.39
  74.9 21.3 %reduce-scatter.3.cloned.1.call-done = bf16[32,2304]{1,0:T(8,128)(2,1)} async-done(((bf16[128,2304]{1,0:T(8,128)(2,1)}), bf16[32,2304]{1,0:T(8,128)(2,1)}) %reduce-scatter.3.cloned.1.call-update) | async-done | bytes 147472 | tf_op jit(solution)/shard_map/reduce_scatter | solution.py:121
  96.2 1.2 fusion.25
  97.3 0.0 copy-done.3
  97.3 1.1 convolution_convert_fusion.2
  98.4 1.9 reshape_broadcast_in_dim_reshape.3
  100.3 14.6 %all_to_all.41 = bf16[8,9,2304]{2,1,0:T(8,128)(2,1)} all-to-all(bf16[8,9,2304]{2,1,0:T(8,128)(2,1)} %reshape_broadcast_in_dim_reshape.3), channel_id=1, replica_groups=mesh['seq'=8,'head'=4] {'seq'}, dimensions={0} | all-to-all | bytes 663552 | tf_op jit(solution)/shard_map/all_to_all | solution.py:153
  115.0 1.9 reshape.132
  116.9 0.0 all-gather.6.cloned.1.call-update
  116.9 0.0 reduce-scatter.5.cloned.1.call-start
  117.0 29.6 %all-gather.6.cloned.1.call-done = bf16[288,2304]{1,0:T(8,128)(2,1)} async-done(((bf16[72,2304]{1,0:T(8,128)(2,1)}), bf16[288,2304]{1,0:T(8,128)(2,1)}) %all-gather.6.cloned.1.call-update) | async-done | bytes 1327120 | tf_op jit(solution)/shard_map/all_gather | solution.py:156
  146.6 4.5 %fusion.52 = f32[288,720]{1,0:T(8,128)} fusion(bf16[288,2304]{1,0:T(8,128)(2,1)} %all-gather.6.cloned.1.call-done, bf16[2304,720]{0,1:T(8,128)(2,1)} %param.20), kind=kOutput, calls=%fused_computation.62 | convolution fusion | flops 955514880 | bytes 5474304 | tf_op jit(solution)/shard_map/dot_general | solution.py:157
  151.1 6.5 %convolution_convert_fusion = bf16[288,2304]{1,0:T(8,128)(2,1)} fusion(bf16[2304,720]{0,1:T(8,128)(2,1)S(1)} %copy-done, bf16[288,2304]{1,0:T(8,128)(2,1)} %all-gather.6.cloned.1.call-done, bf16[2304,720]{0,1:T(8,128)(2,1)} %param.21, f32[288,720]{1,0:T(8,128)} %fusion.52), kind=kOutput, calls=%fused_computation.3 | convolution fusion | flops 1912937472 | bytes 10119168 | tf_op jit(solution)/shard_map/dot_general | solution.py:160
  157.5 0.0 reduce-scatter.5.cloned.1.call-update
  157.6 1.8 fusion.46
  159.4 1.7 copy.82
  161.1 1.7 copy.83
  162.8 0.0 copy-done.6
  162.8 0.2 fusion.36
  163.0 25.4 %reduce-scatter.5.cloned.1.call-done = bf16[72,2304]{1,0:T(8,128)(2,1)} async-done(((bf16[288,2304]{1,0:T(8,128)(2,1)}), bf16[72,2304]{1,0:T(8,128)(2,1)}) %reduce-scatter.5.cloned.1.call-update) | async-done | bytes 331792 | tf_op jit(solution)/shard_map/reduce_scatter | solution.py:163
  188.3 1.9 reshape.133
  190.3 4.2 %all-to-all-start.3 = ((bf16[8,9,2304]{2,1,0:T(8,128)(2,1)}), bf16[8,9,2304]{2,1,0:T(8,128)(2,1)}, u32[]{:S(2)}, u32[]{:S(2)}) async-start(bf16[8,9,2304]{2,1,0:T(8,128)(2,1)} %reshape.133), calls=%async_computation.5 | async-start | bytes 1179648 | tf_op jit(solution)/shard_map/all_to_all | solution.py:164
  194.5 10.4 %all-to-all-done.3 = bf16[8,9,2304]{2,1,0:T(8,128)(2,1)} async-done(((bf16[8,9,2304]{2,1,0:T(8,128)(2,1)}), bf16[8,9,2304]{2,1,0:T(8,128)(2,1)}, u32[]{:S(2)}, u32[]{:S(2)}) %all-to-all-start.3) | async-done | bytes 331808 | tf_op jit(solution)/shard_map/all_to_all | solution.py:164
  204.9 1.9 reshape.134
  206.9 1.2 convolution_multiply_fusion.1
  208.1 1.9 fusion.5
  (11 shorter events, 0.1 us)
Async XLA Ops:
  7.2 143.9 %copy-start = (bf16[2304,720]{0,1:T(8,128)(2,1)S(1)}, bf16[2304,720]{0,1:T(8,128)(2,1)}, u32[]{:S(2)}) copy-start(bf16[2304,720]{0,1:T(8,128)(2,1)} %param.22) | copy-start | bytes 9953284
  7.2 25.3 %copy-start.5 = (s32[128]{0:T(128)S(1)}, s32[128]{0:T(128)}, u32[]{:S(2)}) copy-start(s32[128]{0:T(128)} %param.18) | copy-start | bytes 1540
  7.2 48.4 %all-gather.4.cloned.1.call-start = ((), (), s32[]{:S(2)}) async-start(), calls=%async_computation.6 | async-start | bytes 2654208 | tf_op jit(solution)/shard_map/all_gather | solution.py:82
  29.1 13.0 %all-to-all-start.1 = ((bf16[32,4,576]{2,0,1:T(8,128)(2,1)}), bf16[32,4,576]{2,0,1:T(8,128)(2,1)S(1)}, u32[]{:S(2)}, u32[]{:S(2)}) async-start(bf16[32,4,576]{2,0,1:T(8,128)(2,1)} %copy.77), calls=%async_computation.1 | async-start | bytes 327680 | tf_op jit(solution)/shard_map/all_to_all | solution.py:73
  32.4 63.7 %reduce-scatter.3.cloned.1.call-start = ((), (), s32[]{:S(2)}) async-start(), calls=%async_computation.7 | async-start | bytes 737280 | tf_op jit(solution)/shard_map/reduce_scatter | solution.py:121
  59.5 4.9 %copy-start.2 = (pred[128,1024]{0,1:T(8,128)(4,1)S(1)}, pred[128,1024]{0,1:T(8,128)(4,1)}, u32[]{:S(2)}) copy-start(pred[128,1024]{0,1:T(8,128)(4,1)} %fusion.21) | copy-start | bytes 393220
  69.6 2.8 %copy-start.1 = (bf16[576,2304]{1,0:T(8,128)(2,1)S(1)}, bf16[576,2304]{1,0:T(8,128)(2,1)}, u32[]{:S(2)}) copy-start(bf16[576,2304]{1,0:T(8,128)(2,1)} %param.23) | copy-start | bytes 7962628
  72.3 1.7 copy-start.4
  72.4 25.0 %copy-start.3 = (f32[2304]{0:T(1024)S(1)}, f32[2304]{0:T(1024)}, u32[]{:S(2)}) copy-start(f32[2304]{0:T(1024)} %param.16) | copy-start | bytes 27652
  74.0 72.6 %all-gather.6.cloned.1.call-start = ((), (), s32[]{:S(2)}) async-start(), calls=%async_computation.8 | async-start | bytes 1658880 | tf_op jit(solution)/shard_map/all_gather | solution.py:156
  116.9 71.4 %reduce-scatter.5.cloned.1.call-start = ((), (), s32[]{:S(2)}) async-start(), calls=%async_computation.9 | async-start | bytes 1658880 | tf_op jit(solution)/shard_map/reduce_scatter | solution.py:163
  157.5 5.2 %copy-start.6 = (bf16[2304,8]{0,1:T(8,128)(2,1)S(1)}, bf16[2304,8]{0,1:T(8,128)(2,1)}, u32[]{:S(2)}) copy-start(bf16[2304,8]{0,1:T(8,128)(2,1)} %param.17) | copy-start | bytes 110596
  190.3 14.7 %all-to-all-start.3 = ((bf16[8,9,2304]{2,1,0:T(8,128)(2,1)}), bf16[8,9,2304]{2,1,0:T(8,128)(2,1)}, u32[]{:S(2)}, u32[]{:S(2)}) async-start(bf16[8,9,2304]{2,1,0:T(8,128)(2,1)} %reshape.133), calls=%async_computation.5 | async-start | bytes 1179648 | tf_op jit(solution)/shard_map/all_to_all | solution.py:164
Sparse Core Ops, SparseCore 0:
  27.4 28.1 all-gather.3
  74.1 22.0 reduce-scatter.2
  117.0 29.4 all-gather.5
  157.7 30.6 reduce-scatter.4

commit v11 on v10

--- a/solution.py
+++ b/solution.py
@@ -139,42 +139,36 @@
     route_rank = jnp.sum(before_count * flat_hot, -1)
     slot_ids = (expert_ids.reshape(-1) * CAP + route_rank).reshape(tok_local, route_count)
     slot_total = expert_count * CAP
+    slot_grid = jnp.arange(slot_total, dtype=jnp.int32).reshape(expert_count, CAP)
     dispatch = jnp.any(
-        slot_ids[None, :, :] == jnp.arange(slot_total, dtype=jnp.int32)[:, None, None], -1
+        slot_ids[None, None, :, :] == slot_grid[:, :, None, None], -1
     ).astype(jnp.bfloat16)
-    packed = (
-        jnp.dot(dispatch, normed, preferred_element_type=jnp.float32)
-        .astype(jnp.bfloat16)
-        .reshape(expert_count, CAP, D)
-    )
+    packed = jnp.einsum(
+        "ect,td->ecd", dispatch, normed, preferred_element_type=jnp.float32
+    ).astype(jnp.bfloat16)
     outgoing = jnp.broadcast_to(packed[:, None], (expert_count, replicas, CAP, D)).reshape(
         seq_count, CAP, D
     )
     arrived = lax.all_to_all(outgoing, "seq", split_axis=0, concat_axis=0, tiled=True)
-    slot_count = arrived.shape[1]
-    flat_rows = arrived.reshape(seq_count * slot_count, D)
-    group_rows = lax.all_gather(flat_rows, "head", axis=0, tiled=True)
-    gate_act = jnp.dot(group_rows, gate_weight, preferred_element_type=jnp.float32)
-    up_act = jnp.dot(group_rows, up_weight, preferred_element_type=jnp.float32)
+    group_rows = lax.all_gather(arrived, "head", axis=0, tiled=True)
+    gate_act = jnp.einsum(
+        "rcd,df->rcf", group_rows, gate_weight, preferred_element_type=jnp.float32
+    )
+    up_act = jnp.einsum("rcd,df->rcf", group_rows, up_weight, preferred_element_type=jnp.float32)
     hidden = (jax.nn.silu(gate_act) * up_act).astype(jnp.bfloat16)
-    partial_out = lax.dot_general(
-        hidden, down_weight, (((1,), (1,)), ((), ())), preferred_element_type=jnp.float32
+    partial_out = jnp.einsum(
+        "rcf,df->rcd", hidden, down_weight, preferred_element_type=jnp.float32
     ).astype(jnp.bfloat16)
     shard_out = lax.psum_scatter(partial_out, "head", scatter_dimension=0, tiled=True)
-    returned = lax.all_to_all(
-        shard_out.reshape(seq_count, slot_count, D), "seq", split_axis=0, concat_axis=0, tiled=True
-    )
-    by_slot = jnp.swapaxes(returned.reshape(expert_count, replicas, CAP, D), 1, 2).reshape(
-        slot_total, replicas, D
-    )
-    slot_range = jnp.arange(slot_total, dtype=jnp.int32)[None, :]
-    first_hot = (slot_ids[:, 0:1] == slot_range).astype(jnp.bfloat16)
-    second_hot = (slot_ids[:, 1:2] == slot_range).astype(jnp.bfloat16)
+    returned = lax.all_to_all(shard_out, "seq", split_axis=0, concat_axis=0, tiled=True)
+    by_expert = returned.reshape(expert_count, replicas, CAP, D)
+    first_hot = (slot_ids[:, 0, None, None] == slot_grid[None]).astype(jnp.bfloat16)
+    second_hot = (slot_ids[:, 1, None, None] == slot_grid[None]).astype(jnp.bfloat16)
     first_rows = jnp.sum(
-        jnp.einsum("ts,srd->trd", first_hot, by_slot, preferred_element_type=jnp.float32), 1
+        jnp.einsum("tec,ercd->trd", first_hot, by_expert, preferred_element_type=jnp.float32), 1
     )
     second_rows = jnp.sum(
-        jnp.einsum("ts,srd->trd", second_hot, by_slot, preferred_element_type=jnp.float32), 1
+        jnp.einsum("tec,ercd->trd", second_hot, by_expert, preferred_element_type=jnp.float32), 1
     )
     moe_sum = first_weight[:, None] * first_rows + second_weight[:, None] * second_rows
     residual_out = (middle_wide + residual_scale * moe_sum).astype(jnp.bfloat16)

time: 217 us -> 214 us (0.986)
  local copies, waits for them, and re-layouts: 28.2 us -> 25.7 us
    reduce_scatter x1 -> x0, waiting for transfers between devices: 25.4 us -> none  [per_device(): lax.psum_scatter(partial_out, 'head', scatter_dimension=0, tiled=True)]
    unnamed x4 -> x5, waiting for transfers between devices: 0.07 us -> 25.4 us
    reshape x2 -> x0, local copies, waits for them, and re-layouts: 3.86 us -> none  [the longest x1 1.95 us: per_device(): flat_rows = arrived.reshape(seq_count * slot_count, D)]
    another operation x2 -> x1, local copies, waits for them, and re-layouts: 3.88 us -> 0.08 us  [per_device(): slot_grid[None]]
    unnamed x17 -> x18, local copies, waits for them, and re-layouts: 3.59 us -> 6.09 us
where the time goes in v11:
time: 214 us; the launch traced here: 213 us
  waiting for transfers between devices  99 us (46%)
  blocking collectives  38.5 us (18%)
  local copies, waits for them, and re-layouts  25.7 us (12%)
  matrix products  24.5 us (11%)
  between operations  13.9 us (6%)
  starting transfers between devices  7.7 us (4%)
  other arithmetic  3.62 us (2%)
    all_gather x1, waiting for transfers between devices, per_device(): group_rows = lax.all_gather(arrived, 'head', axis=0, tiled=True)  29.6 us
    unnamed x5, waiting for transfers between devices  25.4 us
    reduce_scatter x1, waiting for transfers between devices, per_device(): lax.psum_scatter(jnp.dot(attention, out_weight, preferred_element_type=jn...  21.3 us
    all_to_all x1, blocking collectives, per_device(): lax.all_to_all(joined_rows, 'head', split_axis=1, concat_axis=0, tiled=True)  15.8 us
    all_to_all x1, blocking collectives, per_device(): lax.all_to_all(outgoing, 'seq', split_axis=0, concat_axis=0, tiled=True)  13.9 us
    all_gather x1, waiting for transfers between devices, per_device(): joined_window = lax.all_gather(joined_head, 'seq', axis=0, tiled=True)  12.4 us
    all_to_all x1, waiting for transfers between devices, per_device(): lax.all_to_all(shard_out, 'seq', split_axis=0, concat_axis=0, tiled=True)  10.4 us
    all_gather x1, blocking collectives, per_device(): all_segments = lax.all_gather(segment_ids, 'seq', axis=0, tiled=True)  8.76 us
  transfers between devices with their start and end apart: 6, of which 5 were waited for; matrix products, arithmetic and copies ran while one was open for 5% of the time, Pallas kernels for 0%

profile of v11, /device:TPU:0, one launch (start us, length us, event | category | flops | bytes accessed | tf_op | source)
XLA Modules:
  0.0 212.9 jit_solution(3600806880690398976)
XLA Ops:
  7.2 0.0 copy-start
  7.2 0.0 copy-start.5
  7.2 0.0 all-gather.4.cloned.1.call-start
  7.2 1.3 reshape.141
  8.5 1.8 reshape.140
  10.3 1.1 pad_maximum_fusion
  11.5 15.8 %all_to_all.40 = bf16[32,4,1152]{2,0,1:T(8,128)(2,1)} all-to-all(bf16[32,4,1152]{2,0,1:T(8,128)(2,1)S(1)} %copy.90), channel_id=1, replica_groups=mesh['seq'=8,'head'=4] {'head'}, dimensions={1} | all-to-all | bytes 589824 | tf_op jit(solution)/shard_map/all_to_all | solution.py:68
  27.2 0.0 all-gather.4.cloned.1.call-update
  27.3 1.1 reshape.145
  28.4 0.7 copy.93
  29.1 3.3 %all-to-all-start.1 = ((bf16[32,4,576]{2,0,1:T(8,128)(2,1)}), bf16[32,4,576]{2,0,1:T(8,128)(2,1)S(1)}, u32[]{:S(2)}, u32[]{:S(2)}) async-start(bf16[32,4,576]{2,0,1:T(8,128)(2,1)} %copy.93), calls=%async_computation.1 | async-start | bytes 327680 | tf_op jit(solution)/shard_map/all_to_all | solution.py:73
  32.4 0.0 reduce-scatter.5.cloned.1.call-start
  32.5 0.0 copy-done.5
  32.5 8.8 %all-gather = s32[8,1,128]{2,1,0:T(1,128)S(1)} all-gather(s32[1,1,128]{2,1,0:T(1,128)S(1)} %bitcast.102), channel_id=1, replica_groups=mesh['seq'=8,'head'=4] {'seq'}, dimensions={0}, use_global_device_ids=true | all-gather | bytes 4608 | tf_op jit(solution)/shard_map/all_gather | solution.py:80
  41.3 0.9 fusion.36
  42.1 0.0 all-to-all-done.1
  42.1 1.0 reshape_reshape.3
  43.2 12.4 %all-gather.4.cloned.1.call-done = bf16[1024,1152]{1,0:T(8,128)(2,1)} async-done(((bf16[128,1152]{1,0:T(8,128)(2,1)}), bf16[1024,1152]{1,0:T(8,128)(2,1)}) %all-gather.4.cloned.1.call-update) | async-done | bytes 2359312 | tf_op jit(solution)/shard_map/all_gather | solution.py:82
  55.6 3.9 %fusion.65 = (bf16[1024,576]{1,0:T(8,128)(2,1)}, bf16[1024,576]{1,0:T(8,128)(2,1)}) fusion(bf16[1024,1152]{1,0:T(8,128)(2,1)} %all-gather.4.cloned.1.call-done), kind=kLoop, calls=%fused_computation.71 | loop fusion | bytes 4718592 | tf_op jit(solution)/shard_map/slice | solution.py:98
  59.5 2.5 %copy.91 = bf16[1024,576]{0,1:T(8,128)(2,1)} copy(bf16[1024,576]{1,0:T(8,128)(2,1)} %get-tuple-element.21) | data formatting | bytes 2359296 | tf_op jit(solution)/shard_map/slice | solution.py:99
  61.9 2.4 %copy.92 = bf16[1024,576]{0,1:T(8,128)(2,1)} copy(bf16[1024,576]{1,0:T(8,128)(2,1)} %get-tuple-element.20) | data formatting | bytes 2359296 | tf_op jit(solution)/shard_map/slice | solution.py:98
  64.4 0.0 copy-done.2
  64.4 5.3 %fusion.67 = (f32[9,128]{1,0:T(8,128)S(1)}, bf16[9,128,1024]{1,2,0:T(8,128)(2,1)}) fusion(pred[128,1024]{0,1:T(8,128)(4,1)S(1)} %copy-done.2, bf16[1024,9,64]{0,2,1:T(8,128)(2,1)} %bitcast.97, bf16[128,9,64]{2,1,0:T(8,128)(2,1)} %reshape_reshape.3), kind=kOutput, calls=%fused_computation.73 | convolution fusion | flops 158073856 | bytes 3822080 | tf_op jit(solution)/shard_map/sub | solution.py:113
  69.6 2.7 %fusion.31 = bf16[128,9,64]{0,2,1:T(8,128)(2,1)S(1)} fusion(bf16[1024,9,64]{0,2,1:T(8,128)(2,1)} %bitcast.96, bf16[9,128,1024]{1,2,0:T(8,128)(2,1)} %get-tuple-element.29, f32[128,9]{0,1:T(8,128)S(1)} %bitcast.103), kind=kOutput, calls=%fused_computation.30 | convolution fusion | flops 151142400 | bytes 3691008 | tf_op jit(solution)/shard_map/hqk,khd->qhd/dot_general | solution.py:32
  72.3 0.0 copy-start.4
  72.4 0.0 copy-start.3
  72.4 0.1 copy-done.1
  72.4 1.5 convolution_convert_fusion.2
  73.9 0.0 reduce-scatter.5.cloned.1.call-update
  74.0 0.0 all-gather.6.cloned.1.call-start
  74.0 0.0 copy-done.4
  74.0 0.1 copy.96
  74.1 0.1 eq.88
  74.2 0.1 fusion.61
  74.3 0.1 reduce_window_sum.11
  74.4 0.2 select_reduce_fusion
  74.6 0.1 reduce_sum.50
  74.7 0.1 copy.97
  74.8 0.1 compare_reduce_fusion
  74.9 21.3 %reduce-scatter.5.cloned.1.call-done = bf16[32,2304]{1,0:T(8,128)(2,1)} async-done(((bf16[128,2304]{1,0:T(8,128)(2,1)}), bf16[32,2304]{1,0:T(8,128)(2,1)}) %reduce-scatter.5.cloned.1.call-update) | async-done | bytes 147472 | tf_op jit(solution)/shard_map/reduce_scatter | solution.py:121
  96.2 1.2 fusion.40
  97.3 0.0 copy-done.3
  97.3 0.4 convolution_convert_fusion.1
  97.7 13.9 %all_to_all.41 = bf16[8,9,2304]{2,1,0:T(8,128)(2,1)S(1)} all-to-all(bf16[8,9,2304]{2,1,0:T(8,128)(2,1)S(1)} %convolution_convert_fusion.1), channel_id=1, replica_groups=mesh['seq'=8,'head'=4] {'seq'}, dimensions={0} | all-to-all | bytes 663552 | tf_op jit(solution)/shard_map/all_to_all | solution.py:152
  111.6 0.8 copy.100
  112.4 0.0 all-gather.6.cloned.1.call-update
  112.5 0.0 reduce-scatter.7.cloned.1.call-start
  112.5 29.6 %all-gather.6.cloned.1.call-done = bf16[32,9,2304]{2,0,1:T(8,128)(2,1)} async-done(((bf16[8,9,2304]{2,0,1:T(8,128)(2,1)}), bf16[32,9,2304]{2,0,1:T(8,128)(2,1)}) %all-gather.6.cloned.1.call-update) | async-done | bytes 1327120 | tf_op jit(solution)/shard_map/all_gather | solution.py:153
  142.1 4.5 %fusion.12 = f32[32,9,720]{2,0,1:T(8,128)} fusion(bf16[32,9,2304]{2,0,1:T(8,128)(2,1)} %all-gather.6.cloned.1.call-done, bf16[2304,720]{0,1:T(8,128)(2,1)} %param.20), kind=kOutput, calls=%fused_computation.19 | convolution fusion | flops 955514880 | bytes 5474304 | tf_op jit(solution)/shard_map/rcd,df->rcf/dot_general | solution.py:154
  146.6 0.0 copy-done
  146.6 6.5 %fusion.1 = bf16[9,4,8,2304]{3,2,1,0:T(8,128)(2,1)} fusion(bf16[2304,720]{0,1:T(8,128)(2,1)S(1)} %copy-done, bf16[32,9,2304]{2,0,1:T(8,128)(2,1)} %all-gather.6.cloned.1.call-done, bf16[2304,720]{0,1:T(8,128)(2,1)} %param.21, f32[32,9,720]{2,0,1:T(8,128)} %fusion.12), kind=kOutput, calls=%fused_computation.4 | convolution fusion | flops 1912937472 | bytes 10119168 | tf_op jit(solution)/shard_map/rcf,df->rcd/dot_general | solution.py:159
  153.1 2.5 %copy.107 = bf16[9,4,8,2304]{3,2,0,1:T(8,128)(2,1)} copy(bf16[9,4,8,2304]{3,2,1,0:T(8,128)(2,1)} %fusion.1) | data formatting | bytes 2654208
  155.6 0.0 reduce-scatter.7.cloned.1.call-update
  155.6 0.1 copy.98
  155.7 1.8 fusion.66
  157.4 1.7 copy.102
  159.1 1.7 copy.103
  160.8 0.2 fusion.55
  161.0 25.3 %reduce-scatter.7.cloned.1.call-done = bf16[8,20736]{1,0:T(8,128)(2,1)} async-done(((bf16[32,20736]{1,0:T(8,128)(2,1)}), bf16[8,20736]{1,0:T(8,128)(2,1)}) %reduce-scatter.7.cloned.1.call-update) | async-done | bytes 331792
  186.3 1.9 copy.101
  188.2 4.2 %all-to-all-start.3 = ((bf16[8,9,2304]{2,1,0:T(8,128)(2,1)}), bf16[8,9,2304]{2,1,0:T(8,128)(2,1)}, u32[]{:S(2)}, u32[]{:S(2)}) async-start(bf16[8,9,2304]{2,1,0:T(8,128)(2,1)} %copy.101), calls=%async_computation.4 | async-start | bytes 1179648 | tf_op jit(solution)/shard_map/all_to_all | solution.py:163
  192.4 10.4 %all-to-all-done.3 = bf16[8,9,2304]{2,1,0:T(8,128)(2,1)} async-done(((bf16[8,9,2304]{2,1,0:T(8,128)(2,1)}), bf16[8,9,2304]{2,1,0:T(8,128)(2,1)}, u32[]{:S(2)}, u32[]{:S(2)}) %all-to-all-start.3) | async-done | bytes 331808 | tf_op jit(solution)/shard_map/all_to_all | solution.py:163
  202.9 1.4 fusion.7
  204.3 2.1 fusion.8
  (12 shorter events, 0.1 us)
Async XLA Ops:
  7.2 139.4 %copy-start = (bf16[2304,720]{0,1:T(8,128)(2,1)S(1)}, bf16[2304,720]{0,1:T(8,128)(2,1)}, u32[]{:S(2)}) copy-start(bf16[2304,720]{0,1:T(8,128)(2,1)} %param.22) | copy-start | bytes 9953284
  7.2 25.3 %copy-start.5 = (s32[128]{0:T(128)S(1)}, s32[128]{0:T(128)}, u32[]{:S(2)}) copy-start(s32[128]{0:T(128)} %param.18) | copy-start | bytes 1540
  7.2 48.4 %all-gather.4.cloned.1.call-start = ((), (), s32[]{:S(2)}) async-start(), calls=%async_computation.6 | async-start | bytes 2654208 | tf_op jit(solution)/shard_map/all_gather | solution.py:82
  29.1 13.0 %all-to-all-start.1 = ((bf16[32,4,576]{2,0,1:T(8,128)(2,1)}), bf16[32,4,576]{2,0,1:T(8,128)(2,1)S(1)}, u32[]{:S(2)}, u32[]{:S(2)}) async-start(bf16[32,4,576]{2,0,1:T(8,128)(2,1)} %copy.93), calls=%async_computation.1 | async-start | bytes 327680 | tf_op jit(solution)/shard_map/all_to_all | solution.py:73
  32.4 63.7 %reduce-scatter.5.cloned.1.call-start = ((), (), s32[]{:S(2)}) async-start(), calls=%async_computation.7 | async-start | bytes 737280 | tf_op jit(solution)/shard_map/reduce_scatter | solution.py:121
  59.5 4.9 %copy-start.2 = (pred[128,1024]{0,1:T(8,128)(4,1)S(1)}, pred[128,1024]{0,1:T(8,128)(4,1)}, u32[]{:S(2)}) copy-start(pred[128,1024]{0,1:T(8,128)(4,1)} %fusion.36) | copy-start | bytes 393220
  69.6 2.8 %copy-start.1 = (bf16[576,2304]{1,0:T(8,128)(2,1)S(1)}, bf16[576,2304]{1,0:T(8,128)(2,1)}, u32[]{:S(2)}) copy-start(bf16[576,2304]{1,0:T(8,128)(2,1)} %param.23) | copy-start | bytes 7962628
  72.3 1.7 copy-start.4
  72.4 25.0 %copy-start.3 = (f32[2304]{0:T(1024)S(1)}, f32[2304]{0:T(1024)}, u32[]{:S(2)}) copy-start(f32[2304]{0:T(1024)} %param.16) | copy-start | bytes 27652
  74.0 68.1 %all-gather.6.cloned.1.call-start = ((), (), s32[]{:S(2)}) async-start(), calls=%async_computation.8 | async-start | bytes 1658880 | tf_op jit(solution)/shard_map/all_gather | solution.py:153
  112.5 73.9 %reduce-scatter.7.cloned.1.call-start = ((), (), s32[]{:S(2)}) async-start(), calls=%async_computation.9 | async-start | bytes 1658880
  153.1 7.8 %copy-start.6 = (bf16[2304,8]{0,1:T(8,128)(2,1)S(1)}, bf16[2304,8]{0,1:T(8,128)(2,1)}, u32[]{:S(2)}) copy-start(bf16[2304,8]{0,1:T(8,128)(2,1)} %param.17) | copy-start | bytes 110596
  188.2 14.7 %all-to-all-start.3 = ((bf16[8,9,2304]{2,1,0:T(8,128)(2,1)}), bf16[8,9,2304]{2,1,0:T(8,128)(2,1)}, u32[]{:S(2)}, u32[]{:S(2)}) async-start(bf16[8,9,2304]{2,1,0:T(8,128)(2,1)} %copy.101), calls=%async_computation.4 | async-start | bytes 1179648 | tf_op jit(solution)/shard_map/all_to_all | solution.py:163
Sparse Core Ops, SparseCore 0:
  27.4 28.1 all-gather.3
  74.1 22.0 reduce-scatter.4
  112.6 29.4 all-gather.5
  155.7 30.6 reduce-scatter.6

commit v12 on v11

--- a/solution.py
+++ b/solution.py
@@ -3,6 +3,7 @@
 import jax
 import jax.numpy as jnp
 from jax import lax
+from jax.experimental.layout import Layout, with_layout_constraint
 from jax.sharding import PartitionSpec as P
 
 D = 2304
@@ -23,14 +24,14 @@
 
 def score_piece(queries, key_piece, piece_allowed):
     raw_scores = jnp.einsum(
-        "qhd,khd->hqk", queries, key_piece, preferred_element_type=jnp.float32
+        "qhd,hdk->hqk", queries, key_piece, preferred_element_type=jnp.float32
     ) * queries.shape[2] ** (-0.5)
     return jnp.where(piece_allowed[None], raw_scores, -jnp.inf)
 
 
 def mix_piece(rounded_piece, value_piece):
     return jnp.einsum(
-        "hqk,khd->qhd", rounded_piece, value_piece, preferred_element_type=jnp.float32
+        "hqk,hdk->qhd", rounded_piece, value_piece, preferred_element_type=jnp.float32
     )
 
 
@@ -58,18 +59,19 @@
     expert_count = router_weight.shape[1]
     replicas = seq_count // expert_count
     seq_place = lax.axis_index("seq")
-    joined_rows = jnp.concatenate(
+    joined_rows_t = jnp.concatenate(
         (
-            key_rows.reshape(tok_local, head_count, group_width),
-            value_rows.reshape(tok_local, head_count, group_width),
+            jnp.transpose(key_rows).reshape(head_count, group_width, tok_local),
+            jnp.transpose(value_rows).reshape(head_count, group_width, tok_local),
         ),
-        2,
+        1,
     )
-    joined_head = lax.all_to_all(
-        joined_rows, "head", split_axis=1, concat_axis=0, tiled=True
-    ).reshape(stretch_len, 2 * group_width)
-    key_head = joined_head[:, :group_width]
-    value_head = joined_head[:, group_width:]
+    joined_head_t = lax.all_to_all(
+        joined_rows_t, "head", split_axis=0, concat_axis=2, tiled=True
+    ).reshape(2 * group_width, stretch_len)
+    joined_head_t = with_layout_constraint(joined_head_t, Layout(major_to_minor=(0, 1)))
+    key_head = jnp.transpose(joined_head_t[:group_width])
+    value_head = jnp.transpose(joined_head_t[group_width:])
     query_head = lax.all_to_all(
         query_rows.reshape(tok_local, head_count, group_width),
         "head",
@@ -79,14 +81,14 @@
     ).reshape(stretch_len, group_width)
     all_segments = lax.all_gather(segment_ids, "seq", axis=0, tiled=True)
     if span_count == seq_count:
-        joined_window = lax.all_gather(joined_head, "seq", axis=0, tiled=True)
+        joined_window_t = lax.all_gather(joined_head_t, "seq", axis=1, tiled=True)
         segment_window = all_segments
         window_first = 0
     else:
-        pieces = [joined_head]
+        pieces = [joined_head_t]
         for distance in range(1, span_count):
-            pieces.append(passed_along(joined_head, "seq", distance))
-        joined_window = jnp.concatenate(pieces[::-1], 0)
+            pieces.append(passed_along(joined_head_t, "seq", distance))
+        joined_window_t = jnp.concatenate(pieces[::-1], 1)
         front_rows = (span_count - 1) * stretch_len
         segment_window = lax.dynamic_slice_in_dim(
             jnp.concatenate((jnp.zeros((front_rows,), jnp.int32), all_segments), 0),
@@ -95,9 +97,10 @@
             0,
         )
         window_first = (seq_place - span_count + 1) * stretch_len
-    key_window = joined_window[:, :group_width]
-    value_window = joined_window[:, group_width:]
     key_total = span_count * stretch_len
+    joined_window_t = with_layout_constraint(joined_window_t, Layout(major_to_minor=(0, 1)))
+    keys_t = joined_window_t[:group_width].reshape(heads_here, HDIM, key_total)
+    values_t = joined_window_t[group_width:].reshape(heads_here, HDIM, key_total)
     query_place = seq_place * stretch_len + jnp.arange(stretch_len, dtype=jnp.int32)
     key_place = window_first + jnp.arange(key_total, dtype=jnp.int32)
     allowed = (
@@ -106,13 +109,11 @@
         & (key_place[None, :] >= 0)
     )
     queries = query_head.reshape(stretch_len, heads_here, HDIM)
-    keys_all = key_window.reshape(key_total, heads_here, HDIM)
-    values_all = value_window.reshape(key_total, heads_here, HDIM)
-    masked = score_piece(queries, keys_all, allowed)
+    masked = score_piece(queries, keys_t, allowed)
     row_max = jnp.max(masked, -1, keepdims=True)
     weights = jnp.where(allowed[None], jnp.exp(masked - row_max), 0.0)
     totals = jnp.sum(weights, -1)
-    mixture = mix_piece(weights.astype(jnp.bfloat16), values_all)
+    mixture = mix_piece(weights.astype(jnp.bfloat16), values_t)
     attention = (
         (mixture / jnp.transpose(totals)[:, :, None])
         .astype(jnp.bfloat16)

time: 214 us -> 210 us (0.981)
  local copies, waits for them, and re-layouts: 25.7 us -> 18.5 us
  waiting for transfers between devices: 99 us -> 103 us
    slice x4 -> x1, local copies, waits for them, and re-layouts: 10.6 us -> 3.24 us  [per_device(): keys_t = joined_window_t[:group_width].reshape(heads_here, HDIM, key_total)]
    unnamed x5, waiting for transfers between devices: 25.4 us -> 28.8 us
    unnamed x18 -> x16, local copies, waits for them, and re-layouts: 6.09 us -> 2.67 us
    reshape x2 -> x3, local copies, waits for them, and re-layouts: 3.06 us -> 4.9 us  [the longest x1 1.84 us: per_device(): joined_head_t = lax.all_to_all(joined_rows_t, 'head', split_axis=0, conca...]
  transfers between devices with their start and end apart: 6 -> 6, of which waited for: 5 -> 5; matrix products, arithmetic and copies ran while one was open for 5% -> 3% of each run, Pallas kernels for 0% -> 0%
where the time goes in v12:
time: 210 us
  waiting for transfers between devices  103 us (49%)
  blocking collectives  38.5 us (18%)
  matrix products  24.5 us (12%)
  local copies, waits for them, and re-layouts  18.5 us (9%)
  between operations  13.9 us (7%)
  starting transfers between devices  7.7 us (4%)
  other arithmetic  3.62 us (2%)
    all_gather x1, waiting for transfers between devices, per_device(): group_rows = lax.all_gather(arrived, 'head', axis=0, tiled=True)  29.6 us
    unnamed x5, waiting for transfers between devices  28.8 us
    reduce_scatter x1, waiting for transfers between devices, per_device(): lax.psum_scatter(jnp.dot(attention, out_weight, preferred_element_type=jn...  21.3 us
    all_to_all x1, blocking collectives, per_device(): lax.all_to_all(joined_rows_t, 'head', split_axis=0, concat_axis=2, tiled=...  15.8 us
    all_to_all x1, blocking collectives, per_device(): lax.all_to_all(outgoing, 'seq', split_axis=0, concat_axis=0, tiled=True)  13.9 us
    all_gather x1, waiting for transfers between devices, per_device(): joined_window_t = lax.all_gather(joined_head_t, 'seq', axis=1, tiled=True)  12.7 us
    all_to_all x1, waiting for transfers between devices, per_device(): lax.all_to_all(shard_out, 'seq', split_axis=0, concat_axis=0, tiled=True)  10.4 us
    all_gather x1, blocking collectives, per_device(): all_segments = lax.all_gather(segment_ids, 'seq', axis=0, tiled=True)  8.76 us
  transfers between devices with their start and end apart: 6, of which 5 were waited for; matrix products, arithmetic and copies ran while one was open for 3% of the time, Pallas kernels for 0%

profile of v12, /device:TPU:0, one launch (start us, length us, event | category | flops | bytes accessed | tf_op | source)
XLA Modules:
  0.0 209.5 jit_solution(672731239730402618)
XLA Ops:
  7.2 0.0 copy-start
  7.2 0.0 copy-start.5
  7.2 0.0 all-gather.4.cloned.1.call-start
  7.2 1.3 reshape.140
  8.5 1.8 reshape.141
  10.3 1.1 pad_maximum_fusion
  11.5 15.8 %all_to_all.40 = bf16[4,1152,32]{1,2,0:T(8,128)(2,1)} all-to-all(bf16[4,1152,32]{1,2,0:T(8,128)(2,1)S(1)} %copy.78), channel_id=1, replica_groups=mesh['seq'=8,'head'=4] {'head'}, dimensions={0} | all-to-all | bytes 589824 | tf_op jit(solution)/shard_map/all_to_all | solution.py:69
  27.3 1.8 copy.79
  29.1 0.0 all-gather.4.cloned.1.call-update
  29.1 1.1 reshape.145
  30.2 0.7 copy.80
  30.9 3.3 %all-to-all-start.1 = ((bf16[32,4,576]{2,0,1:T(8,128)(2,1)}), bf16[32,4,576]{2,0,1:T(8,128)(2,1)S(1)}, u32[]{:S(2)}, u32[]{:S(2)}) async-start(bf16[32,4,576]{2,0,1:T(8,128)(2,1)} %copy.80), calls=%async_computation.1 | async-start | bytes 327680 | tf_op jit(solution)/shard_map/all_to_all | solution.py:75
  34.3 0.0 reduce-scatter.5.cloned.1.call-start
  34.3 0.0 copy-done.5
  34.3 8.8 %all-gather = s32[8,1,128]{2,1,0:T(1,128)S(1)} all-gather(s32[1,1,128]{2,1,0:T(1,128)S(1)} %bitcast.113), channel_id=1, replica_groups=mesh['seq'=8,'head'=4] {'seq'}, dimensions={0}, use_global_device_ids=true | all-gather | bytes 4608 | tf_op jit(solution)/shard_map/all_gather | solution.py:82
  43.1 0.9 fusion.36
  44.0 0.0 all-to-all-done.1
  44.0 1.1 reshape_reshape.3
  45.0 0.0 copy-start.2
  45.0 12.7 %all-gather.4.cloned.1.call-done = bf16[1152,1024]{1,0:T(8,128)(2,1)} async-done(((bf16[1152,128]{1,0:T(8,128)(2,1)}), bf16[1152,1024]{1,0:T(8,128)(2,1)}) %all-gather.4.cloned.1.call-update) | async-done | bytes 2359312 | tf_op jit(solution)/shard_map/all_gather | solution.py:84
  57.7 3.2 %fusion.65 = (bf16[576,1024]{1,0:T(8,128)(2,1)}, bf16[576,1024]{1,0:T(8,128)(2,1)}) fusion(bf16[1152,1024]{1,0:T(8,128)(2,1)} %all-gather.4.cloned.1.call-done), kind=kLoop, calls=%fused_computation.73 | loop fusion | bytes 4718592 | tf_op jit(solution)/shard_map/slice | solution.py:102
  61.0 0.0 copy-done.2
  61.0 5.3 %fusion.66 = (f32[9,128]{1,0:T(8,128)S(1)}, bf16[9,128,1024]{1,2,0:T(8,128)(2,1)}) fusion(pred[128,1024]{0,1:T(8,128)(4,1)S(1)} %copy-done.2, bf16[9,64,1024]{2,1,0:T(8,128)(2,1)} %bitcast.106, bf16[128,9,64]{2,1,0:T(8,128)(2,1)} %reshape_reshape.3), kind=kOutput, calls=%fused_computation.74 | convolution fusion | flops 158073856 | bytes 3822080 | tf_op jit(solution)/shard_map/sub | solution.py:114
  66.3 0.0 copy-start.1
  66.3 2.7 %fusion.31 = bf16[128,9,64]{0,2,1:T(8,128)(2,1)S(1)} fusion(bf16[9,64,1024]{2,1,0:T(8,128)(2,1)} %bitcast.105, bf16[9,128,1024]{1,2,0:T(8,128)(2,1)} %get-tuple-element.14, f32[128,9]{0,1:T(8,128)S(1)} %bitcast.114), kind=kOutput, calls=%fused_computation.30 | convolution fusion | flops 151142400 | bytes 3691008 | tf_op jit(solution)/shard_map/hqk,hdk->qhd/dot_general | solution.py:33
  69.0 0.0 copy-start.4
  69.0 0.0 copy-start.3
  69.0 0.1 copy-done.1
  69.1 1.5 convolution_convert_fusion.2
  70.5 0.0 reduce-scatter.5.cloned.1.call-update
  70.6 0.0 all-gather.6.cloned.1.call-start
  70.6 0.0 copy-done.4
  70.6 0.1 copy.83
  70.7 0.1 eq.88
  70.8 0.1 fusion.61
  70.9 0.1 reduce_window_sum.11
  71.0 0.2 select_reduce_fusion
  71.2 0.1 reduce_sum.50
  71.3 0.1 copy.84
  71.4 0.1 compare_reduce_fusion
  71.5 21.3 %reduce-scatter.5.cloned.1.call-done = bf16[32,2304]{1,0:T(8,128)(2,1)} async-done(((bf16[128,2304]{1,0:T(8,128)(2,1)}), bf16[32,2304]{1,0:T(8,128)(2,1)}) %reduce-scatter.5.cloned.1.call-update) | async-done | bytes 147472 | tf_op jit(solution)/shard_map/reduce_scatter | solution.py:122
  92.8 1.2 fusion.40
  93.9 0.0 copy-done.3
  93.9 0.4 convolution_convert_fusion.1
  94.3 13.9 %all_to_all.41 = bf16[8,9,2304]{2,1,0:T(8,128)(2,1)S(1)} all-to-all(bf16[8,9,2304]{2,1,0:T(8,128)(2,1)S(1)} %convolution_convert_fusion.1), channel_id=1, replica_groups=mesh['seq'=8,'head'=4] {'seq'}, dimensions={0} | all-to-all | bytes 663552 | tf_op jit(solution)/shard_map/all_to_all | solution.py:153
  108.2 0.8 copy.87
  109.1 0.0 all-gather.6.cloned.1.call-update
  109.1 0.0 reduce-scatter.7.cloned.1.call-start
  109.1 29.6 %all-gather.6.cloned.1.call-done = bf16[32,9,2304]{2,0,1:T(8,128)(2,1)} async-done(((bf16[8,9,2304]{2,0,1:T(8,128)(2,1)}), bf16[32,9,2304]{2,0,1:T(8,128)(2,1)}) %all-gather.6.cloned.1.call-update) | async-done | bytes 1327120 | tf_op jit(solution)/shard_map/all_gather | solution.py:154
  138.7 4.5 %fusion.12 = f32[32,9,720]{2,0,1:T(8,128)} fusion(bf16[32,9,2304]{2,0,1:T(8,128)(2,1)} %all-gather.6.cloned.1.call-done, bf16[2304,720]{0,1:T(8,128)(2,1)} %param.20), kind=kOutput, calls=%fused_computation.19 | convolution fusion | flops 955514880 | bytes 5474304 | tf_op jit(solution)/shard_map/rcd,df->rcf/dot_general | solution.py:155
  143.2 0.0 copy-done
  143.2 6.5 %fusion.1 = bf16[9,4,8,2304]{3,2,1,0:T(8,128)(2,1)} fusion(bf16[2304,720]{0,1:T(8,128)(2,1)S(1)} %copy-done, bf16[32,9,2304]{2,0,1:T(8,128)(2,1)} %all-gather.6.cloned.1.call-done, bf16[2304,720]{0,1:T(8,128)(2,1)} %param.21, f32[32,9,720]{2,0,1:T(8,128)} %fusion.12), kind=kOutput, calls=%fused_computation.4 | convolution fusion | flops 1912937472 | bytes 10119168 | tf_op jit(solution)/shard_map/rcf,df->rcd/dot_general | solution.py:160
  149.7 2.5 %copy.92 = bf16[9,4,8,2304]{3,2,0,1:T(8,128)(2,1)} copy(bf16[9,4,8,2304]{3,2,1,0:T(8,128)(2,1)} %fusion.1) | data formatting | bytes 2654208
  152.2 0.0 reduce-scatter.7.cloned.1.call-update
  152.2 0.1 copy.85
  152.3 1.7 slice_bitcast_fusion
  154.0 0.0 copy-done.6
  154.0 0.2 fusion.55
  154.2 28.8 %reduce-scatter.7.cloned.1.call-done = bf16[8,20736]{1,0:T(8,128)(2,1)} async-done(((bf16[32,20736]{1,0:T(8,128)(2,1)}), bf16[8,20736]{1,0:T(8,128)(2,1)}) %reduce-scatter.7.cloned.1.call-update) | async-done | bytes 331792
  183.0 1.9 copy.88
  184.8 4.2 %all-to-all-start.3 = ((bf16[8,9,2304]{2,1,0:T(8,128)(2,1)}), bf16[8,9,2304]{2,1,0:T(8,128)(2,1)}, u32[]{:S(2)}, u32[]{:S(2)}) async-start(bf16[8,9,2304]{2,1,0:T(8,128)(2,1)} %copy.88), calls=%async_computation.4 | async-start | bytes 1179648 | tf_op jit(solution)/shard_map/all_to_all | solution.py:164
  189.1 10.4 %all-to-all-done.3 = bf16[8,9,2304]{2,1,0:T(8,128)(2,1)} async-done(((bf16[8,9,2304]{2,1,0:T(8,128)(2,1)}), bf16[8,9,2304]{2,1,0:T(8,128)(2,1)}, u32[]{:S(2)}, u32[]{:S(2)}) %all-to-all-start.3) | async-done | bytes 331808 | tf_op jit(solution)/shard_map/all_to_all | solution.py:164
  199.5 1.4 fusion.7
  200.9 2.1 fusion.8
  (9 shorter events, 0.1 us)
Async XLA Ops:
  7.2 136.0 %copy-start = (bf16[2304,720]{0,1:T(8,128)(2,1)S(1)}, bf16[2304,720]{0,1:T(8,128)(2,1)}, u32[]{:S(2)}) copy-start(bf16[2304,720]{0,1:T(8,128)(2,1)} %param.22) | copy-start | bytes 9953284
  7.2 27.1 %copy-start.5 = (s32[128]{0:T(128)S(1)}, s32[128]{0:T(128)}, u32[]{:S(2)}) copy-start(s32[128]{0:T(128)} %param.18) | copy-start | bytes 1540
  7.2 50.5 %all-gather.4.cloned.1.call-start = ((), (), s32[]{:S(2)}) async-start(), calls=%async_computation.6 | async-start | bytes 2654208 | tf_op jit(solution)/shard_map/all_gather | solution.py:84
  30.9 13.0 %all-to-all-start.1 = ((bf16[32,4,576]{2,0,1:T(8,128)(2,1)}), bf16[32,4,576]{2,0,1:T(8,128)(2,1)S(1)}, u32[]{:S(2)}, u32[]{:S(2)}) async-start(bf16[32,4,576]{2,0,1:T(8,128)(2,1)} %copy.80), calls=%async_computation.1 | async-start | bytes 327680 | tf_op jit(solution)/shard_map/all_to_all | solution.py:75
  34.3 58.5 %reduce-scatter.5.cloned.1.call-start = ((), (), s32[]{:S(2)}) async-start(), calls=%async_computation.7 | async-start | bytes 737280 | tf_op jit(solution)/shard_map/reduce_scatter | solution.py:122
  45.0 15.9 %copy-start.2 = (pred[128,1024]{0,1:T(8,128)(4,1)S(1)}, pred[128,1024]{0,1:T(8,128)(4,1)}, u32[]{:S(2)}) copy-start(pred[128,1024]{0,1:T(8,128)(4,1)} %fusion.36) | copy-start | bytes 393220
  66.3 2.8 %copy-start.1 = (bf16[576,2304]{1,0:T(8,128)(2,1)S(1)}, bf16[576,2304]{1,0:T(8,128)(2,1)}, u32[]{:S(2)}) copy-start(bf16[576,2304]{1,0:T(8,128)(2,1)} %param.23) | copy-start | bytes 7962628
  69.0 1.6 copy-start.4
  69.0 24.9 %copy-start.3 = (f32[2304]{0:T(1024)S(1)}, f32[2304]{0:T(1024)}, u32[]{:S(2)}) copy-start(f32[2304]{0:T(1024)} %param.16) | copy-start | bytes 27652
  70.6 68.1 %all-gather.6.cloned.1.call-start = ((), (), s32[]{:S(2)}) async-start(), calls=%async_computation.8 | async-start | bytes 1658880 | tf_op jit(solution)/shard_map/all_gather | solution.py:154
  109.1 73.9 %reduce-scatter.7.cloned.1.call-start = ((), (), s32[]{:S(2)}) async-start(), calls=%async_computation.9 | async-start | bytes 1658880
  149.7 4.3 %copy-start.6 = (bf16[2304,8]{0,1:T(8,128)(2,1)S(1)}, bf16[2304,8]{0,1:T(8,128)(2,1)}, u32[]{:S(2)}) copy-start(bf16[2304,8]{0,1:T(8,128)(2,1)} %param.17) | copy-start | bytes 110596
  184.8 14.7 %all-to-all-start.3 = ((bf16[8,9,2304]{2,1,0:T(8,128)(2,1)}), bf16[8,9,2304]{2,1,0:T(8,128)(2,1)}, u32[]{:S(2)}, u32[]{:S(2)}) async-start(bf16[8,9,2304]{2,1,0:T(8,128)(2,1)} %copy.88), calls=%async_computation.4 | async-start | bytes 1179648 | tf_op jit(solution)/shard_map/all_to_all | solution.py:164
Sparse Core Ops, SparseCore 0:
  29.2 28.4 all-gather.3
  70.7 22.0 reduce-scatter.4
  109.2 29.4 all-gather.5
  152.3 30.6 reduce-scatter.6

commit v13 on v12

--- a/solution.py
+++ b/solution.py
@@ -151,16 +151,20 @@
         seq_count, CAP, D
     )
     arrived = lax.all_to_all(outgoing, "seq", split_axis=0, concat_axis=0, tiled=True)
-    group_rows = lax.all_gather(arrived, "head", axis=0, tiled=True)
+    group_rows = lax.all_gather(jnp.swapaxes(arrived, 0, 1), "head", axis=0, tiled=False)
     gate_act = jnp.einsum(
-        "rcd,df->rcf", group_rows, gate_weight, preferred_element_type=jnp.float32
-    )
-    up_act = jnp.einsum("rcd,df->rcf", group_rows, up_weight, preferred_element_type=jnp.float32)
+        "hcsd,df->hcsf", group_rows, gate_weight, preferred_element_type=jnp.float32
+    )
+    up_act = jnp.einsum(
+        "hcsd,df->hcsf", group_rows, up_weight, preferred_element_type=jnp.float32
+    )
     hidden = (jax.nn.silu(gate_act) * up_act).astype(jnp.bfloat16)
     partial_out = jnp.einsum(
-        "rcf,df->rcd", hidden, down_weight, preferred_element_type=jnp.float32
+        "hcsf,df->hcsd", hidden, down_weight, preferred_element_type=jnp.float32
     ).astype(jnp.bfloat16)
-    shard_out = lax.psum_scatter(partial_out, "head", scatter_dimension=0, tiled=True)
+    shard_out = jnp.swapaxes(
+        lax.psum_scatter(partial_out, "head", scatter_dimension=0, tiled=False), 0, 1
+    )
     returned = lax.all_to_all(shard_out, "seq", split_axis=0, concat_axis=0, tiled=True)
     by_expert = returned.reshape(expert_count, replicas, CAP, D)
     first_hot = (slot_ids[:, 0, None, None] == slot_grid[None]).astype(jnp.bfloat16)

time: 210 us -> 204 us (0.971)
  matrix products: 24.5 us -> 20.9 us
  local copies, waits for them, and re-layouts: 18.5 us -> 16.1 us
    unnamed x5 -> x4, waiting for transfers between devices: 28.8 us -> 0.07 us
    reduce_scatter x0 -> x1, waiting for transfers between devices: none -> 28.8 us  [per_device(): lax.psum_scatter(partial_out, 'head', scatter_dimension=0, tiled=False)]
    dot_general x2 -> x3, matrix products: 11 us -> 7.34 us  [the longest x1 3.71 us: per_device(): jnp.einsum('hcsd,df->hcsf', group_rows, gate_weight, preferred_element_ty...]
    transpose x0 -> x2, local copies, waits for them, and re-layouts: none -> 2.72 us  [the longest x1 1.88 us: per_device(): jnp.swapaxes(lax.psum_scatter(partial_out, 'head', scatter_dimension=0, t...]
    unnamed x16 -> x19, local copies, waits for them, and re-layouts: 2.67 us -> 0.21 us
where the time goes in v13:
time: 204 us
  waiting for transfers between devices  103 us (50%)
  blocking collectives  38.5 us (19%)
  matrix products  20.9 us (10%)
  local copies, waits for them, and re-layouts  16.1 us (8%)
  between operations  14 us (7%)
  starting transfers between devices  7.71 us (4%)
  other arithmetic  3.62 us (2%)
    all_gather x1, waiting for transfers between devices, per_device(): lax.all_gather(jnp.swapaxes(arrived, 0, 1), 'head', axis=0, tiled=False)  29.6 us
    reduce_scatter x1, waiting for transfers between devices, per_device(): lax.psum_scatter(partial_out, 'head', scatter_dimension=0, tiled=False)  28.8 us
    reduce_scatter x1, waiting for transfers between devices, per_device(): lax.psum_scatter(jnp.dot(attention, out_weight, preferred_element_type=jn...  21.3 us
    all_to_all x1, blocking collectives, per_device(): lax.all_to_all(joined_rows_t, 'head', split_axis=0, concat_axis=2, tiled=...  15.8 us
    all_to_all x1, blocking collectives, per_device(): lax.all_to_all(outgoing, 'seq', split_axis=0, concat_axis=0, tiled=True)  13.9 us
    all_gather x1, waiting for transfers between devices, per_device(): joined_window_t = lax.all_gather(joined_head_t, 'seq', axis=1, tiled=True)  12.7 us
    all_to_all x1, waiting for transfers between devices, per_device(): lax.all_to_all(shard_out, 'seq', split_axis=0, concat_axis=0, tiled=True)  10.4 us
    all_gather x1, blocking collectives, per_device(): all_segments = lax.all_gather(segment_ids, 'seq', axis=0, tiled=True)  8.76 us
  transfers between devices with their start and end apart: 6, of which 5 were waited for; matrix products, arithmetic and copies ran while one was open for 3% of the time, Pallas kernels for 0%

profile of v13, /device:TPU:0, one launch (start us, length us, event | category | flops | bytes accessed | tf_op | source)
XLA Modules:
  0.0 203.5 jit_solution(4120318202697634740)
XLA Ops:
  7.2 0.0 copy-start
  7.2 0.0 copy-start.5
  7.2 0.0 all-gather.5.cloned.1.call-start
  7.2 1.3 reshape.140
  8.5 1.8 reshape.141
  10.3 1.1 pad_maximum_fusion
  11.4 15.8 %all_to_all.40 = bf16[4,1152,32]{1,2,0:T(8,128)(2,1)} all-to-all(bf16[4,1152,32]{1,2,0:T(8,128)(2,1)S(1)} %copy.77), channel_id=1, replica_groups=mesh['seq'=8,'head'=4] {'head'}, dimensions={0} | all-to-all | bytes 589824 | tf_op jit(solution)/shard_map/all_to_all | solution.py:69
  27.2 1.9 copy.78
  29.1 0.0 all-gather.5.cloned.1.call-update
  29.1 1.1 reshape.145
  30.3 0.7 copy.79
  30.9 3.3 %all-to-all-start.1 = ((bf16[32,4,576]{2,0,1:T(8,128)(2,1)}), bf16[32,4,576]{2,0,1:T(8,128)(2,1)S(1)}, u32[]{:S(2)}, u32[]{:S(2)}) async-start(bf16[32,4,576]{2,0,1:T(8,128)(2,1)} %copy.79), calls=%async_computation.1 | async-start | bytes 327680 | tf_op jit(solution)/shard_map/all_to_all | solution.py:75
  34.3 0.0 reduce-scatter.3.cloned.1.call-start
  34.4 0.0 copy-done.5
  34.4 8.8 %all-gather.1 = s32[8,1,128]{2,1,0:T(1,128)S(1)} all-gather(s32[1,1,128]{2,1,0:T(1,128)S(1)} %bitcast.118), channel_id=1, replica_groups=mesh['seq'=8,'head'=4] {'seq'}, dimensions={0}, use_global_device_ids=true | all-gather | bytes 4608 | tf_op jit(solution)/shard_map/all_gather | solution.py:82
  43.1 0.9 fusion.33
  44.0 0.0 all-to-all-done.1
  44.0 1.1 reshape_reshape.3
  45.1 12.7 %all-gather.5.cloned.1.call-done = bf16[1152,1024]{1,0:T(8,128)(2,1)} async-done(((bf16[1152,128]{1,0:T(8,128)(2,1)}), bf16[1152,1024]{1,0:T(8,128)(2,1)}) %all-gather.5.cloned.1.call-update) | async-done | bytes 2359312 | tf_op jit(solution)/shard_map/all_gather | solution.py:84
  57.8 3.2 %fusion.60 = (bf16[576,1024]{1,0:T(8,128)(2,1)}, bf16[576,1024]{1,0:T(8,128)(2,1)}) fusion(bf16[1152,1024]{1,0:T(8,128)(2,1)} %all-gather.5.cloned.1.call-done), kind=kLoop, calls=%fused_computation.70 | loop fusion | bytes 4718592 | tf_op jit(solution)/shard_map/slice | solution.py:102
  61.0 0.0 copy-done.2
  61.0 5.3 %fusion.61 = (f32[9,128]{1,0:T(8,128)S(1)}, bf16[9,128,1024]{1,2,0:T(8,128)(2,1)}) fusion(pred[128,1024]{0,1:T(8,128)(4,1)S(1)} %copy-done.2, bf16[9,64,1024]{2,1,0:T(8,128)(2,1)} %bitcast.111, bf16[128,9,64]{2,1,0:T(8,128)(2,1)} %reshape_reshape.3), kind=kOutput, calls=%fused_computation.71 | convolution fusion | flops 158073856 | bytes 3822080 | tf_op jit(solution)/shard_map/sub | solution.py:114
  66.3 2.7 %fusion.30 = bf16[128,9,64]{0,2,1:T(8,128)(2,1)S(1)} fusion(bf16[9,64,1024]{2,1,0:T(8,128)(2,1)} %bitcast.110, bf16[9,128,1024]{1,2,0:T(8,128)(2,1)} %get-tuple-element.14, f32[128,9]{0,1:T(8,128)S(1)} %bitcast.121), kind=kOutput, calls=%fused_computation.29 | convolution fusion | flops 151142400 | bytes 3691008 | tf_op jit(solution)/shard_map/hqk,hdk->qhd/dot_general | solution.py:33
  69.0 0.0 copy-start.4
  69.0 0.0 copy-start.3
  69.0 0.1 copy-done.1
  69.1 1.5 convolution_convert_fusion.2
  70.6 0.0 reduce-scatter.3.cloned.1.call-update
  70.6 0.0 all-gather.7.cloned.1.call-start
  70.6 0.0 copy-done.4
  70.7 0.1 copy.82
  70.7 0.1 eq.88
  70.9 0.1 fusion.57
  70.9 0.1 reduce_window_sum.11
  71.0 0.2 select_reduce_fusion
  71.2 0.1 reduce_sum.50
  71.3 0.1 copy.83
  71.4 0.1 compare_reduce_fusion
  71.5 21.3 %reduce-scatter.3.cloned.1.call-done = bf16[32,2304]{1,0:T(8,128)(2,1)} async-done(((bf16[128,2304]{1,0:T(8,128)(2,1)}), bf16[32,2304]{1,0:T(8,128)(2,1)}) %reduce-scatter.3.cloned.1.call-update) | async-done | bytes 147472 | tf_op jit(solution)/shard_map/reduce_scatter | solution.py:122
  92.8 1.2 fusion.36
  94.0 0.0 copy-done.3
  94.0 0.4 convolution_convert_fusion.1
  94.3 13.9 %all_to_all.41 = bf16[8,9,2304]{2,1,0:T(8,128)(2,1)S(1)} all-to-all(bf16[8,9,2304]{2,1,0:T(8,128)(2,1)S(1)} %convolution_convert_fusion.1), channel_id=1, replica_groups=mesh['seq'=8,'head'=4] {'seq'}, dimensions={0} | all-to-all | bytes 663552 | tf_op jit(solution)/shard_map/all_to_all | solution.py:153
  108.2 0.8 copy.86
  109.1 0.0 all-gather.7.cloned.1.call-update
  109.1 0.0 reduce-scatter.5.cloned.1.call-start
  109.2 29.6 %all-gather.7.cloned.1.call-done = bf16[36,8,2304]{2,1,0:T(8,128)(2,1)} async-done(((bf16[9,8,2304]{2,1,0:T(8,128)(2,1)}), bf16[36,8,2304]{2,1,0:T(8,128)(2,1)}) %all-gather.7.cloned.1.call-update) | async-done | bytes 1327120 | tf_op jit(solution)/shard_map/all_gather | solution.py:154
  138.8 3.7 %fusion.11 = f32[4,9,8,720]{3,2,1,0:T(8,128)S(1)} fusion(bf16[4,9,8,2304]{3,2,1,0:T(8,128)(2,1)} %bitcast.119, bf16[2304,720]{0,1:T(8,128)(2,1)} %param.20), kind=kOutput, calls=%fused_computation.18 | convolution fusion | flops 955514880 | bytes 5474304 | tf_op jit(solution)/shard_map/hcsd,df->hcsf/dot_general | solution.py:155
  142.5 0.0 copy-done.6
  142.5 0.0 copy-done.7
  142.5 1.3 fusion.21
  143.9 0.0 copy-start.8
  143.9 2.3 %convolution_convert_fusion = bf16[4,9,8,2304]{3,2,1,0:T(8,128)(2,1)} fusion(bf16[4,9,8,720]{3,2,1,0:T(8,128)(2,1)S(1)} %fusion.21, bf16[2304,720]{0,1:T(8,128)(2,1)S(1)} %copy-done), kind=kOutput, calls=%fused_computation.3 | convolution fusion | flops 956178432 | bytes 5059584 | tf_op jit(solution)/shard_map/hcsf,df->hcsd/dot_general | solution.py:162
  146.2 0.0 reduce-scatter.5.cloned.1.call-update
  146.2 0.1 copy.84
  146.3 1.7 slice_bitcast_fusion
  148.0 0.0 copy-done.8
  148.0 0.2 fusion.51
  148.2 28.8 %reduce-scatter.5.cloned.1.call-done = bf16[1,9,8,2304]{3,2,1,0:T(8,128)(2,1)} async-done(((bf16[4,9,8,2304]{3,2,1,0:T(8,128)(2,1)}), bf16[1,9,8,2304]{3,2,1,0:T(8,128)(2,1)}) %reduce-scatter.5.cloned.1.call-update) | async-done | bytes 331792 | tf_op jit(solution)/shard_map/reduce_scatter | solution.py:166
  177.0 1.9 copy.87
  178.8 4.2 %all-to-all-start.3 = ((bf16[8,9,2304]{2,1,0:T(8,128)(2,1)}), bf16[8,9,2304]{2,1,0:T(8,128)(2,1)}, u32[]{:S(2)}, u32[]{:S(2)}) async-start(bf16[8,9,2304]{2,1,0:T(8,128)(2,1)} %copy.87), calls=%async_computation.5 | async-start | bytes 1179648 | tf_op jit(solution)/shard_map/all_to_all | solution.py:168
  183.1 10.4 %all-to-all-done.3 = bf16[8,9,2304]{2,1,0:T(8,128)(2,1)} async-done(((bf16[8,9,2304]{2,1,0:T(8,128)(2,1)}), bf16[8,9,2304]{2,1,0:T(8,128)(2,1)}, u32[]{:S(2)}, u32[]{:S(2)}) %all-to-all-start.3) | async-done | bytes 331808 | tf_op jit(solution)/shard_map/all_to_all | solution.py:168
  193.5 1.4 fusion.6
  194.9 2.1 %fusion.7 = bf16[32,2304]{1,0:T(8,128)(2,1)} fusion(f32[32,2304]{1,0:T(8,128)S(1)} %fusion.6, bf16[8,9,2304]{2,1,0:T(8,128)(2,1)} %all-to-all-done.3, bf16[32,2304]{1,0:T(8,128)(2,1)S(1)} %get-tuple-element.4, f32[32]{0:T(128)S(1)} %get-tuple-element.11, s32[32]{0:T(128)S(1)} %get-tuple-element.9, s32[8,9]{1,0:T(8,128)S(1)} %copy.84), kind=kOutput, calls=%fused_computation.14 | convolution fusion | flops 11061504 | bytes 922144 | tf_op jit(solution)/shard_map/tec,ercd->trd/dot_general | solution.py:176
  (13 shorter events, 0.1 us)
Async XLA Ops:
  7.2 136.7 %copy-start = (bf16[2304,720]{0,1:T(8,128)(2,1)S(1)}, bf16[2304,720]{0,1:T(8,128)(2,1)}, u32[]{:S(2)}) copy-start(bf16[2304,720]{0,1:T(8,128)(2,1)} %param.22) | copy-start | bytes 9953284
  7.2 27.2 %copy-start.5 = (s32[128]{0:T(128)S(1)}, s32[128]{0:T(128)}, u32[]{:S(2)}) copy-start(s32[128]{0:T(128)} %param.18) | copy-start | bytes 1540
  7.2 50.6 %all-gather.5.cloned.1.call-start = ((), (), s32[]{:S(2)}) async-start(), calls=%async_computation.6 | async-start | bytes 2654208 | tf_op jit(solution)/shard_map/all_gather | solution.py:84
  30.9 13.1 %all-to-all-start.1 = ((bf16[32,4,576]{2,0,1:T(8,128)(2,1)}), bf16[32,4,576]{2,0,1:T(8,128)(2,1)S(1)}, u32[]{:S(2)}, u32[]{:S(2)}) async-start(bf16[32,4,576]{2,0,1:T(8,128)(2,1)} %copy.79), calls=%async_computation.1 | async-start | bytes 327680 | tf_op jit(solution)/shard_map/all_to_all | solution.py:75
  34.3 58.5 %reduce-scatter.3.cloned.1.call-start = ((), (), s32[]{:S(2)}) async-start(), calls=%async_computation.7 | async-start | bytes 737280 | tf_op jit(solution)/shard_map/reduce_scatter | solution.py:122
  45.1 15.9 %copy-start.2 = (pred[128,1024]{0,1:T(8,128)(4,1)S(1)}, pred[128,1024]{0,1:T(8,128)(4,1)}, u32[]{:S(2)}) copy-start(pred[128,1024]{0,1:T(8,128)(4,1)} %fusion.33) | copy-start | bytes 393220
  66.3 2.8 %copy-start.1 = (bf16[576,2304]{1,0:T(8,128)(2,1)S(1)}, bf16[576,2304]{1,0:T(8,128)(2,1)}, u32[]{:S(2)}) copy-start(bf16[576,2304]{1,0:T(8,128)(2,1)} %param.23) | copy-start | bytes 7962628
  69.0 1.7 copy-start.4
  69.0 25.0 %copy-start.3 = (f32[2304]{0:T(1024)S(1)}, f32[2304]{0:T(1024)}, u32[]{:S(2)}) copy-start(f32[2304]{0:T(1024)} %param.16) | copy-start | bytes 27652
  70.6 68.2 %all-gather.7.cloned.1.call-start = ((), (), s32[]{:S(2)}) async-start(), calls=%async_computation.9 | async-start | bytes 1658880 | tf_op jit(solution)/shard_map/all_gather | solution.py:154
  109.1 67.9 %reduce-scatter.5.cloned.1.call-start = ((), (), s32[]{:S(2)}) async-start(), calls=%async_computation.8 | async-start | bytes 1658880 | tf_op jit(solution)/shard_map/reduce_scatter | solution.py:166
  138.8 3.7 %copy-start.6 = (bf16[2304,720]{0,1:T(8,128)(2,1)S(1)}, bf16[2304,720]{0,1:T(8,128)(2,1)}, u32[]{:S(2)}) copy-start(bf16[2304,720]{0,1:T(8,128)(2,1)} %param.21) | copy-start | bytes 9953284
  138.8 3.7 %copy-start.7 = (bf16[36,8,2304]{2,1,0:T(8,128)(2,1)S(1)}, bf16[36,8,2304]{2,1,0:T(8,128)(2,1)}, u32[]{:S(2)}) copy-start(bf16[36,8,2304]{2,1,0:T(8,128)(2,1)} %all-gather.7.cloned.1.call-done) | copy-start | bytes 3981316
  143.9 4.1 %copy-start.8 = (bf16[2304,8]{0,1:T(8,128)(2,1)S(1)}, bf16[2304,8]{0,1:T(8,128)(2,1)}, u32[]{:S(2)}) copy-start(bf16[2304,8]{0,1:T(8,128)(2,1)} %param.17) | copy-start | bytes 110596
  178.8 14.7 %all-to-all-start.3 = ((bf16[8,9,2304]{2,1,0:T(8,128)(2,1)}), bf16[8,9,2304]{2,1,0:T(8,128)(2,1)}, u32[]{:S(2)}, u32[]{:S(2)}) async-start(bf16[8,9,2304]{2,1,0:T(8,128)(2,1)} %copy.87), calls=%async_computation.5 | async-start | bytes 1179648 | tf_op jit(solution)/shard_map/all_to_all | solution.py:168
Sparse Core Ops, SparseCore 0:
  29.2 28.4 all-gather.4
  70.7 22.0 reduce-scatter.2
  109.2 29.4 all-gather.6
  146.3 30.6 reduce-scatter.4

commit v14 on v13

--- a/solution.py
+++ b/solution.py
@@ -3,6 +3,7 @@
 import jax
 import jax.numpy as jnp
 from jax import lax
+from jax.experimental import pallas as pl
 from jax.experimental.layout import Layout, with_layout_constraint
 from jax.sharding import PartitionSpec as P
 
@@ -33,6 +34,40 @@
     return jnp.einsum(
         "hqk,hdk->qhd", rounded_piece, value_piece, preferred_element_type=jnp.float32
     )
+
+
+def attention_project(q3, window_t, allowed, out_weight):
+    heads, tokens, _ = q3.shape
+    group_width = heads * HDIM
+
+    def kernel(q_ref, window_ref, allowed_ref, weight_ref, out_ref):
+        allowed_now = allowed_ref[...] != 0
+        total = jnp.zeros(out_ref.shape, jnp.float32)
+        for head in range(heads):
+            keys = window_ref[pl.ds(head * HDIM, HDIM), :]
+            values = window_ref[pl.ds(group_width + head * HDIM, HDIM), :]
+            raw = jnp.dot(q_ref[head], keys, preferred_element_type=jnp.float32) * HDIM ** (-0.5)
+            masked = jnp.where(allowed_now, raw, -jnp.inf)
+            top = jnp.max(masked, axis=1, keepdims=True)
+            weights = jnp.where(allowed_now, jnp.exp(masked - top), 0.0)
+            sums = jnp.sum(weights, axis=1, keepdims=True)
+            mixed = lax.dot_general(
+                weights.astype(jnp.bfloat16),
+                values,
+                (((1,), (1,)), ((), ())),
+                preferred_element_type=jnp.float32,
+            )
+            attended = (mixed / sums).astype(jnp.bfloat16)
+            total = total + jnp.dot(
+                attended,
+                weight_ref[pl.ds(head * HDIM, HDIM), :],
+                preferred_element_type=jnp.float32,
+            )
+        out_ref[...] = total.astype(out_ref.dtype)
+
+    return pl.pallas_call(
+        kernel, out_shape=jax.ShapeDtypeStruct((tokens, out_weight.shape[1]), jnp.bfloat16)
+    )(q3, window_t, allowed.astype(jnp.int32), out_weight)
 
 
 def per_device(
@@ -99,8 +134,6 @@
         window_first = (seq_place - span_count + 1) * stretch_len
     key_total = span_count * stretch_len
     joined_window_t = with_layout_constraint(joined_window_t, Layout(major_to_minor=(0, 1)))
-    keys_t = joined_window_t[:group_width].reshape(heads_here, HDIM, key_total)
-    values_t = joined_window_t[group_width:].reshape(heads_here, HDIM, key_total)
     query_place = seq_place * stretch_len + jnp.arange(stretch_len, dtype=jnp.int32)
     key_place = window_first + jnp.arange(key_total, dtype=jnp.int32)
     allowed = (
@@ -108,19 +141,9 @@
         & (key_place[None, :] <= query_place[:, None])
         & (key_place[None, :] >= 0)
     )
-    queries = query_head.reshape(stretch_len, heads_here, HDIM)
-    masked = score_piece(queries, keys_t, allowed)
-    row_max = jnp.max(masked, -1, keepdims=True)
-    weights = jnp.where(allowed[None], jnp.exp(masked - row_max), 0.0)
-    totals = jnp.sum(weights, -1)
-    mixture = mix_piece(weights.astype(jnp.bfloat16), values_t)
-    attention = (
-        (mixture / jnp.transpose(totals)[:, :, None])
-        .astype(jnp.bfloat16)
-        .reshape(stretch_len, group_width)
-    )
+    queries = jnp.transpose(query_head.reshape(stretch_len, heads_here, HDIM), (1, 0, 2))
     attended_sum = lax.psum_scatter(
-        jnp.dot(attention, out_weight, preferred_element_type=jnp.float32).astype(jnp.bfloat16),
+        attention_project(queries, joined_window_t, allowed, out_weight),
         "head",
         scatter_dimension=0,
         tiled=True,

time: 204 us -> 201 us (0.985)
  Pallas kernels: 0 us -> 9.87 us
  matrix products: 20.9 us -> 11.4 us
    pallas_call x0 -> x1, Pallas kernels: none -> 9.87 us  [attention_project(): pl.pallas_call(kernel, out_shape=jax.ShapeDtypeStruct((tokens, out_weight...]
    sub x1 -> x0, matrix products: 5.28 us -> none  [per_device(): weights = jnp.where(allowed[None], jnp.exp(masked - row_max), 0.0)]
    dot_general x2 -> x0, matrix products: 4.2 us -> none  [the longest x1 2.71 us: mix_piece(): jnp.einsum('hqk,hdk->qhd', rounded_piece, value_piece, preferred_element_...]
    slice x1 -> x0, local copies, waits for them, and re-layouts: 3.23 us -> none  [per_device(): keys_t = joined_window_t[:group_width].reshape(heads_here, HDIM, key_total)]
  transfers between devices with their start and end apart: 6 -> 6, of which waited for: 5 -> 5; matrix products, arithmetic and copies ran while one was open for 3% -> 4% of each run, Pallas kernels for 0% -> 0%
where the time goes in v14:
time: 201 us
  waiting for transfers between devices  101 us (50%)
  blocking collectives  38.5 us (19%)
  local copies, waits for them, and re-layouts  14.6 us (7%)
  between operations  13.9 us (7%)
  matrix products  11.4 us (6%)
  Pallas kernels  9.87 us (5%)
  starting transfers between devices  7.7 us (4%)
  other arithmetic  3.72 us (2%)
    all_gather x1, waiting for transfers between devices, per_device(): lax.all_gather(jnp.swapaxes(arrived, 0, 1), 'head', axis=0, tiled=False)  29.6 us
    reduce_scatter x1, waiting for transfers between devices, per_device(): lax.psum_scatter(partial_out, 'head', scatter_dimension=0, tiled=False)  28.8 us
    reduce_scatter x1, waiting for transfers between devices, per_device(): lax.psum_scatter(attention_project(queries, joined_window_t, allowed, out...  21.2 us
    all_to_all x1, blocking collectives, per_device(): lax.all_to_all(joined_rows_t, 'head', split_axis=0, concat_axis=2, tiled=...  15.8 us
    all_to_all x1, blocking collectives, per_device(): lax.all_to_all(outgoing, 'seq', split_axis=0, concat_axis=0, tiled=True)  14 us
    all_gather x1, waiting for transfers between devices, per_device(): joined_window_t = lax.all_gather(joined_head_t, 'seq', axis=1, tiled=True)  10.8 us
    all_to_all x1, waiting for transfers between devices, per_device(): lax.all_to_all(shard_out, 'seq', split_axis=0, concat_axis=0, tiled=True)  10.4 us
    pallas_call x1, Pallas kernels, attention_project(): pl.pallas_call(kernel, out_shape=jax.ShapeDtypeStruct((tokens, out_weight...  9.87 us
  transfers between devices with their start and end apart: 6, of which 5 were waited for; matrix products, arithmetic and copies ran while one was open for 4% of the time, Pallas kernels for 0%

profile of v14, /device:TPU:0, one launch (start us, length us, event | category | flops | bytes accessed | tf_op | source)
XLA Modules:
  0.0 200.6 jit_solution(2234687366334357338)
XLA Ops:
  7.2 0.0 copy-start
  7.2 0.0 copy-start.3
  7.2 0.0 all-gather.5.cloned.1.call-start
  7.2 1.3 reshape.82
  8.5 1.8 reshape.83
  10.3 1.1 pad_maximum_fusion
  11.5 15.8 %all_to_all.40 = bf16[4,1152,32]{1,2,0:T(8,128)(2,1)} all-to-all(bf16[4,1152,32]{1,2,0:T(8,128)(2,1)S(1)} %copy.73), channel_id=1, replica_groups=mesh['seq'=8,'head'=4] {'head'}, dimensions={0} | all-to-all | bytes 589824 | tf_op jit(solution)/shard_map/all_to_all | solution.py:104
  27.3 1.9 copy.74
  29.1 0.0 all-gather.5.cloned.1.call-update
  29.1 1.1 reshape.81
  30.3 0.7 copy.71
  31.0 3.3 %all-to-all-start = ((bf16[32,4,576]{2,0,1:T(8,128)(2,1)}), bf16[32,4,576]{2,0,1:T(8,128)(2,1)S(1)}, u32[]{:S(2)}, u32[]{:S(2)}) async-start(bf16[32,4,576]{2,0,1:T(8,128)(2,1)} %copy.71), calls=%async_computation | async-start | bytes 327680 | tf_op jit(solution)/shard_map/all_to_all | solution.py:110
  34.3 0.0 reduce-scatter.3.cloned.1.call-start
  34.4 0.0 copy-done.3
  34.4 8.8 %all-gather.1 = s32[8,1,128]{2,1,0:T(1,128)S(1)} all-gather(s32[1,1,128]{2,1,0:T(1,128)S(1)} %bitcast.92), channel_id=1, replica_groups=mesh['seq'=8,'head'=4] {'seq'}, dimensions={0}, use_global_device_ids=true | all-gather | bytes 4608 | tf_op jit(solution)/shard_map/all_gather | solution.py:117
  43.1 1.0 fusion.18.allowed_ref
  44.1 0.0 all-to-all-done
  44.1 1.0 reshape_reshape.3
  45.2 1.9 copy.87
  47.0 10.8 %all-gather.5.cloned.1.call-done.window_ref = bf16[1152,1024]{1,0:T(8,128)(2,1)} async-done(((bf16[1152,128]{1,0:T(8,128)(2,1)}), bf16[1152,1024]{1,0:T(8,128)(2,1)}) %all-gather.5.cloned.1.call-update) | async-done | bytes 2359312 | tf_op jit(solution)/shard_map/all_gather | solution.py:119
  57.8 0.0 copy-start.2
  57.8 0.0 copy-start.1
  57.8 9.9 %shard_map.139 = bf16[128,2304]{1,0:T(8,128)(2,1)} custom-call(bf16[9,128,64]{2,1,0:T(8,128)(2,1)} %bitcast.85, bf16[1152,1024]{1,0:T(8,128)(2,1)} %all-gather.5.cloned.1.call-done.window_ref, s32[128,1024]{1,0:T(8,128)} %fusion.18.allowed_ref, bf16[576,2304]{1,0:T(8,128)(2,1)} %weight_ref.1), custom_call_target="tpu_custom_call" | custom-call | tf_op jit(solution)/shard_map/pallas_call | solution.py:68
  67.6 0.0 reduce-scatter.3.cloned.1.call-update
  67.7 0.0 all-gather.7.cloned.1.call-start
  67.7 0.0 copy-done.2
  67.7 0.1 copy.75
  67.8 0.1 eq.84
  67.9 0.1 fusion.33
  68.0 0.1 reduce_window_sum.11
  68.1 0.2 select_reduce_fusion
  68.3 0.1 reduce_sum.40
  68.4 0.1 copy.76
  68.5 0.1 compare_reduce_fusion
  68.6 21.2 %reduce-scatter.3.cloned.1.call-done = bf16[32,2304]{1,0:T(8,128)(2,1)} async-done(((bf16[128,2304]{1,0:T(8,128)(2,1)}), bf16[32,2304]{1,0:T(8,128)(2,1)}) %reduce-scatter.3.cloned.1.call-update) | async-done | bytes 147472 | tf_op jit(solution)/shard_map/reduce_scatter | solution.py:145
  89.8 1.2 fusion.19
  90.9 0.0 copy-done.1
  91.0 0.4 convolution_convert_fusion.1
  91.3 14.0 %all_to_all.41 = bf16[8,9,2304]{2,1,0:T(8,128)(2,1)S(1)} all-to-all(bf16[8,9,2304]{2,1,0:T(8,128)(2,1)S(1)} %convolution_convert_fusion.1), channel_id=1, replica_groups=mesh['seq'=8,'head'=4] {'seq'}, dimensions={0} | all-to-all | bytes 663552 | tf_op jit(solution)/shard_map/all_to_all | solution.py:176
  105.3 0.8 copy.79
  106.2 0.0 all-gather.7.cloned.1.call-update
  106.2 0.0 reduce-scatter.5.cloned.1.call-start
  106.2 29.6 %all-gather.7.cloned.1.call-done = bf16[36,8,2304]{2,1,0:T(8,128)(2,1)} async-done(((bf16[9,8,2304]{2,1,0:T(8,128)(2,1)}), bf16[36,8,2304]{2,1,0:T(8,128)(2,1)}) %all-gather.7.cloned.1.call-update) | async-done | bytes 1327120 | tf_op jit(solution)/shard_map/all_gather | solution.py:177
  135.8 0.0 copy-start.4
  135.8 0.0 copy-start.5
  135.8 3.7 %fusion.9 = f32[4,9,8,720]{3,2,1,0:T(8,128)S(1)} fusion(bf16[4,9,8,2304]{3,2,1,0:T(8,128)(2,1)} %bitcast.93, bf16[2304,720]{0,1:T(8,128)(2,1)} %param.20), kind=kOutput, calls=%fused_computation.13 | convolution fusion | flops 955514880 | bytes 5474304 | tf_op jit(solution)/shard_map/hcsd,df->hcsf/dot_general | solution.py:178
  139.5 0.0 copy-done.4
  139.6 0.0 copy-done.5
  139.6 1.3 fusion.14
  140.9 0.0 copy-done
  140.9 0.0 copy-start.6
  140.9 2.3 %convolution_convert_fusion = bf16[4,9,8,2304]{3,2,1,0:T(8,128)(2,1)} fusion(bf16[4,9,8,720]{3,2,1,0:T(8,128)(2,1)S(1)} %fusion.14, bf16[2304,720]{0,1:T(8,128)(2,1)S(1)} %copy-done), kind=kOutput, calls=%fused_computation | convolution fusion | flops 956178432 | bytes 5059584 | tf_op jit(solution)/shard_map/hcsf,df->hcsd/dot_general | solution.py:185
  143.2 0.0 reduce-scatter.5.cloned.1.call-update
  143.2 0.1 copy.77
  143.3 1.7 slice_bitcast_fusion
  145.0 0.0 copy-done.6
  145.0 0.2 fusion.27
  145.3 28.8 %reduce-scatter.5.cloned.1.call-done = bf16[1,9,8,2304]{3,2,1,0:T(8,128)(2,1)} async-done(((bf16[4,9,8,2304]{3,2,1,0:T(8,128)(2,1)}), bf16[1,9,8,2304]{3,2,1,0:T(8,128)(2,1)}) %reduce-scatter.5.cloned.1.call-update) | async-done | bytes 331792 | tf_op jit(solution)/shard_map/reduce_scatter | solution.py:189
  174.0 1.9 copy.80
  175.9 4.2 %all-to-all-start.3 = ((bf16[8,9,2304]{2,1,0:T(8,128)(2,1)}), bf16[8,9,2304]{2,1,0:T(8,128)(2,1)}, u32[]{:S(2)}, u32[]{:S(2)}) async-start(bf16[8,9,2304]{2,1,0:T(8,128)(2,1)} %copy.80), calls=%async_computation.5 | async-start | bytes 1179648 | tf_op jit(solution)/shard_map/all_to_all | solution.py:191
  180.1 10.4 %all-to-all-done.3 = bf16[8,9,2304]{2,1,0:T(8,128)(2,1)} async-done(((bf16[8,9,2304]{2,1,0:T(8,128)(2,1)}), bf16[8,9,2304]{2,1,0:T(8,128)(2,1)}, u32[]{:S(2)}, u32[]{:S(2)}) %all-to-all-start.3) | async-done | bytes 331808 | tf_op jit(solution)/shard_map/all_to_all | solution.py:191
  190.5 1.4 fusion.4
  192.0 2.1 %fusion.5 = bf16[32,2304]{1,0:T(8,128)(2,1)} fusion(f32[32,2304]{1,0:T(8,128)S(1)} %fusion.4, bf16[8,9,2304]{2,1,0:T(8,128)(2,1)} %all-to-all-done.3, bf16[32,2304]{1,0:T(8,128)(2,1)S(1)} %get-tuple-element.4, f32[32]{0:T(128)S(1)} %get-tuple-element.9, s32[32]{0:T(128)S(1)} %get-tuple-element.7, s32[8,9]{1,0:T(8,128)S(1)} %copy.77), kind=kOutput, calls=%fused_computation.9 | convolution fusion | flops 11061504 | bytes 922144 | tf_op jit(solution)/shard_map/tec,ercd->trd/dot_general | solution.py:199
  (8 shorter events, 0.1 us)
Async XLA Ops:
  7.2 133.8 %copy-start = (bf16[2304,720]{0,1:T(8,128)(2,1)S(1)}, bf16[2304,720]{0,1:T(8,128)(2,1)}, u32[]{:S(2)}) copy-start(bf16[2304,720]{0,1:T(8,128)(2,1)} %param.22) | copy-start | bytes 9953284
  7.2 27.2 %copy-start.3 = (s32[128]{0:T(128)S(1)}, s32[128]{0:T(128)}, u32[]{:S(2)}) copy-start(s32[128]{0:T(128)} %param.18) | copy-start | bytes 1540
  7.2 50.6 %all-gather.5.cloned.1.call-start = ((), (), s32[]{:S(2)}) async-start(), calls=%async_computation.6 | async-start | bytes 2654208 | tf_op jit(solution)/shard_map/all_gather | solution.py:119
  31.0 13.2 %all-to-all-start = ((bf16[32,4,576]{2,0,1:T(8,128)(2,1)}), bf16[32,4,576]{2,0,1:T(8,128)(2,1)S(1)}, u32[]{:S(2)}, u32[]{:S(2)}) async-start(bf16[32,4,576]{2,0,1:T(8,128)(2,1)} %copy.71), calls=%async_computation | async-start | bytes 327680 | tf_op jit(solution)/shard_map/all_to_all | solution.py:110
  34.3 55.5 %reduce-scatter.3.cloned.1.call-start = ((), (), s32[]{:S(2)}) async-start(), calls=%async_computation.7 | async-start | bytes 737280 | tf_op jit(solution)/shard_map/reduce_scatter | solution.py:145
  57.8 10.0 %copy-start.2 = (s32[32,2]{0,1:T(2,128)S(1)}, s32[32,2]{0,1:T(2,128)}, u32[]{:S(2)}) copy-start(s32[32,2]{0,1:T(2,128)} %param.19) | copy-start | bytes 772
  57.8 33.2 %copy-start.1 = (f32[2304]{0:T(1024)S(1)}, f32[2304]{0:T(1024)}, u32[]{:S(2)}) copy-start(f32[2304]{0:T(1024)} %param.16) | copy-start | bytes 27652
  67.7 68.1 %all-gather.7.cloned.1.call-start = ((), (), s32[]{:S(2)}) async-start(), calls=%async_computation.9 | async-start | bytes 1658880 | tf_op jit(solution)/shard_map/all_gather | solution.py:177
  106.2 67.8 %reduce-scatter.5.cloned.1.call-start = ((), (), s32[]{:S(2)}) async-start(), calls=%async_computation.8 | async-start | bytes 1658880 | tf_op jit(solution)/shard_map/reduce_scatter | solution.py:189
  135.8 3.7 %copy-start.4 = (bf16[2304,720]{0,1:T(8,128)(2,1)S(1)}, bf16[2304,720]{0,1:T(8,128)(2,1)}, u32[]{:S(2)}) copy-start(bf16[2304,720]{0,1:T(8,128)(2,1)} %param.21) | copy-start | bytes 9953284
  135.8 3.7 %copy-start.5 = (bf16[36,8,2304]{2,1,0:T(8,128)(2,1)S(1)}, bf16[36,8,2304]{2,1,0:T(8,128)(2,1)}, u32[]{:S(2)}) copy-start(bf16[36,8,2304]{2,1,0:T(8,128)(2,1)} %all-gather.7.cloned.1.call-done) | copy-start | bytes 3981316
  140.9 4.1 %copy-start.6 = (bf16[2304,8]{0,1:T(8,128)(2,1)S(1)}, bf16[2304,8]{0,1:T(8,128)(2,1)}, u32[]{:S(2)}) copy-start(bf16[2304,8]{0,1:T(8,128)(2,1)} %param.17) | copy-start | bytes 110596
  175.9 14.7 %all-to-all-start.3 = ((bf16[8,9,2304]{2,1,0:T(8,128)(2,1)}), bf16[8,9,2304]{2,1,0:T(8,128)(2,1)}, u32[]{:S(2)}, u32[]{:S(2)}) async-start(bf16[8,9,2304]{2,1,0:T(8,128)(2,1)} %copy.80), calls=%async_computation.5 | async-start | bytes 1179648 | tf_op jit(solution)/shard_map/all_to_all | solution.py:191
Sparse Core Ops, SparseCore 0:
  29.3 28.4 all-gather.4
  67.8 21.9 reduce-scatter.2
  106.3 29.4 all-gather.6
  143.4 30.6 reduce-scatter.4

commit v15 on v13

--- a/solution.py
+++ b/solution.py
@@ -3,6 +3,8 @@
 import jax
 import jax.numpy as jnp
 from jax import lax
+from jax.experimental import pallas as pl
+from jax.experimental.pallas import tpu as pltpu
 from jax.experimental.layout import Layout, with_layout_constraint
 from jax.sharding import PartitionSpec as P
 
@@ -33,6 +35,51 @@
     return jnp.einsum(
         "hqk,hdk->qhd", rounded_piece, value_piece, preferred_element_type=jnp.float32
     )
+
+
+def attention_project(q3, window_t, allowed, out_weight):
+    heads, tokens, _ = q3.shape
+    key_total = window_t.shape[1]
+    width = out_weight.shape[1]
+
+    def kernel(q_ref, keys_ref, values_ref, allowed_ref, weight_ref, out_ref, total_ref):
+        head = pl.program_id(0)
+
+        @pl.when(head == 0)
+        def _():
+            total_ref[...] = jnp.zeros(total_ref.shape, jnp.float32)
+
+        allowed_now = allowed_ref[...] != 0
+        raw = jnp.dot(q_ref[0], keys_ref[...], preferred_element_type=jnp.float32) * HDIM ** (-0.5)
+        masked = jnp.where(allowed_now, raw, -jnp.inf)
+        top = jnp.max(masked, axis=1, keepdims=True)
+        weights = jnp.where(allowed_now, jnp.exp(masked - top), 0.0)
+        sums = jnp.sum(weights, axis=1, keepdims=True)
+        mixed = lax.dot_general(
+            weights.astype(jnp.bfloat16), values_ref[...], (((1,), (1,)), ((), ())),
+            preferred_element_type=jnp.float32)
+        attended = (mixed / sums).astype(jnp.bfloat16)
+        total_ref[...] += jnp.dot(attended, weight_ref[...], preferred_element_type=jnp.float32)
+
+        @pl.when(head == heads - 1)
+        def _():
+            out_ref[...] = total_ref[...].astype(out_ref.dtype)
+
+    return pl.pallas_call(
+        kernel,
+        grid=(heads,),
+        in_specs=[
+            pl.BlockSpec((1, tokens, HDIM), lambda h: (h, 0, 0)),
+            pl.BlockSpec((HDIM, key_total), lambda h: (h, 0)),
+            pl.BlockSpec((HDIM, key_total), lambda h: (h + heads, 0)),
+            pl.BlockSpec((tokens, key_total), lambda h: (0, 0)),
+            pl.BlockSpec((HDIM, width), lambda h: (h, 0)),
+        ],
+        out_specs=pl.BlockSpec((tokens, width), lambda h: (0, 0)),
+        out_shape=jax.ShapeDtypeStruct((tokens, width), jnp.bfloat16),
+        scratch_shapes=[pltpu.VMEM((tokens, width), jnp.float32)],
+        compiler_params=pltpu.CompilerParams(dimension_semantics=("arbitrary",)),
+    )(q3, window_t, window_t, allowed.astype(jnp.int32), out_weight)
 
 
 def per_device(
@@ -99,8 +146,6 @@
         window_first = (seq_place - span_count + 1) * stretch_len
     key_total = span_count * stretch_len
     joined_window_t = with_layout_constraint(joined_window_t, Layout(major_to_minor=(0, 1)))
-    keys_t = joined_window_t[:group_width].reshape(heads_here, HDIM, key_total)
-    values_t = joined_window_t[group_width:].reshape(heads_here, HDIM, key_total)
     query_place = seq_place * stretch_len + jnp.arange(stretch_len, dtype=jnp.int32)
     key_place = window_first + jnp.arange(key_total, dtype=jnp.int32)
     allowed = (
@@ -108,19 +153,9 @@
         & (key_place[None, :] <= query_place[:, None])
         & (key_place[None, :] >= 0)
     )
-    queries = query_head.reshape(stretch_len, heads_here, HDIM)
-    masked = score_piece(queries, keys_t, allowed)
-    row_max = jnp.max(masked, -1, keepdims=True)
-    weights = jnp.where(allowed[None], jnp.exp(masked - row_max), 0.0)
-    totals = jnp.sum(weights, -1)
-    mixture = mix_piece(weights.astype(jnp.bfloat16), values_t)
-    attention = (
-        (mixture / jnp.transpose(totals)[:, :, None])
-        .astype(jnp.bfloat16)
-        .reshape(stretch_len, group_width)
-    )
+    queries = jnp.transpose(query_head.reshape(stretch_len, heads_here, HDIM), (1, 0, 2))
     attended_sum = lax.psum_scatter(
-        jnp.dot(attention, out_weight, preferred_element_type=jnp.float32).astype(jnp.bfloat16),
+        attention_project(queries, joined_window_t, allowed, out_weight),
         "head",
         scatter_dimension=0,
         tiled=True,

time: 204 us -> 203 us (level)
  Pallas kernels: 0 us -> 11.3 us
  matrix products: 20.9 us -> 11.4 us
    pallas_call x0 -> x1, Pallas kernels: none -> 11.3 us  [attention_project(): pl.pallas_call(kernel, grid=(heads,), in_specs=[pl.BlockSpec((1, tokens,...]
    sub x1 -> x0, matrix products: 5.28 us -> none  [per_device(): weights = jnp.where(allowed[None], jnp.exp(masked - row_max), 0.0)]
    dot_general x2 -> x0, matrix products: 4.2 us -> none  [the longest x1 2.71 us: mix_piece(): jnp.einsum('hqk,hdk->qhd', rounded_piece, value_piece, preferred_element_...]
    slice x1 -> x0, local copies, waits for them, and re-layouts: 3.23 us -> none  [per_device(): keys_t = joined_window_t[:group_width].reshape(heads_here, HDIM, key_total)]
  transfers between devices with their start and end apart: 6 -> 6, of which waited for: 5 -> 5; matrix products, arithmetic and copies ran while one was open for 3% -> 4% of each run, Pallas kernels for 0% -> 0%
where the time goes in v15:
time: 203 us; the launch traced here: 202 us
  waiting for transfers between devices  101 us (50%)
  blocking collectives  38.6 us (19%)
  local copies, waits for them, and re-layouts  14.6 us (7%)
  between operations  13.9 us (7%)
  matrix products  11.4 us (6%)
  Pallas kernels  11.3 us (6%)
  starting transfers between devices  7.7 us (4%)
  other arithmetic  3.72 us (2%)
    all_gather x1, waiting for transfers between devices, per_device(): lax.all_gather(jnp.swapaxes(arrived, 0, 1), 'head', axis=0, tiled=False)  29.6 us
    reduce_scatter x1, waiting for transfers between devices, per_device(): lax.psum_scatter(partial_out, 'head', scatter_dimension=0, tiled=False)  28.8 us
    reduce_scatter x1, waiting for transfers between devices, per_device(): lax.psum_scatter(attention_project(queries, joined_window_t, allowed, out...  21.2 us
    all_to_all x1, blocking collectives, per_device(): lax.all_to_all(joined_rows_t, 'head', split_axis=0, concat_axis=2, tiled=...  15.8 us
    all_to_all x1, blocking collectives, per_device(): lax.all_to_all(outgoing, 'seq', split_axis=0, concat_axis=0, tiled=True)  14 us
    pallas_call x1, Pallas kernels, attention_project(): pl.pallas_call(kernel, grid=(heads,), in_specs=[pl.BlockSpec((1, tokens,...  11.3 us
    all_gather x1, waiting for transfers between devices, per_device(): joined_window_t = lax.all_gather(joined_head_t, 'seq', axis=1, tiled=True)  10.8 us
    all_to_all x1, waiting for transfers between devices, per_device(): lax.all_to_all(shard_out, 'seq', split_axis=0, concat_axis=0, tiled=True)  10.4 us
  transfers between devices with their start and end apart: 6, of which 5 were waited for; matrix products, arithmetic and copies ran while one was open for 4% of the time, Pallas kernels for 0%

profile of v15, /device:TPU:0, one launch (start us, length us, event | category | flops | bytes accessed | tf_op | source)
XLA Modules:
  0.0 202.1 jit_solution(5935363316920443633)
XLA Ops:
  7.2 0.0 copy-start
  7.2 0.0 copy-start.3
  7.2 0.0 all-gather.5.cloned.1.call-start
  7.2 1.3 reshape.82
  8.5 1.8 reshape.83
  10.3 1.1 pad_maximum_fusion
  11.5 15.8 %all_to_all.40 = bf16[4,1152,32]{1,2,0:T(8,128)(2,1)} all-to-all(bf16[4,1152,32]{1,2,0:T(8,128)(2,1)S(1)} %copy.73), channel_id=1, replica_groups=mesh['seq'=8,'head'=4] {'head'}, dimensions={0} | all-to-all | bytes 589824 | tf_op jit(solution)/shard_map/all_to_all | solution.py:116
  27.3 1.9 copy.74
  29.1 0.0 all-gather.5.cloned.1.call-update
  29.1 1.1 reshape.81
  30.3 0.7 copy.71
  31.0 3.3 %all-to-all-start = ((bf16[32,4,576]{2,0,1:T(8,128)(2,1)}), bf16[32,4,576]{2,0,1:T(8,128)(2,1)S(1)}, u32[]{:S(2)}, u32[]{:S(2)}) async-start(bf16[32,4,576]{2,0,1:T(8,128)(2,1)} %copy.71), calls=%async_computation | async-start | bytes 327680 | tf_op jit(solution)/shard_map/all_to_all | solution.py:122
  34.3 0.0 reduce-scatter.3.cloned.1.call-start
  34.4 0.0 copy-done.3
  34.4 8.8 %all-gather.1 = s32[8,1,128]{2,1,0:T(1,128)S(1)} all-gather(s32[1,1,128]{2,1,0:T(1,128)S(1)} %bitcast.92), channel_id=1, replica_groups=mesh['seq'=8,'head'=4] {'seq'}, dimensions={0}, use_global_device_ids=true | all-gather | bytes 4608 | tf_op jit(solution)/shard_map/all_gather | solution.py:129
  43.1 1.0 fusion.18.allowed_ref
  44.1 0.0 all-to-all-done
  44.1 1.0 reshape_reshape.3
  45.2 1.9 copy.87
  47.0 10.8 %all-gather.5.cloned.1.call-done.keys_ref.values_ref = bf16[1152,1024]{1,0:T(8,128)(2,1)} async-done(((bf16[1152,128]{1,0:T(8,128)(2,1)}), bf16[1152,1024]{1,0:T(8,128)(2,1)}) %all-gather.5.cloned.1.call-update) | async-done | bytes 2359312 | tf_op jit(solution)/shard_map/all_gather | solution.py:131
  57.8 0.0 copy-start.2
  57.8 0.0 copy-start.1
  57.8 11.3 %shard_map.139 = bf16[128,2304]{1,0:T(8,128)(2,1)} custom-call(bf16[9,128,64]{2,1,0:T(8,128)(2,1)} %bitcast.85, bf16[1152,1024]{1,0:T(8,128)(2,1)} %all-gather.5.cloned.1.call-done.keys_ref.values_ref, bf16[1152,1024]{1,0:T(8,128)(2,1)} %all-gather.5.cloned.1.call-done.keys_ref.values_ref, s32[128,1024]{1,0:T(8,128)} %fusion.18.allowed_ref, ...), custom_call_target="tpu_custom_call" | custom-call | tf_op jit(solution)/shard_map/pallas_call | solution.py:68
  69.1 0.0 reduce-scatter.3.cloned.1.call-update
  69.1 0.0 all-gather.7.cloned.1.call-start
  69.2 0.0 copy-done.2
  69.2 0.1 copy.75
  69.3 0.1 eq.84
  69.4 0.1 fusion.33
  69.5 0.1 reduce_window_sum.11
  69.6 0.2 select_reduce_fusion
  69.8 0.1 reduce_sum.40
  69.9 0.1 copy.76
  70.0 0.1 compare_reduce_fusion
  70.1 21.2 %reduce-scatter.3.cloned.1.call-done = bf16[32,2304]{1,0:T(8,128)(2,1)} async-done(((bf16[128,2304]{1,0:T(8,128)(2,1)}), bf16[32,2304]{1,0:T(8,128)(2,1)}) %reduce-scatter.3.cloned.1.call-update) | async-done | bytes 147472 | tf_op jit(solution)/shard_map/reduce_scatter | solution.py:157
  91.2 1.2 fusion.19
  92.4 0.0 copy-done.1
  92.4 0.4 convolution_convert_fusion.1
  92.8 14.0 %all_to_all.41 = bf16[8,9,2304]{2,1,0:T(8,128)(2,1)S(1)} all-to-all(bf16[8,9,2304]{2,1,0:T(8,128)(2,1)S(1)} %convolution_convert_fusion.1), channel_id=1, replica_groups=mesh['seq'=8,'head'=4] {'seq'}, dimensions={0} | all-to-all | bytes 663552 | tf_op jit(solution)/shard_map/all_to_all | solution.py:188
  106.8 0.8 copy.79
  107.6 0.0 all-gather.7.cloned.1.call-update
  107.7 0.0 reduce-scatter.5.cloned.1.call-start
  107.7 29.6 %all-gather.7.cloned.1.call-done = bf16[36,8,2304]{2,1,0:T(8,128)(2,1)} async-done(((bf16[9,8,2304]{2,1,0:T(8,128)(2,1)}), bf16[36,8,2304]{2,1,0:T(8,128)(2,1)}) %all-gather.7.cloned.1.call-update) | async-done | bytes 1327120 | tf_op jit(solution)/shard_map/all_gather | solution.py:189
  137.3 0.0 copy-start.4
  137.3 0.0 copy-start.5
  137.3 3.7 %fusion.9 = f32[4,9,8,720]{3,2,1,0:T(8,128)S(1)} fusion(bf16[4,9,8,2304]{3,2,1,0:T(8,128)(2,1)} %bitcast.93, bf16[2304,720]{0,1:T(8,128)(2,1)} %param.20), kind=kOutput, calls=%fused_computation.13 | convolution fusion | flops 955514880 | bytes 5474304 | tf_op jit(solution)/shard_map/hcsd,df->hcsf/dot_general | solution.py:190
  141.0 0.0 copy-done.4
  141.1 0.0 copy-done.5
  141.1 1.3 fusion.14
  142.4 0.0 copy-done
  142.4 0.0 copy-start.6
  142.4 2.3 %convolution_convert_fusion = bf16[4,9,8,2304]{3,2,1,0:T(8,128)(2,1)} fusion(bf16[4,9,8,720]{3,2,1,0:T(8,128)(2,1)S(1)} %fusion.14, bf16[2304,720]{0,1:T(8,128)(2,1)S(1)} %copy-done), kind=kOutput, calls=%fused_computation | convolution fusion | flops 956178432 | bytes 5059584 | tf_op jit(solution)/shard_map/hcsf,df->hcsd/dot_general | solution.py:197
  144.7 0.0 reduce-scatter.5.cloned.1.call-update
  144.7 0.1 copy.77
  144.8 1.7 slice_bitcast_fusion
  146.5 0.0 copy-done.6
  146.5 0.2 fusion.27
  146.8 28.8 %reduce-scatter.5.cloned.1.call-done = bf16[1,9,8,2304]{3,2,1,0:T(8,128)(2,1)} async-done(((bf16[4,9,8,2304]{3,2,1,0:T(8,128)(2,1)}), bf16[1,9,8,2304]{3,2,1,0:T(8,128)(2,1)}) %reduce-scatter.5.cloned.1.call-update) | async-done | bytes 331792 | tf_op jit(solution)/shard_map/reduce_scatter | solution.py:201
  175.5 1.9 copy.80
  177.4 4.2 %all-to-all-start.3 = ((bf16[8,9,2304]{2,1,0:T(8,128)(2,1)}), bf16[8,9,2304]{2,1,0:T(8,128)(2,1)}, u32[]{:S(2)}, u32[]{:S(2)}) async-start(bf16[8,9,2304]{2,1,0:T(8,128)(2,1)} %copy.80), calls=%async_computation.5 | async-start | bytes 1179648 | tf_op jit(solution)/shard_map/all_to_all | solution.py:203
  181.6 10.4 %all-to-all-done.3 = bf16[8,9,2304]{2,1,0:T(8,128)(2,1)} async-done(((bf16[8,9,2304]{2,1,0:T(8,128)(2,1)}), bf16[8,9,2304]{2,1,0:T(8,128)(2,1)}, u32[]{:S(2)}, u32[]{:S(2)}) %all-to-all-start.3) | async-done | bytes 331808 | tf_op jit(solution)/shard_map/all_to_all | solution.py:203
  192.0 1.4 fusion.4
  193.4 2.1 %fusion.5 = bf16[32,2304]{1,0:T(8,128)(2,1)} fusion(f32[32,2304]{1,0:T(8,128)S(1)} %fusion.4, bf16[8,9,2304]{2,1,0:T(8,128)(2,1)} %all-to-all-done.3, bf16[32,2304]{1,0:T(8,128)(2,1)S(1)} %get-tuple-element.4, f32[32]{0:T(128)S(1)} %get-tuple-element.9, s32[32]{0:T(128)S(1)} %get-tuple-element.7, s32[8,9]{1,0:T(8,128)S(1)} %copy.77), kind=kOutput, calls=%fused_computation.9 | convolution fusion | flops 11061504 | bytes 922144 | tf_op jit(solution)/shard_map/tec,ercd->trd/dot_general | solution.py:211
  (8 shorter events, 0.1 us)
Async XLA Ops:
  7.2 135.2 %copy-start = (bf16[2304,720]{0,1:T(8,128)(2,1)S(1)}, bf16[2304,720]{0,1:T(8,128)(2,1)}, u32[]{:S(2)}) copy-start(bf16[2304,720]{0,1:T(8,128)(2,1)} %param.22) | copy-start | bytes 9953284
  7.2 27.2 %copy-start.3 = (s32[128]{0:T(128)S(1)}, s32[128]{0:T(128)}, u32[]{:S(2)}) copy-start(s32[128]{0:T(128)} %param.18) | copy-start | bytes 1540
  7.2 50.6 %all-gather.5.cloned.1.call-start = ((), (), s32[]{:S(2)}) async-start(), calls=%async_computation.6 | async-start | bytes 2654208 | tf_op jit(solution)/shard_map/all_gather | solution.py:131
  31.0 13.2 %all-to-all-start = ((bf16[32,4,576]{2,0,1:T(8,128)(2,1)}), bf16[32,4,576]{2,0,1:T(8,128)(2,1)S(1)}, u32[]{:S(2)}, u32[]{:S(2)}) async-start(bf16[32,4,576]{2,0,1:T(8,128)(2,1)} %copy.71), calls=%async_computation | async-start | bytes 327680 | tf_op jit(solution)/shard_map/all_to_all | solution.py:122
  34.3 56.9 %reduce-scatter.3.cloned.1.call-start = ((), (), s32[]{:S(2)}) async-start(), calls=%async_computation.7 | async-start | bytes 737280 | tf_op jit(solution)/shard_map/reduce_scatter | solution.py:157
  57.8 11.4 %copy-start.2 = (s32[32,2]{0,1:T(2,128)S(1)}, s32[32,2]{0,1:T(2,128)}, u32[]{:S(2)}) copy-start(s32[32,2]{0,1:T(2,128)} %param.19) | copy-start | bytes 772
  57.8 34.6 %copy-start.1 = (f32[2304]{0:T(1024)S(1)}, f32[2304]{0:T(1024)}, u32[]{:S(2)}) copy-start(f32[2304]{0:T(1024)} %param.16) | copy-start | bytes 27652
  69.1 68.2 %all-gather.7.cloned.1.call-start = ((), (), s32[]{:S(2)}) async-start(), calls=%async_computation.9 | async-start | bytes 1658880 | tf_op jit(solution)/shard_map/all_gather | solution.py:189
  107.7 67.9 %reduce-scatter.5.cloned.1.call-start = ((), (), s32[]{:S(2)}) async-start(), calls=%async_computation.8 | async-start | bytes 1658880 | tf_op jit(solution)/shard_map/reduce_scatter | solution.py:201
  137.3 3.7 %copy-start.4 = (bf16[2304,720]{0,1:T(8,128)(2,1)S(1)}, bf16[2304,720]{0,1:T(8,128)(2,1)}, u32[]{:S(2)}) copy-start(bf16[2304,720]{0,1:T(8,128)(2,1)} %param.21) | copy-start | bytes 9953284
  137.3 3.7 %copy-start.5 = (bf16[36,8,2304]{2,1,0:T(8,128)(2,1)S(1)}, bf16[36,8,2304]{2,1,0:T(8,128)(2,1)}, u32[]{:S(2)}) copy-start(bf16[36,8,2304]{2,1,0:T(8,128)(2,1)} %all-gather.7.cloned.1.call-done) | copy-start | bytes 3981316
  142.4 4.1 %copy-start.6 = (bf16[2304,8]{0,1:T(8,128)(2,1)S(1)}, bf16[2304,8]{0,1:T(8,128)(2,1)}, u32[]{:S(2)}) copy-start(bf16[2304,8]{0,1:T(8,128)(2,1)} %param.17) | copy-start | bytes 110596
  177.4 14.7 %all-to-all-start.3 = ((bf16[8,9,2304]{2,1,0:T(8,128)(2,1)}), bf16[8,9,2304]{2,1,0:T(8,128)(2,1)}, u32[]{:S(2)}, u32[]{:S(2)}) async-start(bf16[8,9,2304]{2,1,0:T(8,128)(2,1)} %copy.80), calls=%async_computation.5 | async-start | bytes 1179648 | tf_op jit(solution)/shard_map/all_to_all | solution.py:203
Sparse Core Ops, SparseCore 0:
  29.3 28.4 all-gather.4
  69.3 21.9 reduce-scatter.2
  107.8 29.4 all-gather.6
  144.9 30.6 reduce-scatter.4

commit v16 on v14

--- a/solution.py
+++ b/solution.py
@@ -49,7 +49,7 @@
             raw = jnp.dot(q_ref[head], keys, preferred_element_type=jnp.float32) * HDIM ** (-0.5)
             masked = jnp.where(allowed_now, raw, -jnp.inf)
             top = jnp.max(masked, axis=1, keepdims=True)
-            weights = jnp.where(allowed_now, jnp.exp(masked - top), 0.0)
+            weights = jnp.exp(masked - top)
             sums = jnp.sum(weights, axis=1, keepdims=True)
             mixed = lax.dot_general(
                 weights.astype(jnp.bfloat16),

time: 201 us -> 201 us (level)
  no operation moved by 1% of the time
where the time goes in v16:
time: 201 us; the launch traced here: 200 us
  waiting for transfers between devices  101 us (50%)
  blocking collectives  38.4 us (19%)
  local copies, waits for them, and re-layouts  14.6 us (7%)
  between operations  13.9 us (7%)
  matrix products  11.4 us (6%)
  Pallas kernels  9.61 us (5%)
  starting transfers between devices  7.7 us (4%)
  other arithmetic  3.72 us (2%)
    all_gather x1, waiting for transfers between devices, per_device(): lax.all_gather(jnp.swapaxes(arrived, 0, 1), 'head', axis=0, tiled=False)  29.7 us
    reduce_scatter x1, waiting for transfers between devices, per_device(): lax.psum_scatter(partial_out, 'head', scatter_dimension=0, tiled=False)  28.8 us
    reduce_scatter x1, waiting for transfers between devices, per_device(): lax.psum_scatter(attention_project(queries, joined_window_t, allowed, out...  21.3 us
    all_to_all x1, blocking collectives, per_device(): lax.all_to_all(joined_rows_t, 'head', split_axis=0, concat_axis=2, tiled=...  15.8 us
    all_to_all x1, blocking collectives, per_device(): lax.all_to_all(outgoing, 'seq', split_axis=0, concat_axis=0, tiled=True)  13.8 us
    all_gather x1, waiting for transfers between devices, per_device(): joined_window_t = lax.all_gather(joined_head_t, 'seq', axis=1, tiled=True)  10.8 us
    all_to_all x1, waiting for transfers between devices, per_device(): lax.all_to_all(shard_out, 'seq', split_axis=0, concat_axis=0, tiled=True)  10.4 us
    pallas_call x1, Pallas kernels, attention_project(): pl.pallas_call(kernel, out_shape=jax.ShapeDtypeStruct((tokens, out_weight...  9.61 us
  transfers between devices with their start and end apart: 6, of which 5 were waited for; matrix products, arithmetic and copies ran while one was open for 4% of the time, Pallas kernels for 0%

profile of v16, /device:TPU:0, one launch (start us, length us, event | category | flops | bytes accessed | tf_op | source)
XLA Modules:
  0.0 200.3 jit_solution(5539887444085911906)
XLA Ops:
  7.2 0.0 copy-start
  7.2 0.0 copy-start.3
  7.2 0.0 all-gather.5.cloned.1.call-start
  7.2 1.3 reshape.82
  8.5 1.8 reshape.83
  10.3 1.1 pad_maximum_fusion
  11.5 15.8 %all_to_all.40 = bf16[4,1152,32]{1,2,0:T(8,128)(2,1)} all-to-all(bf16[4,1152,32]{1,2,0:T(8,128)(2,1)S(1)} %copy.73), channel_id=1, replica_groups=mesh['seq'=8,'head'=4] {'head'}, dimensions={0} | all-to-all | bytes 589824 | tf_op jit(solution)/shard_map/all_to_all | solution.py:104
  27.3 1.9 copy.74
  29.1 0.0 all-gather.5.cloned.1.call-update
  29.1 1.1 reshape.81
  30.3 0.7 copy.71
  31.0 3.3 %all-to-all-start = ((bf16[32,4,576]{2,0,1:T(8,128)(2,1)}), bf16[32,4,576]{2,0,1:T(8,128)(2,1)S(1)}, u32[]{:S(2)}, u32[]{:S(2)}) async-start(bf16[32,4,576]{2,0,1:T(8,128)(2,1)} %copy.71), calls=%async_computation | async-start | bytes 327680 | tf_op jit(solution)/shard_map/all_to_all | solution.py:110
  34.3 0.0 reduce-scatter.3.cloned.1.call-start
  34.4 0.0 copy-done.3
  34.4 8.8 %all-gather.1 = s32[8,1,128]{2,1,0:T(1,128)S(1)} all-gather(s32[1,1,128]{2,1,0:T(1,128)S(1)} %bitcast.92), channel_id=1, replica_groups=mesh['seq'=8,'head'=4] {'seq'}, dimensions={0}, use_global_device_ids=true | all-gather | bytes 4608 | tf_op jit(solution)/shard_map/all_gather | solution.py:117
  43.1 1.0 fusion.18.allowed_ref
  44.1 0.0 all-to-all-done
  44.1 1.0 reshape_reshape.3
  45.2 1.9 copy.87
  47.0 10.8 %all-gather.5.cloned.1.call-done.window_ref = bf16[1152,1024]{1,0:T(8,128)(2,1)} async-done(((bf16[1152,128]{1,0:T(8,128)(2,1)}), bf16[1152,1024]{1,0:T(8,128)(2,1)}) %all-gather.5.cloned.1.call-update) | async-done | bytes 2359312 | tf_op jit(solution)/shard_map/all_gather | solution.py:119
  57.8 0.0 copy-start.2
  57.8 0.0 copy-start.1
  57.8 9.6 %shard_map.139 = bf16[128,2304]{1,0:T(8,128)(2,1)} custom-call(bf16[9,128,64]{2,1,0:T(8,128)(2,1)} %bitcast.85, bf16[1152,1024]{1,0:T(8,128)(2,1)} %all-gather.5.cloned.1.call-done.window_ref, s32[128,1024]{1,0:T(8,128)} %fusion.18.allowed_ref, bf16[576,2304]{1,0:T(8,128)(2,1)} %weight_ref.1), custom_call_target="tpu_custom_call" | custom-call | tf_op jit(solution)/shard_map/pallas_call | solution.py:68
  67.4 0.0 reduce-scatter.3.cloned.1.call-update
  67.4 0.0 all-gather.7.cloned.1.call-start
  67.5 0.0 copy-done.2
  67.5 0.1 copy.75
  67.6 0.1 eq.84
  67.7 0.1 fusion.33
  67.7 0.1 reduce_window_sum.11
  67.8 0.2 select_reduce_fusion
  68.0 0.1 reduce_sum.40
  68.1 0.1 copy.76
  68.2 0.1 compare_reduce_fusion
  68.3 21.3 %reduce-scatter.3.cloned.1.call-done = bf16[32,2304]{1,0:T(8,128)(2,1)} async-done(((bf16[128,2304]{1,0:T(8,128)(2,1)}), bf16[32,2304]{1,0:T(8,128)(2,1)}) %reduce-scatter.3.cloned.1.call-update) | async-done | bytes 147472 | tf_op jit(solution)/shard_map/reduce_scatter | solution.py:145
  89.6 1.2 fusion.19
  90.8 0.0 copy-done.1
  90.8 0.4 convolution_convert_fusion.1
  91.2 13.8 %all_to_all.41 = bf16[8,9,2304]{2,1,0:T(8,128)(2,1)S(1)} all-to-all(bf16[8,9,2304]{2,1,0:T(8,128)(2,1)S(1)} %convolution_convert_fusion.1), channel_id=1, replica_groups=mesh['seq'=8,'head'=4] {'seq'}, dimensions={0} | all-to-all | bytes 663552 | tf_op jit(solution)/shard_map/all_to_all | solution.py:176
  104.9 0.8 copy.79
  105.8 0.0 all-gather.7.cloned.1.call-update
  105.8 0.0 reduce-scatter.5.cloned.1.call-start
  105.9 29.7 %all-gather.7.cloned.1.call-done = bf16[36,8,2304]{2,1,0:T(8,128)(2,1)} async-done(((bf16[9,8,2304]{2,1,0:T(8,128)(2,1)}), bf16[36,8,2304]{2,1,0:T(8,128)(2,1)}) %all-gather.7.cloned.1.call-update) | async-done | bytes 1327120 | tf_op jit(solution)/shard_map/all_gather | solution.py:177
  135.5 0.0 copy-start.4
  135.5 0.0 copy-start.5
  135.5 3.7 %fusion.9 = f32[4,9,8,720]{3,2,1,0:T(8,128)S(1)} fusion(bf16[4,9,8,2304]{3,2,1,0:T(8,128)(2,1)} %bitcast.93, bf16[2304,720]{0,1:T(8,128)(2,1)} %param.20), kind=kOutput, calls=%fused_computation.13 | convolution fusion | flops 955514880 | bytes 5474304 | tf_op jit(solution)/shard_map/hcsd,df->hcsf/dot_general | solution.py:178
  139.3 0.0 copy-done.4
  139.3 0.0 copy-done.5
  139.3 1.3 fusion.14
  140.6 0.0 copy-done
  140.6 0.0 copy-start.6
  140.6 2.3 %convolution_convert_fusion = bf16[4,9,8,2304]{3,2,1,0:T(8,128)(2,1)} fusion(bf16[4,9,8,720]{3,2,1,0:T(8,128)(2,1)S(1)} %fusion.14, bf16[2304,720]{0,1:T(8,128)(2,1)S(1)} %copy-done), kind=kOutput, calls=%fused_computation | convolution fusion | flops 956178432 | bytes 5059584 | tf_op jit(solution)/shard_map/hcsf,df->hcsd/dot_general | solution.py:185
  142.9 0.0 reduce-scatter.5.cloned.1.call-update
  143.0 0.1 copy.77
  143.0 1.7 slice_bitcast_fusion
  144.8 0.0 copy-done.6
  144.8 0.2 fusion.27
  145.0 28.8 %reduce-scatter.5.cloned.1.call-done = bf16[1,9,8,2304]{3,2,1,0:T(8,128)(2,1)} async-done(((bf16[4,9,8,2304]{3,2,1,0:T(8,128)(2,1)}), bf16[1,9,8,2304]{3,2,1,0:T(8,128)(2,1)}) %reduce-scatter.5.cloned.1.call-update) | async-done | bytes 331792 | tf_op jit(solution)/shard_map/reduce_scatter | solution.py:189
  173.7 1.9 copy.80
  175.6 4.2 %all-to-all-start.3 = ((bf16[8,9,2304]{2,1,0:T(8,128)(2,1)}), bf16[8,9,2304]{2,1,0:T(8,128)(2,1)}, u32[]{:S(2)}, u32[]{:S(2)}) async-start(bf16[8,9,2304]{2,1,0:T(8,128)(2,1)} %copy.80), calls=%async_computation.5 | async-start | bytes 1179648 | tf_op jit(solution)/shard_map/all_to_all | solution.py:191
  179.8 10.4 %all-to-all-done.3 = bf16[8,9,2304]{2,1,0:T(8,128)(2,1)} async-done(((bf16[8,9,2304]{2,1,0:T(8,128)(2,1)}), bf16[8,9,2304]{2,1,0:T(8,128)(2,1)}, u32[]{:S(2)}, u32[]{:S(2)}) %all-to-all-start.3) | async-done | bytes 331808 | tf_op jit(solution)/shard_map/all_to_all | solution.py:191
  190.3 1.4 fusion.4
  191.7 2.1 %fusion.5 = bf16[32,2304]{1,0:T(8,128)(2,1)} fusion(f32[32,2304]{1,0:T(8,128)S(1)} %fusion.4, bf16[8,9,2304]{2,1,0:T(8,128)(2,1)} %all-to-all-done.3, bf16[32,2304]{1,0:T(8,128)(2,1)S(1)} %get-tuple-element.4, f32[32]{0:T(128)S(1)} %get-tuple-element.9, s32[32]{0:T(128)S(1)} %get-tuple-element.7, s32[8,9]{1,0:T(8,128)S(1)} %copy.77), kind=kOutput, calls=%fused_computation.9 | convolution fusion | flops 11061504 | bytes 922144 | tf_op jit(solution)/shard_map/tec,ercd->trd/dot_general | solution.py:199
  (8 shorter events, 0.1 us)
Async XLA Ops:
  7.2 133.5 %copy-start = (bf16[2304,720]{0,1:T(8,128)(2,1)S(1)}, bf16[2304,720]{0,1:T(8,128)(2,1)}, u32[]{:S(2)}) copy-start(bf16[2304,720]{0,1:T(8,128)(2,1)} %param.22) | copy-start | bytes 9953284
  7.2 27.2 %copy-start.3 = (s32[128]{0:T(128)S(1)}, s32[128]{0:T(128)}, u32[]{:S(2)}) copy-start(s32[128]{0:T(128)} %param.18) | copy-start | bytes 1540
  7.2 50.6 %all-gather.5.cloned.1.call-start = ((), (), s32[]{:S(2)}) async-start(), calls=%async_computation.6 | async-start | bytes 2654208 | tf_op jit(solution)/shard_map/all_gather | solution.py:119
  31.0 13.2 %all-to-all-start = ((bf16[32,4,576]{2,0,1:T(8,128)(2,1)}), bf16[32,4,576]{2,0,1:T(8,128)(2,1)S(1)}, u32[]{:S(2)}, u32[]{:S(2)}) async-start(bf16[32,4,576]{2,0,1:T(8,128)(2,1)} %copy.71), calls=%async_computation | async-start | bytes 327680 | tf_op jit(solution)/shard_map/all_to_all | solution.py:110
  34.3 55.3 %reduce-scatter.3.cloned.1.call-start = ((), (), s32[]{:S(2)}) async-start(), calls=%async_computation.7 | async-start | bytes 737280 | tf_op jit(solution)/shard_map/reduce_scatter | solution.py:145
  57.8 9.7 %copy-start.2 = (s32[32,2]{0,1:T(2,128)S(1)}, s32[32,2]{0,1:T(2,128)}, u32[]{:S(2)}) copy-start(s32[32,2]{0,1:T(2,128)} %param.19) | copy-start | bytes 772
  57.8 33.0 %copy-start.1 = (f32[2304]{0:T(1024)S(1)}, f32[2304]{0:T(1024)}, u32[]{:S(2)}) copy-start(f32[2304]{0:T(1024)} %param.16) | copy-start | bytes 27652
  67.4 68.1 %all-gather.7.cloned.1.call-start = ((), (), s32[]{:S(2)}) async-start(), calls=%async_computation.9 | async-start | bytes 1658880 | tf_op jit(solution)/shard_map/all_gather | solution.py:177
  105.8 67.9 %reduce-scatter.5.cloned.1.call-start = ((), (), s32[]{:S(2)}) async-start(), calls=%async_computation.8 | async-start | bytes 1658880 | tf_op jit(solution)/shard_map/reduce_scatter | solution.py:189
  135.5 3.7 %copy-start.4 = (bf16[2304,720]{0,1:T(8,128)(2,1)S(1)}, bf16[2304,720]{0,1:T(8,128)(2,1)}, u32[]{:S(2)}) copy-start(bf16[2304,720]{0,1:T(8,128)(2,1)} %param.21) | copy-start | bytes 9953284
  135.5 3.7 %copy-start.5 = (bf16[36,8,2304]{2,1,0:T(8,128)(2,1)S(1)}, bf16[36,8,2304]{2,1,0:T(8,128)(2,1)}, u32[]{:S(2)}) copy-start(bf16[36,8,2304]{2,1,0:T(8,128)(2,1)} %all-gather.7.cloned.1.call-done) | copy-start | bytes 3981316
  140.6 4.1 %copy-start.6 = (bf16[2304,8]{0,1:T(8,128)(2,1)S(1)}, bf16[2304,8]{0,1:T(8,128)(2,1)}, u32[]{:S(2)}) copy-start(bf16[2304,8]{0,1:T(8,128)(2,1)} %param.17) | copy-start | bytes 110596
  175.6 14.7 %all-to-all-start.3 = ((bf16[8,9,2304]{2,1,0:T(8,128)(2,1)}), bf16[8,9,2304]{2,1,0:T(8,128)(2,1)}, u32[]{:S(2)}, u32[]{:S(2)}) async-start(bf16[8,9,2304]{2,1,0:T(8,128)(2,1)} %copy.80), calls=%async_computation.5 | async-start | bytes 1179648 | tf_op jit(solution)/shard_map/all_to_all | solution.py:191
Sparse Core Ops, SparseCore 0:
  29.3 28.4 all-gather.4
  67.5 22.0 reduce-scatter.2
  105.9 29.5 all-gather.6
  143.1 30.6 reduce-scatter.4

commit v17 on v16

--- a/solution.py
+++ b/solution.py
@@ -4,6 +4,7 @@
 import jax.numpy as jnp
 from jax import lax
 from jax.experimental import pallas as pl
+from jax.experimental.pallas import tpu as pltpu
 from jax.experimental.layout import Layout, with_layout_constraint
 from jax.sharding import PartitionSpec as P
 
@@ -40,9 +41,8 @@
     heads, tokens, _ = q3.shape
     group_width = heads * HDIM
 
-    def kernel(q_ref, window_ref, allowed_ref, weight_ref, out_ref):
+    def kernel(q_ref, window_ref, allowed_ref, weight_ref, out_ref, gathered_ref):
         allowed_now = allowed_ref[...] != 0
-        total = jnp.zeros(out_ref.shape, jnp.float32)
         for head in range(heads):
             keys = window_ref[pl.ds(head * HDIM, HDIM), :]
             values = window_ref[pl.ds(group_width + head * HDIM, HDIM), :]
@@ -57,16 +57,21 @@
                 (((1,), (1,)), ((), ())),
                 preferred_element_type=jnp.float32,
             )
-            attended = (mixed / sums).astype(jnp.bfloat16)
-            total = total + jnp.dot(
-                attended,
-                weight_ref[pl.ds(head * HDIM, HDIM), :],
-                preferred_element_type=jnp.float32,
+            attended = (mixed / sums).astype(jnp.bfloat16).astype(jnp.float32)
+            gathered_ref[pl.ds(head * HDIM, HDIM), :] = jnp.transpose(attended).astype(
+                jnp.bfloat16
             )
-        out_ref[...] = total.astype(out_ref.dtype)
+        out_ref[...] = lax.dot_general(
+            gathered_ref[...],
+            weight_ref[...],
+            (((0,), (0,)), ((), ())),
+            preferred_element_type=jnp.float32,
+        ).astype(out_ref.dtype)
 
     return pl.pallas_call(
-        kernel, out_shape=jax.ShapeDtypeStruct((tokens, out_weight.shape[1]), jnp.bfloat16)
+        kernel,
+        out_shape=jax.ShapeDtypeStruct((tokens, out_weight.shape[1]), jnp.bfloat16),
+        scratch_shapes=[pltpu.VMEM((group_width, tokens), jnp.bfloat16)],
     )(q3, window_t, allowed.astype(jnp.int32), out_weight)
 
 

time: 201 us -> 198 us (0.985)
  Pallas kernels: 9.61 us -> 6.19 us
    pallas_call x1, Pallas kernels: 9.61 us -> 6.19 us  [attention_project(): pl.pallas_call(kernel, out_shape=jax.ShapeDtypeStruct((tokens, out_weight...]
where the time goes in v17:
time: 198 us; the launch traced here: 197 us
  waiting for transfers between devices  101 us (51%)
  blocking collectives  38.5 us (19%)
  local copies, waits for them, and re-layouts  14.6 us (7%)
  between operations  13.9 us (7%)
  matrix products  11.4 us (6%)
  starting transfers between devices  7.7 us (4%)
  Pallas kernels  6.19 us (3%)
  other arithmetic  3.72 us (2%)
    all_gather x1, waiting for transfers between devices, per_device(): lax.all_gather(jnp.swapaxes(arrived, 0, 1), 'head', axis=0, tiled=False)  29.6 us
    reduce_scatter x1, waiting for transfers between devices, per_device(): lax.psum_scatter(partial_out, 'head', scatter_dimension=0, tiled=False)  28.8 us
    reduce_scatter x1, waiting for transfers between devices, per_device(): lax.psum_scatter(attention_project(queries, joined_window_t, allowed, out...  21.3 us
    all_to_all x1, blocking collectives, per_device(): lax.all_to_all(joined_rows_t, 'head', split_axis=0, concat_axis=2, tiled=...  15.8 us
    all_to_all x1, blocking collectives, per_device(): lax.all_to_all(outgoing, 'seq', split_axis=0, concat_axis=0, tiled=True)  13.9 us
    all_gather x1, waiting for transfers between devices, per_device(): joined_window_t = lax.all_gather(joined_head_t, 'seq', axis=1, tiled=True)  10.8 us
    all_to_all x1, waiting for transfers between devices, per_device(): lax.all_to_all(shard_out, 'seq', split_axis=0, concat_axis=0, tiled=True)  10.4 us
    all_gather x1, blocking collectives, per_device(): all_segments = lax.all_gather(segment_ids, 'seq', axis=0, tiled=True)  8.76 us
  transfers between devices with their start and end apart: 6, of which 5 were waited for; matrix products, arithmetic and copies ran while one was open for 4% of the time, Pallas kernels for 0%

profile of v17, /device:TPU:0, one launch (start us, length us, event | category | flops | bytes accessed | tf_op | source)
XLA Modules:
  0.0 196.9 jit_solution(7855085059491665560)
XLA Ops:
  7.2 0.0 copy-start
  7.2 0.0 copy-start.3
  7.2 0.0 all-gather.5.cloned.1.call-start
  7.2 1.3 reshape.82
  8.5 1.8 reshape.83
  10.3 1.1 pad_maximum_fusion
  11.5 15.8 %all_to_all.40 = bf16[4,1152,32]{1,2,0:T(8,128)(2,1)} all-to-all(bf16[4,1152,32]{1,2,0:T(8,128)(2,1)S(1)} %copy.73), channel_id=1, replica_groups=mesh['seq'=8,'head'=4] {'head'}, dimensions={0} | all-to-all | bytes 589824 | tf_op jit(solution)/shard_map/all_to_all | solution.py:109
  27.3 1.9 copy.74
  29.1 0.0 all-gather.5.cloned.1.call-update
  29.1 1.1 reshape.81
  30.3 0.7 copy.71
  31.0 3.3 %all-to-all-start = ((bf16[32,4,576]{2,0,1:T(8,128)(2,1)}), bf16[32,4,576]{2,0,1:T(8,128)(2,1)S(1)}, u32[]{:S(2)}, u32[]{:S(2)}) async-start(bf16[32,4,576]{2,0,1:T(8,128)(2,1)} %copy.71), calls=%async_computation | async-start | bytes 327680 | tf_op jit(solution)/shard_map/all_to_all | solution.py:115
  34.3 0.0 reduce-scatter.3.cloned.1.call-start
  34.4 0.0 copy-done.3
  34.4 8.8 %all-gather.1 = s32[8,1,128]{2,1,0:T(1,128)S(1)} all-gather(s32[1,1,128]{2,1,0:T(1,128)S(1)} %bitcast.92), channel_id=1, replica_groups=mesh['seq'=8,'head'=4] {'seq'}, dimensions={0}, use_global_device_ids=true | all-gather | bytes 4608 | tf_op jit(solution)/shard_map/all_gather | solution.py:122
  43.1 1.0 fusion.18.allowed_ref
  44.1 0.0 all-to-all-done
  44.1 1.0 reshape_reshape.3
  45.2 1.9 copy.87
  47.0 10.8 %all-gather.5.cloned.1.call-done.window_ref = bf16[1152,1024]{1,0:T(8,128)(2,1)} async-done(((bf16[1152,128]{1,0:T(8,128)(2,1)}), bf16[1152,1024]{1,0:T(8,128)(2,1)}) %all-gather.5.cloned.1.call-update) | async-done | bytes 2359312 | tf_op jit(solution)/shard_map/all_gather | solution.py:124
  57.8 0.0 copy-start.2
  57.8 0.0 copy-start.1
  57.8 6.2 %shard_map.139 = bf16[128,2304]{1,0:T(8,128)(2,1)} custom-call(bf16[9,128,64]{2,1,0:T(8,128)(2,1)} %bitcast.85, bf16[1152,1024]{1,0:T(8,128)(2,1)} %all-gather.5.cloned.1.call-done.window_ref, s32[128,1024]{1,0:T(8,128)} %fusion.18.allowed_ref, bf16[576,2304]{1,0:T(8,128)(2,1)} %weight_ref.1), custom_call_target="tpu_custom_call" | custom-call | tf_op jit(solution)/shard_map/pallas_call | solution.py:71
  64.0 0.0 reduce-scatter.3.cloned.1.call-update
  64.0 0.0 all-gather.7.cloned.1.call-start
  64.0 0.0 copy-done.2
  64.0 0.1 copy.75
  64.1 0.1 eq.84
  64.2 0.1 fusion.33
  64.3 0.1 reduce_window_sum.11
  64.4 0.2 select_reduce_fusion
  64.6 0.1 reduce_sum.40
  64.7 0.1 copy.76
  64.8 0.1 compare_reduce_fusion
  64.9 21.3 %reduce-scatter.3.cloned.1.call-done = bf16[32,2304]{1,0:T(8,128)(2,1)} async-done(((bf16[128,2304]{1,0:T(8,128)(2,1)}), bf16[32,2304]{1,0:T(8,128)(2,1)}) %reduce-scatter.3.cloned.1.call-update) | async-done | bytes 147472 | tf_op jit(solution)/shard_map/reduce_scatter | solution.py:150
  86.2 1.2 fusion.19
  87.3 0.0 copy-done.1
  87.4 0.4 convolution_convert_fusion.1
  87.7 13.9 %all_to_all.41 = bf16[8,9,2304]{2,1,0:T(8,128)(2,1)S(1)} all-to-all(bf16[8,9,2304]{2,1,0:T(8,128)(2,1)S(1)} %convolution_convert_fusion.1), channel_id=1, replica_groups=mesh['seq'=8,'head'=4] {'seq'}, dimensions={0} | all-to-all | bytes 663552 | tf_op jit(solution)/shard_map/all_to_all | solution.py:181
  101.6 0.8 copy.79
  102.5 0.0 all-gather.7.cloned.1.call-update
  102.5 0.0 reduce-scatter.5.cloned.1.call-start
  102.6 29.6 %all-gather.7.cloned.1.call-done = bf16[36,8,2304]{2,1,0:T(8,128)(2,1)} async-done(((bf16[9,8,2304]{2,1,0:T(8,128)(2,1)}), bf16[36,8,2304]{2,1,0:T(8,128)(2,1)}) %all-gather.7.cloned.1.call-update) | async-done | bytes 1327120 | tf_op jit(solution)/shard_map/all_gather | solution.py:182
  132.2 0.0 copy-start.4
  132.2 0.0 copy-start.5
  132.2 3.7 %fusion.9 = f32[4,9,8,720]{3,2,1,0:T(8,128)S(1)} fusion(bf16[4,9,8,2304]{3,2,1,0:T(8,128)(2,1)} %bitcast.93, bf16[2304,720]{0,1:T(8,128)(2,1)} %param.20), kind=kOutput, calls=%fused_computation.13 | convolution fusion | flops 955514880 | bytes 5474304 | tf_op jit(solution)/shard_map/hcsd,df->hcsf/dot_general | solution.py:183
  135.9 0.0 copy-done.4
  135.9 0.0 copy-done.5
  135.9 1.3 fusion.14
  137.3 0.0 copy-done
  137.3 0.0 copy-start.6
  137.3 2.3 %convolution_convert_fusion = bf16[4,9,8,2304]{3,2,1,0:T(8,128)(2,1)} fusion(bf16[4,9,8,720]{3,2,1,0:T(8,128)(2,1)S(1)} %fusion.14, bf16[2304,720]{0,1:T(8,128)(2,1)S(1)} %copy-done), kind=kOutput, calls=%fused_computation | convolution fusion | flops 956178432 | bytes 5059584 | tf_op jit(solution)/shard_map/hcsf,df->hcsd/dot_general | solution.py:190
  139.6 0.0 reduce-scatter.5.cloned.1.call-update
  139.6 0.1 copy.77
  139.7 1.7 slice_bitcast_fusion
  141.4 0.0 copy-done.6
  141.4 0.2 fusion.27
  141.6 28.8 %reduce-scatter.5.cloned.1.call-done = bf16[1,9,8,2304]{3,2,1,0:T(8,128)(2,1)} async-done(((bf16[4,9,8,2304]{3,2,1,0:T(8,128)(2,1)}), bf16[1,9,8,2304]{3,2,1,0:T(8,128)(2,1)}) %reduce-scatter.5.cloned.1.call-update) | async-done | bytes 331792 | tf_op jit(solution)/shard_map/reduce_scatter | solution.py:194
  170.4 1.9 copy.80
  172.3 4.2 %all-to-all-start.3 = ((bf16[8,9,2304]{2,1,0:T(8,128)(2,1)}), bf16[8,9,2304]{2,1,0:T(8,128)(2,1)}, u32[]{:S(2)}, u32[]{:S(2)}) async-start(bf16[8,9,2304]{2,1,0:T(8,128)(2,1)} %copy.80), calls=%async_computation.5 | async-start | bytes 1179648 | tf_op jit(solution)/shard_map/all_to_all | solution.py:196
  176.5 10.4 %all-to-all-done.3 = bf16[8,9,2304]{2,1,0:T(8,128)(2,1)} async-done(((bf16[8,9,2304]{2,1,0:T(8,128)(2,1)}), bf16[8,9,2304]{2,1,0:T(8,128)(2,1)}, u32[]{:S(2)}, u32[]{:S(2)}) %all-to-all-start.3) | async-done | bytes 331808 | tf_op jit(solution)/shard_map/all_to_all | solution.py:196
  186.9 1.4 fusion.4
  188.3 2.1 %fusion.5 = bf16[32,2304]{1,0:T(8,128)(2,1)} fusion(f32[32,2304]{1,0:T(8,128)S(1)} %fusion.4, bf16[8,9,2304]{2,1,0:T(8,128)(2,1)} %all-to-all-done.3, bf16[32,2304]{1,0:T(8,128)(2,1)S(1)} %get-tuple-element.4, f32[32]{0:T(128)S(1)} %get-tuple-element.9, s32[32]{0:T(128)S(1)} %get-tuple-element.7, s32[8,9]{1,0:T(8,128)S(1)} %copy.77), kind=kOutput, calls=%fused_computation.9 | convolution fusion | flops 11061504 | bytes 922144 | tf_op jit(solution)/shard_map/tec,ercd->trd/dot_general | solution.py:204
  (8 shorter events, 0.1 us)
Async XLA Ops:
  7.2 130.1 %copy-start = (bf16[2304,720]{0,1:T(8,128)(2,1)S(1)}, bf16[2304,720]{0,1:T(8,128)(2,1)}, u32[]{:S(2)}) copy-start(bf16[2304,720]{0,1:T(8,128)(2,1)} %param.22) | copy-start | bytes 9953284
  7.2 27.2 %copy-start.3 = (s32[128]{0:T(128)S(1)}, s32[128]{0:T(128)}, u32[]{:S(2)}) copy-start(s32[128]{0:T(128)} %param.18) | copy-start | bytes 1540
  7.2 50.6 %all-gather.5.cloned.1.call-start = ((), (), s32[]{:S(2)}) async-start(), calls=%async_computation.6 | async-start | bytes 2654208 | tf_op jit(solution)/shard_map/all_gather | solution.py:124
  31.0 13.2 %all-to-all-start = ((bf16[32,4,576]{2,0,1:T(8,128)(2,1)}), bf16[32,4,576]{2,0,1:T(8,128)(2,1)S(1)}, u32[]{:S(2)}, u32[]{:S(2)}) async-start(bf16[32,4,576]{2,0,1:T(8,128)(2,1)} %copy.71), calls=%async_computation | async-start | bytes 327680 | tf_op jit(solution)/shard_map/all_to_all | solution.py:115
  34.3 51.9 %reduce-scatter.3.cloned.1.call-start = ((), (), s32[]{:S(2)}) async-start(), calls=%async_computation.7 | async-start | bytes 737280 | tf_op jit(solution)/shard_map/reduce_scatter | solution.py:150
  57.8 6.3 %copy-start.2 = (s32[32,2]{0,1:T(2,128)S(1)}, s32[32,2]{0,1:T(2,128)}, u32[]{:S(2)}) copy-start(s32[32,2]{0,1:T(2,128)} %param.19) | copy-start | bytes 772
  57.8 29.6 %copy-start.1 = (f32[2304]{0:T(1024)S(1)}, f32[2304]{0:T(1024)}, u32[]{:S(2)}) copy-start(f32[2304]{0:T(1024)} %param.16) | copy-start | bytes 27652
  64.0 68.2 %all-gather.7.cloned.1.call-start = ((), (), s32[]{:S(2)}) async-start(), calls=%async_computation.9 | async-start | bytes 1658880 | tf_op jit(solution)/shard_map/all_gather | solution.py:182
  102.5 67.9 %reduce-scatter.5.cloned.1.call-start = ((), (), s32[]{:S(2)}) async-start(), calls=%async_computation.8 | async-start | bytes 1658880 | tf_op jit(solution)/shard_map/reduce_scatter | solution.py:194
  132.2 3.7 %copy-start.4 = (bf16[2304,720]{0,1:T(8,128)(2,1)S(1)}, bf16[2304,720]{0,1:T(8,128)(2,1)}, u32[]{:S(2)}) copy-start(bf16[2304,720]{0,1:T(8,128)(2,1)} %param.21) | copy-start | bytes 9953284
  132.2 3.7 %copy-start.5 = (bf16[36,8,2304]{2,1,0:T(8,128)(2,1)S(1)}, bf16[36,8,2304]{2,1,0:T(8,128)(2,1)}, u32[]{:S(2)}) copy-start(bf16[36,8,2304]{2,1,0:T(8,128)(2,1)} %all-gather.7.cloned.1.call-done) | copy-start | bytes 3981316
  137.3 4.1 %copy-start.6 = (bf16[2304,8]{0,1:T(8,128)(2,1)S(1)}, bf16[2304,8]{0,1:T(8,128)(2,1)}, u32[]{:S(2)}) copy-start(bf16[2304,8]{0,1:T(8,128)(2,1)} %param.17) | copy-start | bytes 110596
  172.3 14.7 %all-to-all-start.3 = ((bf16[8,9,2304]{2,1,0:T(8,128)(2,1)}), bf16[8,9,2304]{2,1,0:T(8,128)(2,1)}, u32[]{:S(2)}, u32[]{:S(2)}) async-start(bf16[8,9,2304]{2,1,0:T(8,128)(2,1)} %copy.80), calls=%async_computation.5 | async-start | bytes 1179648 | tf_op jit(solution)/shard_map/all_to_all | solution.py:196
Sparse Core Ops, SparseCore 0:
  29.3 28.4 all-gather.4
  64.1 22.0 reduce-scatter.2
  102.6 29.5 all-gather.6
  139.7 30.6 reduce-scatter.4

commit v18 on v17

--- a/solution.py
+++ b/solution.py
@@ -46,21 +46,18 @@
         for head in range(heads):
             keys = window_ref[pl.ds(head * HDIM, HDIM), :]
             values = window_ref[pl.ds(group_width + head * HDIM, HDIM), :]
-            raw = jnp.dot(q_ref[head], keys, preferred_element_type=jnp.float32) * HDIM ** (-0.5)
+            raw = lax.dot_general(
+                keys,
+                q_ref[head],
+                (((0,), (1,)), ((), ())),
+                preferred_element_type=jnp.float32,
+            ) * HDIM ** (-0.5)
             masked = jnp.where(allowed_now, raw, -jnp.inf)
-            top = jnp.max(masked, axis=1, keepdims=True)
+            top = jnp.max(masked, axis=0, keepdims=True)
             weights = jnp.exp(masked - top)
-            sums = jnp.sum(weights, axis=1, keepdims=True)
-            mixed = lax.dot_general(
-                weights.astype(jnp.bfloat16),
-                values,
-                (((1,), (1,)), ((), ())),
-                preferred_element_type=jnp.float32,
-            )
-            attended = (mixed / sums).astype(jnp.bfloat16).astype(jnp.float32)
-            gathered_ref[pl.ds(head * HDIM, HDIM), :] = jnp.transpose(attended).astype(
-                jnp.bfloat16
-            )
+            sums = jnp.sum(weights, axis=0, keepdims=True)
+            mixed = jnp.dot(values, weights.astype(jnp.bfloat16), preferred_element_type=jnp.float32)
+            gathered_ref[pl.ds(head * HDIM, HDIM), :] = (mixed / sums).astype(jnp.bfloat16)
         out_ref[...] = lax.dot_general(
             gathered_ref[...],
             weight_ref[...],
@@ -72,7 +69,7 @@
         kernel,
         out_shape=jax.ShapeDtypeStruct((tokens, out_weight.shape[1]), jnp.bfloat16),
         scratch_shapes=[pltpu.VMEM((group_width, tokens), jnp.bfloat16)],
-    )(q3, window_t, allowed.astype(jnp.int32), out_weight)
+    )(q3, window_t, jnp.transpose(allowed).astype(jnp.int32), out_weight)
 
 
 def per_device(

time: 198 us -> 199 us (level)
  no operation moved by 1% of the time
where the time goes in v18:
time: 199 us; the launch traced here: 198 us
  waiting for transfers between devices  101 us (51%)
  blocking collectives  38.5 us (19%)
  local copies, waits for them, and re-layouts  14.6 us (7%)
  between operations  13.9 us (7%)
  matrix products  11.4 us (6%)
  starting transfers between devices  7.7 us (4%)
  Pallas kernels  7.27 us (4%)
  other arithmetic  3.76 us (2%)
    all_gather x1, waiting for transfers between devices, per_device(): lax.all_gather(jnp.swapaxes(arrived, 0, 1), 'head', axis=0, tiled=False)  29.6 us
    reduce_scatter x1, waiting for transfers between devices, per_device(): lax.psum_scatter(partial_out, 'head', scatter_dimension=0, tiled=False)  28.8 us
    reduce_scatter x1, waiting for transfers between devices, per_device(): lax.psum_scatter(attention_project(queries, joined_window_t, allowed, out...  21.3 us
    all_to_all x1, blocking collectives, per_device(): lax.all_to_all(joined_rows_t, 'head', split_axis=0, concat_axis=2, tiled=...  15.8 us
    all_to_all x1, blocking collectives, per_device(): lax.all_to_all(outgoing, 'seq', split_axis=0, concat_axis=0, tiled=True)  13.9 us
    all_gather x1, waiting for transfers between devices, per_device(): joined_window_t = lax.all_gather(joined_head_t, 'seq', axis=1, tiled=True)  10.7 us
    all_to_all x1, waiting for transfers between devices, per_device(): lax.all_to_all(shard_out, 'seq', split_axis=0, concat_axis=0, tiled=True)  10.4 us
    all_gather x1, blocking collectives, per_device(): all_segments = lax.all_gather(segment_ids, 'seq', axis=0, tiled=True)  8.76 us
  transfers between devices with their start and end apart: 6, of which 5 were waited for; matrix products, arithmetic and copies ran while one was open for 4% of the time, Pallas kernels for 0%

profile of v18, /device:TPU:0, one launch (start us, length us, event | category | flops | bytes accessed | tf_op | source)
XLA Modules:
  0.0 198.0 jit_solution(2885177653198217891)
XLA Ops:
  7.2 0.0 copy-start
  7.2 0.0 copy-start.3
  7.2 0.0 all-gather.5.cloned.1.call-start
  7.2 1.3 reshape.82
  8.5 1.8 reshape.83
  10.3 1.1 pad_maximum_fusion
  11.5 15.8 %all_to_all.40 = bf16[4,1152,32]{1,2,0:T(8,128)(2,1)} all-to-all(bf16[4,1152,32]{1,2,0:T(8,128)(2,1)S(1)} %copy.73), channel_id=1, replica_groups=mesh['seq'=8,'head'=4] {'head'}, dimensions={0} | all-to-all | bytes 589824 | tf_op jit(solution)/shard_map/all_to_all | solution.py:106
  27.3 1.9 copy.74
  29.1 0.0 all-gather.5.cloned.1.call-update
  29.1 1.1 reshape.81
  30.3 0.7 copy.71
  31.0 3.3 %all-to-all-start = ((bf16[32,4,576]{2,0,1:T(8,128)(2,1)}), bf16[32,4,576]{2,0,1:T(8,128)(2,1)S(1)}, u32[]{:S(2)}, u32[]{:S(2)}) async-start(bf16[32,4,576]{2,0,1:T(8,128)(2,1)} %copy.71), calls=%async_computation | async-start | bytes 327680 | tf_op jit(solution)/shard_map/all_to_all | solution.py:112
  34.3 0.0 reduce-scatter.3.cloned.1.call-start
  34.4 0.0 copy-done.3
  34.4 8.8 %all-gather.1 = s32[8,1,128]{2,1,0:T(1,128)S(1)} all-gather(s32[1,1,128]{2,1,0:T(1,128)S(1)} %bitcast.92), channel_id=1, replica_groups=mesh['seq'=8,'head'=4] {'seq'}, dimensions={0}, use_global_device_ids=true | all-gather | bytes 4608 | tf_op jit(solution)/shard_map/all_gather | solution.py:119
  43.1 1.0 fusion.18.allowed_ref
  44.1 0.0 all-to-all-done
  44.1 1.0 reshape_reshape.3
  45.2 1.9 copy.87
  47.0 10.7 %all-gather.5.cloned.1.call-done.window_ref = bf16[1152,1024]{1,0:T(8,128)(2,1)} async-done(((bf16[1152,128]{1,0:T(8,128)(2,1)}), bf16[1152,1024]{1,0:T(8,128)(2,1)}) %all-gather.5.cloned.1.call-update) | async-done | bytes 2359312 | tf_op jit(solution)/shard_map/all_gather | solution.py:121
  57.8 0.0 copy-start.2
  57.8 0.0 copy-start.1
  57.8 7.3 %shard_map.139 = bf16[128,2304]{1,0:T(8,128)(2,1)} custom-call(bf16[9,128,64]{2,1,0:T(8,128)(2,1)} %bitcast.85, bf16[1152,1024]{1,0:T(8,128)(2,1)} %all-gather.5.cloned.1.call-done.window_ref, s32[1024,128]{1,0:T(8,128)} %fusion.18.allowed_ref, bf16[576,2304]{1,0:T(8,128)(2,1)} %weight_ref.1), custom_call_target="tpu_custom_call" | custom-call | tf_op jit(solution)/shard_map/pallas_call | solution.py:68
  65.0 0.0 reduce-scatter.3.cloned.1.call-update
  65.1 0.0 all-gather.7.cloned.1.call-start
  65.1 0.0 copy-done.2
  65.1 0.1 copy.75
  65.2 0.1 eq.85
  65.3 0.1 fusion.33
  65.4 0.1 reduce_window_sum.11
  65.5 0.2 select_reduce_fusion
  65.7 0.1 reduce_sum.40
  65.8 0.1 copy.76
  65.9 0.1 compare_reduce_fusion
  66.0 21.3 %reduce-scatter.3.cloned.1.call-done = bf16[32,2304]{1,0:T(8,128)(2,1)} async-done(((bf16[128,2304]{1,0:T(8,128)(2,1)}), bf16[32,2304]{1,0:T(8,128)(2,1)}) %reduce-scatter.3.cloned.1.call-update) | async-done | bytes 147472 | tf_op jit(solution)/shard_map/reduce_scatter | solution.py:147
  87.3 1.2 fusion.19
  88.4 0.0 copy-done.1
  88.4 0.4 convolution_convert_fusion.1
  88.8 13.9 %all_to_all.41 = bf16[8,9,2304]{2,1,0:T(8,128)(2,1)S(1)} all-to-all(bf16[8,9,2304]{2,1,0:T(8,128)(2,1)S(1)} %convolution_convert_fusion.1), channel_id=1, replica_groups=mesh['seq'=8,'head'=4] {'seq'}, dimensions={0} | all-to-all | bytes 663552 | tf_op jit(solution)/shard_map/all_to_all | solution.py:178
  102.7 0.8 copy.79
  103.6 0.0 all-gather.7.cloned.1.call-update
  103.6 0.0 reduce-scatter.5.cloned.1.call-start
  103.6 29.6 %all-gather.7.cloned.1.call-done = bf16[36,8,2304]{2,1,0:T(8,128)(2,1)} async-done(((bf16[9,8,2304]{2,1,0:T(8,128)(2,1)}), bf16[36,8,2304]{2,1,0:T(8,128)(2,1)}) %all-gather.7.cloned.1.call-update) | async-done | bytes 1327120 | tf_op jit(solution)/shard_map/all_gather | solution.py:179
  133.2 0.0 copy-start.4
  133.2 0.0 copy-start.5
  133.2 3.7 %fusion.9 = f32[4,9,8,720]{3,2,1,0:T(8,128)S(1)} fusion(bf16[4,9,8,2304]{3,2,1,0:T(8,128)(2,1)} %bitcast.93, bf16[2304,720]{0,1:T(8,128)(2,1)} %param.20), kind=kOutput, calls=%fused_computation.13 | convolution fusion | flops 955514880 | bytes 5474304 | tf_op jit(solution)/shard_map/hcsd,df->hcsf/dot_general | solution.py:180
  137.0 0.0 copy-done.4
  137.0 0.0 copy-done.5
  137.0 1.3 fusion.14
  138.3 0.0 copy-done
  138.3 0.0 copy-start.6
  138.4 2.3 %convolution_convert_fusion = bf16[4,9,8,2304]{3,2,1,0:T(8,128)(2,1)} fusion(bf16[4,9,8,720]{3,2,1,0:T(8,128)(2,1)S(1)} %fusion.14, bf16[2304,720]{0,1:T(8,128)(2,1)S(1)} %copy-done), kind=kOutput, calls=%fused_computation | convolution fusion | flops 956178432 | bytes 5059584 | tf_op jit(solution)/shard_map/hcsf,df->hcsd/dot_general | solution.py:187
  140.6 0.0 reduce-scatter.5.cloned.1.call-update
  140.7 0.1 copy.77
  140.8 1.7 slice_bitcast_fusion
  142.5 0.0 copy-done.6
  142.5 0.2 fusion.27
  142.7 28.8 %reduce-scatter.5.cloned.1.call-done = bf16[1,9,8,2304]{3,2,1,0:T(8,128)(2,1)} async-done(((bf16[4,9,8,2304]{3,2,1,0:T(8,128)(2,1)}), bf16[1,9,8,2304]{3,2,1,0:T(8,128)(2,1)}) %reduce-scatter.5.cloned.1.call-update) | async-done | bytes 331792 | tf_op jit(solution)/shard_map/reduce_scatter | solution.py:191
  171.4 1.9 copy.80
  173.3 4.2 %all-to-all-start.3 = ((bf16[8,9,2304]{2,1,0:T(8,128)(2,1)}), bf16[8,9,2304]{2,1,0:T(8,128)(2,1)}, u32[]{:S(2)}, u32[]{:S(2)}) async-start(bf16[8,9,2304]{2,1,0:T(8,128)(2,1)} %copy.80), calls=%async_computation.5 | async-start | bytes 1179648 | tf_op jit(solution)/shard_map/all_to_all | solution.py:193
  177.5 10.4 %all-to-all-done.3 = bf16[8,9,2304]{2,1,0:T(8,128)(2,1)} async-done(((bf16[8,9,2304]{2,1,0:T(8,128)(2,1)}), bf16[8,9,2304]{2,1,0:T(8,128)(2,1)}, u32[]{:S(2)}, u32[]{:S(2)}) %all-to-all-start.3) | async-done | bytes 331808 | tf_op jit(solution)/shard_map/all_to_all | solution.py:193
  188.0 1.4 fusion.4
  189.4 2.1 %fusion.5 = bf16[32,2304]{1,0:T(8,128)(2,1)} fusion(f32[32,2304]{1,0:T(8,128)S(1)} %fusion.4, bf16[8,9,2304]{2,1,0:T(8,128)(2,1)} %all-to-all-done.3, bf16[32,2304]{1,0:T(8,128)(2,1)S(1)} %get-tuple-element.4, f32[32]{0:T(128)S(1)} %get-tuple-element.9, s32[32]{0:T(128)S(1)} %get-tuple-element.7, s32[8,9]{1,0:T(8,128)S(1)} %copy.77), kind=kOutput, calls=%fused_computation.9 | convolution fusion | flops 11061504 | bytes 922144 | tf_op jit(solution)/shard_map/tec,ercd->trd/dot_general | solution.py:201
  (8 shorter events, 0.1 us)
Async XLA Ops:
  7.2 131.2 %copy-start = (bf16[2304,720]{0,1:T(8,128)(2,1)S(1)}, bf16[2304,720]{0,1:T(8,128)(2,1)}, u32[]{:S(2)}) copy-start(bf16[2304,720]{0,1:T(8,128)(2,1)} %param.22) | copy-start | bytes 9953284
  7.2 27.2 %copy-start.3 = (s32[128]{0:T(128)S(1)}, s32[128]{0:T(128)}, u32[]{:S(2)}) copy-start(s32[128]{0:T(128)} %param.18) | copy-start | bytes 1540
  7.2 50.6 %all-gather.5.cloned.1.call-start = ((), (), s32[]{:S(2)}) async-start(), calls=%async_computation.6 | async-start | bytes 2654208 | tf_op jit(solution)/shard_map/all_gather | solution.py:121
  31.0 13.2 %all-to-all-start = ((bf16[32,4,576]{2,0,1:T(8,128)(2,1)}), bf16[32,4,576]{2,0,1:T(8,128)(2,1)S(1)}, u32[]{:S(2)}, u32[]{:S(2)}) async-start(bf16[32,4,576]{2,0,1:T(8,128)(2,1)} %copy.71), calls=%async_computation | async-start | bytes 327680 | tf_op jit(solution)/shard_map/all_to_all | solution.py:112
  34.3 53.0 %reduce-scatter.3.cloned.1.call-start = ((), (), s32[]{:S(2)}) async-start(), calls=%async_computation.7 | async-start | bytes 737280 | tf_op jit(solution)/shard_map/reduce_scatter | solution.py:147
  57.8 7.3 %copy-start.2 = (s32[32,2]{0,1:T(2,128)S(1)}, s32[32,2]{0,1:T(2,128)}, u32[]{:S(2)}) copy-start(s32[32,2]{0,1:T(2,128)} %param.19) | copy-start | bytes 772
  57.8 30.7 %copy-start.1 = (f32[2304]{0:T(1024)S(1)}, f32[2304]{0:T(1024)}, u32[]{:S(2)}) copy-start(f32[2304]{0:T(1024)} %param.16) | copy-start | bytes 27652
  65.1 68.2 %all-gather.7.cloned.1.call-start = ((), (), s32[]{:S(2)}) async-start(), calls=%async_computation.9 | async-start | bytes 1658880 | tf_op jit(solution)/shard_map/all_gather | solution.py:179
  103.6 67.9 %reduce-scatter.5.cloned.1.call-start = ((), (), s32[]{:S(2)}) async-start(), calls=%async_computation.8 | async-start | bytes 1658880 | tf_op jit(solution)/shard_map/reduce_scatter | solution.py:191
  133.2 3.7 %copy-start.4 = (bf16[2304,720]{0,1:T(8,128)(2,1)S(1)}, bf16[2304,720]{0,1:T(8,128)(2,1)}, u32[]{:S(2)}) copy-start(bf16[2304,720]{0,1:T(8,128)(2,1)} %param.21) | copy-start | bytes 9953284
  133.2 3.7 %copy-start.5 = (bf16[36,8,2304]{2,1,0:T(8,128)(2,1)S(1)}, bf16[36,8,2304]{2,1,0:T(8,128)(2,1)}, u32[]{:S(2)}) copy-start(bf16[36,8,2304]{2,1,0:T(8,128)(2,1)} %all-gather.7.cloned.1.call-done) | copy-start | bytes 3981316
  138.3 4.1 %copy-start.6 = (bf16[2304,8]{0,1:T(8,128)(2,1)S(1)}, bf16[2304,8]{0,1:T(8,128)(2,1)}, u32[]{:S(2)}) copy-start(bf16[2304,8]{0,1:T(8,128)(2,1)} %param.17) | copy-start | bytes 110596
  173.3 14.7 %all-to-all-start.3 = ((bf16[8,9,2304]{2,1,0:T(8,128)(2,1)}), bf16[8,9,2304]{2,1,0:T(8,128)(2,1)}, u32[]{:S(2)}, u32[]{:S(2)}) async-start(bf16[8,9,2304]{2,1,0:T(8,128)(2,1)} %copy.80), calls=%async_computation.5 | async-start | bytes 1179648 | tf_op jit(solution)/shard_map/all_to_all | solution.py:193
Sparse Core Ops, SparseCore 0:
  29.3 28.4 all-gather.4
  65.2 22.0 reduce-scatter.2
  103.7 29.4 all-gather.6
  140.8 30.6 reduce-scatter.4

commit v19 on v17

--- a/solution.py
+++ b/solution.py
@@ -37,12 +37,18 @@
     )
 
 
-def attention_project(q3, window_t, allowed, out_weight):
+def attention_project(q3, window_t, query_info, key_info, out_weight):
     heads, tokens, _ = q3.shape
     group_width = heads * HDIM
 
-    def kernel(q_ref, window_ref, allowed_ref, weight_ref, out_ref, gathered_ref):
-        allowed_now = allowed_ref[...] != 0
+    def kernel(q_ref, window_ref, query_ref, key_ref, weight_ref, out_ref, gathered_ref):
+        query_now = query_ref[...]
+        key_now = key_ref[...]
+        allowed_now = (
+            (key_now[0:1, :] == query_now[:, 0:1])
+            & (key_now[1:2, :] <= query_now[:, 1:2])
+            & (key_now[1:2, :] >= 0)
+        )
         for head in range(heads):
             keys = window_ref[pl.ds(head * HDIM, HDIM), :]
             values = window_ref[pl.ds(group_width + head * HDIM, HDIM), :]
@@ -72,7 +78,7 @@
         kernel,
         out_shape=jax.ShapeDtypeStruct((tokens, out_weight.shape[1]), jnp.bfloat16),
         scratch_shapes=[pltpu.VMEM((group_width, tokens), jnp.bfloat16)],
-    )(q3, window_t, allowed.astype(jnp.int32), out_weight)
+    )(q3, window_t, query_info, key_info, out_weight)
 
 
 def per_device(
@@ -148,7 +154,13 @@
     )
     queries = jnp.transpose(query_head.reshape(stretch_len, heads_here, HDIM), (1, 0, 2))
     attended_sum = lax.psum_scatter(
-        attention_project(queries, joined_window_t, allowed, out_weight),
+        attention_project(
+            queries,
+            joined_window_t,
+            jnp.stack((segment_ids, query_place), 1),
+            jnp.stack((segment_window, key_place), 0),
+            out_weight,
+        ),
         "head",
         scatter_dimension=0,
         tiled=True,

time: 198 us -> 198 us (level)
  transfers between devices with their start and end apart: 6 -> 6, of which waited for: 5 -> 5; matrix products, arithmetic and copies ran while one was open for 4% -> 5% of each run, Pallas kernels for 0% -> 0%
where the time goes in v19:
time: 198 us; the launch traced here: 197 us
  waiting for transfers between devices  101 us (51%)
  blocking collectives  38.4 us (19%)
  local copies, waits for them, and re-layouts  15.3 us (8%)
  between operations  14 us (7%)
  matrix products  11.4 us (6%)
  starting transfers between devices  7.7 us (4%)
  Pallas kernels  6.25 us (3%)
  other arithmetic  3.38 us (2%)
    all_gather x1, waiting for transfers between devices, per_device(): lax.all_gather(jnp.swapaxes(arrived, 0, 1), 'head', axis=0, tiled=False)  29.6 us
    reduce_scatter x1, waiting for transfers between devices, per_device(): lax.psum_scatter(partial_out, 'head', scatter_dimension=0, tiled=False)  28.8 us
    reduce_scatter x1, waiting for transfers between devices, per_device(): lax.psum_scatter(attention_project(queries, joined_window_t, jnp.stack((s...  21.3 us
    all_to_all x1, blocking collectives, per_device(): lax.all_to_all(joined_rows_t, 'head', split_axis=0, concat_axis=2, tiled=...  15.8 us
    all_to_all x1, blocking collectives, per_device(): lax.all_to_all(outgoing, 'seq', split_axis=0, concat_axis=0, tiled=True)  13.9 us
    all_to_all x1, waiting for transfers between devices, per_device(): lax.all_to_all(shard_out, 'seq', split_axis=0, concat_axis=0, tiled=True)  10.4 us
    all_gather x1, waiting for transfers between devices, per_device(): joined_window_t = lax.all_gather(joined_head_t, 'seq', axis=1, tiled=True)  10.4 us
    all_gather x1, blocking collectives, per_device(): all_segments = lax.all_gather(segment_ids, 'seq', axis=0, tiled=True)  8.75 us
  transfers between devices with their start and end apart: 6, of which 5 were waited for; matrix products, arithmetic and copies ran while one was open for 5% of the time, Pallas kernels for 0%

profile of v19, /device:TPU:0, one launch (start us, length us, event | category | flops | bytes accessed | tf_op | source)
XLA Modules:
  0.0 197.0 jit_solution(628485744788200056)
XLA Ops:
  7.2 0.0 copy-start
  7.2 0.0 copy-start.3
  7.2 0.0 all-gather.5.cloned.1.call-start
  7.2 1.3 reshape.83
  8.5 1.8 reshape.84
  10.3 1.1 pad_maximum_fusion
  11.5 15.8 %all_to_all.40 = bf16[4,1152,32]{1,2,0:T(8,128)(2,1)} all-to-all(bf16[4,1152,32]{1,2,0:T(8,128)(2,1)S(1)} %copy.78), channel_id=1, replica_groups=mesh['seq'=8,'head'=4] {'head'}, dimensions={0} | all-to-all | bytes 589824 | tf_op jit(solution)/shard_map/all_to_all | solution.py:115
  27.3 1.9 copy.79
  29.1 0.0 all-gather.5.cloned.1.call-update
  29.2 1.1 reshape.82
  30.3 0.7 copy.76
  31.0 3.3 %all-to-all-start = ((bf16[32,4,576]{2,0,1:T(8,128)(2,1)}), bf16[32,4,576]{2,0,1:T(8,128)(2,1)S(1)}, u32[]{:S(2)}, u32[]{:S(2)}) async-start(bf16[32,4,576]{2,0,1:T(8,128)(2,1)} %copy.76), calls=%async_computation | async-start | bytes 327680 | tf_op jit(solution)/shard_map/all_to_all | solution.py:121
  34.3 0.0 reduce-scatter.3.cloned.1.call-start
  34.4 0.0 copy-done.3
  34.4 0.7 copy.80.query_ref
  35.2 8.7 %all-gather.1 = s32[8,1,128]{2,1,0:T(1,128)S(1)} all-gather(s32[1,1,128]{2,1,0:T(1,128)S(1)} %bitcast.94), channel_id=1, replica_groups=mesh['seq'=8,'head'=4] {'seq'}, dimensions={0}, use_global_device_ids=true | all-gather | bytes 4608 | tf_op jit(solution)/shard_map/all_gather | solution.py:128
  43.9 0.6 pad_add_fusion.key_ref
  44.5 0.0 all-to-all-done
  44.5 1.0 reshape_reshape.3
  45.6 1.8 copy.93
  47.4 10.4 %all-gather.5.cloned.1.call-done.window_ref = bf16[1152,1024]{1,0:T(8,128)(2,1)} async-done(((bf16[1152,128]{1,0:T(8,128)(2,1)}), bf16[1152,1024]{1,0:T(8,128)(2,1)}) %all-gather.5.cloned.1.call-update) | async-done | bytes 2359312 | tf_op jit(solution)/shard_map/all_gather | solution.py:130
  57.8 0.0 copy-start.2
  57.8 0.0 copy-start.1
  57.8 6.2 %shard_map.139 = bf16[128,2304]{1,0:T(8,128)(2,1)} custom-call(bf16[9,128,64]{2,1,0:T(8,128)(2,1)} %bitcast.86, bf16[1152,1024]{1,0:T(8,128)(2,1)} %all-gather.5.cloned.1.call-done.window_ref, s32[128,2]{1,0:T(8,128)} %copy.80.query_ref, s32[2,1024]{1,0:T(2,128)} %pad_add_fusion.key_ref, bf16[576,2304]{1,0:T(8,128)(2,1)} %weight_ref.1), custom_call_target="tpu_custom_call" | custom-call | tf_op jit(solution)/shard_map/pallas_call | solution.py:77
  64.0 0.0 reduce-scatter.3.cloned.1.call-update
  64.1 0.0 all-gather.7.cloned.1.call-start
  64.1 0.0 copy-done.2
  64.1 0.1 copy.81
  64.2 0.1 eq.68
  64.3 0.1 fusion.31
  64.4 0.1 reduce_window_sum.11
  64.5 0.2 select_reduce_fusion
  64.7 0.1 reduce_sum.40
  64.8 0.1 copy.82
  64.9 0.1 compare_reduce_fusion
  65.0 21.3 %reduce-scatter.3.cloned.1.call-done = bf16[32,2304]{1,0:T(8,128)(2,1)} async-done(((bf16[128,2304]{1,0:T(8,128)(2,1)}), bf16[32,2304]{1,0:T(8,128)(2,1)}) %reduce-scatter.3.cloned.1.call-update) | async-done | bytes 147472 | tf_op jit(solution)/shard_map/reduce_scatter | solution.py:156
  86.3 1.2 fusion.17
  87.4 0.0 copy-done.1
  87.4 0.4 convolution_convert_fusion.1
  87.8 13.9 %all_to_all.41 = bf16[8,9,2304]{2,1,0:T(8,128)(2,1)S(1)} all-to-all(bf16[8,9,2304]{2,1,0:T(8,128)(2,1)S(1)} %convolution_convert_fusion.1), channel_id=1, replica_groups=mesh['seq'=8,'head'=4] {'seq'}, dimensions={0} | all-to-all | bytes 663552 | tf_op jit(solution)/shard_map/all_to_all | solution.py:193
  101.7 0.8 copy.85
  102.6 0.0 all-gather.7.cloned.1.call-update
  102.6 0.0 reduce-scatter.5.cloned.1.call-start
  102.6 29.6 %all-gather.7.cloned.1.call-done = bf16[36,8,2304]{2,1,0:T(8,128)(2,1)} async-done(((bf16[9,8,2304]{2,1,0:T(8,128)(2,1)}), bf16[36,8,2304]{2,1,0:T(8,128)(2,1)}) %all-gather.7.cloned.1.call-update) | async-done | bytes 1327120 | tf_op jit(solution)/shard_map/all_gather | solution.py:194
  132.2 0.0 copy-start.4
  132.2 0.0 copy-start.5
  132.2 3.7 %fusion.9 = f32[4,9,8,720]{3,2,1,0:T(8,128)S(1)} fusion(bf16[4,9,8,2304]{3,2,1,0:T(8,128)(2,1)} %bitcast.95, bf16[2304,720]{0,1:T(8,128)(2,1)} %param.20), kind=kOutput, calls=%fused_computation.13 | convolution fusion | flops 955514880 | bytes 5474304 | tf_op jit(solution)/shard_map/hcsd,df->hcsf/dot_general | solution.py:195
  136.0 0.0 copy-done.4
  136.0 0.0 copy-done.5
  136.0 1.3 fusion.14
  137.3 0.0 copy-done
  137.3 0.0 copy-start.6
  137.4 2.3 %convolution_convert_fusion = bf16[4,9,8,2304]{3,2,1,0:T(8,128)(2,1)} fusion(bf16[4,9,8,720]{3,2,1,0:T(8,128)(2,1)S(1)} %fusion.14, bf16[2304,720]{0,1:T(8,128)(2,1)S(1)} %copy-done), kind=kOutput, calls=%fused_computation | convolution fusion | flops 956178432 | bytes 5059584 | tf_op jit(solution)/shard_map/hcsf,df->hcsd/dot_general | solution.py:202
  139.6 0.0 reduce-scatter.5.cloned.1.call-update
  139.7 0.1 copy.83
  139.7 1.7 slice_bitcast_fusion
  141.5 0.0 copy-done.6
  141.5 0.2 fusion.25
  141.7 28.8 %reduce-scatter.5.cloned.1.call-done = bf16[1,9,8,2304]{3,2,1,0:T(8,128)(2,1)} async-done(((bf16[4,9,8,2304]{3,2,1,0:T(8,128)(2,1)}), bf16[1,9,8,2304]{3,2,1,0:T(8,128)(2,1)}) %reduce-scatter.5.cloned.1.call-update) | async-done | bytes 331792 | tf_op jit(solution)/shard_map/reduce_scatter | solution.py:206
  170.4 1.9 copy.86
  172.3 4.2 %all-to-all-start.3 = ((bf16[8,9,2304]{2,1,0:T(8,128)(2,1)}), bf16[8,9,2304]{2,1,0:T(8,128)(2,1)}, u32[]{:S(2)}, u32[]{:S(2)}) async-start(bf16[8,9,2304]{2,1,0:T(8,128)(2,1)} %copy.86), calls=%async_computation.5 | async-start | bytes 1179648 | tf_op jit(solution)/shard_map/all_to_all | solution.py:208
  176.5 10.4 %all-to-all-done.3 = bf16[8,9,2304]{2,1,0:T(8,128)(2,1)} async-done(((bf16[8,9,2304]{2,1,0:T(8,128)(2,1)}), bf16[8,9,2304]{2,1,0:T(8,128)(2,1)}, u32[]{:S(2)}, u32[]{:S(2)}) %all-to-all-start.3) | async-done | bytes 331808 | tf_op jit(solution)/shard_map/all_to_all | solution.py:208
  187.0 1.4 fusion.4
  188.4 2.1 %fusion.5 = bf16[32,2304]{1,0:T(8,128)(2,1)} fusion(f32[32,2304]{1,0:T(8,128)S(1)} %fusion.4, bf16[8,9,2304]{2,1,0:T(8,128)(2,1)} %all-to-all-done.3, bf16[32,2304]{1,0:T(8,128)(2,1)S(1)} %get-tuple-element.4, f32[32]{0:T(128)S(1)} %get-tuple-element.9, s32[32]{0:T(128)S(1)} %get-tuple-element.7, s32[8,9]{1,0:T(8,128)S(1)} %copy.83), kind=kOutput, calls=%fused_computation.9 | convolution fusion | flops 11061504 | bytes 922144 | tf_op jit(solution)/shard_map/tec,ercd->trd/dot_general | solution.py:216
  (10 shorter events, 0.1 us)
Async XLA Ops:
  7.2 130.2 %copy-start = (bf16[2304,720]{0,1:T(8,128)(2,1)S(1)}, bf16[2304,720]{0,1:T(8,128)(2,1)}, u32[]{:S(2)}) copy-start(bf16[2304,720]{0,1:T(8,128)(2,1)} %param.22) | copy-start | bytes 9953284
  7.2 27.2 %copy-start.3 = (s32[128]{0:T(128)S(1)}, s32[128]{0:T(128)}, u32[]{:S(2)}) copy-start(s32[128]{0:T(128)} %param.18) | copy-start | bytes 1540
  7.2 50.6 %all-gather.5.cloned.1.call-start = ((), (), s32[]{:S(2)}) async-start(), calls=%async_computation.6 | async-start | bytes 2654208 | tf_op jit(solution)/shard_map/all_gather | solution.py:130
  31.0 13.5 %all-to-all-start = ((bf16[32,4,576]{2,0,1:T(8,128)(2,1)}), bf16[32,4,576]{2,0,1:T(8,128)(2,1)S(1)}, u32[]{:S(2)}, u32[]{:S(2)}) async-start(bf16[32,4,576]{2,0,1:T(8,128)(2,1)} %copy.76), calls=%async_computation | async-start | bytes 327680 | tf_op jit(solution)/shard_map/all_to_all | solution.py:121
  34.3 51.9 %reduce-scatter.3.cloned.1.call-start = ((), (), s32[]{:S(2)}) async-start(), calls=%async_computation.7 | async-start | bytes 737280 | tf_op jit(solution)/shard_map/reduce_scatter | solution.py:156
  57.8 6.3 %copy-start.2 = (s32[32,2]{0,1:T(2,128)S(1)}, s32[32,2]{0,1:T(2,128)}, u32[]{:S(2)}) copy-start(s32[32,2]{0,1:T(2,128)} %param.19) | copy-start | bytes 772
  57.8 29.6 %copy-start.1 = (f32[2304]{0:T(1024)S(1)}, f32[2304]{0:T(1024)}, u32[]{:S(2)}) copy-start(f32[2304]{0:T(1024)} %param.16) | copy-start | bytes 27652
  64.1 68.2 %all-gather.7.cloned.1.call-start = ((), (), s32[]{:S(2)}) async-start(), calls=%async_computation.9 | async-start | bytes 1658880 | tf_op jit(solution)/shard_map/all_gather | solution.py:194
  102.6 67.9 %reduce-scatter.5.cloned.1.call-start = ((), (), s32[]{:S(2)}) async-start(), calls=%async_computation.8 | async-start | bytes 1658880 | tf_op jit(solution)/shard_map/reduce_scatter | solution.py:206
  132.2 3.7 %copy-start.4 = (bf16[2304,720]{0,1:T(8,128)(2,1)S(1)}, bf16[2304,720]{0,1:T(8,128)(2,1)}, u32[]{:S(2)}) copy-start(bf16[2304,720]{0,1:T(8,128)(2,1)} %param.21) | copy-start | bytes 9953284
  132.2 3.7 %copy-start.5 = (bf16[36,8,2304]{2,1,0:T(8,128)(2,1)S(1)}, bf16[36,8,2304]{2,1,0:T(8,128)(2,1)}, u32[]{:S(2)}) copy-start(bf16[36,8,2304]{2,1,0:T(8,128)(2,1)} %all-gather.7.cloned.1.call-done) | copy-start | bytes 3981316
  137.3 4.1 %copy-start.6 = (bf16[2304,8]{0,1:T(8,128)(2,1)S(1)}, bf16[2304,8]{0,1:T(8,128)(2,1)}, u32[]{:S(2)}) copy-start(bf16[2304,8]{0,1:T(8,128)(2,1)} %param.17) | copy-start | bytes 110596
  172.3 14.7 %all-to-all-start.3 = ((bf16[8,9,2304]{2,1,0:T(8,128)(2,1)}), bf16[8,9,2304]{2,1,0:T(8,128)(2,1)}, u32[]{:S(2)}, u32[]{:S(2)}) async-start(bf16[8,9,2304]{2,1,0:T(8,128)(2,1)} %copy.86), calls=%async_computation.5 | async-start | bytes 1179648 | tf_op jit(solution)/shard_map/all_to_all | solution.py:208
Sparse Core Ops, SparseCore 0:
  29.3 28.4 all-gather.4
  64.2 22.0 reduce-scatter.2
  102.7 29.4 all-gather.6
  139.8 30.6 reduce-scatter.4
